TPU v7x, 32 devices: a whole 2x2x4 slice. The times are simulated.
32 devices in a mesh: dp: 4 (over y, x), expert: 8 (over z, core).
Axes of the slice: x: 2, y: 2, z: 4, core: 2. Of those that a mesh axis runs over, the one named last changes fastest.
Arguments:
- tokens: bfloat16 [4096, 7168], P(('dp', 'expert')), may hold values from -6 to 6
- steering: float32 [7168], replicated, may hold values from -6 to 6
- norm_gain: float32 [7168], replicated, may hold values from 0.1 to 1.9
- route_ids: int32 [4096, 8], P(('dp', 'expert')), may hold values from 0 to 255, as said below
- route_gates: int32 [4096, 8], P(('dp', 'expert')), may hold values from 1 to 65535
- gate_weight: bfloat16 [7168, 8192], P(None, 'expert'), may hold values from -0.0625 to 0.0625
- up_weight: bfloat16 [7168, 8192], P(None, 'expert'), may hold values from -0.0625 to 0.0625
- down_weight: bfloat16 [8192, 7168], P('expert'), may hold values from -0.125 to 0.125
- out_grad: bfloat16 [4096, 7168], P(('dp', 'expert')), may hold values from -6 to 6
Outputs:
- layer_out: bfloat16 [4096, 7168], P(('dp', 'expert'))
- in_grad: bfloat16 [4096, 7168], P(('dp', 'expert'))
- steer_grad: float32 [7168], replicated
Inputs may be any that keep to these rules, and one draw needn't show every extreme that they name: `route_ids`: each row names 8 different experts. Among the 128 rows of one device no expert below 4 is named more than 8 times. One expert below 4, the same for every device, is named exactly 8 times by every device's rows, and on some devices every expert below 4 is named exactly 8 times.
All inputs are finite; a program needn't handle non-finite values.
Results may differ from a plain program's by a relative error of at most 0.0021.
Values may be sent and summed in bfloat16 or wider, within the bound.
No kernel may reach another device: no remote copies, remote signals or barrier semaphores. Data moves between devices by JAX's collectives and lax.ppermute only.
A program may use at most 128 MiB of HBM per device.

v0:
```python
import jax
import jax.numpy as jnp
from jax import lax
from jax.sharding import PartitionSpec as P

EXP_FLIGHT = 4
CAP = 8


EPSILON = 1e-06
GATE_UNIT = 1.0 / 65536.0


def slot_tables(route_ids, route_gates, flight, capacity):
    count_rows = route_ids.shape[0]
    expert_range = jnp.arange(flight, dtype=jnp.int32)
    hit_mask = route_ids[:, :, None] == expert_range[None, None, :]
    member = jnp.any(hit_mask, axis=1)
    scaled = route_gates.astype(jnp.float32) * GATE_UNIT
    weights = jnp.sum(jnp.where(hit_mask, scaled[:, :, None], 0.0), axis=1)
    position = jnp.cumsum(member.astype(jnp.int32), axis=0) - 1
    slot_of = jnp.where(member, position, capacity)
    slot_range = jnp.arange(capacity, dtype=jnp.int32)
    matches = slot_of[:, :, None] == slot_range[None, None, :]
    row_range = jnp.arange(count_rows, dtype=jnp.int32)
    slot_table = jnp.sum(jnp.where(matches, row_range[:, None, None], 0), axis=0)
    filled = jnp.any(matches, axis=0)
    combine = jnp.where(matches, weights[:, :, None], 0.0).reshape(count_rows, flight * capacity)
    return (slot_table, filled, combine)


def dispatch_rows(values, slot_table, filled):
    picked = values[slot_table]
    return jnp.where(filled[:, :, None], picked, jnp.zeros((), values.dtype))


def normalize(tokens, steering, norm_gain):
    residual = tokens.astype(jnp.float32) + steering
    inverse = lax.rsqrt(jnp.mean(residual * residual, axis=-1, keepdims=True) + EPSILON)
    normed = (residual * inverse * norm_gain).astype(jnp.bfloat16)
    return (residual, inverse, normed)


def norm_backward(residual, inverse, norm_gain, back_normed, out_grad):
    scaled = back_normed * norm_gain
    inner_mean = jnp.mean(scaled * residual, axis=-1, keepdims=True)
    cubed = inverse * inverse * inverse
    return out_grad.astype(jnp.float32) + inverse * scaled - residual * cubed * inner_mean


def share_forward(token_rows, gate_cols, up_cols, down_rows):
    gate_pre = jnp.dot(token_rows, gate_cols, preferred_element_type=jnp.float32)
    up_pre = jnp.dot(token_rows, up_cols, preferred_element_type=jnp.float32)
    hidden = (jax.nn.silu(gate_pre) * up_pre).astype(jnp.bfloat16)
    forward = jnp.dot(hidden, down_rows, preferred_element_type=jnp.float32).astype(jnp.bfloat16)
    return (forward, gate_pre, up_pre)


def share_backward(grad_rows, gate_pre, up_pre, gate_cols, up_cols, down_rows):
    contract = (((1,), (1,)), ((), ()))
    back_hidden = lax.dot_general(
        grad_rows, down_rows, contract, preferred_element_type=jnp.float32
    )
    sigmoid = jax.nn.sigmoid(gate_pre)
    back_up = (back_hidden * gate_pre * sigmoid).astype(jnp.bfloat16)
    back_gate = (back_hidden * up_pre * sigmoid * (1.0 + gate_pre * (1.0 - sigmoid))).astype(
        jnp.bfloat16
    )
    backward = lax.dot_general(back_gate, gate_cols, contract, preferred_element_type=jnp.float32)
    backward = backward + lax.dot_general(
        back_up, up_cols, contract, preferred_element_type=jnp.float32
    )
    return backward.astype(jnp.bfloat16)


def apply_combine(combine, partial_sums):
    return jnp.dot(combine, partial_sums, precision=lax.Precision.HIGHEST)


def shards(
    tokens,
    steering,
    norm_gain,
    route_ids,
    route_gates,
    gate_weight,
    up_weight,
    down_weight,
    out_grad,
):
    expert_count = lax.axis_size("expert")
    flight = EXP_FLIGHT
    group_size = expert_count // flight
    capacity = CAP
    feature_count = tokens.shape[1]
    residual, inverse, normed = normalize(tokens, steering, norm_gain)
    slot_table, filled, combine = slot_tables(route_ids, route_gates, flight, capacity)
    packed = jnp.stack(
        [dispatch_rows(normed, slot_table, filled), dispatch_rows(out_grad, slot_table, filled)],
        axis=1,
    )
    sending = jnp.repeat(packed, group_size, axis=0)
    arrived = lax.all_to_all(sending, "expert", split_axis=0, concat_axis=0, tiled=True)
    local_rows = arrived[:, 0].reshape(expert_count * capacity, feature_count)
    local_grads = arrived[:, 1].reshape(expert_count * capacity, feature_count)
    forward, gate_pre, up_pre = share_forward(local_rows, gate_weight, up_weight, down_weight)
    came_out = lax.all_to_all(
        forward.reshape(expert_count, capacity, feature_count),
        "expert",
        split_axis=0,
        concat_axis=0,
        tiled=True,
    )
    backward = share_backward(local_grads, gate_pre, up_pre, gate_weight, up_weight, down_weight)
    came_grad = lax.all_to_all(
        backward.reshape(expert_count, capacity, feature_count),
        "expert",
        split_axis=0,
        concat_axis=0,
        tiled=True,
    )
    out_sums = (
        came_out.reshape(flight, group_size, capacity, feature_count)
        .astype(jnp.float32)
        .sum(axis=1)
    )
    grad_sums = (
        came_grad.reshape(flight, group_size, capacity, feature_count)
        .astype(jnp.float32)
        .sum(axis=1)
    )
    mixture = apply_combine(combine, out_sums.reshape(flight * capacity, feature_count))
    back_normed = apply_combine(combine, grad_sums.reshape(flight * capacity, feature_count))
    layer_out = (residual + mixture).astype(jnp.bfloat16)
    total_grad = norm_backward(residual, inverse, norm_gain, back_normed, out_grad)
    steer_grad = lax.psum(jnp.sum(total_grad, axis=0), ("dp", "expert"))
    return (layer_out, total_grad.astype(jnp.bfloat16), steer_grad)


def solution(mesh):
    in_specs = (
        P(("dp", "expert"), None),
        P(),
        P(),
        P(("dp", "expert"), None),
        P(("dp", "expert"), None),
        P(None, "expert"),
        P(None, "expert"),
        P("expert", None),
        P(("dp", "expert"), None),
    )
    out_specs = (P(("dp", "expert"), None), P(("dp", "expert"), None), P())
    return jax.shard_map(shards, mesh=mesh, in_specs=in_specs, out_specs=out_specs, check_vma=False)
```

profile of v0, /device:TPU:0, one launch (start us, length us, event | category | flops | bytes accessed | tf_op | source)
XLA Modules:
  0.0 191.6 jit_solution(9282980750656883561)
XLA Ops:
  0.6 0.7 fusion.16
  1.3 0.1 copy.20
  1.5 0.2 reduce_window_sum.11
  1.6 0.1 copy.21
  1.7 0.2 select_reduce_fusion
  1.9 0.2 fusion.15
  2.0 0.1 reshape.94
  2.1 2.1 %multiply_reduce_fusion.1 = f32[128]{0:T(128)S(1)} fusion(bf16[128,7168]{1,0:T(8,128)(2,1)} %param.9, f32[7168]{0:T(1024)} %param.10), kind=kLoop, calls=%fused_computation.15 | loop fusion | flops 3669888 | bytes 1864192 | tf_op jit(solution)/shard_map/reduce_sum | solution.py:39
  4.2 2.1 %multiply_convert_fusion = bf16[128,7168]{1,0:T(8,128)(2,1)S(1)} fusion(bf16[128,7168]{1,0:T(8,128)(2,1)} %param.9, f32[7168]{0:T(1024)} %param.11, f32[128]{0:T(128)S(1)} %get-tuple-element.6, f32[7168]{0:T(1024)} %param.10), kind=kLoop, calls=%fused_computation.14 | loop fusion | flops 4587520 | bytes 3727872 | tf_op jit(solution)/shard_map/convert_element_type | solution.py:40
  6.3 0.8 gather_fusion
  7.1 3.0 %gather_fusion.1 = bf16[32,7168]{1,0:T(8,128)(2,1)S(1)} fusion(bf16[128,7168]{1,0:T(8,128)(2,1)} %param.17, s32[1024]{0:T(1024)S(1)} %pad_clamp_fusion), kind=kCustom, calls=%fused_computation.1 | custom fusion | bytes 917632 | tf_op jit(solution)/shard_map/gather | solution.py:33
  10.1 0.1 bitcast_select_fusion.1
  10.3 0.1 pad_maximum_fusion
  10.4 0.1 copy.22
  10.4 0.2 broadcast_in_dim.84
  10.6 49.6 %all_to_all.15 = bf16[8,2,8,7168]{3,2,1,0:T(8,128)(2,1)S(1)} all-to-all(bf16[8,2,8,7168]{3,2,1,0:T(8,128)(2,1)S(1)} %bitcast.44), channel_id=1, replica_groups=mesh['dp'=4,'expert'=8] {'expert'}, dimensions={0} | all-to-all | bytes 3670016 | tf_op jit(solution)/shard_map/all_to_all | solution.py:103
  60.2 7.9 %fusion.8 = f32[64,1024]{1,0:T(8,128)S(1)} fusion(bf16[7168,1024]{1,0:T(8,128)(2,1)} %param.14, bf16[8,2,8,7168]{3,2,1,0:T(8,128)(2,1)S(1)} %all_to_all.15), kind=kOutput, calls=%fused_computation.24 | convolution fusion | flops 939524096 | bytes 15859712 | tf_op jit(solution)/shard_map/dot_general | solution.py:52
  68.0 9.7 %fusion.6 = f32[64,1024]{1,0:T(8,128)S(1)} fusion(bf16[1024,7168]{1,0:T(8,128)(2,1)} %param.16, bf16[8,2,8,7168]{3,2,1,0:T(8,128)(2,1)S(1)} %all_to_all.15), kind=kOutput, calls=%fused_computation.20 | convolution fusion | flops 939524096 | bytes 15859712 | tf_op jit(solution)/shard_map/dot_general | solution.py:61
  77.8 7.9 %fusion.7 = f32[64,1024]{1,0:T(8,128)S(1)} fusion(bf16[7168,1024]{1,0:T(8,128)(2,1)} %param.15, bf16[8,2,8,7168]{3,2,1,0:T(8,128)(2,1)S(1)} %all_to_all.15), kind=kOutput, calls=%fused_computation.23 | convolution fusion | flops 939524096 | bytes 15859712 | tf_op jit(solution)/shard_map/dot_general | solution.py:53
  85.6 9.7 %fusion.9 = f32[64,7168]{1,0:T(8,128)S(1)} fusion(bf16[7168,1024]{1,0:T(8,128)(2,1)} %param.14, f32[64,1024]{1,0:T(8,128)S(1)} %fusion.8, f32[64,1024]{1,0:T(8,128)S(1)} %fusion.6, f32[64,1024]{1,0:T(8,128)S(1)} %fusion.7), kind=kOutput, calls=%fused_computation.31 | convolution fusion | flops 940179456 | bytes 17301504 | tf_op jit(solution)/shard_map/dot_general | solution.py:69
  95.4 10.9 %fusion.5 = bf16[8,8,7168]{2,1,0:T(8,128)(2,1)} fusion(f32[64,7168]{1,0:T(8,128)S(1)} %fusion.9, bf16[7168,1024]{1,0:T(8,128)(2,1)} %param.15, f32[64,1024]{1,0:T(8,128)S(1)} %fusion.6, f32[64,1024]{1,0:T(8,128)S(1)} %fusion.8), kind=kOutput, calls=%fused_computation.11 | convolution fusion | flops 940834816 | bytes 17956864 | tf_op jit(solution)/shard_map/dot_general | solution.py:70
  106.3 3.6 %all-to-all-start.2 = ((bf16[8,8,7168]{2,1,0:T(8,128)(2,1)}), bf16[8,8,7168]{2,1,0:T(8,128)(2,1)S(1)}, u32[]{:S(2)}, u32[]{:S(2)}) async-start(bf16[8,8,7168]{2,1,0:T(8,128)(2,1)} %fusion.5), calls=%async_computation.2 | async-start | bytes 1835008 | tf_op jit(solution)/shard_map/all_to_all | solution.py:115
  109.8 0.0 copy-start.6
  109.8 0.0 copy-start.5
  109.9 8.8 %fusion.4 = bf16[8,8,7168]{2,1,0:T(8,128)(2,1)} fusion(bf16[1024,7168]{1,0:T(8,128)(2,1)} %param.16, f32[64,1024]{1,0:T(8,128)S(1)} %fusion.7, f32[64,1024]{1,0:T(8,128)S(1)} %fusion.8), kind=kOutput, calls=%fused_computation.10 | convolution fusion | flops 940376064 | bytes 16121856 | tf_op jit(solution)/shard_map/dot_general | solution.py:55
  118.6 0.0 copy-start
  118.6 0.0 copy-start.3
  118.6 0.0 copy-start.4
  118.6 14.9 %all-to-all-done.2 = bf16[8,8,7168]{2,1,0:T(8,128)(2,1)S(1)} async-done(((bf16[8,8,7168]{2,1,0:T(8,128)(2,1)}), bf16[8,8,7168]{2,1,0:T(8,128)(2,1)S(1)}, u32[]{:S(2)}, u32[]{:S(2)}) %all-to-all-start.2) | async-done | bytes 917536 | tf_op jit(solution)/shard_map/all_to_all | solution.py:115
  133.5 0.0 copy-start.2
  133.5 0.9 copy-done.2
  134.4 3.6 %all-to-all-start.1 = ((bf16[8,8,7168]{2,1,0:T(8,128)(2,1)}), bf16[8,8,7168]{2,1,0:T(8,128)(2,1)S(1)}, u32[]{:S(2)}, u32[]{:S(2)}) async-start(bf16[8,8,7168]{2,1,0:T(8,128)(2,1)} %fusion.4), calls=%async_computation.1 | async-start | bytes 1835008 | tf_op jit(solution)/shard_map/all_to_all | solution.py:107
  138.0 0.0 copy-done.6
  138.0 0.0 copy-done.5
  138.1 1.4 convert_reduce_fusion
  139.5 0.0 copy-done
  139.5 0.0 copy-done.3
  139.5 0.0 copy-done.4
  139.5 0.0 copy-start.1
  139.5 3.6 %multiply_reduce_fusion = (f32[128]{0:T(128)S(1)}, f32[128,7168]{1,0:T(8,128)S(1)}) fusion(bf16[128,7168]{1,0:T(8,128)(2,1)S(1)} %copy-done, f32[7168]{0:T(1024)S(1)} %copy-done.3, f32[7168]{0:T(1024)S(1)} %copy-done.4, f32[4,8,7168]{2,1,0:T(8,128)S(1)} %convert_reduce_fusion, f32[128,4]{0,1:T(4,128)S(1)} %select_reduce_fusion.1, ...), kind=kOutput, calls=%fused_computation.13 | convolution fusion | flops 356917120 | bytes 6484480 | tf_op jit(solution)/shard_map/dot_general | solution.py:77
  143.2 0.0 copy-done.1
  143.2 2.6 %fusion.28 = (f32[7168]{0:T(1024)S(1)}, bf16[128,7168]{1,0:T(8,128)(2,1)}) fusion(f32[128]{0:T(128)S(1)} %broadcast_multiply_fusion, f32[128]{0:T(128)S(1)} %get-tuple-element.5, f32[7168]{0:T(1024)S(1)} %copy-done.3, bf16[128,7168]{1,0:T(8,128)(2,1)S(1)} %copy-done, f32[128,7168]{1,0:T(8,128)S(1)} %get-tuple-element.10, f32[128]{0:T(128)S(1)} %get-tuple-element.6, ...), kind=kLoop, calls=%fused_computation.61 | loop fusion | flops 9167872 | bytes 9233920 | tf_op jit(solution)/shard_map/reduce_sum | solution.py:136
  145.8 41.3 %psum.7 = f32[7168]{0:T(1024)} all-reduce(f32[7168]{0:T(1024)S(1)} %get-tuple-element.3), channel_id=1, replica_groups=mesh['dp'=4,'expert'=8] {'dp','expert'}, use_global_device_ids=true, to_apply=%region_10.11 | all-reduce | flops 7168 | bytes 57344 | tf_op jit(solution)/shard_map/psum | solution.py:136
  187.2 0.0 all-to-all-done.1
  187.2 0.1 convert_reduce_fusion.1
  187.3 4.4 %fusion.2 = bf16[128,7168]{1,0:T(8,128)(2,1)} fusion(f32[4,8,7168]{2,1,0:T(8,128)S(1)} %convert_reduce_fusion.1, bf16[128,7168]{1,0:T(8,128)(2,1)S(1)} %copy-done, f32[7168]{0:T(1024)S(1)} %copy-done.3, f32[128,4]{0,1:T(4,128)S(1)} %select_reduce_fusion.1, s32[128,4]{0,1:T(4,128)S(1)} %add_select_fusion), kind=kOutput, calls=%fused_computation.6 | convolution fusion | flops 355999744 | bytes 4620288 | tf_op jit(solution)/shard_map/dot_general | solution.py:77
  (8 shorter events, 0.1 us)
Async XLA Ops:
  106.3 27.2 %all-to-all-start.2 = ((bf16[8,8,7168]{2,1,0:T(8,128)(2,1)}), bf16[8,8,7168]{2,1,0:T(8,128)(2,1)S(1)}, u32[]{:S(2)}, u32[]{:S(2)}) async-start(bf16[8,8,7168]{2,1,0:T(8,128)(2,1)} %fusion.5), calls=%async_computation.2 | async-start | bytes 1835008 | tf_op jit(solution)/shard_map/all_to_all | solution.py:115
  109.8 28.2 %copy-start.6 = (s32[128,8]{0,1:T(8,128)S(1)}, s32[128,8]{0,1:T(8,128)}, u32[]{:S(2)}) copy-start(s32[128,8]{0,1:T(8,128)} %param.13) | copy-start | bytes 12292
  109.8 28.2 %copy-start.5 = (s32[128,8]{0,1:T(8,128)S(1)}, s32[128,8]{0,1:T(8,128)}, u32[]{:S(2)}) copy-start(s32[128,8]{0,1:T(8,128)} %param.12) | copy-start | bytes 12292
  118.6 20.9 %copy-start = (bf16[128,7168]{1,0:T(8,128)(2,1)S(1)}, bf16[128,7168]{1,0:T(8,128)(2,1)}, u32[]{:S(2)}) copy-start(bf16[128,7168]{1,0:T(8,128)(2,1)} %param.9) | copy-start | bytes 5505028
  118.6 20.9 %copy-start.3 = (f32[7168]{0:T(1024)S(1)}, f32[7168]{0:T(1024)}, u32[]{:S(2)}) copy-start(f32[7168]{0:T(1024)} %param.10) | copy-start | bytes 86020
  118.6 20.9 %copy-start.4 = (f32[7168]{0:T(1024)S(1)}, f32[7168]{0:T(1024)}, u32[]{:S(2)}) copy-start(f32[7168]{0:T(1024)} %param.11) | copy-start | bytes 86020
  133.5 0.9 copy-start.2
  134.4 52.7 %all-to-all-start.1 = ((bf16[8,8,7168]{2,1,0:T(8,128)(2,1)}), bf16[8,8,7168]{2,1,0:T(8,128)(2,1)S(1)}, u32[]{:S(2)}, u32[]{:S(2)}) async-start(bf16[8,8,7168]{2,1,0:T(8,128)(2,1)} %fusion.4), calls=%async_computation.1 | async-start | bytes 1835008 | tf_op jit(solution)/shard_map/all_to_all | solution.py:107
  139.5 3.7 %copy-start.1 = (bf16[128,7168]{1,0:T(8,128)(2,1)S(1)}, bf16[128,7168]{1,0:T(8,128)(2,1)}, u32[]{:S(2)}) copy-start(bf16[128,7168]{1,0:T(8,128)(2,1)} %param.17) | copy-start | bytes 5505028
where the time goes:
time: 192 us
  blocking collectives  90.9 us (47%)
  matrix products  62.8 us (33%)
  waiting for transfers between devices  14.9 us (8%)
  other arithmetic  9.82 us (5%)
  starting transfers between devices  7.11 us (4%)
  local copies, waits for them, and re-layouts  5.27 us (3%)
    all_to_all x1, blocking collectives, shards(): lax.all_to_all(sending, 'expert', split_axis=0, concat_axis=0, tiled=True)  49.6 us
    psum x1, blocking collectives, shards(): steer_grad = lax.psum(jnp.sum(total_grad, axis=0), ('dp', 'expert'))  41.3 us
    all_to_all x1, waiting for transfers between devices, shards(): lax.all_to_all(backward.reshape(expert_count, capacity, feature_count), '...  14.9 us
    dot_general x1, matrix products, share_backward(): lax.dot_general(back_up, up_cols, contract, preferred_element_type=jnp.fl...  10.9 us
    dot_general x1, matrix products, share_backward(): lax.dot_general(back_gate, gate_cols, contract, preferred_element_type=jn...  9.73 us
    dot_general x1, matrix products, share_backward(): lax.dot_general(grad_rows, down_rows, contract, preferred_element_type=jn...  9.72 us
    dot_general x1, matrix products, share_forward(): jnp.dot(hidden, down_rows, preferred_element_type=jnp.float32)  8.77 us
    dot_general x2, matrix products, apply_combine(): return jnp.dot(combine, partial_sums, precision=lax.Precision.HIGHEST)  8 us
  transfers between devices with their start and end apart: 2, of which 1 were waited for; matrix products, arithmetic and copies ran while one was open for 9% of the time, Pallas kernels for 0%

commit v1 on v0

--- a/solution.py
+++ b/solution.py
@@ -2,6 +2,8 @@
 import jax.numpy as jnp
 from jax import lax
 from jax.sharding import PartitionSpec as P
+from jax.experimental import pallas as pl
+from jax.experimental.pallas import tpu as pltpu
 
 EXP_FLIGHT = 4
 CAP = 8
@@ -71,6 +73,60 @@
         back_up, up_cols, contract, preferred_element_type=jnp.float32
     )
     return backward.astype(jnp.bfloat16)
+
+
+def _expert_kernel(x_ref, y_ref, g_ref, u_ref, d_ref, out_ref, back_ref, acc_o, acc_b):
+    j = pl.program_id(1)
+    @pl.when(j == 0)
+    def _():
+        acc_o[...] = jnp.zeros_like(acc_o)
+        acc_b[...] = jnp.zeros_like(acc_b)
+    x = x_ref[...]
+    y = y_ref[...]
+    gw = g_ref[...]
+    uw = u_ref[...]
+    dw = d_ref[...]
+    nt = (((1,), (1,)), ((), ()))
+    g = jnp.dot(x, gw, preferred_element_type=jnp.float32)
+    u = jnp.dot(x, uw, preferred_element_type=jnp.float32)
+    sig = jax.nn.sigmoid(g)
+    hidden = (g * sig * u).astype(jnp.bfloat16)
+    bh = lax.dot_general(y, dw, nt, preferred_element_type=jnp.float32)
+    back_up = (bh * g * sig).astype(jnp.bfloat16)
+    back_gate = (bh * u * sig * (1.0 + g * (1.0 - sig))).astype(jnp.bfloat16)
+    acc_o[...] += jnp.dot(hidden, dw, preferred_element_type=jnp.float32)
+    acc_b[...] += (lax.dot_general(back_gate, gw, nt, preferred_element_type=jnp.float32)
+                   + lax.dot_general(back_up, uw, nt, preferred_element_type=jnp.float32))
+    @pl.when(j == pl.num_programs(1) - 1)
+    def _():
+        out_ref[...] = acc_o[...].astype(out_ref.dtype)
+        back_ref[...] = acc_b[...].astype(back_ref.dtype)
+
+def expert_share(x, y, gw, uw, dw):
+    rows, feat = x.shape
+    hid = gw.shape[1]
+    rb = min(rows, 128)
+    hb = min(hid, 256)
+    return pl.pallas_call(
+        _expert_kernel,
+        grid=(rows // rb, hid // hb),
+        in_specs=[
+            pl.BlockSpec((rb, feat), lambda i, j: (i, 0)),
+            pl.BlockSpec((rb, feat), lambda i, j: (i, 0)),
+            pl.BlockSpec((feat, hb), lambda i, j: (0, j)),
+            pl.BlockSpec((feat, hb), lambda i, j: (0, j)),
+            pl.BlockSpec((hb, feat), lambda i, j: (j, 0)),
+        ],
+        out_specs=[
+            pl.BlockSpec((rb, feat), lambda i, j: (i, 0)),
+            pl.BlockSpec((rb, feat), lambda i, j: (i, 0)),
+        ],
+        out_shape=[jax.ShapeDtypeStruct((rows, feat), jnp.bfloat16)] * 2,
+        scratch_shapes=[pltpu.VMEM((rb, feat), jnp.float32)] * 2,
+        compiler_params=pltpu.CompilerParams(
+            dimension_semantics=("arbitrary", "arbitrary"), vmem_limit_bytes=56 * 1024 * 1024
+        ),
+    )(x, y, gw, uw, dw)
 
 
 def apply_combine(combine, partial_sums):
@@ -103,7 +159,7 @@
     arrived = lax.all_to_all(sending, "expert", split_axis=0, concat_axis=0, tiled=True)
     local_rows = arrived[:, 0].reshape(expert_count * capacity, feature_count)
     local_grads = arrived[:, 1].reshape(expert_count * capacity, feature_count)
-    forward, gate_pre, up_pre = share_forward(local_rows, gate_weight, up_weight, down_weight)
+    forward, backward = expert_share(local_rows, local_grads, gate_weight, up_weight, down_weight)
     came_out = lax.all_to_all(
         forward.reshape(expert_count, capacity, feature_count),
         "expert",
@@ -111,7 +167,6 @@
         concat_axis=0,
         tiled=True,
     )
-    backward = share_backward(local_grads, gate_pre, up_pre, gate_weight, up_weight, down_weight)
     came_grad = lax.all_to_all(
         backward.reshape(expert_count, capacity, feature_count),
         "expert",

time: 192 us -> 179 us (0.932)
  matrix products: 62.8 us -> 7.99 us
  Pallas kernels: 0 us -> 32 us
  blocking collectives: 90.9 us -> 119 us
  waiting for transfers between devices: 14.9 us -> 0.01 us
  starting transfers between devices: 7.11 us -> 3.73 us
    dot_general x6 -> x0, matrix products: 54.8 us -> none  [the longest x1 10.9 us: share_backward(): lax.dot_general(back_up, up_cols, contract, preferred_element_type=jnp.fl...]
    pallas_call x0 -> x1, Pallas kernels: none -> 32 us  [expert_share(): pl.pallas_call(_expert_kernel, grid=(rows // rb, hid // hb), in_specs=[pl...]
    all_to_all x0 -> x1, blocking collectives: none -> 28.1 us  [shards(): lax.all_to_all(backward.reshape(expert_count, capacity, feature_count), '...]
    all_to_all x1 -> x0, waiting for transfers between devices: 14.9 us -> none  [shards(): lax.all_to_all(backward.reshape(expert_count, capacity, feature_count), '...]
    all_to_all x1 -> x0, starting transfers between devices: 3.55 us -> none  [shards(): lax.all_to_all(backward.reshape(expert_count, capacity, feature_count), '...]
  transfers between devices with their start and end apart: 2 -> 1, of which waited for: 1 -> 0; matrix products, arithmetic and copies ran while one was open for 9% -> 4% of each run, Pallas kernels for 0% -> 0%
where the time goes in v1:
time: 179 us
  blocking collectives  119 us (66%)
  Pallas kernels  32 us (18%)
  other arithmetic  9.82 us (5%)
  matrix products  7.99 us (4%)
  local copies, waits for them, and re-layouts  5.69 us (3%)
  starting transfers between devices  3.73 us (2%)
    all_to_all x1, blocking collectives, shards(): lax.all_to_all(sending, 'expert', split_axis=0, concat_axis=0, tiled=True)  49.6 us
    psum x1, blocking collectives, shards(): steer_grad = lax.psum(jnp.sum(total_grad, axis=0), ('dp', 'expert'))  41.1 us
    pallas_call x1, Pallas kernels, expert_share(): pl.pallas_call(_expert_kernel, grid=(rows // rb, hid // hb), in_specs=[pl...  32 us
    all_to_all x1, blocking collectives, shards(): lax.all_to_all(backward.reshape(expert_count, capacity, feature_count), '...  28.1 us
    dot_general x2, matrix products, apply_combine(): return jnp.dot(combine, partial_sums, precision=lax.Precision.HIGHEST)  7.99 us
    gather x2, local copies, waits for them, and re-layouts, dispatch_rows(): picked = values[slot_table]  3.82 us
    all_to_all x1, starting transfers between devices, shards(): lax.all_to_all(forward.reshape(expert_count, capacity, feature_count), 'e...  3.73 us
  transfers between devices with their start and end apart: 1, of which 0 were waited for; matrix products, arithmetic and copies ran while one was open for 4% of the time, Pallas kernels for 0%

profile of v1, /device:TPU:0, one launch (start us, length us, event | category | flops | bytes accessed | tf_op | source)
XLA Modules:
  0.0 178.9 jit_solution(13707995987383138351)
XLA Ops:
  0.6 0.7 fusion.6
  1.3 0.1 copy.23
  1.5 0.2 reduce_window_sum.11
  1.6 0.1 copy.24
  1.7 0.2 select_reduce_fusion
  1.9 0.2 fusion.5
  2.0 0.1 reshape.94
  2.1 2.1 %multiply_reduce_fusion.1 = f32[128]{0:T(128)S(1)} fusion(bf16[128,7168]{1,0:T(8,128)(2,1)} %param.9, f32[7168]{0:T(1024)} %param.10), kind=kLoop, calls=%fused_computation.10 | loop fusion | flops 3669888 | bytes 1864192 | tf_op jit(solution)/shard_map/reduce_sum | solution.py:41
  4.2 2.1 %multiply_convert_fusion = bf16[128,7168]{1,0:T(8,128)(2,1)S(1)} fusion(bf16[128,7168]{1,0:T(8,128)(2,1)} %param.9, f32[7168]{0:T(1024)} %param.11, f32[128]{0:T(128)S(1)} %get-tuple-element.12, f32[7168]{0:T(1024)} %param.10), kind=kLoop, calls=%fused_computation.9 | loop fusion | flops 4587520 | bytes 3727872 | tf_op jit(solution)/shard_map/convert_element_type | solution.py:42
  6.3 0.8 gather_fusion
  7.1 3.0 %gather_fusion.1 = bf16[32,7168]{1,0:T(8,128)(2,1)S(1)} fusion(bf16[128,7168]{1,0:T(8,128)(2,1)} %param.17, s32[1024]{0:T(1024)S(1)} %pad_clamp_fusion), kind=kCustom, calls=%fused_computation.1 | custom fusion | bytes 917632 | tf_op jit(solution)/shard_map/gather | solution.py:35
  10.1 0.1 bitcast_select_fusion.1
  10.3 0.1 pad_maximum_fusion
  10.4 0.1 copy.25
  10.4 0.2 broadcast_in_dim.84
  10.6 49.6 %all_to_all.15 = bf16[8,2,8,7168]{3,2,1,0:T(8,128)(2,1)S(1)} all-to-all(bf16[8,2,8,7168]{3,2,1,0:T(8,128)(2,1)S(1)} %bitcast.33), channel_id=1, replica_groups=mesh['dp'=4,'expert'=8] {'expert'}, dimensions={0} | all-to-all | bytes 3670016 | tf_op jit(solution)/shard_map/all_to_all | solution.py:159
  60.2 1.3 slice_bitcast_fusion
  61.5 32.0 %shard_map.112 = (bf16[64,7168]{1,0:T(8,128)(2,1)}, bf16[64,7168]{1,0:T(8,128)(2,1)}) custom-call(bf16[64,7168]{1,0:T(8,128)(2,1)} %get-tuple-element.10.x_ref, bf16[64,7168]{1,0:T(8,128)(2,1)} %get-tuple-element.9.y_ref, bf16[7168,1024]{1,0:T(8,128)(2,1)} %g_ref.1, bf16[7168,1024]{1,0:T(8,128)(2,1)} %u_ref.1, bf16[1024,7168]{1,0:T(8,128)(2,1)} %d_ref.1), custom_call_target="tpu_custom_call" | custom-call | tf_op jit(solution)/shard_map/pallas_call | solution.py:110
  93.6 0.0 copy-start.5
  93.6 0.0 copy-start.4
  93.6 0.0 copy-start
  93.6 0.0 copy-start.2
  93.6 0.0 copy-start.3
  93.6 28.1 %all_to_all.16 = bf16[8,8,7168]{2,1,0:T(8,128)(2,1)} all-to-all(bf16[8,8,7168]{2,1,0:T(8,128)(2,1)} %bitcast.35), channel_id=1, replica_groups=mesh['dp'=4,'expert'=8] {'expert'}, dimensions={0} | all-to-all | bytes 1835008 | tf_op jit(solution)/shard_map/all_to_all | solution.py:170
  121.7 3.7 %all-to-all-start.1 = ((bf16[8,8,7168]{2,1,0:T(8,128)(2,1)}), bf16[8,8,7168]{2,1,0:T(8,128)(2,1)S(1)}, u32[]{:S(2)}, u32[]{:S(2)}) async-start(bf16[8,8,7168]{2,1,0:T(8,128)(2,1)} %bitcast.34), calls=%async_computation.1 | async-start | bytes 1835008 | tf_op jit(solution)/shard_map/all_to_all | solution.py:163
  125.5 0.0 copy-done.5
  125.5 0.0 copy-done.4
  125.5 1.4 convert_reduce_fusion
  127.0 0.0 copy-done
  127.0 0.0 copy-done.2
  127.0 0.0 copy-done.3
  127.0 0.0 copy-start.1
  127.0 3.6 %multiply_reduce_fusion = (f32[128]{0:T(128)S(1)}, f32[128,7168]{1,0:T(8,128)S(1)}) fusion(bf16[128,7168]{1,0:T(8,128)(2,1)S(1)} %copy-done, f32[7168]{0:T(1024)S(1)} %copy-done.2, f32[7168]{0:T(1024)S(1)} %copy-done.3, f32[4,8,7168]{2,1,0:T(8,128)S(1)} %convert_reduce_fusion, f32[128,4]{0,1:T(4,128)S(1)} %select_reduce_fusion.1, ...), kind=kOutput, calls=%fused_computation.8 | convolution fusion | flops 356917120 | bytes 6484480 | tf_op jit(solution)/shard_map/dot_general | solution.py:133
  130.6 0.0 copy-done.1
  130.7 2.6 %fusion.15 = (f32[7168]{0:T(1024)S(1)}, bf16[128,7168]{1,0:T(8,128)(2,1)}) fusion(f32[128]{0:T(128)S(1)} %broadcast_multiply_fusion, f32[128]{0:T(128)S(1)} %get-tuple-element.11, f32[7168]{0:T(1024)S(1)} %copy-done.2, bf16[128,7168]{1,0:T(8,128)(2,1)S(1)} %copy-done, f32[128,7168]{1,0:T(8,128)S(1)} %get-tuple-element.16, f32[128]{0:T(128)S(1)} %get-tuple-element.12, ...), kind=kLoop, calls=%fused_computation.42 | loop fusion | flops 9167872 | bytes 9233920 | tf_op jit(solution)/shard_map/reduce_sum | solution.py:191
  133.3 41.1 %psum.7 = f32[7168]{0:T(1024)} all-reduce(f32[7168]{0:T(1024)S(1)} %get-tuple-element.7), channel_id=1, replica_groups=mesh['dp'=4,'expert'=8] {'dp','expert'}, use_global_device_ids=true, to_apply=%region_10.11 | all-reduce | flops 7168 | bytes 57344 | tf_op jit(solution)/shard_map/psum | solution.py:191
  174.4 0.0 all-to-all-done.1
  174.4 0.1 convert_reduce_fusion.1
  174.6 4.4 %fusion.2 = bf16[128,7168]{1,0:T(8,128)(2,1)} fusion(f32[4,8,7168]{2,1,0:T(8,128)S(1)} %convert_reduce_fusion.1, bf16[128,7168]{1,0:T(8,128)(2,1)S(1)} %copy-done, f32[7168]{0:T(1024)S(1)} %copy-done.2, f32[128,4]{0,1:T(4,128)S(1)} %select_reduce_fusion.1, s32[128,4]{0,1:T(4,128)S(1)} %add_select_fusion), kind=kOutput, calls=%fused_computation.6 | convolution fusion | flops 355999744 | bytes 4620288 | tf_op jit(solution)/shard_map/dot_general | solution.py:133
  (8 shorter events, 0.1 us)
Async XLA Ops:
  93.6 31.9 %copy-start.5 = (s32[128,8]{0,1:T(8,128)S(1)}, s32[128,8]{0,1:T(8,128)}, u32[]{:S(2)}) copy-start(s32[128,8]{0,1:T(8,128)} %param.13) | copy-start | bytes 12292
  93.6 31.9 %copy-start.4 = (s32[128,8]{0,1:T(8,128)S(1)}, s32[128,8]{0,1:T(8,128)}, u32[]{:S(2)}) copy-start(s32[128,8]{0,1:T(8,128)} %param.12) | copy-start | bytes 12292
  93.6 33.4 %copy-start = (bf16[128,7168]{1,0:T(8,128)(2,1)S(1)}, bf16[128,7168]{1,0:T(8,128)(2,1)}, u32[]{:S(2)}) copy-start(bf16[128,7168]{1,0:T(8,128)(2,1)} %param.9) | copy-start | bytes 5505028
  93.6 33.4 %copy-start.2 = (f32[7168]{0:T(1024)S(1)}, f32[7168]{0:T(1024)}, u32[]{:S(2)}) copy-start(f32[7168]{0:T(1024)} %param.10) | copy-start | bytes 86020
  93.6 33.4 %copy-start.3 = (f32[7168]{0:T(1024)S(1)}, f32[7168]{0:T(1024)}, u32[]{:S(2)}) copy-start(f32[7168]{0:T(1024)} %param.11) | copy-start | bytes 86020
  121.7 52.7 %all-to-all-start.1 = ((bf16[8,8,7168]{2,1,0:T(8,128)(2,1)}), bf16[8,8,7168]{2,1,0:T(8,128)(2,1)S(1)}, u32[]{:S(2)}, u32[]{:S(2)}) async-start(bf16[8,8,7168]{2,1,0:T(8,128)(2,1)} %bitcast.34), calls=%async_computation.1 | async-start | bytes 1835008 | tf_op jit(solution)/shard_map/all_to_all | solution.py:163
  127.0 3.7 %copy-start.1 = (bf16[128,7168]{1,0:T(8,128)(2,1)S(1)}, bf16[128,7168]{1,0:T(8,128)(2,1)}, u32[]{:S(2)}) copy-start(bf16[128,7168]{1,0:T(8,128)(2,1)} %param.17) | copy-start | bytes 5505028

commit v2 on v1

--- a/solution.py
+++ b/solution.py
@@ -133,6 +133,32 @@
     return jnp.dot(combine, partial_sums, precision=lax.Precision.HIGHEST)
 
 
+def group_perm(expert_count, group_size, shift):
+    return [
+        (d, (d // group_size) * group_size + (d % group_size + shift) % group_size)
+        for d in range(expert_count)
+    ]
+
+
+def group_gather(piece, member, expert_count, group_size):
+    got = [piece]
+    for shift in range(1, group_size):
+        got.append(lax.ppermute(piece, "expert", group_perm(expert_count, group_size, shift)))
+    stacked = jnp.stack(got)
+    order = (member - jnp.arange(group_size, dtype=jnp.int32)) % group_size
+    return jnp.take(stacked, order, axis=0)
+
+
+def group_reduce_scatter(pieces, member, expert_count, group_size, axis):
+    total = lax.dynamic_index_in_dim(pieces, member, axis, keepdims=False).astype(jnp.float32)
+    for shift in range(1, group_size):
+        target = (member + shift) % group_size
+        part = lax.dynamic_index_in_dim(pieces, target, axis, keepdims=False)
+        moved = lax.ppermute(part, "expert", group_perm(expert_count, group_size, shift))
+        total = total + moved.astype(jnp.float32)
+    return total
+
+
 def shards(
     tokens,
     steering,
@@ -149,43 +175,46 @@
     group_size = expert_count // flight
     capacity = CAP
     feature_count = tokens.shape[1]
+    piece = feature_count // group_size
+    member = lax.axis_index("expert") % group_size
     residual, inverse, normed = normalize(tokens, steering, norm_gain)
     slot_table, filled, combine = slot_tables(route_ids, route_gates, flight, capacity)
     packed = jnp.stack(
         [dispatch_rows(normed, slot_table, filled), dispatch_rows(out_grad, slot_table, filled)],
         axis=1,
     )
-    sending = jnp.repeat(packed, group_size, axis=0)
+    sending = (
+        packed.reshape(flight, 2, capacity, group_size, piece)
+        .transpose(0, 3, 1, 2, 4)
+        .reshape(expert_count, 2, capacity, piece)
+    )
     arrived = lax.all_to_all(sending, "expert", split_axis=0, concat_axis=0, tiled=True)
-    local_rows = arrived[:, 0].reshape(expert_count * capacity, feature_count)
-    local_grads = arrived[:, 1].reshape(expert_count * capacity, feature_count)
+    whole = group_gather(arrived, member, expert_count, group_size)
+    rows = whole.transpose(1, 2, 3, 0, 4).reshape(expert_count, 2, capacity, feature_count)
+    local_rows = rows[:, 0].reshape(expert_count * capacity, feature_count)
+    local_grads = rows[:, 1].reshape(expert_count * capacity, feature_count)
     forward, backward = expert_share(local_rows, local_grads, gate_weight, up_weight, down_weight)
-    came_out = lax.all_to_all(
-        forward.reshape(expert_count, capacity, feature_count),
-        "expert",
-        split_axis=0,
-        concat_axis=0,
-        tiled=True,
-    )
-    came_grad = lax.all_to_all(
-        backward.reshape(expert_count, capacity, feature_count),
-        "expert",
-        split_axis=0,
-        concat_axis=0,
-        tiled=True,
-    )
-    out_sums = (
-        came_out.reshape(flight, group_size, capacity, feature_count)
+    both = jnp.stack(
+        [
+            forward.reshape(expert_count, capacity, feature_count),
+            backward.reshape(expert_count, capacity, feature_count),
+        ],
+        axis=1,
+    ).reshape(expert_count, 2, capacity, group_size, piece)
+    summed = group_reduce_scatter(both, member, expert_count, group_size, 3)
+    came = lax.all_to_all(
+        summed.astype(jnp.bfloat16), "expert", split_axis=0, concat_axis=0, tiled=True
+    )
+    sums = (
+        came.reshape(flight, group_size, 2, capacity, piece)
+        .transpose(0, 2, 3, 1, 4)
+        .reshape(flight, 2, capacity * feature_count)
         .astype(jnp.float32)
-        .sum(axis=1)
-    )
-    grad_sums = (
-        came_grad.reshape(flight, group_size, capacity, feature_count)
-        .astype(jnp.float32)
-        .sum(axis=1)
-    )
-    mixture = apply_combine(combine, out_sums.reshape(flight * capacity, feature_count))
-    back_normed = apply_combine(combine, grad_sums.reshape(flight * capacity, feature_count))
+    )
+    out_sums = sums[:, 0].reshape(flight * capacity, feature_count)
+    grad_sums = sums[:, 1].reshape(flight * capacity, feature_count)
+    mixture = apply_combine(combine, out_sums)
+    back_normed = apply_combine(combine, grad_sums)
     layer_out = (residual + mixture).astype(jnp.bfloat16)
     total_grad = norm_backward(residual, inverse, norm_gain, back_normed, out_grad)
     steer_grad = lax.psum(jnp.sum(total_grad, axis=0), ("dp", "expert"))

time: 179 us -> 177 us (0.989)
  blocking collectives: 119 us -> 68.4 us
  waiting for transfers between devices: 0.01 us -> 28.3 us
  local copies, waits for them, and re-layouts: 5.69 us -> 22 us
  other arithmetic: 9.82 us -> 15.2 us
  matrix products: 7.99 us -> 5.15 us
    all_to_all x1 -> x0, blocking collectives: 28.1 us -> none  [shards(): lax.all_to_all(backward.reshape(expert_count, capacity, feature_count), '...]
    all_to_all x1, waiting for transfers between devices: 0.01 us -> 23.4 us  [shards(): lax.all_to_all(summed.astype(jnp.bfloat16), 'expert', split_axis=0, conca...]
    all_to_all x1, blocking collectives: 49.6 us -> 29.9 us  [shards(): lax.all_to_all(sending, 'expert', split_axis=0, concat_axis=0, tiled=True)]
    ppermute x0 -> x2, waiting for transfers between devices: none -> 4.89 us  [the longest x1 2.56 us: group_gather(): lax.ppermute(piece, 'expert', group_perm(expert_count, group_size, shift))]
    slice x0 -> x1, local copies, waits for them, and re-layouts: none -> 4.76 us  [shards(): grad_sums = sums[:, 1].reshape(flight * capacity, feature_count)]
    another operation x0 -> x2, other arithmetic: none -> 4.17 us  [the longest x1 2.58 us: group_gather(): stacked = jnp.stack(got)]
    gather x0 -> x1, local copies, waits for them, and re-layouts: none -> 3.39 us  [group_gather(): return jnp.take(stacked, order, axis=0)]
    dot_general x2, matrix products: 7.99 us -> 5.15 us  [apply_combine(): return jnp.dot(combine, partial_sums, precision=lax.Precision.HIGHEST)]
  transfers between devices with their start and end apart: 1 -> 3, of which waited for: 0 -> 3; matrix products, arithmetic and copies ran while one was open for 4% -> 0% of each run, Pallas kernels for 0% -> 0%
where the time goes in v2:
time: 177 us; the launch traced here: 176 us
  blocking collectives  68.4 us (39%)
  Pallas kernels  32 us (18%)
  waiting for transfers between devices  28.3 us (16%)
  local copies, waits for them, and re-layouts  22 us (12%)
  other arithmetic  15.2 us (9%)
  matrix products  5.15 us (3%)
  starting transfers between devices  3.94 us (2%)
    psum x1, blocking collectives, shards(): steer_grad = lax.psum(jnp.sum(total_grad, axis=0), ('dp', 'expert'))  38.5 us
    pallas_call x1, Pallas kernels, expert_share(): pl.pallas_call(_expert_kernel, grid=(rows // rb, hid // hb), in_specs=[pl...  32 us
    all_to_all x1, blocking collectives, shards(): lax.all_to_all(sending, 'expert', split_axis=0, concat_axis=0, tiled=True)  29.9 us
    all_to_all x1, waiting for transfers between devices, shards(): lax.all_to_all(summed.astype(jnp.bfloat16), 'expert', split_axis=0, conca...  23.4 us
    gather x2, local copies, waits for them, and re-layouts, dispatch_rows(): picked = values[slot_table]  5.96 us
    dot_general x2, matrix products, apply_combine(): return jnp.dot(combine, partial_sums, precision=lax.Precision.HIGHEST)  5.15 us
    slice x1, local copies, waits for them, and re-layouts, shards(): grad_sums = sums[:, 1].reshape(flight * capacity, feature_count)  4.76 us
    all_to_all x1, starting transfers between devices, shards(): lax.all_to_all(summed.astype(jnp.bfloat16), 'expert', split_axis=0, conca...  3.73 us
  transfers between devices with their start and end apart: 3, of which 3 were waited for; matrix products, arithmetic and copies ran while one was open for 0% of the time, Pallas kernels for 0%

profile of v2, /device:TPU:0, one launch (start us, length us, event | category | flops | bytes accessed | tf_op | source)
XLA Modules:
  0.0 175.9 jit_solution(15873183798750054230)
XLA Ops:
  0.6 0.0 copy-start.2
  0.6 0.0 copy-start
  0.7 0.0 copy-start.3
  0.7 0.8 fusion.11
  1.5 0.1 copy.37
  1.6 0.2 reduce_window_sum.11
  1.8 0.1 copy.38
  1.9 0.2 select_reduce_fusion
  2.0 0.2 fusion.10
  2.2 0.1 reshape.211
  2.3 2.1 %multiply_reduce_fusion.1 = f32[128]{0:T(128)S(1)} fusion(bf16[128,7168]{1,0:T(8,128)(2,1)} %param.9, f32[7168]{0:T(1024)} %param.10), kind=kLoop, calls=%fused_computation.9 | loop fusion | flops 3669888 | bytes 1864192 | tf_op jit(solution)/shard_map/reduce_sum | solution.py:41
  4.4 0.0 copy-done.2
  4.4 0.0 copy-done
  4.4 0.0 copy-done.3
  4.4 1.8 %multiply_convert_fusion = bf16[128,7168]{1,0:T(8,128)(2,1)} fusion(bf16[128,7168]{1,0:T(8,128)(2,1)S(1)} %copy-done, f32[7168]{0:T(1024)S(1)} %copy-done.3, f32[128]{0:T(128)S(1)} %get-tuple-element.16, f32[7168]{0:T(1024)S(1)} %copy-done.2), kind=kLoop, calls=%fused_computation.8 | loop fusion | flops 4587520 | bytes 3727872 | tf_op jit(solution)/shard_map/convert_element_type | solution.py:42
  6.2 3.0 %gather_fusion = bf16[32,7168]{1,0:T(8,128)(2,1)S(1)} fusion(bf16[128,7168]{1,0:T(8,128)(2,1)} %multiply_convert_fusion, s32[1024]{0:T(1024)S(1)} %pad_clamp_fusion.1), kind=kCustom, calls=%fused_computation | custom fusion | bytes 917632 | tf_op jit(solution)/shard_map/gather | solution.py:35
  9.2 3.0 %gather_fusion.1 = bf16[32,7168]{1,0:T(8,128)(2,1)S(1)} fusion(bf16[128,7168]{1,0:T(8,128)(2,1)} %param.17, s32[1024]{0:T(1024)S(1)} %pad_clamp_fusion.1), kind=kCustom, calls=%fused_computation.1 | custom fusion | bytes 917632 | tf_op jit(solution)/shard_map/gather | solution.py:35
  12.2 0.1 bitcast_select_fusion.1
  12.4 0.1 fusion.4
  12.4 29.9 %all_to_all.10 = bf16[8,2,8,3584]{3,2,1,0:T(8,128)(2,1)S(1)} all-to-all(bf16[8,2,8,3584]{3,2,1,0:T(8,128)(2,1)S(1)} %bitcast.50), channel_id=1, replica_groups=mesh['dp'=4,'expert'=8] {'expert'}, dimensions={0} | all-to-all | bytes 1835008 | tf_op jit(solution)/shard_map/all_to_all | solution.py:191
  42.3 0.0 collective-permute-start
  42.4 2.6 %collective-permute-done = bf16[8,2,8,3584]{3,2,1,0:T(8,128)(2,1)} collective-permute-done((bf16[8,2,8,3584]{3,2,1,0:T(8,128)(2,1)S(1)}, bf16[8,2,8,3584]{3,2,1,0:T(8,128)(2,1)}, u32[]{:S(2)}, u32[]{:S(2)}) %collective-permute-start) | collective-permute-done | bytes 917536 | tf_op jit(solution)/shard_map/ppermute | solution.py:146
  44.9 2.6 %pad_maximum_fusion = bf16[2,8,2,8,3584]{4,3,2,1,0:T(8,128)(2,1)} fusion(bf16[1,8,2,8,3584]{4,3,2,1,0:T(8,128)(2,1)} %bitcast.8, bf16[1,8,2,8,3584]{4,3,2,1,0:T(8,128)(2,1)S(1)} %bitcast.48), kind=kLoop, calls=%fused_computation.15 | loop fusion | flops 917504 | bytes 3670016 | tf_op jit(solution)/shard_map/stack | solution.py:147
  47.5 3.4 %gather_fusion.2 = bf16[2,8,2,8,3584]{4,3,2,1,0:T(8,128)(2,1)} fusion(bf16[2,8,2,8,3584]{4,3,2,1,0:T(8,128)(2,1)} %pad_maximum_fusion, s32[1024]{0:T(1024)S(1)} %pad_clamp_fusion), kind=kCustom, calls=%fused_computation.2 | custom fusion | bytes 3670024 | tf_op jit(solution)/shard_map/jit(_take)/gather | solution.py:149
  50.9 1.7 select_bitcast_fusion
  52.6 0.2 copy.48
  52.8 1.3 slice_bitcast_fusion
  54.2 32.0 %shard_map.112 = (bf16[64,7168]{1,0:T(8,128)(2,1)}, bf16[64,7168]{1,0:T(8,128)(2,1)}) custom-call(bf16[64,7168]{1,0:T(8,128)(2,1)} %get-tuple-element.14.x_ref, bf16[64,7168]{1,0:T(8,128)(2,1)} %get-tuple-element.13.y_ref, bf16[7168,1024]{1,0:T(8,128)(2,1)} %g_ref.1, bf16[7168,1024]{1,0:T(8,128)(2,1)} %u_ref.1, bf16[1024,7168]{1,0:T(8,128)(2,1)} %d_ref.1), custom_call_target="tpu_custom_call" | custom-call | tf_op jit(solution)/shard_map/pallas_call | solution.py:110
  86.2 1.6 fusion.3
  87.8 0.1 copy.53
  87.9 0.2 collective-permute-start.1
  88.1 2.3 %collective-permute-done.1 = bf16[8,2,8,3584]{3,2,1,0:T(8,128)(2,1)S(1)} collective-permute-done((bf16[8,2,8,3584]{3,2,1,0:T(8,128)(2,1)S(1)}, bf16[8,2,8,3584]{3,2,1,0:T(8,128)(2,1)S(1)}, u32[]{:S(2)}, u32[]{:S(2)}) %collective-permute-start.1) | collective-permute-done | bytes 917536 | tf_op jit(solution)/shard_map/ppermute | solution.py:157
  90.4 1.1 fusion.1
  91.6 3.7 %all-to-all-start.1 = ((bf16[8,2,8,3584]{3,2,1,0:T(8,128)(2,1)}), bf16[8,2,8,3584]{3,2,1,0:T(8,128)(2,1)S(1)}, u32[]{:S(2)}, u32[]{:S(2)}) async-start(bf16[8,2,8,3584]{3,2,1,0:T(8,128)(2,1)} %fusion.1), calls=%async_computation.1 | async-start | bytes 1835008 | tf_op jit(solution)/shard_map/all_to_all | solution.py:205
  95.3 0.0 copy-done.5
  95.3 0.0 copy-done.4
  95.4 23.4 %all-to-all-done.1 = bf16[8,2,8,3584]{3,2,1,0:T(8,128)(2,1)S(1)} async-done(((bf16[8,2,8,3584]{3,2,1,0:T(8,128)(2,1)}), bf16[8,2,8,3584]{3,2,1,0:T(8,128)(2,1)S(1)}, u32[]{:S(2)}, u32[]{:S(2)}) %all-to-all-start.1) | async-done | bytes 917536 | tf_op jit(solution)/shard_map/all_to_all | solution.py:205
  118.8 1.9 %copy.44 = bf16[4,2,8,2,3584]{4,3,2,1,0:T(2,128)(2,1)} copy(bf16[4,2,8,2,3584]{4,2,1,3,0:T(8,128)(2,1)S(1)} %bitcast.49) | data formatting | bytes 1835008 | tf_op jit(solution)/shard_map/transpose | solution.py:210
  120.7 2.4 %reshape.207 = bf16[4,2,57344]{2,1,0:T(2,128)(2,1)S(1)} reshape(bf16[4,2,8,2,3584]{4,3,2,1,0:T(2,128)(2,1)} %copy.44) | data formatting | bytes 1835008 | tf_op jit(solution)/shard_map/reshape | solution.py:211
  123.1 4.8 %slice_reduce_fusion = (bf16[4,57344]{1,0:T(4,128)(2,1)}, bf16[4,57344]{1,0:T(4,128)(2,1)S(1)}) fusion(bf16[4,2,57344]{2,1,0:T(2,128)(2,1)S(1)} %reshape.207), kind=kLoop, calls=%fused_computation.21 | loop fusion | bytes 1835008 | tf_op jit(solution)/shard_map/slice | solution.py:215
  127.8 1.4 reshape_squeeze.15
  129.2 0.0 copy-start.1
  129.2 2.2 %multiply_reduce_fusion = (f32[128]{0:T(128)S(1)}, f32[128,7168]{1,0:T(8,128)S(1)}) fusion(bf16[128,7168]{1,0:T(8,128)(2,1)S(1)} %copy-done, f32[7168]{0:T(1024)S(1)} %copy-done.2, f32[7168]{0:T(1024)S(1)} %copy-done.3, bf16[32,7168]{1,0:T(8,128)(2,1)S(1)} %reshape_squeeze.15, f32[128,4]{0,1:T(4,128)S(1)} %select_reduce_fusion.1, ...), kind=kOutput, calls=%fused_computation.7 | convolution fusion | flops 356917120 | bytes 6025728 | tf_op jit(solution)/shard_map/dot_general | solution.py:133
  131.4 0.0 copy-done.1
  131.4 2.6 %fusion.23 = (f32[7168]{0:T(1024)S(1)}, bf16[128,7168]{1,0:T(8,128)(2,1)}) fusion(f32[128]{0:T(128)S(1)} %broadcast_multiply_fusion, f32[128]{0:T(128)S(1)} %get-tuple-element.15, f32[7168]{0:T(1024)S(1)} %copy-done.2, bf16[128,7168]{1,0:T(8,128)(2,1)S(1)} %copy-done, f32[128,7168]{1,0:T(8,128)S(1)} %get-tuple-element.20, f32[128]{0:T(128)S(1)} %get-tuple-element.16, ...), kind=kLoop, calls=%fused_computation.72 | loop fusion | flops 9167872 | bytes 9233920 | tf_op jit(solution)/shard_map/reduce_sum | solution.py:220
  134.0 38.5 %psum.7 = f32[7168]{0:T(1024)} all-reduce(f32[7168]{0:T(1024)S(1)} %get-tuple-element.9), channel_id=1, replica_groups=mesh['dp'=4,'expert'=8] {'dp','expert'}, use_global_device_ids=true, to_apply=%region_8.9 | all-reduce | flops 7168 | bytes 57344 | tf_op jit(solution)/shard_map/psum | solution.py:220
  172.5 0.4 reshape_squeeze.14
  172.9 3.0 %fusion = bf16[128,7168]{1,0:T(8,128)(2,1)} fusion(bf16[32,7168]{1,0:T(8,128)(2,1)S(1)} %reshape_squeeze.14, bf16[128,7168]{1,0:T(8,128)(2,1)S(1)} %copy-done, f32[7168]{0:T(1024)S(1)} %copy-done.2, f32[128,4]{0,1:T(4,128)S(1)} %select_reduce_fusion.1, s32[128,4]{0,1:T(4,128)S(1)} %add_select_fusion), kind=kOutput, calls=%fused_computation.5 | convolution fusion | flops 355999744 | bytes 4161536 | tf_op jit(solution)/shard_map/dot_general | solution.py:133
  (14 shorter events, 0.2 us)
Async XLA Ops:
  0.6 3.7 %copy-start.2 = (f32[7168]{0:T(1024)S(1)}, f32[7168]{0:T(1024)}, u32[]{:S(2)}) copy-start(f32[7168]{0:T(1024)} %param.10) | copy-start | bytes 86020
  0.6 3.7 %copy-start = (bf16[128,7168]{1,0:T(8,128)(2,1)S(1)}, bf16[128,7168]{1,0:T(8,128)(2,1)}, u32[]{:S(2)}) copy-start(bf16[128,7168]{1,0:T(8,128)(2,1)} %param.9) | copy-start | bytes 5505028
  0.7 3.7 %copy-start.3 = (f32[7168]{0:T(1024)S(1)}, f32[7168]{0:T(1024)}, u32[]{:S(2)}) copy-start(f32[7168]{0:T(1024)} %param.11) | copy-start | bytes 86020
  42.3 2.6 %collective-permute-start = (bf16[8,2,8,3584]{3,2,1,0:T(8,128)(2,1)S(1)}, bf16[8,2,8,3584]{3,2,1,0:T(8,128)(2,1)}, u32[]{:S(2)}, u32[]{:S(2)}) collective-permute-start(bf16[8,2,8,3584]{3,2,1,0:T(8,128)(2,1)S(1)} %all_to_all.10), channel_id=1, source_target_pairs={{0,1},{1,0},{2,3},{3,2},{4,5},{5,4},{6,7},{7,6},{8,9},{9,8},{10,11... | collective-permute-start | bytes 2752520 | tf_op jit(solution)/shard_map/ppermute | solution.py:146
  87.9 2.5 %collective-permute-start.1 = (bf16[8,2,8,3584]{3,2,1,0:T(8,128)(2,1)S(1)}, bf16[8,2,8,3584]{3,2,1,0:T(8,128)(2,1)S(1)}, u32[]{:S(2)}, u32[]{:S(2)}) collective-permute-start(bf16[8,2,8,3584]{3,2,1,0:T(8,128)(2,1)S(1)} %bitcast.51), channel_id=1, source_target_pairs={{0,1},{1,0},{2,3},{3,2},{4,5},{5,4},{6,7},{7,6},{8,9},{9,8},{10,11... | collective-permute-start | bytes 2752520 | tf_op jit(solution)/shard_map/ppermute | solution.py:157
  90.4 4.9 %copy-start.5 = (s32[128,8]{0,1:T(8,128)S(1)}, s32[128,8]{0,1:T(8,128)}, u32[]{:S(2)}) copy-start(s32[128,8]{0,1:T(8,128)} %param.13) | copy-start | bytes 12292
  90.4 4.9 %copy-start.4 = (s32[128,8]{0,1:T(8,128)S(1)}, s32[128,8]{0,1:T(8,128)}, u32[]{:S(2)}) copy-start(s32[128,8]{0,1:T(8,128)} %param.12) | copy-start | bytes 12292
  91.6 27.2 %all-to-all-start.1 = ((bf16[8,2,8,3584]{3,2,1,0:T(8,128)(2,1)}), bf16[8,2,8,3584]{3,2,1,0:T(8,128)(2,1)S(1)}, u32[]{:S(2)}, u32[]{:S(2)}) async-start(bf16[8,2,8,3584]{3,2,1,0:T(8,128)(2,1)} %fusion.1), calls=%async_computation.1 | async-start | bytes 1835008 | tf_op jit(solution)/shard_map/all_to_all | solution.py:205
  129.2 2.2 %copy-start.1 = (bf16[128,7168]{1,0:T(8,128)(2,1)S(1)}, bf16[128,7168]{1,0:T(8,128)(2,1)}, u32[]{:S(2)}) copy-start(bf16[128,7168]{1,0:T(8,128)(2,1)} %param.17) | copy-start | bytes 5505028

commit v3 on v2

--- a/solution.py
+++ b/solution.py
@@ -159,6 +159,19 @@
     return total
 
 
+def butterfly_sum(value, axes):
+    for axis in axes:
+        size = lax.axis_size(axis)
+        if size & (size - 1):
+            value = lax.psum(value, axis)
+            continue
+        bit = 1
+        while bit < size:
+            value = value + lax.ppermute(value, axis, [(i, i ^ bit) for i in range(size)])
+            bit *= 2
+    return value
+
+
 def shards(
     tokens,
     steering,
@@ -217,7 +230,7 @@
     back_normed = apply_combine(combine, grad_sums)
     layer_out = (residual + mixture).astype(jnp.bfloat16)
     total_grad = norm_backward(residual, inverse, norm_gain, back_normed, out_grad)
-    steer_grad = lax.psum(jnp.sum(total_grad, axis=0), ("dp", "expert"))
+    steer_grad = butterfly_sum(jnp.sum(total_grad, axis=0), ("expert", "dp"))
     return (layer_out, total_grad.astype(jnp.bfloat16), steer_grad)
 
 

time: 177 us -> 153 us (0.86)
  blocking collectives: 68.4 us -> 29.9 us
  waiting for transfers between devices: 28.3 us -> 40.2 us
  starting transfers between devices: 3.94 us -> 6.96 us
    psum x1 -> x0, blocking collectives: 38.5 us -> none  [shards(): steer_grad = lax.psum(jnp.sum(total_grad, axis=0), ('dp', 'expert'))]
    ppermute x0 -> x5, waiting for transfers between devices: none -> 11.8 us  [butterfly_sum(): lax.ppermute(value, axis, [(i, i ^ bit) for i in range(size)])]
    ppermute x0 -> x5, starting transfers between devices: none -> 3.02 us  [butterfly_sum(): lax.ppermute(value, axis, [(i, i ^ bit) for i in range(size)])]
  transfers between devices with their start and end apart: 3 -> 8, of which waited for: 3 -> 7; matrix products, arithmetic and copies ran while one was open for 0% -> 2% of each run, Pallas kernels for 0% -> 0%
where the time goes in v3:
time: 153 us
  waiting for transfers between devices  40.2 us (26%)
  Pallas kernels  32 us (21%)
  blocking collectives  29.9 us (20%)
  local copies, waits for them, and re-layouts  22 us (14%)
  other arithmetic  15.8 us (10%)
  starting transfers between devices  6.96 us (5%)
  matrix products  5.15 us (3%)
    pallas_call x1, Pallas kernels, expert_share(): pl.pallas_call(_expert_kernel, grid=(rows // rb, hid // hb), in_specs=[pl...  32 us
    all_to_all x1, blocking collectives, shards(): lax.all_to_all(sending, 'expert', split_axis=0, concat_axis=0, tiled=True)  29.9 us
    all_to_all x1, waiting for transfers between devices, shards(): lax.all_to_all(summed.astype(jnp.bfloat16), 'expert', split_axis=0, conca...  23.4 us
    ppermute x5, waiting for transfers between devices, butterfly_sum(): lax.ppermute(value, axis, [(i, i ^ bit) for i in range(size)])  11.8 us
    gather x2, local copies, waits for them, and re-layouts, dispatch_rows(): picked = values[slot_table]  5.96 us
    dot_general x2, matrix products, apply_combine(): return jnp.dot(combine, partial_sums, precision=lax.Precision.HIGHEST)  5.15 us
    slice x1, local copies, waits for them, and re-layouts, shards(): grad_sums = sums[:, 1].reshape(flight * capacity, feature_count)  4.76 us
    all_to_all x1, starting transfers between devices, shards(): lax.all_to_all(summed.astype(jnp.bfloat16), 'expert', split_axis=0, conca...  3.73 us
  transfers between devices with their start and end apart: 8, of which 7 were waited for; matrix products, arithmetic and copies ran while one was open for 2% of the time, Pallas kernels for 0%

profile of v3, /device:TPU:0, one launch (start us, length us, event | category | flops | bytes accessed | tf_op | source)
XLA Modules:
  0.0 152.9 jit_solution(1878149663419073564)
XLA Ops:
  0.6 0.0 copy-start.2
  0.6 0.0 copy-start
  0.7 0.8 fusion.11
  1.5 0.1 copy.37
  1.6 0.2 reduce_window_sum.11
  1.8 0.1 copy.38
  1.9 0.2 select_reduce_fusion
  2.0 0.2 fusion.10
  2.2 0.1 reshape.211
  2.3 2.1 %multiply_reduce_fusion.1 = f32[128]{0:T(128)S(1)} fusion(bf16[128,7168]{1,0:T(8,128)(2,1)} %param.9, f32[7168]{0:T(1024)} %param.10), kind=kLoop, calls=%fused_computation.9 | loop fusion | flops 3669888 | bytes 1864192 | tf_op jit(solution)/shard_map/reduce_sum | solution.py:41
  4.4 1.8 %multiply_convert_fusion = bf16[128,7168]{1,0:T(8,128)(2,1)} fusion(bf16[128,7168]{1,0:T(8,128)(2,1)S(1)} %copy-done, f32[7168]{0:T(1024)S(1)} %copy-done.3, f32[128]{0:T(128)S(1)} %get-tuple-element.16, f32[7168]{0:T(1024)S(1)} %copy-done.2), kind=kLoop, calls=%fused_computation.8 | loop fusion | flops 4587520 | bytes 3727872 | tf_op jit(solution)/shard_map/convert_element_type | solution.py:42
  6.2 3.0 %gather_fusion = bf16[32,7168]{1,0:T(8,128)(2,1)S(1)} fusion(bf16[128,7168]{1,0:T(8,128)(2,1)} %multiply_convert_fusion, s32[1024]{0:T(1024)S(1)} %pad_clamp_fusion.1), kind=kCustom, calls=%fused_computation | custom fusion | bytes 917632 | tf_op jit(solution)/shard_map/gather | solution.py:35
  9.2 3.0 %gather_fusion.1 = bf16[32,7168]{1,0:T(8,128)(2,1)S(1)} fusion(bf16[128,7168]{1,0:T(8,128)(2,1)} %param.17, s32[1024]{0:T(1024)S(1)} %pad_clamp_fusion.1), kind=kCustom, calls=%fused_computation.1 | custom fusion | bytes 917632 | tf_op jit(solution)/shard_map/gather | solution.py:35
  12.2 0.1 bitcast_select_fusion.1
  12.4 0.1 fusion.4
  12.4 29.9 %all_to_all.10 = bf16[8,2,8,3584]{3,2,1,0:T(8,128)(2,1)S(1)} all-to-all(bf16[8,2,8,3584]{3,2,1,0:T(8,128)(2,1)S(1)} %bitcast.50), channel_id=1, replica_groups=mesh['dp'=4,'expert'=8] {'expert'}, dimensions={0} | all-to-all | bytes 1835008 | tf_op jit(solution)/shard_map/all_to_all | solution.py:204
  42.3 0.0 collective-permute-start
  42.4 2.6 %collective-permute-done = bf16[8,2,8,3584]{3,2,1,0:T(8,128)(2,1)} collective-permute-done((bf16[8,2,8,3584]{3,2,1,0:T(8,128)(2,1)S(1)}, bf16[8,2,8,3584]{3,2,1,0:T(8,128)(2,1)}, u32[]{:S(2)}, u32[]{:S(2)}) %collective-permute-start) | collective-permute-done | bytes 917536 | tf_op jit(solution)/shard_map/ppermute | solution.py:146
  44.9 2.6 %pad_maximum_fusion = bf16[2,8,2,8,3584]{4,3,2,1,0:T(8,128)(2,1)} fusion(bf16[1,8,2,8,3584]{4,3,2,1,0:T(8,128)(2,1)} %bitcast.8, bf16[1,8,2,8,3584]{4,3,2,1,0:T(8,128)(2,1)S(1)} %bitcast.48), kind=kLoop, calls=%fused_computation.15 | loop fusion | flops 917504 | bytes 3670016 | tf_op jit(solution)/shard_map/stack | solution.py:147
  47.5 3.4 %gather_fusion.2 = bf16[2,8,2,8,3584]{4,3,2,1,0:T(8,128)(2,1)} fusion(bf16[2,8,2,8,3584]{4,3,2,1,0:T(8,128)(2,1)} %pad_maximum_fusion, s32[1024]{0:T(1024)S(1)} %pad_clamp_fusion), kind=kCustom, calls=%fused_computation.2 | custom fusion | bytes 3670024 | tf_op jit(solution)/shard_map/jit(_take)/gather | solution.py:149
  50.9 1.7 %select_bitcast_fusion = bf16[2,8,2,1,8,3584]{5,4,3,2,1,0:T(8,128)(2,1)S(1)} fusion(bf16[2,8,2,8,3584]{4,3,2,1,0:T(8,128)(2,1)} %gather_fusion.2, pred[2]{0:T(512)(128)(4,1)S(1)} %compare_and_fusion), kind=kLoop, calls=%fused_computation.18 | loop fusion | flops 917504 | bytes 3670018
  52.6 0.2 copy.48
  52.8 1.3 slice_bitcast_fusion
  54.2 32.0 %shard_map.112 = (bf16[64,7168]{1,0:T(8,128)(2,1)}, bf16[64,7168]{1,0:T(8,128)(2,1)}) custom-call(bf16[64,7168]{1,0:T(8,128)(2,1)} %get-tuple-element.14.x_ref, bf16[64,7168]{1,0:T(8,128)(2,1)} %get-tuple-element.13.y_ref, bf16[7168,1024]{1,0:T(8,128)(2,1)} %g_ref.1, bf16[7168,1024]{1,0:T(8,128)(2,1)} %u_ref.1, bf16[1024,7168]{1,0:T(8,128)(2,1)} %d_ref.1), custom_call_target="tpu_custom_call" | custom-call | tf_op jit(solution)/shard_map/pallas_call | solution.py:110
  86.2 1.6 %fusion.3 = (bf16[8,2,8,1,3584]{4,2,3,0,1:T(8,128)(2,1)S(1)}, bf16[8,2,8,1,3584]{4,2,3,0,1:T(8,128)(2,1)S(1)}) fusion(s32[]{:T(128)S(6)} %select_n.140, bf16[8,1,8,2,3584]{4,2,3,0,1:T(8,128)(2,1)} %bitcast.52, bf16[8,1,8,2,3584]{4,2,3,0,1:T(8,128)(2,1)} %bitcast.53, s32[]{:T(128)S(6)} %select_n.142), kind=kLoop, calls=%fused_computation.20 | loop fusion | flops 917504 | bytes 3670024 | tf_op jit(solution)/shard_map/stack | solution.py:210
  87.8 0.1 copy.53
  87.9 0.2 collective-permute-start.1
  88.1 2.3 %collective-permute-done.1 = bf16[8,2,8,3584]{3,2,1,0:T(8,128)(2,1)S(1)} collective-permute-done((bf16[8,2,8,3584]{3,2,1,0:T(8,128)(2,1)S(1)}, bf16[8,2,8,3584]{3,2,1,0:T(8,128)(2,1)S(1)}, u32[]{:S(2)}, u32[]{:S(2)}) %collective-permute-start.1) | collective-permute-done | bytes 917536 | tf_op jit(solution)/shard_map/ppermute | solution.py:157
  90.4 1.1 fusion.1
  91.6 3.7 %all-to-all-start.1 = ((bf16[8,2,8,3584]{3,2,1,0:T(8,128)(2,1)}), bf16[8,2,8,3584]{3,2,1,0:T(8,128)(2,1)S(1)}, u32[]{:S(2)}, u32[]{:S(2)}) async-start(bf16[8,2,8,3584]{3,2,1,0:T(8,128)(2,1)} %fusion.1), calls=%async_computation.1 | async-start | bytes 1835008 | tf_op jit(solution)/shard_map/all_to_all | solution.py:218
  95.4 23.4 %all-to-all-done.1 = bf16[8,2,8,3584]{3,2,1,0:T(8,128)(2,1)S(1)} async-done(((bf16[8,2,8,3584]{3,2,1,0:T(8,128)(2,1)}), bf16[8,2,8,3584]{3,2,1,0:T(8,128)(2,1)S(1)}, u32[]{:S(2)}, u32[]{:S(2)}) %all-to-all-start.1) | async-done | bytes 917536 | tf_op jit(solution)/shard_map/all_to_all | solution.py:218
  118.8 1.9 %copy.44 = bf16[4,2,8,2,3584]{4,3,2,1,0:T(2,128)(2,1)} copy(bf16[4,2,8,2,3584]{4,2,1,3,0:T(8,128)(2,1)S(1)} %bitcast.49) | data formatting | bytes 1835008 | tf_op jit(solution)/shard_map/transpose | solution.py:223
  120.7 2.4 %reshape.207 = bf16[4,2,57344]{2,1,0:T(2,128)(2,1)S(1)} reshape(bf16[4,2,8,2,3584]{4,3,2,1,0:T(2,128)(2,1)} %copy.44) | data formatting | bytes 1835008 | tf_op jit(solution)/shard_map/reshape | solution.py:224
  123.1 4.8 %slice_reduce_fusion = (bf16[4,57344]{1,0:T(4,128)(2,1)}, bf16[4,57344]{1,0:T(4,128)(2,1)S(1)}) fusion(bf16[4,2,57344]{2,1,0:T(2,128)(2,1)S(1)} %reshape.207), kind=kLoop, calls=%fused_computation.21 | loop fusion | bytes 1835008 | tf_op jit(solution)/shard_map/slice | solution.py:228
  127.8 1.4 reshape_squeeze.15
  129.2 0.0 copy-start.1
  129.2 2.2 %multiply_reduce_fusion = (f32[128]{0:T(128)S(1)}, f32[128,7168]{1,0:T(8,128)S(1)}) fusion(bf16[128,7168]{1,0:T(8,128)(2,1)S(1)} %copy-done, f32[7168]{0:T(1024)S(1)} %copy-done.2, f32[7168]{0:T(1024)S(1)} %copy-done.3, bf16[32,7168]{1,0:T(8,128)(2,1)S(1)} %reshape_squeeze.15, f32[128,4]{0,1:T(4,128)S(1)} %select_reduce_fusion.1, ...), kind=kOutput, calls=%fused_computation.7 | convolution fusion | flops 356917120 | bytes 6025728 | tf_op jit(solution)/shard_map/dot_general | solution.py:133
  131.4 2.6 %fusion.23 = (f32[7168]{0:T(1024)S(1)}, bf16[128,7168]{1,0:T(8,128)(2,1)}) fusion(f32[128]{0:T(128)S(1)} %broadcast_multiply_fusion, f32[128]{0:T(128)S(1)} %get-tuple-element.15, f32[7168]{0:T(1024)S(1)} %copy-done.2, bf16[128,7168]{1,0:T(8,128)(2,1)S(1)} %copy-done, f32[128,7168]{1,0:T(8,128)S(1)} %get-tuple-element.20, f32[128]{0:T(128)S(1)} %get-tuple-element.16, ...), kind=kLoop, calls=%fused_computation.72 | loop fusion | flops 9167872 | bytes 9233920 | tf_op jit(solution)/shard_map/reduce_sum | solution.py:233
  134.0 0.0 collective-permute-start.2
  134.0 1.2 collective-permute-done.2
  135.3 3.9 %collective-permute-done.3 = f32[7168]{0:T(1024)S(1)} collective-permute-done((f32[7168]{0:T(1024)S(1)}, f32[7168]{0:T(1024)S(1)}, u32[]{:S(2)}, u32[]{:S(2)}) %collective-permute-start.3) | collective-permute-done | bytes 28704 | tf_op jit(solution)/shard_map/ppermute | solution.py:170
  139.1 4.8 %collective-permute-done.4 = f32[7168]{0:T(1024)S(1)} collective-permute-done((f32[7168]{0:T(1024)S(1)}, f32[7168]{0:T(1024)S(1)}, u32[]{:S(2)}, u32[]{:S(2)}) %collective-permute-start.4) | collective-permute-done | bytes 28704 | tf_op jit(solution)/shard_map/ppermute | solution.py:170
  143.9 1.5 collective-permute-start.5
  145.4 0.4 reshape_squeeze.14
  145.8 2.0 %collective-permute-done.5 = f32[7168]{0:T(1024)S(1)} collective-permute-done((f32[7168]{0:T(1024)S(1)}, f32[7168]{0:T(1024)S(1)}, u32[]{:S(2)}, u32[]{:S(2)}) %collective-permute-start.5) | collective-permute-done | bytes 28704 | tf_op jit(solution)/shard_map/ppermute | solution.py:170
  147.8 1.5 collective-permute-start.6
  149.3 3.0 %fusion = bf16[128,7168]{1,0:T(8,128)(2,1)} fusion(bf16[32,7168]{1,0:T(8,128)(2,1)S(1)} %reshape_squeeze.14, bf16[128,7168]{1,0:T(8,128)(2,1)S(1)} %copy-done, f32[7168]{0:T(1024)S(1)} %copy-done.2, f32[128,4]{0,1:T(4,128)S(1)} %select_reduce_fusion.1, s32[128,4]{0,1:T(4,128)S(1)} %add_select_fusion), kind=kOutput, calls=%fused_computation.5 | convolution fusion | flops 355999744 | bytes 4161536 | tf_op jit(solution)/shard_map/dot_general | solution.py:133
  152.3 0.6 add.132
  (28 shorter events, 0.2 us)
Async XLA Ops:
  0.6 3.7 %copy-start.2 = (f32[7168]{0:T(1024)S(1)}, f32[7168]{0:T(1024)}, u32[]{:S(2)}) copy-start(f32[7168]{0:T(1024)} %param.10) | copy-start | bytes 86020
  0.6 3.7 %copy-start = (bf16[128,7168]{1,0:T(8,128)(2,1)S(1)}, bf16[128,7168]{1,0:T(8,128)(2,1)}, u32[]{:S(2)}) copy-start(bf16[128,7168]{1,0:T(8,128)(2,1)} %param.9) | copy-start | bytes 5505028
  0.7 3.7 %copy-start.3 = (f32[7168]{0:T(1024)S(1)}, f32[7168]{0:T(1024)}, u32[]{:S(2)}) copy-start(f32[7168]{0:T(1024)} %param.11) | copy-start | bytes 86020
  42.3 2.6 %collective-permute-start = (bf16[8,2,8,3584]{3,2,1,0:T(8,128)(2,1)S(1)}, bf16[8,2,8,3584]{3,2,1,0:T(8,128)(2,1)}, u32[]{:S(2)}, u32[]{:S(2)}) collective-permute-start(bf16[8,2,8,3584]{3,2,1,0:T(8,128)(2,1)S(1)} %all_to_all.10), channel_id=1, source_target_pairs={{0,1},{1,0},{2,3},{3,2},{4,5},{5,4},{6,7},{7,6},{8,9},{9,8},{10,11... | collective-permute-start | bytes 2752520 | tf_op jit(solution)/shard_map/ppermute | solution.py:146
  87.9 2.5 %collective-permute-start.1 = (bf16[8,2,8,3584]{3,2,1,0:T(8,128)(2,1)S(1)}, bf16[8,2,8,3584]{3,2,1,0:T(8,128)(2,1)S(1)}, u32[]{:S(2)}, u32[]{:S(2)}) collective-permute-start(bf16[8,2,8,3584]{3,2,1,0:T(8,128)(2,1)S(1)} %bitcast.51), channel_id=1, source_target_pairs={{0,1},{1,0},{2,3},{3,2},{4,5},{5,4},{6,7},{7,6},{8,9},{9,8},{10,11... | collective-permute-start | bytes 2752520 | tf_op jit(solution)/shard_map/ppermute | solution.py:157
  90.4 4.9 %copy-start.5 = (s32[128,8]{0,1:T(8,128)S(1)}, s32[128,8]{0,1:T(8,128)}, u32[]{:S(2)}) copy-start(s32[128,8]{0,1:T(8,128)} %param.13) | copy-start | bytes 12292
  90.4 4.9 %copy-start.4 = (s32[128,8]{0,1:T(8,128)S(1)}, s32[128,8]{0,1:T(8,128)}, u32[]{:S(2)}) copy-start(s32[128,8]{0,1:T(8,128)} %param.12) | copy-start | bytes 12292
  91.6 27.2 %all-to-all-start.1 = ((bf16[8,2,8,3584]{3,2,1,0:T(8,128)(2,1)}), bf16[8,2,8,3584]{3,2,1,0:T(8,128)(2,1)S(1)}, u32[]{:S(2)}, u32[]{:S(2)}) async-start(bf16[8,2,8,3584]{3,2,1,0:T(8,128)(2,1)} %fusion.1), calls=%async_computation.1 | async-start | bytes 1835008 | tf_op jit(solution)/shard_map/all_to_all | solution.py:218
  129.2 2.2 %copy-start.1 = (bf16[128,7168]{1,0:T(8,128)(2,1)S(1)}, bf16[128,7168]{1,0:T(8,128)(2,1)}, u32[]{:S(2)}) copy-start(bf16[128,7168]{1,0:T(8,128)(2,1)} %param.17) | copy-start | bytes 5505028
  134.0 1.2 collective-permute-start.2
  135.2 3.9 %collective-permute-start.3 = (f32[7168]{0:T(1024)S(1)}, f32[7168]{0:T(1024)S(1)}, u32[]{:S(2)}, u32[]{:S(2)}) collective-permute-start(f32[7168]{0:T(1024)S(1)} %add.128), channel_id=1, source_target_pairs={{0,2},{1,3},{2,0},{3,1},{4,6},{5,7},{6,4},{7,5},{8,10},{9,11},{10,... | collective-permute-start | bytes 86024 | tf_op jit(solution)/shard_map/ppermute | solution.py:170
  139.1 4.8 %collective-permute-start.4 = (f32[7168]{0:T(1024)S(1)}, f32[7168]{0:T(1024)S(1)}, u32[]{:S(2)}, u32[]{:S(2)}) collective-permute-start(f32[7168]{0:T(1024)S(1)} %add.129), channel_id=1, source_target_pairs={{0,4},{1,5},{2,6},{3,7},{4,0},{5,1},{6,2},{7,3},{8,12},{9,13},{10,... | collective-permute-start | bytes 86024 | tf_op jit(solution)/shard_map/ppermute | solution.py:170
  143.9 3.9 %collective-permute-start.5 = (f32[7168]{0:T(1024)S(1)}, f32[7168]{0:T(1024)S(1)}, u32[]{:S(2)}, u32[]{:S(2)}) collective-permute-start(f32[7168]{0:T(1024)S(1)} %add.130), channel_id=1, source_target_pairs={{0,8},{8,0},{16,24},{24,16},{1,9},{9,1},{17,25},{25,17},{2,10},{10... | collective-permute-start | bytes 86024 | tf_op jit(solution)/shard_map/ppermute | solution.py:170
  147.8 4.5 %collective-permute-start.6 = (f32[7168]{0:T(1024)S(1)}, f32[7168]{0:T(1024)S(1)}, u32[]{:S(2)}, u32[]{:S(2)}) collective-permute-start(f32[7168]{0:T(1024)S(1)} %add.131), channel_id=1, source_target_pairs={{0,16},{8,24},{16,0},{24,8},{1,17},{9,25},{17,1},{25,9},{2,18},{10... | collective-permute-start | bytes 86024 | tf_op jit(solution)/shard_map/ppermute | solution.py:170

commit v4 on v3

--- a/solution.py
+++ b/solution.py
@@ -172,6 +172,102 @@
     return value
 
 
+def by_features(
+    normed, out_grad, slot_table, filled, gate_weight, up_weight, down_weight,
+    member, expert_count, group_size,
+):
+    flight, capacity = slot_table.shape
+    feature_count = normed.shape[1]
+    piece = feature_count // group_size
+    packed = jnp.stack(
+        [dispatch_rows(normed, slot_table, filled), dispatch_rows(out_grad, slot_table, filled)],
+        axis=1,
+    )
+    sending = (
+        packed.reshape(flight, 2, capacity, group_size, piece)
+        .transpose(0, 3, 1, 2, 4)
+        .reshape(expert_count, 2, capacity, piece)
+    )
+    arrived = lax.all_to_all(sending, "expert", split_axis=0, concat_axis=0, tiled=True)
+    whole = group_gather(arrived, member, expert_count, group_size)
+    rows = whole.transpose(1, 2, 3, 0, 4).reshape(expert_count, 2, capacity, feature_count)
+    local_rows = rows[:, 0].reshape(expert_count * capacity, feature_count)
+    local_grads = rows[:, 1].reshape(expert_count * capacity, feature_count)
+    forward, backward = expert_share(local_rows, local_grads, gate_weight, up_weight, down_weight)
+    both = jnp.stack(
+        [
+            forward.reshape(expert_count, capacity, feature_count),
+            backward.reshape(expert_count, capacity, feature_count),
+        ],
+        axis=1,
+    ).reshape(expert_count, 2, capacity, group_size, piece)
+    summed = group_reduce_scatter(both, member, expert_count, group_size, 3)
+    came = lax.all_to_all(
+        summed.astype(jnp.bfloat16), "expert", split_axis=0, concat_axis=0, tiled=True
+    )
+    sums = (
+        came.reshape(flight, group_size, 2, capacity, piece)
+        .transpose(0, 2, 3, 1, 4)
+        .reshape(flight, 2, capacity * feature_count)
+        .astype(jnp.float32)
+    )
+    out_sums = sums[:, 0].reshape(flight * capacity, feature_count)
+    grad_sums = sums[:, 1].reshape(flight * capacity, feature_count)
+    return out_sums, grad_sums
+
+
+def by_slots(
+    normed, out_grad, slot_table, filled, gate_weight, up_weight, down_weight,
+    member, expert_count, group_size,
+):
+    flight, capacity = slot_table.shape
+    feature_count = normed.shape[1]
+    half = capacity // group_size
+    sending = jnp.stack(
+        [dispatch_rows(normed, slot_table, filled), dispatch_rows(out_grad, slot_table, filled)],
+        axis=1,
+    )
+    sending = (
+        sending.reshape(flight, 2, group_size, half, feature_count)
+        .transpose(0, 2, 1, 3, 4)
+        .reshape(expert_count, 2, half, feature_count)
+    )
+    arrived = lax.all_to_all(sending, "expert", split_axis=0, concat_axis=0, tiled=True)
+    got = [arrived]
+    for shift in range(1, group_size):
+        got.append(lax.ppermute(arrived, "expert", group_perm(expert_count, group_size, shift)))
+    rows = jnp.stack(got, axis=1)
+    local_rows = rows[:, :, 0].reshape(expert_count * group_size * half, feature_count)
+    local_grads = rows[:, :, 1].reshape(expert_count * group_size * half, feature_count)
+    forward, backward = expert_share(local_rows, local_grads, gate_weight, up_weight, down_weight)
+    both = jnp.stack(
+        [
+            forward.reshape(expert_count, group_size, half, feature_count),
+            backward.reshape(expert_count, group_size, half, feature_count),
+        ],
+        axis=2,
+    )
+    total = both[:, 0].astype(jnp.float32)
+    for shift in range(1, group_size):
+        back_shift = (group_size - shift) % group_size
+        moved = lax.ppermute(
+            both[:, shift], "expert", group_perm(expert_count, group_size, back_shift)
+        )
+        total = total + moved.astype(jnp.float32)
+    came = lax.all_to_all(
+        total.astype(jnp.bfloat16), "expert", split_axis=0, concat_axis=0, tiled=True
+    )
+    sums = (
+        came.reshape(flight, group_size, 2, half, feature_count)
+        .transpose(0, 2, 1, 3, 4)
+        .reshape(flight, 2, capacity * feature_count)
+        .astype(jnp.float32)
+    )
+    out_sums = sums[:, 0].reshape(flight * capacity, feature_count)
+    grad_sums = sums[:, 1].reshape(flight * capacity, feature_count)
+    return out_sums, grad_sums
+
+
 def shards(
     tokens,
     steering,
@@ -192,40 +288,16 @@
     member = lax.axis_index("expert") % group_size
     residual, inverse, normed = normalize(tokens, steering, norm_gain)
     slot_table, filled, combine = slot_tables(route_ids, route_gates, flight, capacity)
-    packed = jnp.stack(
-        [dispatch_rows(normed, slot_table, filled), dispatch_rows(out_grad, slot_table, filled)],
-        axis=1,
-    )
-    sending = (
-        packed.reshape(flight, 2, capacity, group_size, piece)
-        .transpose(0, 3, 1, 2, 4)
-        .reshape(expert_count, 2, capacity, piece)
-    )
-    arrived = lax.all_to_all(sending, "expert", split_axis=0, concat_axis=0, tiled=True)
-    whole = group_gather(arrived, member, expert_count, group_size)
-    rows = whole.transpose(1, 2, 3, 0, 4).reshape(expert_count, 2, capacity, feature_count)
-    local_rows = rows[:, 0].reshape(expert_count * capacity, feature_count)
-    local_grads = rows[:, 1].reshape(expert_count * capacity, feature_count)
-    forward, backward = expert_share(local_rows, local_grads, gate_weight, up_weight, down_weight)
-    both = jnp.stack(
-        [
-            forward.reshape(expert_count, capacity, feature_count),
-            backward.reshape(expert_count, capacity, feature_count),
-        ],
-        axis=1,
-    ).reshape(expert_count, 2, capacity, group_size, piece)
-    summed = group_reduce_scatter(both, member, expert_count, group_size, 3)
-    came = lax.all_to_all(
-        summed.astype(jnp.bfloat16), "expert", split_axis=0, concat_axis=0, tiled=True
-    )
-    sums = (
-        came.reshape(flight, group_size, 2, capacity, piece)
-        .transpose(0, 2, 3, 1, 4)
-        .reshape(flight, 2, capacity * feature_count)
-        .astype(jnp.float32)
-    )
-    out_sums = sums[:, 0].reshape(flight * capacity, feature_count)
-    grad_sums = sums[:, 1].reshape(flight * capacity, feature_count)
+    if capacity % group_size == 0:
+        out_sums, grad_sums = by_slots(
+            normed, out_grad, slot_table, filled, gate_weight, up_weight, down_weight,
+            member, expert_count, group_size,
+        )
+    else:
+        out_sums, grad_sums = by_features(
+            normed, out_grad, slot_table, filled, gate_weight, up_weight, down_weight,
+            member, expert_count, group_size,
+        )
     mixture = apply_combine(combine, out_sums)
     back_normed = apply_combine(combine, grad_sums)
     layer_out = (residual + mixture).astype(jnp.bfloat16)

time: 153 us -> 150 us (0.980)
  other arithmetic: 15.8 us -> 12.1 us
    another operation x3 -> x7, local copies, waits for them, and re-layouts: 3.1 us -> 7.98 us  [the longest x3 3.97 us: by_slots(): jnp.stack([forward.reshape(expert_count, group_size, half, feature_count)...]
    gather x1 -> x0, local copies, waits for them, and re-layouts: 3.39 us -> none  [group_gather(): return jnp.take(stacked, order, axis=0)]
    another operation x3 -> x2, other arithmetic: 4.21 us -> 1.49 us  [the longest x1 1.32 us: by_slots(): rows = jnp.stack(got, axis=1)]
    gather x2, local copies, waits for them, and re-layouts: 5.96 us -> 3.82 us  [dispatch_rows(): picked = values[slot_table]]
    transpose x1 -> x0, local copies, waits for them, and re-layouts: 1.87 us -> none  [shards(): sums = came.reshape(flight, group_size, 2, capacity, piece).transpose(0,...]
    unnamed x1 -> x0, other arithmetic: 1.74 us -> none
    slice x1 -> x4, local copies, waits for them, and re-layouts: 4.76 us -> 6.06 us  [the longest x1 4.76 us: by_slots(): grad_sums = sums[:, 1].reshape(flight * capacity, feature_count)]
where the time goes in v4:
time: 150 us
  waiting for transfers between devices  40 us (27%)
  Pallas kernels  32 us (21%)
  blocking collectives  29.9 us (20%)
  local copies, waits for them, and re-layouts  22.4 us (15%)
  other arithmetic  12.1 us (8%)
  starting transfers between devices  7 us (5%)
  matrix products  5.16 us (3%)
    pallas_call x1, Pallas kernels, expert_share(): pl.pallas_call(_expert_kernel, grid=(rows // rb, hid // hb), in_specs=[pl...  32 us
    all_to_all x1, blocking collectives, by_slots(): lax.all_to_all(sending, 'expert', split_axis=0, concat_axis=0, tiled=True)  29.9 us
    all_to_all x1, waiting for transfers between devices, by_slots(): lax.all_to_all(total.astype(jnp.bfloat16), 'expert', split_axis=0, concat...  23.4 us
    ppermute x5, waiting for transfers between devices, butterfly_sum(): lax.ppermute(value, axis, [(i, i ^ bit) for i in range(size)])  11.8 us
    dot_general x2, matrix products, apply_combine(): return jnp.dot(combine, partial_sums, precision=lax.Precision.HIGHEST)  5.16 us
    slice x1, local copies, waits for them, and re-layouts, by_slots(): grad_sums = sums[:, 1].reshape(flight * capacity, feature_count)  4.76 us
    another operation x3, local copies, waits for them, and re-layouts, by_slots(): jnp.stack([forward.reshape(expert_count, group_size, half, feature_count)...  3.97 us
    gather x2, local copies, waits for them, and re-layouts, dispatch_rows(): picked = values[slot_table]  3.82 us
  transfers between devices with their start and end apart: 8, of which 7 were waited for; matrix products, arithmetic and copies ran while one was open for 2% of the time, Pallas kernels for 0%

profile of v4, /device:TPU:0, one launch (start us, length us, event | category | flops | bytes accessed | tf_op | source)
XLA Modules:
  0.0 149.6 jit_solution(13125218821385124856)
XLA Ops:
  0.6 0.7 fusion.10
  1.3 0.1 copy.53
  1.5 0.2 reduce_window_sum.11
  1.6 0.1 copy.54
  1.7 0.2 select_reduce_fusion
  1.9 0.2 fusion.9
  2.0 0.1 reshape.148
  2.1 2.1 %multiply_reduce_fusion.1 = f32[128]{0:T(128)S(1)} fusion(bf16[128,7168]{1,0:T(8,128)(2,1)} %param.9, f32[7168]{0:T(1024)} %param.10), kind=kLoop, calls=%fused_computation.8 | loop fusion | flops 3669888 | bytes 1864192 | tf_op jit(solution)/shard_map/reduce_sum | solution.py:41
  4.2 2.1 %multiply_convert_fusion = bf16[128,7168]{1,0:T(8,128)(2,1)S(1)} fusion(bf16[128,7168]{1,0:T(8,128)(2,1)} %param.9, f32[7168]{0:T(1024)} %param.11, f32[128]{0:T(128)S(1)} %get-tuple-element.16, f32[7168]{0:T(1024)} %param.10), kind=kLoop, calls=%fused_computation.7 | loop fusion | flops 4587520 | bytes 3727872 | tf_op jit(solution)/shard_map/convert_element_type | solution.py:42
  6.3 0.8 gather_fusion
  7.1 3.0 %gather_fusion.1 = bf16[32,7168]{1,0:T(8,128)(2,1)S(1)} fusion(bf16[128,7168]{1,0:T(8,128)(2,1)} %param.17, s32[1024]{0:T(1024)S(1)} %pad_clamp_fusion), kind=kCustom, calls=%fused_computation.1 | custom fusion | bytes 917632 | tf_op jit(solution)/shard_map/gather | solution.py:35
  10.1 0.1 bitcast_select_fusion.1
  10.3 0.2 fusion.4
  10.5 0.4 fusion.3
  10.9 29.9 %all_to_all.10 = bf16[8,2,4,7168]{3,2,1,0:T(4,128)(2,1)S(1)} all-to-all(bf16[8,2,4,7168]{3,2,1,0:T(4,128)(2,1)S(1)} %bitcast.42), channel_id=1, replica_groups=mesh['dp'=4,'expert'=8] {'expert'}, dimensions={0} | all-to-all | bytes 1835008 | tf_op jit(solution)/shard_map/all_to_all | solution.py:235
  40.8 2.5 %collective-permute-done = bf16[8,2,4,7168]{3,2,1,0:T(4,128)(2,1)S(1)} collective-permute-done((bf16[8,2,4,7168]{3,2,1,0:T(4,128)(2,1)S(1)}, bf16[8,2,4,7168]{3,2,1,0:T(4,128)(2,1)S(1)}, u32[]{:S(2)}, u32[]{:S(2)}) %collective-permute-start) | collective-permute-done | bytes 917536 | tf_op jit(solution)/shard_map/ppermute | solution.py:238
  43.3 1.3 pad_maximum_fusion
  44.6 0.3 copy.57
  44.9 1.1 reshape_squeeze.12.x_ref
  46.0 0.3 copy.58
  46.4 1.1 reshape_squeeze.13.y_ref
  47.5 32.0 %shard_map.112 = (bf16[64,7168]{1,0:T(8,128)(2,1)}, bf16[64,7168]{1,0:T(8,128)(2,1)}) custom-call(bf16[64,7168]{1,0:T(8,128)(2,1)} %reshape_squeeze.12.x_ref, bf16[64,7168]{1,0:T(8,128)(2,1)} %reshape_squeeze.13.y_ref, bf16[7168,1024]{1,0:T(8,128)(2,1)} %g_ref.1, bf16[7168,1024]{1,0:T(8,128)(2,1)} %u_ref.1, bf16[1024,7168]{1,0:T(8,128)(2,1)} %d_ref.1), custom_call_target="tpu_custom_call" | custom-call | tf_op jit(solution)/shard_map/pallas_call | solution.py:110
  79.5 1.8 %stack_reshape.6 = bf16[8,2,1,4,7168]{4,3,1,0,2:T(4,128)(2,1)S(1)} reshape(bf16[64,7168]{1,0:T(8,128)(2,1)} %get-tuple-element.5) | data formatting | bytes 1835008 | tf_op jit(solution)/shard_map/stack;reshape | solution.py:243
  81.3 0.3 constant_dynamic-update-slice_fusion.1
  81.7 1.8 %stack_reshape.7 = bf16[8,2,1,4,7168]{4,3,1,0,2:T(4,128)(2,1)S(1)} reshape(bf16[64,7168]{1,0:T(8,128)(2,1)} %get-tuple-element.6) | data formatting | bytes 1835008 | tf_op jit(solution)/shard_map/stack;reshape | solution.py:243
  83.5 0.4 constant_dynamic-update-slice_fusion
  83.9 0.7 fusion.20
  84.5 0.3 copy.70
  84.9 0.2 collective-permute-start.1
  85.1 2.3 %collective-permute-done.1 = bf16[8,2,4,7168]{3,2,1,0:T(4,128)(2,1)S(1)} collective-permute-done((bf16[8,2,4,7168]{3,2,1,0:T(4,128)(2,1)S(1)}, bf16[8,2,4,7168]{3,2,1,0:T(4,128)(2,1)S(1)}, u32[]{:S(2)}, u32[]{:S(2)}) %collective-permute-start.1) | collective-permute-done | bytes 917536 | tf_op jit(solution)/shard_map/ppermute | solution.py:253
  87.4 1.4 fusion.1
  88.8 3.8 %all-to-all-start.1 = ((bf16[8,2,4,7168]{3,2,1,0:T(4,128)(2,1)}), bf16[8,2,4,7168]{3,2,1,0:T(4,128)(2,1)S(1)}, u32[]{:S(2)}, u32[]{:S(2)}) async-start(bf16[8,2,4,7168]{3,2,1,0:T(4,128)(2,1)} %fusion.1), calls=%async_computation.1 | async-start | bytes 1835008 | tf_op jit(solution)/shard_map/all_to_all | solution.py:257
  92.6 23.4 %all-to-all-done.1 = bf16[8,2,4,7168]{3,2,1,0:T(4,128)(2,1)S(1)} async-done(((bf16[8,2,4,7168]{3,2,1,0:T(4,128)(2,1)}), bf16[8,2,4,7168]{3,2,1,0:T(4,128)(2,1)S(1)}, u32[]{:S(2)}, u32[]{:S(2)}) %all-to-all-start.1) | async-done | bytes 917536 | tf_op jit(solution)/shard_map/all_to_all | solution.py:257
  116.1 1.3 copy.71
  117.3 2.4 %reshape.144 = bf16[4,2,57344]{2,1,0:T(2,128)(2,1)S(1)} reshape(bf16[4,2,2,4,7168]{4,3,2,1,0:T(4,128)(2,1)} %bitcast.43) | data formatting | bytes 1835008 | tf_op jit(solution)/shard_map/reshape | solution.py:263
  119.7 4.8 %slice_reduce_fusion = (bf16[4,57344]{1,0:T(4,128)(2,1)}, bf16[4,57344]{1,0:T(4,128)(2,1)S(1)}) fusion(bf16[4,2,57344]{2,1,0:T(2,128)(2,1)S(1)} %reshape.144), kind=kLoop, calls=%fused_computation.15 | loop fusion | bytes 1835008 | tf_op jit(solution)/shard_map/slice | solution.py:267
  124.5 1.4 reshape_squeeze.15
  125.9 2.2 %multiply_reduce_fusion = (f32[128]{0:T(128)S(1)}, f32[128,7168]{1,0:T(8,128)S(1)}) fusion(bf16[128,7168]{1,0:T(8,128)(2,1)S(1)} %copy-done, f32[7168]{0:T(1024)S(1)} %copy-done.2, f32[7168]{0:T(1024)S(1)} %copy-done.3, bf16[32,7168]{1,0:T(8,128)(2,1)S(1)} %reshape_squeeze.15, f32[128,4]{0,1:T(4,128)S(1)} %select_reduce_fusion.1, ...), kind=kOutput, calls=%fused_computation.6 | convolution fusion | flops 356917120 | bytes 6025728 | tf_op jit(solution)/shard_map/dot_general | solution.py:133
  128.1 2.6 %fusion.19 = (f32[7168]{0:T(1024)S(1)}, bf16[128,7168]{1,0:T(8,128)(2,1)}) fusion(f32[128]{0:T(128)S(1)} %broadcast_multiply_fusion, f32[128]{0:T(128)S(1)} %get-tuple-element.15, f32[7168]{0:T(1024)S(1)} %copy-done.2, bf16[128,7168]{1,0:T(8,128)(2,1)S(1)} %copy-done, f32[128,7168]{1,0:T(8,128)S(1)} %get-tuple-element.20, f32[128]{0:T(128)S(1)} %get-tuple-element.16, ...), kind=kLoop, calls=%fused_computation.55 | loop fusion | flops 9167872 | bytes 9233920 | tf_op jit(solution)/shard_map/reduce_sum | solution.py:305
  130.7 1.2 collective-permute-done.2
  131.9 3.9 %collective-permute-done.3 = f32[7168]{0:T(1024)S(1)} collective-permute-done((f32[7168]{0:T(1024)S(1)}, f32[7168]{0:T(1024)S(1)}, u32[]{:S(2)}, u32[]{:S(2)}) %collective-permute-start.3) | collective-permute-done | bytes 28704 | tf_op jit(solution)/shard_map/ppermute | solution.py:170
  135.8 4.8 %collective-permute-done.4 = f32[7168]{0:T(1024)S(1)} collective-permute-done((f32[7168]{0:T(1024)S(1)}, f32[7168]{0:T(1024)S(1)}, u32[]{:S(2)}, u32[]{:S(2)}) %collective-permute-start.4) | collective-permute-done | bytes 28704 | tf_op jit(solution)/shard_map/ppermute | solution.py:170
  140.6 1.5 collective-permute-start.5
  142.1 0.4 reshape_squeeze.14
  142.4 2.0 %collective-permute-done.5 = f32[7168]{0:T(1024)S(1)} collective-permute-done((f32[7168]{0:T(1024)S(1)}, f32[7168]{0:T(1024)S(1)}, u32[]{:S(2)}, u32[]{:S(2)}) %collective-permute-start.5) | collective-permute-done | bytes 28704 | tf_op jit(solution)/shard_map/ppermute | solution.py:170
  144.4 1.5 %collective-permute-start.6 = (f32[7168]{0:T(1024)S(1)}, f32[7168]{0:T(1024)S(1)}, u32[]{:S(2)}, u32[]{:S(2)}) collective-permute-start(f32[7168]{0:T(1024)S(1)} %add.73), channel_id=1, source_target_pairs={{0,16},{8,24},{16,0},{24,8},{1,17},{9,25},{17,1},{25,9},{2,18},{10... | collective-permute-start | bytes 86024 | tf_op jit(solution)/shard_map/ppermute | solution.py:170
  146.0 3.0 %fusion = bf16[128,7168]{1,0:T(8,128)(2,1)} fusion(bf16[32,7168]{1,0:T(8,128)(2,1)S(1)} %reshape_squeeze.14, bf16[128,7168]{1,0:T(8,128)(2,1)S(1)} %copy-done, f32[7168]{0:T(1024)S(1)} %copy-done.2, f32[128,4]{0,1:T(4,128)S(1)} %select_reduce_fusion.1, s32[128,4]{0,1:T(4,128)S(1)} %add_select_fusion), kind=kOutput, calls=%fused_computation.4 | convolution fusion | flops 355999744 | bytes 4161536 | tf_op jit(solution)/shard_map/dot_general | solution.py:133
  148.9 0.6 add.74
  (29 shorter events, 0.1 us)
Async XLA Ops:
  40.8 2.5 %collective-permute-start = (bf16[8,2,4,7168]{3,2,1,0:T(4,128)(2,1)S(1)}, bf16[8,2,4,7168]{3,2,1,0:T(4,128)(2,1)S(1)}, u32[]{:S(2)}, u32[]{:S(2)}) collective-permute-start(bf16[8,2,4,7168]{3,2,1,0:T(4,128)(2,1)S(1)} %all_to_all.10), channel_id=1, source_target_pairs={{0,1},{1,0},{2,3},{3,2},{4,5},{5,4},{6,7},{7,6},{8,9},{9,8},{10,11... | collective-permute-start | bytes 2752520 | tf_op jit(solution)/shard_map/ppermute | solution.py:238
  84.5 8.1 %copy-start.5 = (s32[128,8]{0,1:T(8,128)S(1)}, s32[128,8]{0,1:T(8,128)}, u32[]{:S(2)}) copy-start(s32[128,8]{0,1:T(8,128)} %param.13) | copy-start | bytes 12292
  84.5 8.1 %copy-start.4 = (s32[128,8]{0,1:T(8,128)S(1)}, s32[128,8]{0,1:T(8,128)}, u32[]{:S(2)}) copy-start(s32[128,8]{0,1:T(8,128)} %param.12) | copy-start | bytes 12292
  84.9 2.5 %collective-permute-start.1 = (bf16[8,2,4,7168]{3,2,1,0:T(4,128)(2,1)S(1)}, bf16[8,2,4,7168]{3,2,1,0:T(4,128)(2,1)S(1)}, u32[]{:S(2)}, u32[]{:S(2)}) collective-permute-start(bf16[8,2,4,7168]{3,2,1,0:T(4,128)(2,1)S(1)} %bitcast.45), channel_id=1, source_target_pairs={{0,1},{1,0},{2,3},{3,2},{4,5},{5,4},{6,7},{7,6},{8,9},{9,8},{10,11... | collective-permute-start | bytes 2752520 | tf_op jit(solution)/shard_map/ppermute | solution.py:253
  88.8 27.2 %all-to-all-start.1 = ((bf16[8,2,4,7168]{3,2,1,0:T(4,128)(2,1)}), bf16[8,2,4,7168]{3,2,1,0:T(4,128)(2,1)S(1)}, u32[]{:S(2)}, u32[]{:S(2)}) async-start(bf16[8,2,4,7168]{3,2,1,0:T(4,128)(2,1)} %fusion.1), calls=%async_computation.1 | async-start | bytes 1835008 | tf_op jit(solution)/shard_map/all_to_all | solution.py:257
  116.0 9.8 %copy-start = (bf16[128,7168]{1,0:T(8,128)(2,1)S(1)}, bf16[128,7168]{1,0:T(8,128)(2,1)}, u32[]{:S(2)}) copy-start(bf16[128,7168]{1,0:T(8,128)(2,1)} %param.9) | copy-start | bytes 5505028
  116.0 9.8 %copy-start.2 = (f32[7168]{0:T(1024)S(1)}, f32[7168]{0:T(1024)}, u32[]{:S(2)}) copy-start(f32[7168]{0:T(1024)} %param.10) | copy-start | bytes 86020
  116.1 9.8 %copy-start.3 = (f32[7168]{0:T(1024)S(1)}, f32[7168]{0:T(1024)}, u32[]{:S(2)}) copy-start(f32[7168]{0:T(1024)} %param.11) | copy-start | bytes 86020
  125.9 2.2 %copy-start.1 = (bf16[128,7168]{1,0:T(8,128)(2,1)S(1)}, bf16[128,7168]{1,0:T(8,128)(2,1)}, u32[]{:S(2)}) copy-start(bf16[128,7168]{1,0:T(8,128)(2,1)} %param.17) | copy-start | bytes 5505028
  130.7 1.2 collective-permute-start.2
  131.9 3.9 %collective-permute-start.3 = (f32[7168]{0:T(1024)S(1)}, f32[7168]{0:T(1024)S(1)}, u32[]{:S(2)}, u32[]{:S(2)}) collective-permute-start(f32[7168]{0:T(1024)S(1)} %add.70), channel_id=1, source_target_pairs={{0,2},{1,3},{2,0},{3,1},{4,6},{5,7},{6,4},{7,5},{8,10},{9,11},{10,... | collective-permute-start | bytes 86024 | tf_op jit(solution)/shard_map/ppermute | solution.py:170
  135.8 4.8 %collective-permute-start.4 = (f32[7168]{0:T(1024)S(1)}, f32[7168]{0:T(1024)S(1)}, u32[]{:S(2)}, u32[]{:S(2)}) collective-permute-start(f32[7168]{0:T(1024)S(1)} %add.71), channel_id=1, source_target_pairs={{0,4},{1,5},{2,6},{3,7},{4,0},{5,1},{6,2},{7,3},{8,12},{9,13},{10,... | collective-permute-start | bytes 86024 | tf_op jit(solution)/shard_map/ppermute | solution.py:170
  140.6 3.9 %collective-permute-start.5 = (f32[7168]{0:T(1024)S(1)}, f32[7168]{0:T(1024)S(1)}, u32[]{:S(2)}, u32[]{:S(2)}) collective-permute-start(f32[7168]{0:T(1024)S(1)} %add.72), channel_id=1, source_target_pairs={{0,8},{8,0},{16,24},{24,16},{1,9},{9,1},{17,25},{25,17},{2,10},{10... | collective-permute-start | bytes 86024 | tf_op jit(solution)/shard_map/ppermute | solution.py:170
  144.4 4.5 %collective-permute-start.6 = (f32[7168]{0:T(1024)S(1)}, f32[7168]{0:T(1024)S(1)}, u32[]{:S(2)}, u32[]{:S(2)}) collective-permute-start(f32[7168]{0:T(1024)S(1)} %add.73), channel_id=1, source_target_pairs={{0,16},{8,24},{16,0},{24,8},{1,17},{9,25},{17,1},{25,9},{2,18},{10... | collective-permute-start | bytes 86024 | tf_op jit(solution)/shard_map/ppermute | solution.py:170

commit v5 on v4

--- a/solution.py
+++ b/solution.py
@@ -216,55 +216,32 @@
     return out_sums, grad_sums
 
 
-def by_slots(
+def by_pair(
     normed, out_grad, slot_table, filled, gate_weight, up_weight, down_weight,
     member, expert_count, group_size,
 ):
     flight, capacity = slot_table.shape
     feature_count = normed.shape[1]
-    half = capacity // group_size
     sending = jnp.stack(
         [dispatch_rows(normed, slot_table, filled), dispatch_rows(out_grad, slot_table, filled)],
         axis=1,
-    )
-    sending = (
-        sending.reshape(flight, 2, group_size, half, feature_count)
-        .transpose(0, 2, 1, 3, 4)
-        .reshape(expert_count, 2, half, feature_count)
-    )
+    ).reshape(expert_count, capacity, feature_count)
     arrived = lax.all_to_all(sending, "expert", split_axis=0, concat_axis=0, tiled=True)
-    got = [arrived]
-    for shift in range(1, group_size):
-        got.append(lax.ppermute(arrived, "expert", group_perm(expert_count, group_size, shift)))
-    rows = jnp.stack(got, axis=1)
-    local_rows = rows[:, :, 0].reshape(expert_count * group_size * half, feature_count)
-    local_grads = rows[:, :, 1].reshape(expert_count * group_size * half, feature_count)
+    swap = group_perm(expert_count, group_size, 1)
+    partner = lax.ppermute(arrived, "expert", swap)
+    first = member == 0
+    local_rows = jnp.where(first, arrived, partner).reshape(expert_count * capacity, feature_count)
+    local_grads = jnp.where(first, partner, arrived).reshape(expert_count * capacity, feature_count)
     forward, backward = expert_share(local_rows, local_grads, gate_weight, up_weight, down_weight)
-    both = jnp.stack(
-        [
-            forward.reshape(expert_count, group_size, half, feature_count),
-            backward.reshape(expert_count, group_size, half, feature_count),
-        ],
-        axis=2,
-    )
-    total = both[:, 0].astype(jnp.float32)
-    for shift in range(1, group_size):
-        back_shift = (group_size - shift) % group_size
-        moved = lax.ppermute(
-            both[:, shift], "expert", group_perm(expert_count, group_size, back_shift)
-        )
-        total = total + moved.astype(jnp.float32)
+    keep = jnp.where(first, forward, backward)
+    give = jnp.where(first, backward, forward)
+    total = keep.astype(jnp.float32) + lax.ppermute(give, "expert", swap).astype(jnp.float32)
     came = lax.all_to_all(
-        total.astype(jnp.bfloat16), "expert", split_axis=0, concat_axis=0, tiled=True
-    )
-    sums = (
-        came.reshape(flight, group_size, 2, half, feature_count)
-        .transpose(0, 2, 1, 3, 4)
-        .reshape(flight, 2, capacity * feature_count)
-        .astype(jnp.float32)
-    )
-    out_sums = sums[:, 0].reshape(flight * capacity, feature_count)
-    grad_sums = sums[:, 1].reshape(flight * capacity, feature_count)
+        total.astype(jnp.bfloat16).reshape(expert_count, capacity, feature_count),
+        "expert", split_axis=0, concat_axis=0, tiled=True,
+    ).reshape(flight, 2, capacity, feature_count)
+    out_sums = came[:, 0].reshape(flight * capacity, feature_count).astype(jnp.float32)
+    grad_sums = came[:, 1].reshape(flight * capacity, feature_count).astype(jnp.float32)
     return out_sums, grad_sums
 
 
@@ -288,8 +265,8 @@
     member = lax.axis_index("expert") % group_size
     residual, inverse, normed = normalize(tokens, steering, norm_gain)
     slot_table, filled, combine = slot_tables(route_ids, route_gates, flight, capacity)
-    if capacity % group_size == 0:
-        out_sums, grad_sums = by_slots(
+    if group_size == 2:
+        out_sums, grad_sums = by_pair(
             normed, out_grad, slot_table, filled, gate_weight, up_weight, down_weight,
             member, expert_count, group_size,
         )

time: 150 us -> 134 us (0.89)
  local copies, waits for them, and re-layouts: 22.4 us -> 4.17 us
  other arithmetic: 12.1 us -> 14.1 us
    another operation x7 -> x1, local copies, waits for them, and re-layouts: 7.98 us -> 0.06 us  [by_pair(): jnp.stack([dispatch_rows(normed, slot_table, filled), dispatch_rows(out_g...]
    slice x4 -> x0, local copies, waits for them, and re-layouts: 6.06 us -> none  [the longest x1 4.76 us: by_slots(): grad_sums = sums[:, 1].reshape(flight * capacity, feature_count)]
    reshape x0 -> x2, other arithmetic: none -> 3.78 us  [the longest x1 2.43 us: by_pair(): total.astype(jnp.bfloat16).reshape(expert_count, capacity, feature_count)]
    reshape x2 -> x0, local copies, waits for them, and re-layouts: 3.63 us -> none  [the longest x1 2.37 us: by_slots(): sums = came.reshape(flight, group_size, 2, half, feature_count).transpose...]
where the time goes in v5:
time: 134 us
  waiting for transfers between devices  40.5 us (30%)
  Pallas kernels  32.1 us (24%)
  blocking collectives  29.9 us (22%)
  other arithmetic  14.1 us (11%)
  starting transfers between devices  6.95 us (5%)
  matrix products  5.15 us (4%)
  local copies, waits for them, and re-layouts  4.17 us (3%)
    pallas_call x1, Pallas kernels, expert_share(): pl.pallas_call(_expert_kernel, grid=(rows // rb, hid // hb), in_specs=[pl...  32.1 us
    all_to_all x1, blocking collectives, by_pair(): lax.all_to_all(sending, 'expert', split_axis=0, concat_axis=0, tiled=True)  29.9 us
    all_to_all x1, waiting for transfers between devices, by_pair(): lax.all_to_all(total.astype(jnp.bfloat16).reshape(expert_count, capacity,...  23.4 us
    ppermute x5, waiting for transfers between devices, butterfly_sum(): lax.ppermute(value, axis, [(i, i ^ bit) for i in range(size)])  12.2 us
    dot_general x2, matrix products, apply_combine(): return jnp.dot(combine, partial_sums, precision=lax.Precision.HIGHEST)  5.15 us
    gather x2, local copies, waits for them, and re-layouts, dispatch_rows(): picked = values[slot_table]  3.82 us
    all_to_all x1, starting transfers between devices, by_pair(): lax.all_to_all(total.astype(jnp.bfloat16).reshape(expert_count, capacity,...  3.73 us
    ppermute x5, starting transfers between devices, butterfly_sum(): lax.ppermute(value, axis, [(i, i ^ bit) for i in range(size)])  3.02 us
  transfers between devices with their start and end apart: 8, of which 7 were waited for; matrix products, arithmetic and copies ran while one was open for 2% of the time, Pallas kernels for 0%

profile of v5, /device:TPU:0, one launch (start us, length us, event | category | flops | bytes accessed | tf_op | source)
XLA Modules:
  0.0 133.6 jit_solution(1639728871936895017)
XLA Ops:
  0.6 0.7 fusion.7
  1.3 0.1 copy.23
  1.5 0.2 reduce_window_sum.11
  1.6 0.1 copy.24
  1.7 0.2 select_reduce_fusion
  1.9 0.2 fusion.6
  2.0 0.1 reshape.152
  2.1 2.1 %multiply_reduce_fusion.1 = f32[128]{0:T(128)S(1)} fusion(bf16[128,7168]{1,0:T(8,128)(2,1)} %param.9, f32[7168]{0:T(1024)} %param.10), kind=kLoop, calls=%fused_computation.8 | loop fusion | flops 3669888 | bytes 1864192 | tf_op jit(solution)/shard_map/reduce_sum | solution.py:41
  4.2 2.1 %multiply_convert_fusion = bf16[128,7168]{1,0:T(8,128)(2,1)S(1)} fusion(bf16[128,7168]{1,0:T(8,128)(2,1)} %param.9, f32[7168]{0:T(1024)} %param.11, f32[128]{0:T(128)S(1)} %get-tuple-element.12, f32[7168]{0:T(1024)} %param.10), kind=kLoop, calls=%fused_computation.7 | loop fusion | flops 4587520 | bytes 3727872 | tf_op jit(solution)/shard_map/convert_element_type | solution.py:42
  6.3 0.8 gather_fusion
  7.1 3.0 %gather_fusion.1 = bf16[32,7168]{1,0:T(8,128)(2,1)S(1)} fusion(bf16[128,7168]{1,0:T(8,128)(2,1)} %param.17, s32[1024]{0:T(1024)S(1)} %pad_clamp_fusion), kind=kCustom, calls=%fused_computation.1 | custom fusion | bytes 917632 | tf_op jit(solution)/shard_map/gather | solution.py:35
  10.1 0.1 bitcast_select_fusion.1
  10.3 0.1 pad_maximum_fusion
  10.4 0.1 copy.25
  10.4 29.9 %all_to_all.10 = bf16[8,8,7168]{2,1,0:T(8,128)(2,1)S(1)} all-to-all(bf16[8,8,7168]{2,1,0:T(8,128)(2,1)S(1)} %bitcast.31), channel_id=1, replica_groups=mesh['dp'=4,'expert'=8] {'expert'}, dimensions={0} | all-to-all | bytes 1835008 | tf_op jit(solution)/shard_map/all_to_all | solution.py:229
  40.3 0.0 collective-permute-start
  40.3 2.5 %collective-permute-done = bf16[8,8,7168]{2,1,0:T(8,128)(2,1)S(1)} collective-permute-done((bf16[8,8,7168]{2,1,0:T(8,128)(2,1)S(1)}, bf16[8,8,7168]{2,1,0:T(8,128)(2,1)S(1)}, u32[]{:S(2)}, u32[]{:S(2)}) %collective-permute-start) | collective-permute-done | bytes 917536 | tf_op jit(solution)/shard_map/ppermute | solution.py:231
  42.8 1.3 %select_bitcast_fusion = (bf16[64,7168]{1,0:T(8,128)(2,1)}, bf16[64,7168]{1,0:T(8,128)(2,1)}) fusion(bf16[8,8,7168]{2,1,0:T(8,128)(2,1)S(1)} %collective-permute-done, bf16[8,8,7168]{2,1,0:T(8,128)(2,1)S(1)} %all_to_all.10, pred[]{:T(512)S(6)} %eq.49), kind=kLoop, calls=%fused_computation.13 | loop fusion | flops 917504 | bytes 3670017 | tf_op jit(solution)/shard_map/reshape | solution.py:234
  44.2 32.1 %shard_map.112 = (bf16[64,7168]{1,0:T(8,128)(2,1)}, bf16[64,7168]{1,0:T(8,128)(2,1)}) custom-call(bf16[64,7168]{1,0:T(8,128)(2,1)} %get-tuple-element.10.x_ref, bf16[64,7168]{1,0:T(8,128)(2,1)} %get-tuple-element.9.y_ref, bf16[7168,1024]{1,0:T(8,128)(2,1)} %g_ref.1, bf16[7168,1024]{1,0:T(8,128)(2,1)} %u_ref.1, bf16[1024,7168]{1,0:T(8,128)(2,1)} %d_ref.1), custom_call_target="tpu_custom_call" | custom-call | tf_op jit(solution)/shard_map/pallas_call | solution.py:110
  76.2 0.0 copy-start.5
  76.2 0.0 copy-start.2
  76.2 0.0 copy-start.3
  76.2 1.4 %broadcast_select_fusion = bf16[64,7168]{1,0:T(8,128)(2,1)S(1)} fusion(bf16[64,7168]{1,0:T(8,128)(2,1)} %get-tuple-element.6, bf16[64,7168]{1,0:T(8,128)(2,1)} %get-tuple-element.5, pred[]{:T(512)S(6)} %eq.49), kind=kLoop, calls=%fused_computation.15 | loop fusion | flops 458752 | bytes 2752513 | tf_op jit(solution)/shard_map/jit(_where)/select_n | solution.py:237
  77.7 0.2 collective-permute-start.1
  77.9 2.3 %collective-permute-done.1 = bf16[64,7168]{1,0:T(8,128)(2,1)S(1)} collective-permute-done((bf16[64,7168]{1,0:T(8,128)(2,1)S(1)}, bf16[64,7168]{1,0:T(8,128)(2,1)S(1)}, u32[]{:S(2)}, u32[]{:S(2)}) %collective-permute-start.1) | collective-permute-done | bytes 917536 | tf_op jit(solution)/shard_map/ppermute | solution.py:238
  80.2 2.4 %fusion.1 = bf16[8,8,7168]{2,1,0:T(8,128)(2,1)} fusion(bf16[64,7168]{1,0:T(8,128)(2,1)S(1)} %collective-permute-done.1, bf16[64,7168]{1,0:T(8,128)(2,1)} %get-tuple-element.5, bf16[64,7168]{1,0:T(8,128)(2,1)} %get-tuple-element.6, pred[]{:T(512)S(6)} %eq.49), kind=kLoop, calls=%fused_computation.11 | loop fusion | flops 2293760 | bytes 3670017 | tf_op jit(solution)/shard_map/reshape | solution.py:240
  82.6 3.7 %all-to-all-start.1 = ((bf16[8,8,7168]{2,1,0:T(8,128)(2,1)}), bf16[8,8,7168]{2,1,0:T(8,128)(2,1)S(1)}, u32[]{:S(2)}, u32[]{:S(2)}) async-start(bf16[8,8,7168]{2,1,0:T(8,128)(2,1)} %fusion.1), calls=%async_computation.1 | async-start | bytes 1835008 | tf_op jit(solution)/shard_map/all_to_all | solution.py:239
  86.4 0.0 copy-done.5
  86.4 0.0 copy-done.4
  86.4 23.4 %all-to-all-done.1 = bf16[8,8,7168]{2,1,0:T(8,128)(2,1)S(1)} async-done(((bf16[8,8,7168]{2,1,0:T(8,128)(2,1)}), bf16[8,8,7168]{2,1,0:T(8,128)(2,1)S(1)}, u32[]{:S(2)}, u32[]{:S(2)}) %all-to-all-start.1) | async-done | bytes 917536 | tf_op jit(solution)/shard_map/all_to_all | solution.py:239
  109.9 0.0 copy-done
  109.9 0.0 copy-done.2
  109.9 0.0 copy-done.3
  109.9 2.2 %multiply_reduce_fusion = (f32[128]{0:T(128)S(1)}, f32[128,7168]{1,0:T(8,128)S(1)}) fusion(bf16[128,7168]{1,0:T(8,128)(2,1)S(1)} %copy-done, f32[7168]{0:T(1024)S(1)} %copy-done.2, f32[7168]{0:T(1024)S(1)} %copy-done.3, bf16[4,2,8,7168]{3,2,1,0:T(8,128)(2,1)S(1)} %bitcast.32, f32[128,4]{0,1:T(4,128)S(1)} %select_reduce_fusion.1, s32[128,4]{0,1:T(4,128)S(1)} %add_select_fusion), kind=kOutput, calls=%fused_computation.6 | convolution fusion | flops 356917120 | bytes 6025728 | tf_op jit(solution)/shard_map/dot_general | solution.py:133
  112.1 0.0 copy-done.1
  112.1 2.6 %fusion.16 = (f32[7168]{0:T(1024)S(1)}, bf16[128,7168]{1,0:T(8,128)(2,1)}) fusion(f32[128]{0:T(128)S(1)} %broadcast_multiply_fusion, f32[128]{0:T(128)S(1)} %get-tuple-element.11, f32[7168]{0:T(1024)S(1)} %copy-done.2, bf16[128,7168]{1,0:T(8,128)(2,1)S(1)} %copy-done, f32[128,7168]{1,0:T(8,128)S(1)} %get-tuple-element.16, f32[128]{0:T(128)S(1)} %get-tuple-element.12, ...), kind=kLoop, calls=%fused_computation.45 | loop fusion | flops 9167872 | bytes 9233920 | tf_op jit(solution)/shard_map/reduce_sum | solution.py:282
  114.7 0.0 collective-permute-start.2
  114.7 1.2 collective-permute-done.2
  115.9 0.0 collective-permute-start.3
  115.9 3.9 %collective-permute-done.3 = f32[7168]{0:T(1024)S(1)} collective-permute-done((f32[7168]{0:T(1024)S(1)}, f32[7168]{0:T(1024)S(1)}, u32[]{:S(2)}, u32[]{:S(2)}) %collective-permute-start.3) | collective-permute-done | bytes 28704 | tf_op jit(solution)/shard_map/ppermute | solution.py:170
  119.8 0.0 collective-permute-start.4
  119.8 4.8 %collective-permute-done.4 = f32[7168]{0:T(1024)S(1)} collective-permute-done((f32[7168]{0:T(1024)S(1)}, f32[7168]{0:T(1024)S(1)}, u32[]{:S(2)}, u32[]{:S(2)}) %collective-permute-start.4) | collective-permute-done | bytes 28704 | tf_op jit(solution)/shard_map/ppermute | solution.py:170
  124.6 1.5 %collective-permute-start.5 = (f32[7168]{0:T(1024)S(1)}, f32[7168]{0:T(1024)S(1)}, u32[]{:S(2)}, u32[]{:S(2)}) collective-permute-start(f32[7168]{0:T(1024)S(1)} %add.77), channel_id=1, source_target_pairs={{0,8},{8,0},{16,24},{24,16},{1,9},{9,1},{17,25},{25,17},{2,10},{10... | collective-permute-start | bytes 86024 | tf_op jit(solution)/shard_map/ppermute | solution.py:170
  126.1 2.4 %collective-permute-done.5 = f32[7168]{0:T(1024)S(1)} collective-permute-done((f32[7168]{0:T(1024)S(1)}, f32[7168]{0:T(1024)S(1)}, u32[]{:S(2)}, u32[]{:S(2)}) %collective-permute-start.5) | collective-permute-done | bytes 28704 | tf_op jit(solution)/shard_map/ppermute | solution.py:170
  128.5 1.5 %collective-permute-start.6 = (f32[7168]{0:T(1024)S(1)}, f32[7168]{0:T(1024)S(1)}, u32[]{:S(2)}, u32[]{:S(2)}) collective-permute-start(f32[7168]{0:T(1024)S(1)} %add.78), channel_id=1, source_target_pairs={{0,16},{8,24},{16,0},{24,8},{1,17},{9,25},{17,1},{25,9},{2,18},{10... | collective-permute-start | bytes 86024 | tf_op jit(solution)/shard_map/ppermute | solution.py:170
  130.0 3.0 %fusion = bf16[128,7168]{1,0:T(8,128)(2,1)} fusion(bf16[128,7168]{1,0:T(8,128)(2,1)S(1)} %copy-done, f32[7168]{0:T(1024)S(1)} %copy-done.2, bf16[4,2,8,7168]{3,2,1,0:T(8,128)(2,1)S(1)} %bitcast.33, f32[128,4]{0,1:T(4,128)S(1)} %select_reduce_fusion.1, s32[128,4]{0,1:T(4,128)S(1)} %add_select_fusion), kind=kOutput, calls=%fused_computation.4 | convolution fusion | flops 355999744 | bytes 4161536 | tf_op jit(solution)/shard_map/dot_general | solution.py:133
  133.0 0.0 collective-permute-done.6
  133.0 0.6 add.79
  (15 shorter events, 0.1 us)
Async XLA Ops:
  40.3 2.5 %collective-permute-start = (bf16[8,8,7168]{2,1,0:T(8,128)(2,1)S(1)}, bf16[8,8,7168]{2,1,0:T(8,128)(2,1)S(1)}, u32[]{:S(2)}, u32[]{:S(2)}) collective-permute-start(bf16[8,8,7168]{2,1,0:T(8,128)(2,1)S(1)} %all_to_all.10), channel_id=1, source_target_pairs={{0,1},{1,0},{2,3},{3,2},{4,5},{5,4},{6,7},{7,6},{8,9},{9,8},{10,11... | collective-permute-start | bytes 2752520 | tf_op jit(solution)/shard_map/ppermute | solution.py:231
  76.2 10.2 %copy-start.5 = (s32[128,8]{0,1:T(8,128)S(1)}, s32[128,8]{0,1:T(8,128)}, u32[]{:S(2)}) copy-start(s32[128,8]{0,1:T(8,128)} %param.13) | copy-start | bytes 12292
  76.2 10.2 %copy-start.4 = (s32[128,8]{0,1:T(8,128)S(1)}, s32[128,8]{0,1:T(8,128)}, u32[]{:S(2)}) copy-start(s32[128,8]{0,1:T(8,128)} %param.12) | copy-start | bytes 12292
  76.2 33.7 %copy-start = (bf16[128,7168]{1,0:T(8,128)(2,1)S(1)}, bf16[128,7168]{1,0:T(8,128)(2,1)}, u32[]{:S(2)}) copy-start(bf16[128,7168]{1,0:T(8,128)(2,1)} %param.9) | copy-start | bytes 5505028
  76.2 33.7 %copy-start.2 = (f32[7168]{0:T(1024)S(1)}, f32[7168]{0:T(1024)}, u32[]{:S(2)}) copy-start(f32[7168]{0:T(1024)} %param.10) | copy-start | bytes 86020
  76.2 33.7 %copy-start.3 = (f32[7168]{0:T(1024)S(1)}, f32[7168]{0:T(1024)}, u32[]{:S(2)}) copy-start(f32[7168]{0:T(1024)} %param.11) | copy-start | bytes 86020
  77.7 2.5 %collective-permute-start.1 = (bf16[64,7168]{1,0:T(8,128)(2,1)S(1)}, bf16[64,7168]{1,0:T(8,128)(2,1)S(1)}, u32[]{:S(2)}, u32[]{:S(2)}) collective-permute-start(bf16[64,7168]{1,0:T(8,128)(2,1)S(1)} %broadcast_select_fusion), channel_id=1, source_target_pairs={{0,1},{1,0},{2,3},{3,2},{4,5},{5,4},{6,7},{7,6},{8,9},{9,8},{10,11... | collective-permute-start | bytes 2752520 | tf_op jit(solution)/shard_map/ppermute | solution.py:238
  82.6 27.2 %all-to-all-start.1 = ((bf16[8,8,7168]{2,1,0:T(8,128)(2,1)}), bf16[8,8,7168]{2,1,0:T(8,128)(2,1)S(1)}, u32[]{:S(2)}, u32[]{:S(2)}) async-start(bf16[8,8,7168]{2,1,0:T(8,128)(2,1)} %fusion.1), calls=%async_computation.1 | async-start | bytes 1835008 | tf_op jit(solution)/shard_map/all_to_all | solution.py:239
  109.9 2.2 %copy-start.1 = (bf16[128,7168]{1,0:T(8,128)(2,1)S(1)}, bf16[128,7168]{1,0:T(8,128)(2,1)}, u32[]{:S(2)}) copy-start(bf16[128,7168]{1,0:T(8,128)(2,1)} %param.17) | copy-start | bytes 5505028
  114.7 1.2 collective-permute-start.2
  115.9 3.9 %collective-permute-start.3 = (f32[7168]{0:T(1024)S(1)}, f32[7168]{0:T(1024)S(1)}, u32[]{:S(2)}, u32[]{:S(2)}) collective-permute-start(f32[7168]{0:T(1024)S(1)} %add.75), channel_id=1, source_target_pairs={{0,2},{1,3},{2,0},{3,1},{4,6},{5,7},{6,4},{7,5},{8,10},{9,11},{10,... | collective-permute-start | bytes 86024 | tf_op jit(solution)/shard_map/ppermute | solution.py:170
  119.8 4.8 %collective-permute-start.4 = (f32[7168]{0:T(1024)S(1)}, f32[7168]{0:T(1024)S(1)}, u32[]{:S(2)}, u32[]{:S(2)}) collective-permute-start(f32[7168]{0:T(1024)S(1)} %add.76), channel_id=1, source_target_pairs={{0,4},{1,5},{2,6},{3,7},{4,0},{5,1},{6,2},{7,3},{8,12},{9,13},{10,... | collective-permute-start | bytes 86024 | tf_op jit(solution)/shard_map/ppermute | solution.py:170
  124.6 3.9 %collective-permute-start.5 = (f32[7168]{0:T(1024)S(1)}, f32[7168]{0:T(1024)S(1)}, u32[]{:S(2)}, u32[]{:S(2)}) collective-permute-start(f32[7168]{0:T(1024)S(1)} %add.77), channel_id=1, source_target_pairs={{0,8},{8,0},{16,24},{24,16},{1,9},{9,1},{17,25},{25,17},{2,10},{10... | collective-permute-start | bytes 86024 | tf_op jit(solution)/shard_map/ppermute | solution.py:170
  128.5 4.5 %collective-permute-start.6 = (f32[7168]{0:T(1024)S(1)}, f32[7168]{0:T(1024)S(1)}, u32[]{:S(2)}, u32[]{:S(2)}) collective-permute-start(f32[7168]{0:T(1024)S(1)} %add.78), channel_id=1, source_target_pairs={{0,16},{8,24},{16,0},{24,8},{1,17},{9,25},{17,1},{25,9},{2,18},{10... | collective-permute-start | bytes 86024 | tf_op jit(solution)/shard_map/ppermute | solution.py:170

commit v6 on v5

--- a/solution.py
+++ b/solution.py
@@ -216,6 +216,27 @@
     return out_sums, grad_sums
 
 
+def exchange(chunks, axis):
+    size = lax.axis_size(axis)
+    me = lax.axis_index(axis)
+    moved = [lax.dynamic_index_in_dim(chunks, me, 0, keepdims=False)]
+    for shift in range(1, size):
+        part = lax.dynamic_index_in_dim(chunks, (me + shift) % size, 0, keepdims=False)
+        moved.append(lax.ppermute(part, axis, [(i, (i + shift) % size) for i in range(size)]))
+    stacked = jnp.stack(moved)
+    order = (me - jnp.arange(size, dtype=jnp.int32)) % size
+    return jnp.take(stacked, order, axis=0)
+
+
+def pick_rows(values, slot_table, filled):
+    token_range = jnp.arange(values.shape[0], dtype=jnp.int32)
+    onehot = (slot_table[:, :, None] == token_range[None, None, :]) & filled[:, :, None]
+    picked = jnp.einsum(
+        "fct,td->fcd", onehot.astype(values.dtype), values, preferred_element_type=jnp.float32
+    )
+    return picked.astype(values.dtype)
+
+
 def by_pair(
     normed, out_grad, slot_table, filled, gate_weight, up_weight, down_weight,
     member, expert_count, group_size,
@@ -223,10 +244,10 @@
     flight, capacity = slot_table.shape
     feature_count = normed.shape[1]
     sending = jnp.stack(
-        [dispatch_rows(normed, slot_table, filled), dispatch_rows(out_grad, slot_table, filled)],
+        [pick_rows(normed, slot_table, filled), pick_rows(out_grad, slot_table, filled)],
         axis=1,
     ).reshape(expert_count, capacity, feature_count)
-    arrived = lax.all_to_all(sending, "expert", split_axis=0, concat_axis=0, tiled=True)
+    arrived = exchange(sending, "expert")
     swap = group_perm(expert_count, group_size, 1)
     partner = lax.ppermute(arrived, "expert", swap)
     first = member == 0
@@ -236,9 +257,8 @@
     keep = jnp.where(first, forward, backward)
     give = jnp.where(first, backward, forward)
     total = keep.astype(jnp.float32) + lax.ppermute(give, "expert", swap).astype(jnp.float32)
-    came = lax.all_to_all(
-        total.astype(jnp.bfloat16).reshape(expert_count, capacity, feature_count),
-        "expert", split_axis=0, concat_axis=0, tiled=True,
+    came = exchange(
+        total.astype(jnp.bfloat16).reshape(expert_count, capacity, feature_count), "expert"
     ).reshape(flight, 2, capacity, feature_count)
     out_sums = came[:, 0].reshape(flight * capacity, feature_count).astype(jnp.float32)
     grad_sums = came[:, 1].reshape(flight * capacity, feature_count).astype(jnp.float32)

time: 134 us -> 130 us (0.970)
  blocking collectives: 29.9 us -> 0 us
  starting transfers between devices: 6.95 us -> 36 us
  waiting for transfers between devices: 40.5 us -> 24.5 us
  local copies, waits for them, and re-layouts: 4.17 us -> 14.4 us
  matrix products: 5.15 us -> 7.84 us
    all_to_all x1 -> x0, blocking collectives: 29.9 us -> none  [by_pair(): lax.all_to_all(sending, 'expert', split_axis=0, concat_axis=0, tiled=True)]
    ppermute x0 -> x14, starting transfers between devices: none -> 23.9 us  [exchange(): lax.ppermute(part, axis, [(i, (i + shift) % size) for i in range(size)])]
    all_to_all x1 -> x0, waiting for transfers between devices: 23.4 us -> none  [by_pair(): lax.all_to_all(total.astype(jnp.bfloat16).reshape(expert_count, capacity,...]
    ppermute x0 -> x14, waiting for transfers between devices: none -> 11.4 us  [exchange(): lax.ppermute(part, axis, [(i, (i + shift) % size) for i in range(size)])]
    unnamed x12 -> x24, local copies, waits for them, and re-layouts: 0.03 us -> 7.88 us
    ppermute x5, starting transfers between devices: 3.02 us -> 10.1 us  [butterfly_sum(): lax.ppermute(value, axis, [(i, i ^ bit) for i in range(size)])]
    all_to_all x1 -> x0, starting transfers between devices: 3.73 us -> none  [by_pair(): lax.all_to_all(total.astype(jnp.bfloat16).reshape(expert_count, capacity,...]
    ppermute x5, waiting for transfers between devices: 12.2 us -> 8.51 us  [butterfly_sum(): lax.ppermute(value, axis, [(i, i ^ bit) for i in range(size)])]
  transfers between devices with their start and end apart: 8 -> 21, of which waited for: 7 -> 8; matrix products, arithmetic and copies ran while one was open for 2% -> 8% of each run, Pallas kernels for 0% -> 0%
where the time goes in v6:
time: 130 us; the launch traced here: 129 us
  starting transfers between devices  36 us (28%)
  Pallas kernels  32.1 us (25%)
  waiting for transfers between devices  24.5 us (19%)
  local copies, waits for them, and re-layouts  14.4 us (11%)
  other arithmetic  13.4 us (10%)
  matrix products  7.84 us (6%)
    pallas_call x1, Pallas kernels, expert_share(): pl.pallas_call(_expert_kernel, grid=(rows // rb, hid // hb), in_specs=[pl...  32.1 us
    ppermute x14, starting transfers between devices, exchange(): lax.ppermute(part, axis, [(i, (i + shift) % size) for i in range(size)])  23.9 us
    ppermute x14, waiting for transfers between devices, exchange(): lax.ppermute(part, axis, [(i, (i + shift) % size) for i in range(size)])  11.4 us
    ppermute x5, starting transfers between devices, butterfly_sum(): lax.ppermute(value, axis, [(i, i ^ bit) for i in range(size)])  10.1 us
    ppermute x5, waiting for transfers between devices, butterfly_sum(): lax.ppermute(value, axis, [(i, i ^ bit) for i in range(size)])  8.51 us
    unnamed x24, local copies, waits for them, and re-layouts  7.88 us
    dot_general x2, matrix products, apply_combine(): return jnp.dot(combine, partial_sums, precision=lax.Precision.HIGHEST)  5.15 us
    gather x2, local copies, waits for them, and re-layouts, exchange(): return jnp.take(stacked, order, axis=0)  3.57 us
  transfers between devices with their start and end apart: 21, of which 8 were waited for; matrix products, arithmetic and copies ran while one was open for 8% of the time, Pallas kernels for 0%

profile of v6, /device:TPU:0, one launch (start us, length us, event | category | flops | bytes accessed | tf_op | source)
XLA Modules:
  0.0 129.3 jit_solution(12645677519723572821)
XLA Ops:
  0.8 0.8 fusion.15
  2.3 2.1 %multiply_reduce_fusion.1 = f32[128]{0:T(128)S(1)} fusion(bf16[128,7168]{1,0:T(8,128)(2,1)} %param.11, f32[7168]{0:T(1024)} %param.12), kind=kLoop, calls=%fused_computation.12 | loop fusion | flops 3669888 | bytes 1864192 | tf_op jit(solution)/shard_map/reduce_sum | solution.py:41
  4.3 1.9 %fusion.2 = bf16[4,1,8,7168]{3,2,0,1:T(8,128)(2,1)S(1)} fusion(bf16[128,7168]{1,0:T(8,128)(2,1)} %param.19, s32[4,8]{1,0:T(4,128)S(1)} %select_reduce_fusion, pred[4,8]{1,0:T(4,128)(4,1)S(1)} %fusion.14), kind=kOutput, calls=%fused_computation.8 | convolution fusion | flops 58957824 | bytes 2293920 | tf_op jit(solution)/shard_map/fct,td->fcd/dot_general | solution.py:234
  6.3 0.8 fusion.1
  7.3 0.7 dynamic-slice_bitcast_fusion.7
  8.5 2.6 %collective-permute-start.1 = (bf16[8,7168]{1,0:T(8,128)(2,1)S(1)}, bf16[8,7168]{1,0:T(8,128)(2,1)S(1)}, u32[]{:S(2)}, u32[]{:S(2)}) collective-permute-start(bf16[8,7168]{1,0:T(8,128)(2,1)S(1)} %get-tuple-element.25), channel_id=1, source_target_pairs={{0,2},{1,3},{2,4},{3,5},{4,6},{5,7},{6,0},{7,1},{8,10},{9,11},{10,... | collective-permute-start | bytes 344072 | tf_op jit(solution)/shard_map/ppermute | solution.py:225
  11.1 2.6 %collective-permute-start.2 = (bf16[8,7168]{1,0:T(8,128)(2,1)S(1)}, bf16[8,7168]{1,0:T(8,128)(2,1)S(1)}, u32[]{:S(2)}, u32[]{:S(2)}) collective-permute-start(bf16[8,7168]{1,0:T(8,128)(2,1)S(1)} %get-tuple-element.24), channel_id=1, source_target_pairs={{0,3},{1,4},{2,5},{3,6},{4,7},{5,0},{6,1},{7,2},{8,11},{9,12},{10,... | collective-permute-start | bytes 344072 | tf_op jit(solution)/shard_map/ppermute | solution.py:225
  13.6 1.2 collective-permute-start.3
  14.9 1.1 collective-permute-start.4
  16.1 1.9 %collective-permute-start.5 = (bf16[8,7168]{1,0:T(8,128)(2,1)S(1)}, bf16[8,7168]{1,0:T(8,128)(2,1)S(1)}, u32[]{:S(2)}, u32[]{:S(2)}) collective-permute-start(bf16[8,7168]{1,0:T(8,128)(2,1)S(1)} %get-tuple-element.21), channel_id=1, source_target_pairs={{0,6},{1,7},{2,0},{3,1},{4,2},{5,3},{6,4},{7,5},{8,14},{9,15},{10,... | collective-permute-start | bytes 344072 | tf_op jit(solution)/shard_map/ppermute | solution.py:225
  18.6 1.2 collective-permute-start.6
  20.5 5.6 %collective-permute-done.2 = bf16[8,7168]{1,0:T(8,128)(2,1)S(1)} collective-permute-done((bf16[8,7168]{1,0:T(8,128)(2,1)S(1)}, bf16[8,7168]{1,0:T(8,128)(2,1)S(1)}, u32[]{:S(2)}, u32[]{:S(2)}) %collective-permute-start.2) | collective-permute-done | bytes 114720 | tf_op jit(solution)/shard_map/ppermute | solution.py:225
  26.7 0.7 bitcast_dynamic-update-slice_fusion.10
  27.4 0.7 bitcast_dynamic-update-slice_fusion.9
  28.0 0.7 bitcast_dynamic-update-slice_fusion.8
  28.7 0.7 bitcast_dynamic-update-slice_fusion.7
  29.3 1.8 %gather_fusion = bf16[8,8,7168]{2,1,0:T(8,128)(2,1)S(1)} fusion(bf16[8,8,7168]{2,1,0:T(8,128)(2,1)} %bitcast_dynamic-update-slice_fusion.7, s32[1024]{0:T(1024)S(1)} %pad_clamp_fusion), kind=kCustom, calls=%fused_computation.clone | custom fusion | bytes 1835040 | tf_op jit(solution)/shard_map/jit(_take)/gather | solution.py:228
  31.1 1.1 broadcast_select_fusion
  32.2 1.6 %collective-permute-start.7 = (bf16[8,8,7168]{2,1,0:T(8,128)(2,1)}, bf16[8,8,7168]{2,1,0:T(8,128)(2,1)}, u32[]{:S(2)}, u32[]{:S(2)}) collective-permute-start(bf16[8,8,7168]{2,1,0:T(8,128)(2,1)} %broadcast_select_fusion), channel_id=1, source_target_pairs={{0,1},{1,0},{2,3},{3,2},{4,5},{5,4},{6,7},{7,6},{8,9},{9,8},{10,11... | collective-permute-start | bytes 2752520 | tf_op jit(solution)/shard_map/ppermute | solution.py:252
  33.8 2.4 %collective-permute-done.7 = bf16[8,8,7168]{2,1,0:T(8,128)(2,1)} collective-permute-done((bf16[8,8,7168]{2,1,0:T(8,128)(2,1)}, bf16[8,8,7168]{2,1,0:T(8,128)(2,1)}, u32[]{:S(2)}, u32[]{:S(2)}) %collective-permute-start.7) | collective-permute-done | bytes 917536 | tf_op jit(solution)/shard_map/ppermute | solution.py:252
  36.3 2.6 %select_bitcast_fusion = (bf16[64,7168]{1,0:T(8,128)(2,1)}, bf16[64,7168]{1,0:T(8,128)(2,1)}) fusion(bf16[8,8,7168]{2,1,0:T(8,128)(2,1)} %collective-permute-done.7, pred[]{:T(512)S(6)} %eq.86, bf16[8,8,7168]{2,1,0:T(8,128)(2,1)S(1)} %gather_fusion, pred[8]{0:T(512)(128)(4,1)S(1)} %compare_and_fusion), kind=kLoop, calls=%fused_computation.22 | loop fusion | flops 1376256 | bytes 3670025 | tf_op jit(solution)/shard_map/reshape | solution.py:255
  38.9 32.1 %shard_map.112 = (bf16[64,7168]{1,0:T(8,128)(2,1)}, bf16[64,7168]{1,0:T(8,128)(2,1)}) custom-call(bf16[64,7168]{1,0:T(8,128)(2,1)} %get-tuple-element.11.x_ref, bf16[64,7168]{1,0:T(8,128)(2,1)} %get-tuple-element.10.y_ref, bf16[7168,1024]{1,0:T(8,128)(2,1)} %g_ref.1, bf16[7168,1024]{1,0:T(8,128)(2,1)} %u_ref.1, bf16[1024,7168]{1,0:T(8,128)(2,1)} %d_ref.1), custom_call_target="tpu_custom_call" | custom-call | tf_op jit(solution)/shard_map/pallas_call | solution.py:110
  70.9 1.3 %broadcast_select_fusion.2 = bf16[64,7168]{1,0:T(8,128)(2,1)S(1)} fusion(bf16[64,7168]{1,0:T(8,128)(2,1)} %get-tuple-element.7, bf16[64,7168]{1,0:T(8,128)(2,1)} %get-tuple-element.6, pred[]{:T(512)S(6)} %eq.86), kind=kLoop, calls=%fused_computation.26 | loop fusion | flops 458752 | bytes 2752513 | tf_op jit(solution)/shard_map/jit(_where)/select_n | solution.py:258
  72.7 2.1 %collective-permute-done.8 = bf16[64,7168]{1,0:T(8,128)(2,1)S(1)} collective-permute-done((bf16[64,7168]{1,0:T(8,128)(2,1)S(1)}, bf16[64,7168]{1,0:T(8,128)(2,1)S(1)}, u32[]{:S(2)}, u32[]{:S(2)}) %collective-permute-start.8) | collective-permute-done | bytes 917536 | tf_op jit(solution)/shard_map/ppermute | solution.py:259
  74.8 1.5 %fusion.9 = bf16[8,8,7168]{2,1,0:T(8,128)(2,1)S(1)} fusion(bf16[64,7168]{1,0:T(8,128)(2,1)S(1)} %collective-permute-done.8, bf16[64,7168]{1,0:T(8,128)(2,1)} %get-tuple-element.6, bf16[64,7168]{1,0:T(8,128)(2,1)} %get-tuple-element.7, pred[]{:T(512)S(6)} %eq.86), kind=kLoop, calls=%fused_computation.20 | loop fusion | flops 2293760 | bytes 3670017 | tf_op jit(solution)/shard_map/reshape | solution.py:261
  76.3 0.7 dynamic-slice_bitcast_fusion
  77.4 4.2 %collective-permute-start.10 = (bf16[8,7168]{1,0:T(8,128)(2,1)S(1)}, bf16[8,7168]{1,0:T(8,128)(2,1)S(1)}, u32[]{:S(2)}, u32[]{:S(2)}) collective-permute-start(bf16[8,7168]{1,0:T(8,128)(2,1)S(1)} %get-tuple-element.17), channel_id=1, source_target_pairs={{0,2},{1,3},{2,4},{3,5},{4,6},{5,7},{6,0},{7,1},{8,10},{9,11},{10,... | collective-permute-start | bytes 344072 | tf_op jit(solution)/shard_map/ppermute | solution.py:225
  81.6 2.6 %collective-permute-start.11 = (bf16[8,7168]{1,0:T(8,128)(2,1)S(1)}, bf16[8,7168]{1,0:T(8,128)(2,1)S(1)}, u32[]{:S(2)}, u32[]{:S(2)}) collective-permute-start(bf16[8,7168]{1,0:T(8,128)(2,1)S(1)} %get-tuple-element.16), channel_id=1, source_target_pairs={{0,3},{1,4},{2,5},{3,6},{4,7},{5,0},{6,1},{7,2},{8,11},{9,12},{10,... | collective-permute-start | bytes 344072 | tf_op jit(solution)/shard_map/ppermute | solution.py:225
  84.2 0.9 collective-permute-start.12
  85.1 1.8 %collective-permute-start.13 = (bf16[8,7168]{1,0:T(8,128)(2,1)S(1)}, bf16[8,7168]{1,0:T(8,128)(2,1)S(1)}, u32[]{:S(2)}, u32[]{:S(2)}) collective-permute-start(bf16[8,7168]{1,0:T(8,128)(2,1)S(1)} %get-tuple-element.14), channel_id=1, source_target_pairs={{0,5},{1,6},{2,7},{3,0},{4,1},{5,2},{6,3},{7,4},{8,13},{9,14},{10,... | collective-permute-start | bytes 344072 | tf_op jit(solution)/shard_map/ppermute | solution.py:225
  86.9 1.0 collective-permute-start.14
  88.6 1.9 %collective-permute-start.15 = (bf16[8,7168]{1,0:T(8,128)(2,1)S(1)}, bf16[8,7168]{1,0:T(8,128)(2,1)S(1)}, u32[]{:S(2)}, u32[]{:S(2)}) collective-permute-start(bf16[8,7168]{1,0:T(8,128)(2,1)S(1)} %get-tuple-element.12), channel_id=1, source_target_pairs={{0,7},{1,0},{2,1},{3,2},{4,3},{5,4},{6,5},{7,6},{8,15},{9,8},{10,9... | collective-permute-start | bytes 344072 | tf_op jit(solution)/shard_map/ppermute | solution.py:225
  91.1 5.8 %collective-permute-done.11 = bf16[8,7168]{1,0:T(8,128)(2,1)S(1)} collective-permute-done((bf16[8,7168]{1,0:T(8,128)(2,1)S(1)}, bf16[8,7168]{1,0:T(8,128)(2,1)S(1)}, u32[]{:S(2)}, u32[]{:S(2)}) %collective-permute-start.11) | collective-permute-done | bytes 114720 | tf_op jit(solution)/shard_map/ppermute | solution.py:225
  98.3 0.7 bitcast_dynamic-update-slice_fusion.2
  98.9 0.7 bitcast_dynamic-update-slice_fusion.1
  100.2 1.8 %gather_fusion.1 = bf16[8,8,7168]{2,1,0:T(8,128)(2,1)S(1)} fusion(bf16[8,8,7168]{2,1,0:T(8,128)(2,1)} %bitcast_dynamic-update-slice_fusion, s32[1024]{0:T(1024)S(1)} %pad_clamp_fusion), kind=kCustom, calls=%fused_computation.1.clone | custom fusion | bytes 1835040 | tf_op jit(solution)/shard_map/jit(_take)/gather | solution.py:228
  102.2 2.2 %multiply_reduce_fusion = (f32[128]{0:T(128)S(1)}, f32[128,7168]{1,0:T(8,128)S(1)}) fusion(bf16[128,7168]{1,0:T(8,128)(2,1)S(1)} %copy-done, f32[7168]{0:T(1024)S(1)} %copy-done.2, f32[7168]{0:T(1024)S(1)} %copy-done.3, bf16[4,2,8,7168]{3,2,1,0:T(8,128)(2,1)S(1)} %bitcast.90, f32[128,4]{0,1:T(4,128)S(1)} %select_reduce_fusion.1, ...), kind=kOutput, calls=%fused_computation.10 | convolution fusion | flops 356917120 | bytes 6025728 | tf_op jit(solution)/shard_map/dot_general | solution.py:133
  104.4 2.6 %fusion.32 = (f32[7168]{0:T(1024)S(1)}, bf16[128,7168]{1,0:T(8,128)(2,1)}) fusion(f32[128]{0:T(128)S(1)} %broadcast_multiply_fusion, f32[128]{0:T(128)S(1)} %get-tuple-element.28, f32[7168]{0:T(1024)S(1)} %copy-done.2, bf16[128,7168]{1,0:T(8,128)(2,1)S(1)} %copy-done, f32[128,7168]{1,0:T(8,128)S(1)} %get-tuple-element.31, f32[128]{0:T(128)S(1)} %get-tuple-element.29, ...), kind=kLoop, calls=%fused_computation.95 | loop fusion | flops 9167872 | bytes 9233920 | tf_op jit(solution)/shard_map/reduce_sum | solution.py:302
  107.0 1.6 %collective-permute-start.16 = (f32[7168]{0:T(1024)S(1)}, f32[7168]{0:T(1024)S(1)}, u32[]{:S(2)}, u32[]{:S(2)}) collective-permute-start(f32[7168]{0:T(1024)S(1)} %get-tuple-element.8), channel_id=1, source_target_pairs={{0,1},{1,0},{2,3},{3,2},{4,5},{5,4},{6,7},{7,6},{8,9},{9,8},{10,11... | collective-permute-start | bytes 86024 | tf_op jit(solution)/shard_map/ppermute | solution.py:170
  108.6 0.9 collective-permute-done.16
  109.5 4.2 %collective-permute-start.17 = (f32[7168]{0:T(1024)S(1)}, f32[7168]{0:T(1024)S(1)}, u32[]{:S(2)}, u32[]{:S(2)}) collective-permute-start(f32[7168]{0:T(1024)S(1)} %add.186), channel_id=1, source_target_pairs={{0,2},{1,3},{2,0},{3,1},{4,6},{5,7},{6,4},{7,5},{8,10},{9,11},{10,... | collective-permute-start | bytes 86024 | tf_op jit(solution)/shard_map/ppermute | solution.py:170
  113.7 1.8 %collective-permute-done.17 = f32[7168]{0:T(1024)S(1)} collective-permute-done((f32[7168]{0:T(1024)S(1)}, f32[7168]{0:T(1024)S(1)}, u32[]{:S(2)}, u32[]{:S(2)}) %collective-permute-start.17) | collective-permute-done | bytes 28704 | tf_op jit(solution)/shard_map/ppermute | solution.py:170
  115.5 1.3 %collective-permute-start.18 = (f32[7168]{0:T(1024)S(1)}, f32[7168]{0:T(1024)S(1)}, u32[]{:S(2)}, u32[]{:S(2)}) collective-permute-start(f32[7168]{0:T(1024)S(1)} %add.187), channel_id=1, source_target_pairs={{0,4},{1,5},{2,6},{3,7},{4,0},{5,1},{6,2},{7,3},{8,12},{9,13},{10,... | collective-permute-start | bytes 86024 | tf_op jit(solution)/shard_map/ppermute | solution.py:170
  116.9 3.4 %collective-permute-done.18 = f32[7168]{0:T(1024)S(1)} collective-permute-done((f32[7168]{0:T(1024)S(1)}, f32[7168]{0:T(1024)S(1)}, u32[]{:S(2)}, u32[]{:S(2)}) %collective-permute-start.18) | collective-permute-done | bytes 28704 | tf_op jit(solution)/shard_map/ppermute | solution.py:170
  120.3 1.5 %collective-permute-start.19 = (f32[7168]{0:T(1024)S(1)}, f32[7168]{0:T(1024)S(1)}, u32[]{:S(2)}, u32[]{:S(2)}) collective-permute-start(f32[7168]{0:T(1024)S(1)} %add.188), channel_id=1, source_target_pairs={{0,8},{8,0},{16,24},{24,16},{1,9},{9,1},{17,25},{25,17},{2,10},{10... | collective-permute-start | bytes 86024 | tf_op jit(solution)/shard_map/ppermute | solution.py:170
  121.8 2.4 %collective-permute-done.19 = f32[7168]{0:T(1024)S(1)} collective-permute-done((f32[7168]{0:T(1024)S(1)}, f32[7168]{0:T(1024)S(1)}, u32[]{:S(2)}, u32[]{:S(2)}) %collective-permute-start.19) | collective-permute-done | bytes 28704 | tf_op jit(solution)/shard_map/ppermute | solution.py:170
  124.2 1.5 %collective-permute-start.20 = (f32[7168]{0:T(1024)S(1)}, f32[7168]{0:T(1024)S(1)}, u32[]{:S(2)}, u32[]{:S(2)}) collective-permute-start(f32[7168]{0:T(1024)S(1)} %add.189), channel_id=1, source_target_pairs={{0,16},{8,24},{16,0},{24,8},{1,17},{9,25},{17,1},{25,9},{2,18},{10... | collective-permute-start | bytes 86024 | tf_op jit(solution)/shard_map/ppermute | solution.py:170
  125.7 3.0 %fusion = bf16[128,7168]{1,0:T(8,128)(2,1)} fusion(bf16[128,7168]{1,0:T(8,128)(2,1)S(1)} %copy-done, f32[7168]{0:T(1024)S(1)} %copy-done.2, bf16[4,2,8,7168]{3,2,1,0:T(8,128)(2,1)S(1)} %bitcast.91, f32[128,4]{0,1:T(4,128)S(1)} %select_reduce_fusion.1, s32[128,4]{0,1:T(4,128)S(1)} %add_select_fusion), kind=kOutput, calls=%fused_computation.4 | convolution fusion | flops 355999744 | bytes 4161536 | tf_op jit(solution)/shard_map/dot_general | solution.py:133
  (58 shorter events, 8.3 us)
Async XLA Ops:
  0.6 5.6 %copy-start = (bf16[128,7168]{1,0:T(8,128)(2,1)S(1)}, bf16[128,7168]{1,0:T(8,128)(2,1)}, u32[]{:S(2)}) copy-start(bf16[128,7168]{1,0:T(8,128)(2,1)} %param.11) | copy-start | bytes 5505028
  0.6 5.6 %copy-start.2 = (f32[7168]{0:T(1024)S(1)}, f32[7168]{0:T(1024)}, u32[]{:S(2)}) copy-start(f32[7168]{0:T(1024)} %param.12) | copy-start | bytes 86020
  0.7 5.6 %copy-start.3 = (f32[7168]{0:T(1024)S(1)}, f32[7168]{0:T(1024)}, u32[]{:S(2)}) copy-start(f32[7168]{0:T(1024)} %param.13) | copy-start | bytes 86020
  8.0 8.1 %collective-permute-start = (bf16[8,7168]{1,0:T(8,128)(2,1)S(1)}, bf16[8,7168]{1,0:T(8,128)(2,1)S(1)}, u32[]{:S(2)}, u32[]{:S(2)}) collective-permute-start(bf16[8,7168]{1,0:T(8,128)(2,1)S(1)} %get-tuple-element.26), channel_id=1, source_target_pairs={{0,1},{1,2},{2,3},{3,4},{4,5},{5,6},{6,7},{7,0},{8,9},{9,10},{10,1... | collective-permute-start | bytes 344072 | tf_op jit(solution)/shard_map/ppermute | solution.py:225
  8.5 10.1 %collective-permute-start.1 = (bf16[8,7168]{1,0:T(8,128)(2,1)S(1)}, bf16[8,7168]{1,0:T(8,128)(2,1)S(1)}, u32[]{:S(2)}, u32[]{:S(2)}) collective-permute-start(bf16[8,7168]{1,0:T(8,128)(2,1)S(1)} %get-tuple-element.25), channel_id=1, source_target_pairs={{0,2},{1,3},{2,4},{3,5},{4,6},{5,7},{6,0},{7,1},{8,10},{9,11},{10,... | collective-permute-start | bytes 344072 | tf_op jit(solution)/shard_map/ppermute | solution.py:225
  11.1 15.0 %collective-permute-start.2 = (bf16[8,7168]{1,0:T(8,128)(2,1)S(1)}, bf16[8,7168]{1,0:T(8,128)(2,1)S(1)}, u32[]{:S(2)}, u32[]{:S(2)}) collective-permute-start(bf16[8,7168]{1,0:T(8,128)(2,1)S(1)} %get-tuple-element.24), channel_id=1, source_target_pairs={{0,3},{1,4},{2,5},{3,6},{4,7},{5,0},{6,1},{7,2},{8,11},{9,12},{10,... | collective-permute-start | bytes 344072 | tf_op jit(solution)/shard_map/ppermute | solution.py:225
  13.6 13.1 %collective-permute-start.3 = (bf16[8,7168]{1,0:T(8,128)(2,1)S(1)}, bf16[8,7168]{1,0:T(8,128)(2,1)S(1)}, u32[]{:S(2)}, u32[]{:S(2)}) collective-permute-start(bf16[8,7168]{1,0:T(8,128)(2,1)S(1)} %get-tuple-element.23), channel_id=1, source_target_pairs={{0,4},{1,5},{2,6},{3,7},{4,0},{5,1},{6,2},{7,3},{8,12},{9,13},{10,... | collective-permute-start | bytes 344072 | tf_op jit(solution)/shard_map/ppermute | solution.py:225
  14.9 12.5 %collective-permute-start.4 = (bf16[8,7168]{1,0:T(8,128)(2,1)S(1)}, bf16[8,7168]{1,0:T(8,128)(2,1)S(1)}, u32[]{:S(2)}, u32[]{:S(2)}) collective-permute-start(bf16[8,7168]{1,0:T(8,128)(2,1)S(1)} %get-tuple-element.22), channel_id=1, source_target_pairs={{0,5},{1,6},{2,7},{3,0},{4,1},{5,2},{6,3},{7,4},{8,13},{9,14},{10,... | collective-permute-start | bytes 344072 | tf_op jit(solution)/shard_map/ppermute | solution.py:225
  16.1 12.0 %collective-permute-start.5 = (bf16[8,7168]{1,0:T(8,128)(2,1)S(1)}, bf16[8,7168]{1,0:T(8,128)(2,1)S(1)}, u32[]{:S(2)}, u32[]{:S(2)}) collective-permute-start(bf16[8,7168]{1,0:T(8,128)(2,1)S(1)} %get-tuple-element.21), channel_id=1, source_target_pairs={{0,6},{1,7},{2,0},{3,1},{4,2},{5,3},{6,4},{7,5},{8,14},{9,15},{10,... | collective-permute-start | bytes 344072 | tf_op jit(solution)/shard_map/ppermute | solution.py:225
  18.6 10.1 %collective-permute-start.6 = (bf16[8,7168]{1,0:T(8,128)(2,1)S(1)}, bf16[8,7168]{1,0:T(8,128)(2,1)S(1)}, u32[]{:S(2)}, u32[]{:S(2)}) collective-permute-start(bf16[8,7168]{1,0:T(8,128)(2,1)S(1)} %get-tuple-element.20), channel_id=1, source_target_pairs={{0,7},{1,0},{2,1},{3,2},{4,3},{5,4},{6,5},{7,6},{8,15},{9,8},{10,9... | collective-permute-start | bytes 344072 | tf_op jit(solution)/shard_map/ppermute | solution.py:225
  32.2 4.1 %collective-permute-start.7 = (bf16[8,8,7168]{2,1,0:T(8,128)(2,1)}, bf16[8,8,7168]{2,1,0:T(8,128)(2,1)}, u32[]{:S(2)}, u32[]{:S(2)}) collective-permute-start(bf16[8,8,7168]{2,1,0:T(8,128)(2,1)} %broadcast_select_fusion), channel_id=1, source_target_pairs={{0,1},{1,0},{2,3},{3,2},{4,5},{5,4},{6,7},{7,6},{8,9},{9,8},{10,11... | collective-permute-start | bytes 2752520 | tf_op jit(solution)/shard_map/ppermute | solution.py:252
  70.9 6.5 %copy-start.5 = (s32[128,8]{0,1:T(8,128)S(1)}, s32[128,8]{0,1:T(8,128)}, u32[]{:S(2)}) copy-start(s32[128,8]{0,1:T(8,128)} %param.15) | copy-start | bytes 12292
  70.9 6.5 %copy-start.4 = (s32[128,8]{0,1:T(8,128)S(1)}, s32[128,8]{0,1:T(8,128)}, u32[]{:S(2)}) copy-start(s32[128,8]{0,1:T(8,128)} %param.14) | copy-start | bytes 12292
  72.2 2.5 %collective-permute-start.8 = (bf16[64,7168]{1,0:T(8,128)(2,1)S(1)}, bf16[64,7168]{1,0:T(8,128)(2,1)S(1)}, u32[]{:S(2)}, u32[]{:S(2)}) collective-permute-start(bf16[64,7168]{1,0:T(8,128)(2,1)S(1)} %broadcast_select_fusion.2), channel_id=1, source_target_pairs={{0,1},{1,0},{2,3},{3,2},{4,5},{5,4},{6,7},{7,6},{8,9},{9,8},{10,11... | collective-permute-start | bytes 2752520 | tf_op jit(solution)/shard_map/ppermute | solution.py:259
  77.0 9.9 %collective-permute-start.9 = (bf16[8,7168]{1,0:T(8,128)(2,1)S(1)}, bf16[8,7168]{1,0:T(8,128)(2,1)S(1)}, u32[]{:S(2)}, u32[]{:S(2)}) collective-permute-start(bf16[8,7168]{1,0:T(8,128)(2,1)S(1)} %get-tuple-element.18), channel_id=1, source_target_pairs={{0,1},{1,2},{2,3},{3,4},{4,5},{5,6},{6,7},{7,0},{8,9},{9,10},{10,1... | collective-permute-start | bytes 344072 | tf_op jit(solution)/shard_map/ppermute | solution.py:225
  77.4 11.2 %collective-permute-start.10 = (bf16[8,7168]{1,0:T(8,128)(2,1)S(1)}, bf16[8,7168]{1,0:T(8,128)(2,1)S(1)}, u32[]{:S(2)}, u32[]{:S(2)}) collective-permute-start(bf16[8,7168]{1,0:T(8,128)(2,1)S(1)} %get-tuple-element.17), channel_id=1, source_target_pairs={{0,2},{1,3},{2,4},{3,5},{4,6},{5,7},{6,0},{7,1},{8,10},{9,11},{10,... | collective-permute-start | bytes 344072 | tf_op jit(solution)/shard_map/ppermute | solution.py:225
  81.6 15.4 %collective-permute-start.11 = (bf16[8,7168]{1,0:T(8,128)(2,1)S(1)}, bf16[8,7168]{1,0:T(8,128)(2,1)S(1)}, u32[]{:S(2)}, u32[]{:S(2)}) collective-permute-start(bf16[8,7168]{1,0:T(8,128)(2,1)S(1)} %get-tuple-element.16), channel_id=1, source_target_pairs={{0,3},{1,4},{2,5},{3,6},{4,7},{5,0},{6,1},{7,2},{8,11},{9,12},{10,... | collective-permute-start | bytes 344072 | tf_op jit(solution)/shard_map/ppermute | solution.py:225
  84.2 13.4 %collective-permute-start.12 = (bf16[8,7168]{1,0:T(8,128)(2,1)S(1)}, bf16[8,7168]{1,0:T(8,128)(2,1)S(1)}, u32[]{:S(2)}, u32[]{:S(2)}) collective-permute-start(bf16[8,7168]{1,0:T(8,128)(2,1)S(1)} %get-tuple-element.15), channel_id=1, source_target_pairs={{0,4},{1,5},{2,6},{3,7},{4,0},{5,1},{6,2},{7,3},{8,12},{9,13},{10,... | collective-permute-start | bytes 344072 | tf_op jit(solution)/shard_map/ppermute | solution.py:225
  85.1 13.2 %collective-permute-start.13 = (bf16[8,7168]{1,0:T(8,128)(2,1)S(1)}, bf16[8,7168]{1,0:T(8,128)(2,1)S(1)}, u32[]{:S(2)}, u32[]{:S(2)}) collective-permute-start(bf16[8,7168]{1,0:T(8,128)(2,1)S(1)} %get-tuple-element.14), channel_id=1, source_target_pairs={{0,5},{1,6},{2,7},{3,0},{4,1},{5,2},{6,3},{7,4},{8,13},{9,14},{10,... | collective-permute-start | bytes 344072 | tf_op jit(solution)/shard_map/ppermute | solution.py:225
  86.9 12.0 %collective-permute-start.14 = (bf16[8,7168]{1,0:T(8,128)(2,1)S(1)}, bf16[8,7168]{1,0:T(8,128)(2,1)S(1)}, u32[]{:S(2)}, u32[]{:S(2)}) collective-permute-start(bf16[8,7168]{1,0:T(8,128)(2,1)S(1)} %get-tuple-element.13), channel_id=1, source_target_pairs={{0,6},{1,7},{2,0},{3,1},{4,2},{5,3},{6,4},{7,5},{8,14},{9,15},{10,... | collective-permute-start | bytes 344072 | tf_op jit(solution)/shard_map/ppermute | solution.py:225
  88.6 11.0 %collective-permute-start.15 = (bf16[8,7168]{1,0:T(8,128)(2,1)S(1)}, bf16[8,7168]{1,0:T(8,128)(2,1)S(1)}, u32[]{:S(2)}, u32[]{:S(2)}) collective-permute-start(bf16[8,7168]{1,0:T(8,128)(2,1)S(1)} %get-tuple-element.12), channel_id=1, source_target_pairs={{0,7},{1,0},{2,1},{3,2},{4,3},{5,4},{6,5},{7,6},{8,15},{9,8},{10,9... | collective-permute-start | bytes 344072 | tf_op jit(solution)/shard_map/ppermute | solution.py:225
  102.0 2.3 %copy-start.1 = (bf16[128,7168]{1,0:T(8,128)(2,1)S(1)}, bf16[128,7168]{1,0:T(8,128)(2,1)}, u32[]{:S(2)}) copy-start(bf16[128,7168]{1,0:T(8,128)(2,1)} %param.19) | copy-start | bytes 5505028
  107.0 2.5 %collective-permute-start.16 = (f32[7168]{0:T(1024)S(1)}, f32[7168]{0:T(1024)S(1)}, u32[]{:S(2)}, u32[]{:S(2)}) collective-permute-start(f32[7168]{0:T(1024)S(1)} %get-tuple-element.8), channel_id=1, source_target_pairs={{0,1},{1,0},{2,3},{3,2},{4,5},{5,4},{6,7},{7,6},{8,9},{9,8},{10,11... | collective-permute-start | bytes 86024 | tf_op jit(solution)/shard_map/ppermute | solution.py:170
  109.5 6.0 %collective-permute-start.17 = (f32[7168]{0:T(1024)S(1)}, f32[7168]{0:T(1024)S(1)}, u32[]{:S(2)}, u32[]{:S(2)}) collective-permute-start(f32[7168]{0:T(1024)S(1)} %add.186), channel_id=1, source_target_pairs={{0,2},{1,3},{2,0},{3,1},{4,6},{5,7},{6,4},{7,5},{8,10},{9,11},{10,... | collective-permute-start | bytes 86024 | tf_op jit(solution)/shard_map/ppermute | solution.py:170
  115.5 4.8 %collective-permute-start.18 = (f32[7168]{0:T(1024)S(1)}, f32[7168]{0:T(1024)S(1)}, u32[]{:S(2)}, u32[]{:S(2)}) collective-permute-start(f32[7168]{0:T(1024)S(1)} %add.187), channel_id=1, source_target_pairs={{0,4},{1,5},{2,6},{3,7},{4,0},{5,1},{6,2},{7,3},{8,12},{9,13},{10,... | collective-permute-start | bytes 86024 | tf_op jit(solution)/shard_map/ppermute | solution.py:170
  120.3 3.9 %collective-permute-start.19 = (f32[7168]{0:T(1024)S(1)}, f32[7168]{0:T(1024)S(1)}, u32[]{:S(2)}, u32[]{:S(2)}) collective-permute-start(f32[7168]{0:T(1024)S(1)} %add.188), channel_id=1, source_target_pairs={{0,8},{8,0},{16,24},{24,16},{1,9},{9,1},{17,25},{25,17},{2,10},{10... | collective-permute-start | bytes 86024 | tf_op jit(solution)/shard_map/ppermute | solution.py:170
  124.2 4.5 %collective-permute-start.20 = (f32[7168]{0:T(1024)S(1)}, f32[7168]{0:T(1024)S(1)}, u32[]{:S(2)}, u32[]{:S(2)}) collective-permute-start(f32[7168]{0:T(1024)S(1)} %add.189), channel_id=1, source_target_pairs={{0,16},{8,24},{16,0},{24,8},{1,17},{9,25},{17,1},{25,9},{2,18},{10... | collective-permute-start | bytes 86024 | tf_op jit(solution)/shard_map/ppermute | solution.py:170

commit v7 on v6

--- a/solution.py
+++ b/solution.py
@@ -237,6 +237,22 @@
     return picked.astype(values.dtype)
 
 
+def collect(chunks, kind, flight, group_size):
+    size = lax.axis_size("expert")
+    me = lax.axis_index("expert")
+    own = jnp.where(me % group_size == kind, chunks[me % size], jnp.zeros_like(chunks[0]))
+    moved = [own]
+    for shift in range(1, size):
+        part = lax.dynamic_index_in_dim(chunks, (me + shift) % size, 0, keepdims=False)
+        pairs = [(i, (i + shift) % size) for i in range(size) if i % group_size == kind]
+        moved.append(lax.ppermute(part, "expert", pairs))
+    stacked = jnp.stack(moved)
+    senders = jnp.arange(flight, dtype=jnp.int32) * group_size + kind
+    order = (me - senders) % size
+    picked = jnp.take(stacked, order, axis=0)
+    return picked.reshape(flight * chunks.shape[1], chunks.shape[2])
+
+
 def by_pair(
     normed, out_grad, slot_table, filled, gate_weight, up_weight, down_weight,
     member, expert_count, group_size,
@@ -257,11 +273,9 @@
     keep = jnp.where(first, forward, backward)
     give = jnp.where(first, backward, forward)
     total = keep.astype(jnp.float32) + lax.ppermute(give, "expert", swap).astype(jnp.float32)
-    came = exchange(
-        total.astype(jnp.bfloat16).reshape(expert_count, capacity, feature_count), "expert"
-    ).reshape(flight, 2, capacity, feature_count)
-    out_sums = came[:, 0].reshape(flight * capacity, feature_count).astype(jnp.float32)
-    grad_sums = came[:, 1].reshape(flight * capacity, feature_count).astype(jnp.float32)
+    total = total.astype(jnp.bfloat16).reshape(expert_count, capacity, feature_count)
+    grad_sums = collect(total, 1, flight, group_size).astype(jnp.float32)
+    out_sums = collect(total, 0, flight, group_size).astype(jnp.float32)
     return out_sums, grad_sums
 
 

time: 130 us -> 153 us (1.18)
  starting transfers between devices: 36 us -> 51.7 us
  waiting for transfers between devices: 24.5 us -> 31.6 us
    ppermute x0 -> x14, starting transfers between devices: none -> 36 us  [collect(): moved.append(lax.ppermute(part, 'expert', pairs))]
    ppermute x14 -> x7, starting transfers between devices: 23.9 us -> 11.1 us  [exchange(): lax.ppermute(part, axis, [(i, (i + shift) % size) for i in range(size)])]
    ppermute x0 -> x14, waiting for transfers between devices: none -> 11.8 us  [collect(): moved.append(lax.ppermute(part, 'expert', pairs))]
    ppermute x5, starting transfers between devices: 10.1 us -> 2.53 us  [butterfly_sum(): lax.ppermute(value, axis, [(i, i ^ bit) for i in range(size)])]
    ppermute x14 -> x7, waiting for transfers between devices: 11.4 us -> 5.59 us  [exchange(): lax.ppermute(part, axis, [(i, (i + shift) % size) for i in range(size)])]
    gather x0 -> x2, local copies, waits for them, and re-layouts: none -> 2.33 us  [collect(): picked = jnp.take(stacked, order, axis=0)]
    gather x2 -> x1, local copies, waits for them, and re-layouts: 3.57 us -> 1.78 us  [exchange(): return jnp.take(stacked, order, axis=0)]
    unnamed x24 -> x40, local copies, waits for them, and re-layouts: 7.88 us -> 7.7 us
  transfers between devices with their start and end apart: 21 -> 28, of which waited for: 8 -> 10; matrix products, arithmetic and copies ran while one was open for 8% -> 11% of each run, Pallas kernels for 0% -> 0%
where the time goes in v7:
time: 153 us; the launch traced here: 152 us
  starting transfers between devices  51.7 us (34%)
  Pallas kernels  32.1 us (21%)
  waiting for transfers between devices  31.6 us (21%)
  other arithmetic  14.5 us (9%)
  local copies, waits for them, and re-layouts  13.4 us (9%)
  matrix products  7.88 us (5%)
    ppermute x14, starting transfers between devices, collect(): moved.append(lax.ppermute(part, 'expert', pairs))  36 us
    pallas_call x1, Pallas kernels, expert_share(): pl.pallas_call(_expert_kernel, grid=(rows // rb, hid // hb), in_specs=[pl...  32.1 us
    ppermute x14, waiting for transfers between devices, collect(): moved.append(lax.ppermute(part, 'expert', pairs))  11.8 us
    ppermute x7, starting transfers between devices, exchange(): lax.ppermute(part, axis, [(i, (i + shift) % size) for i in range(size)])  11.1 us
    ppermute x5, waiting for transfers between devices, butterfly_sum(): lax.ppermute(value, axis, [(i, i ^ bit) for i in range(size)])  9.59 us
    unnamed x40, local copies, waits for them, and re-layouts  7.7 us
    ppermute x7, waiting for transfers between devices, exchange(): lax.ppermute(part, axis, [(i, (i + shift) % size) for i in range(size)])  5.59 us
    dot_general x2, matrix products, apply_combine(): return jnp.dot(combine, partial_sums, precision=lax.Precision.HIGHEST)  5.18 us
  transfers between devices with their start and end apart: 28, of which 10 were waited for; matrix products, arithmetic and copies ran while one was open for 11% of the time, Pallas kernels for 0%

profile of v7, /device:TPU:0, one launch (start us, length us, event | category | flops | bytes accessed | tf_op | source)
XLA Modules:
  0.0 152.4 jit_solution(13658844746773324346)
XLA Ops:
  0.8 0.8 fusion.21
  2.3 2.1 %multiply_reduce_fusion.1 = f32[128]{0:T(128)S(1)} fusion(bf16[128,7168]{1,0:T(8,128)(2,1)} %param.11, f32[7168]{0:T(1024)} %param.12), kind=kLoop, calls=%fused_computation.15 | loop fusion | flops 3669888 | bytes 1864192 | tf_op jit(solution)/shard_map/reduce_sum | solution.py:41
  4.3 1.9 %fusion.4 = bf16[4,1,8,7168]{3,2,0,1:T(8,128)(2,1)S(1)} fusion(bf16[128,7168]{1,0:T(8,128)(2,1)} %param.19, s32[4,8]{1,0:T(4,128)S(1)} %select_reduce_fusion, pred[4,8]{1,0:T(4,128)(4,1)S(1)} %fusion.20), kind=kOutput, calls=%fused_computation.11 | convolution fusion | flops 58957824 | bytes 2293920 | tf_op jit(solution)/shard_map/fct,td->fcd/dot_general | solution.py:234
  6.3 0.8 fusion.3
  7.3 0.7 dynamic-slice_bitcast_fusion.7
  8.5 2.6 %collective-permute-start.1 = (bf16[8,7168]{1,0:T(8,128)(2,1)S(1)}, bf16[8,7168]{1,0:T(8,128)(2,1)S(1)}, u32[]{:S(2)}, u32[]{:S(2)}) collective-permute-start(bf16[8,7168]{1,0:T(8,128)(2,1)S(1)} %get-tuple-element.26), channel_id=1, source_target_pairs={{0,2},{1,3},{2,4},{3,5},{4,6},{5,7},{6,0},{7,1},{8,10},{9,11},{10,... | collective-permute-start | bytes 344072 | tf_op jit(solution)/shard_map/ppermute | solution.py:225
  11.1 2.6 %collective-permute-start.2 = (bf16[8,7168]{1,0:T(8,128)(2,1)S(1)}, bf16[8,7168]{1,0:T(8,128)(2,1)S(1)}, u32[]{:S(2)}, u32[]{:S(2)}) collective-permute-start(bf16[8,7168]{1,0:T(8,128)(2,1)S(1)} %get-tuple-element.25), channel_id=1, source_target_pairs={{0,3},{1,4},{2,5},{3,6},{4,7},{5,0},{6,1},{7,2},{8,11},{9,12},{10,... | collective-permute-start | bytes 344072 | tf_op jit(solution)/shard_map/ppermute | solution.py:225
  13.7 1.2 collective-permute-start.3
  14.9 1.1 collective-permute-start.4
  16.1 1.9 %collective-permute-start.5 = (bf16[8,7168]{1,0:T(8,128)(2,1)S(1)}, bf16[8,7168]{1,0:T(8,128)(2,1)S(1)}, u32[]{:S(2)}, u32[]{:S(2)}) collective-permute-start(bf16[8,7168]{1,0:T(8,128)(2,1)S(1)} %get-tuple-element.22), channel_id=1, source_target_pairs={{0,6},{1,7},{2,0},{3,1},{4,2},{5,3},{6,4},{7,5},{8,14},{9,15},{10,... | collective-permute-start | bytes 344072 | tf_op jit(solution)/shard_map/ppermute | solution.py:225
  18.6 1.2 collective-permute-start.6
  20.5 5.6 %collective-permute-done.2 = bf16[8,7168]{1,0:T(8,128)(2,1)S(1)} collective-permute-done((bf16[8,7168]{1,0:T(8,128)(2,1)S(1)}, bf16[8,7168]{1,0:T(8,128)(2,1)S(1)}, u32[]{:S(2)}, u32[]{:S(2)}) %collective-permute-start.2) | collective-permute-done | bytes 114720 | tf_op jit(solution)/shard_map/ppermute | solution.py:225
  29.3 1.8 %gather_fusion = bf16[8,8,7168]{2,1,0:T(8,128)(2,1)S(1)} fusion(bf16[8,8,7168]{2,1,0:T(8,128)(2,1)} %bitcast_dynamic-update-slice_fusion.14, s32[1024]{0:T(1024)S(1)} %pad_clamp_fusion.2), kind=kCustom, calls=%fused_computation.2 | custom fusion | bytes 1835040 | tf_op jit(solution)/shard_map/jit(_take)/gather | solution.py:228
  31.1 1.1 broadcast_select_fusion
  32.2 1.6 %collective-permute-start.7 = (bf16[8,8,7168]{2,1,0:T(8,128)(2,1)}, bf16[8,8,7168]{2,1,0:T(8,128)(2,1)}, u32[]{:S(2)}, u32[]{:S(2)}) collective-permute-start(bf16[8,8,7168]{2,1,0:T(8,128)(2,1)} %broadcast_select_fusion), channel_id=1, source_target_pairs={{0,1},{1,0},{2,3},{3,2},{4,5},{5,4},{6,7},{7,6},{8,9},{9,8},{10,11... | collective-permute-start | bytes 2752520 | tf_op jit(solution)/shard_map/ppermute | solution.py:268
  33.8 2.4 %collective-permute-done.7 = bf16[8,8,7168]{2,1,0:T(8,128)(2,1)} collective-permute-done((bf16[8,8,7168]{2,1,0:T(8,128)(2,1)}, bf16[8,8,7168]{2,1,0:T(8,128)(2,1)}, u32[]{:S(2)}, u32[]{:S(2)}) %collective-permute-start.7) | collective-permute-done | bytes 917536 | tf_op jit(solution)/shard_map/ppermute | solution.py:268
  36.3 2.6 %select_bitcast_fusion = (bf16[64,7168]{1,0:T(8,128)(2,1)}, bf16[64,7168]{1,0:T(8,128)(2,1)}) fusion(bf16[8,8,7168]{2,1,0:T(8,128)(2,1)} %collective-permute-done.7, pred[]{:T(512)S(6)} %eq.91, bf16[8,8,7168]{2,1,0:T(8,128)(2,1)S(1)} %gather_fusion, pred[8]{0:T(512)(128)(4,1)S(1)} %compare_and_fusion.2), kind=kLoop, calls=%fused_computation.25 | loop fusion | flops 1376256 | bytes 3670025 | tf_op jit(solution)/shard_map/reshape | solution.py:271
  38.9 32.1 %shard_map.112 = (bf16[64,7168]{1,0:T(8,128)(2,1)}, bf16[64,7168]{1,0:T(8,128)(2,1)}) custom-call(bf16[64,7168]{1,0:T(8,128)(2,1)} %get-tuple-element.11.x_ref, bf16[64,7168]{1,0:T(8,128)(2,1)} %get-tuple-element.10.y_ref, bf16[7168,1024]{1,0:T(8,128)(2,1)} %g_ref.1, bf16[7168,1024]{1,0:T(8,128)(2,1)} %u_ref.1, bf16[1024,7168]{1,0:T(8,128)(2,1)} %d_ref.1), custom_call_target="tpu_custom_call" | custom-call | tf_op jit(solution)/shard_map/pallas_call | solution.py:110
  71.0 1.3 broadcast_select_fusion.1
  72.8 2.1 %collective-permute-done.8 = bf16[64,7168]{1,0:T(8,128)(2,1)} collective-permute-done((bf16[64,7168]{1,0:T(8,128)(2,1)S(1)}, bf16[64,7168]{1,0:T(8,128)(2,1)}, u32[]{:S(2)}, u32[]{:S(2)}) %collective-permute-start.8) | collective-permute-done | bytes 917536 | tf_op jit(solution)/shard_map/ppermute | solution.py:275
  74.9 1.8 %fusion.11 = bf16[8,8,7168]{2,1,0:T(8,128)(2,1)S(1)} fusion(bf16[64,7168]{1,0:T(8,128)(2,1)} %collective-permute-done.8, bf16[64,7168]{1,0:T(8,128)(2,1)} %get-tuple-element.6, bf16[64,7168]{1,0:T(8,128)(2,1)} %get-tuple-element.7, pred[]{:T(512)S(6)} %eq.91), kind=kLoop, calls=%fused_computation.23 | loop fusion | flops 2293760 | bytes 3670017 | tf_op jit(solution)/shard_map/reshape | solution.py:276
  76.7 0.8 select_dynamic-update-slice_fusion
  77.6 1.3 collective-permute-start.16
  78.9 7.5 %collective-permute-start.9 = (bf16[8,7168]{1,0:T(8,128)(2,1)}, bf16[8,7168]{1,0:T(8,128)(2,1)}, u32[]{:S(2)}, u32[]{:S(2)}) collective-permute-start(bf16[8,7168]{1,0:T(8,128)(2,1)} %get-tuple-element.19), channel_id=1, source_target_pairs={{0,1},{2,3},{4,5},{6,7},{8,9},{10,11},{12,13},{14,15},{16,17},{18,... | collective-permute-start | bytes 344072 | tf_op jit(solution)/shard_map/ppermute | solution.py:248
  87.0 1.9 %collective-permute-start.10 = (bf16[8,7168]{1,0:T(8,128)(2,1)}, bf16[8,7168]{1,0:T(8,128)(2,1)S(1)}, u32[]{:S(2)}, u32[]{:S(2)}) collective-permute-start(bf16[8,7168]{1,0:T(8,128)(2,1)} %get-tuple-element.18), channel_id=1, source_target_pairs={{0,2},{2,4},{4,6},{6,0},{8,10},{10,12},{12,14},{14,8},{16,18},{18,... | collective-permute-start | bytes 344072 | tf_op jit(solution)/shard_map/ppermute | solution.py:248
  89.0 1.3 collective-permute-start.18
  90.3 6.6 %collective-permute-start.11 = (bf16[8,7168]{1,0:T(8,128)(2,1)}, bf16[8,7168]{1,0:T(8,128)(2,1)S(1)}, u32[]{:S(2)}, u32[]{:S(2)}) collective-permute-start(bf16[8,7168]{1,0:T(8,128)(2,1)} %get-tuple-element.17), channel_id=1, source_target_pairs={{0,3},{2,5},{4,7},{6,1},{8,11},{10,13},{12,15},{14,9},{16,19},{18,... | collective-permute-start | bytes 344072 | tf_op jit(solution)/shard_map/ppermute | solution.py:248
  97.6 3.9 %collective-permute-start.12 = (bf16[8,7168]{1,0:T(8,128)(2,1)}, bf16[8,7168]{1,0:T(8,128)(2,1)}, u32[]{:S(2)}, u32[]{:S(2)}) collective-permute-start(bf16[8,7168]{1,0:T(8,128)(2,1)} %get-tuple-element.16), channel_id=1, source_target_pairs={{0,4},{2,6},{4,0},{6,2},{8,12},{10,14},{12,8},{14,10},{16,20},{18,... | collective-permute-start | bytes 344072 | tf_op jit(solution)/shard_map/ppermute | solution.py:248
  101.6 1.3 collective-permute-start.20
  102.9 5.0 %collective-permute-done.20 = bf16[8,7168]{1,0:T(8,128)(2,1)S(1)} collective-permute-done((bf16[8,7168]{1,0:T(8,128)(2,1)}, bf16[8,7168]{1,0:T(8,128)(2,1)S(1)}, u32[]{:S(2)}, u32[]{:S(2)}) %collective-permute-start.20) | collective-permute-done | bytes 114720 | tf_op jit(solution)/shard_map/ppermute | solution.py:248
  108.6 1.3 collective-permute-start.22
  109.9 6.8 %collective-permute-done.22 = bf16[8,7168]{1,0:T(8,128)(2,1)S(1)} collective-permute-done((bf16[8,7168]{1,0:T(8,128)(2,1)S(1)}, bf16[8,7168]{1,0:T(8,128)(2,1)S(1)}, u32[]{:S(2)}, u32[]{:S(2)}) %collective-permute-start.22) | collective-permute-done | bytes 114720 | tf_op jit(solution)/shard_map/ppermute | solution.py:248
  116.7 4.3 %collective-permute-start.13 = (bf16[8,7168]{1,0:T(8,128)(2,1)}, bf16[8,7168]{1,0:T(8,128)(2,1)}, u32[]{:S(2)}, u32[]{:S(2)}) collective-permute-start(bf16[8,7168]{1,0:T(8,128)(2,1)} %get-tuple-element.15), channel_id=1, source_target_pairs={{0,5},{2,7},{4,1},{6,3},{8,13},{10,15},{12,9},{14,11},{16,21},{18,... | collective-permute-start | bytes 344072 | tf_op jit(solution)/shard_map/ppermute | solution.py:248
  121.1 0.9 copy-done.3
  122.0 1.8 %gather_fusion.2 = bf16[4,8,7168]{2,1,0:T(8,128)(2,1)S(1)} fusion(bf16[8,8,7168]{2,1,0:T(8,128)(2,1)} %copy-done.3, s32[1024]{0:T(1024)S(1)} %get-tuple-element.33), kind=kCustom, calls=%fused_computation.1.clone | custom fusion | bytes 917520 | tf_op jit(solution)/shard_map/jit(_take)/gather | solution.py:252
  123.8 2.2 %multiply_reduce_fusion = (f32[128]{0:T(128)S(1)}, f32[128,7168]{1,0:T(8,128)S(1)}) fusion(bf16[128,7168]{1,0:T(8,128)(2,1)S(1)} %copy-done, f32[7168]{0:T(1024)S(1)} %copy-done.2, f32[7168]{0:T(1024)S(1)} %copy-done.8, bf16[4,8,7168]{2,1,0:T(8,128)(2,1)S(1)} %gather_fusion.2, pred[4]{0:T(512)(128)(4,1)S(1)} %compare_and_fusion, ...), kind=kOutput, calls=%fused_computation.13 | convolution fusion | flops 357146496 | bytes 6025732 | tf_op jit(solution)/shard_map/dot_general | solution.py:133
  126.0 3.1 %collective-permute-start.14 = (bf16[8,7168]{1,0:T(8,128)(2,1)S(1)}, bf16[8,7168]{1,0:T(8,128)(2,1)S(1)}, u32[]{:S(2)}, u32[]{:S(2)}) collective-permute-start(bf16[8,7168]{1,0:T(8,128)(2,1)S(1)} %copy-done.7), channel_id=1, source_target_pairs={{0,6},{2,0},{4,2},{6,4},{8,14},{10,8},{12,10},{14,12},{16,22},{18,... | collective-permute-start | bytes 344072 | tf_op jit(solution)/shard_map/ppermute | solution.py:248
  129.1 0.9 bitcast_dynamic-update-slice_fusion.13
  130.0 1.5 collective-permute-start.15
  131.5 2.6 %fusion.44 = (f32[7168]{0:T(1024)S(1)}, bf16[128,7168]{1,0:T(8,128)(2,1)}) fusion(f32[128]{0:T(128)S(1)} %broadcast_multiply_fusion, f32[128]{0:T(128)S(1)} %get-tuple-element.29, f32[7168]{0:T(1024)S(1)} %copy-done.2, bf16[128,7168]{1,0:T(8,128)(2,1)S(1)} %copy-done, f32[128,7168]{1,0:T(8,128)S(1)} %get-tuple-element.32, f32[128]{0:T(128)S(1)} %get-tuple-element.30, ...), kind=kLoop, calls=%fused_computation.130 | loop fusion | flops 9167872 | bytes 9233920 | tf_op jit(solution)/shard_map/reduce_sum | solution.py:316
  134.2 0.9 bitcast_dynamic-update-slice_fusion.10
  135.4 0.8 collective-permute-start.24
  136.2 0.9 bitcast_dynamic-update-slice_fusion.9
  137.1 2.1 %collective-permute-done.24 = f32[7168]{0:T(1024)S(1)} collective-permute-done((f32[7168]{0:T(1024)S(1)}, f32[7168]{0:T(1024)S(1)}, u32[]{:S(2)}, u32[]{:S(2)}) %collective-permute-start.24) | collective-permute-done | bytes 28704 | tf_op jit(solution)/shard_map/ppermute | solution.py:170
  139.3 0.9 collective-permute-start.25
  140.2 3.9 %collective-permute-done.25 = f32[7168]{0:T(1024)S(1)} collective-permute-done((f32[7168]{0:T(1024)S(1)}, f32[7168]{0:T(1024)S(1)}, u32[]{:S(2)}, u32[]{:S(2)}) %collective-permute-start.25) | collective-permute-done | bytes 28704 | tf_op jit(solution)/shard_map/ppermute | solution.py:170
  145.0 2.9 %collective-permute-done.26 = f32[7168]{0:T(1024)S(1)} collective-permute-done((f32[7168]{0:T(1024)S(1)}, f32[7168]{0:T(1024)S(1)}, u32[]{:S(2)}, u32[]{:S(2)}) %collective-permute-start.26) | collective-permute-done | bytes 28704 | tf_op jit(solution)/shard_map/ppermute | solution.py:170
  148.3 3.0 %fusion.2 = bf16[128,7168]{1,0:T(8,128)(2,1)} fusion(bf16[128,7168]{1,0:T(8,128)(2,1)S(1)} %copy-done, f32[7168]{0:T(1024)S(1)} %copy-done.2, bf16[4,8,7168]{2,1,0:T(8,128)(2,1)S(1)} %gather_fusion.1, pred[4]{0:T(512)(128)(4,1)S(1)} %compare_and_fusion.1, f32[128,4]{0,1:T(4,128)S(1)} %select_reduce_fusion.1, s32[128,4]{0,1:T(4,128)S(1)} %add_select_fusion), kind=kOutput, calls=%fused_computation.7 | convolution fusion | flops 356229120 | bytes 4161540 | tf_op jit(solution)/shard_map/dot_general | solution.py:133
  (94 shorter events, 11.4 us)
Async XLA Ops:
  0.6 5.6 %copy-start = (bf16[128,7168]{1,0:T(8,128)(2,1)S(1)}, bf16[128,7168]{1,0:T(8,128)(2,1)}, u32[]{:S(2)}) copy-start(bf16[128,7168]{1,0:T(8,128)(2,1)} %param.11) | copy-start | bytes 5505028
  0.6 5.6 %copy-start.2 = (f32[7168]{0:T(1024)S(1)}, f32[7168]{0:T(1024)}, u32[]{:S(2)}) copy-start(f32[7168]{0:T(1024)} %param.12) | copy-start | bytes 86020
  0.7 5.6 %copy-start.8 = (f32[7168]{0:T(1024)S(1)}, f32[7168]{0:T(1024)}, u32[]{:S(2)}) copy-start(f32[7168]{0:T(1024)} %param.13) | copy-start | bytes 86020
  8.0 8.1 %collective-permute-start = (bf16[8,7168]{1,0:T(8,128)(2,1)S(1)}, bf16[8,7168]{1,0:T(8,128)(2,1)S(1)}, u32[]{:S(2)}, u32[]{:S(2)}) collective-permute-start(bf16[8,7168]{1,0:T(8,128)(2,1)S(1)} %get-tuple-element.27), channel_id=1, source_target_pairs={{0,1},{1,2},{2,3},{3,4},{4,5},{5,6},{6,7},{7,0},{8,9},{9,10},{10,1... | collective-permute-start | bytes 344072 | tf_op jit(solution)/shard_map/ppermute | solution.py:225
  8.5 10.1 %collective-permute-start.1 = (bf16[8,7168]{1,0:T(8,128)(2,1)S(1)}, bf16[8,7168]{1,0:T(8,128)(2,1)S(1)}, u32[]{:S(2)}, u32[]{:S(2)}) collective-permute-start(bf16[8,7168]{1,0:T(8,128)(2,1)S(1)} %get-tuple-element.26), channel_id=1, source_target_pairs={{0,2},{1,3},{2,4},{3,5},{4,6},{5,7},{6,0},{7,1},{8,10},{9,11},{10,... | collective-permute-start | bytes 344072 | tf_op jit(solution)/shard_map/ppermute | solution.py:225
  11.1 15.0 %collective-permute-start.2 = (bf16[8,7168]{1,0:T(8,128)(2,1)S(1)}, bf16[8,7168]{1,0:T(8,128)(2,1)S(1)}, u32[]{:S(2)}, u32[]{:S(2)}) collective-permute-start(bf16[8,7168]{1,0:T(8,128)(2,1)S(1)} %get-tuple-element.25), channel_id=1, source_target_pairs={{0,3},{1,4},{2,5},{3,6},{4,7},{5,0},{6,1},{7,2},{8,11},{9,12},{10,... | collective-permute-start | bytes 344072 | tf_op jit(solution)/shard_map/ppermute | solution.py:225
  13.7 13.1 %collective-permute-start.3 = (bf16[8,7168]{1,0:T(8,128)(2,1)S(1)}, bf16[8,7168]{1,0:T(8,128)(2,1)S(1)}, u32[]{:S(2)}, u32[]{:S(2)}) collective-permute-start(bf16[8,7168]{1,0:T(8,128)(2,1)S(1)} %get-tuple-element.24), channel_id=1, source_target_pairs={{0,4},{1,5},{2,6},{3,7},{4,0},{5,1},{6,2},{7,3},{8,12},{9,13},{10,... | collective-permute-start | bytes 344072 | tf_op jit(solution)/shard_map/ppermute | solution.py:225
  14.9 12.5 %collective-permute-start.4 = (bf16[8,7168]{1,0:T(8,128)(2,1)S(1)}, bf16[8,7168]{1,0:T(8,128)(2,1)S(1)}, u32[]{:S(2)}, u32[]{:S(2)}) collective-permute-start(bf16[8,7168]{1,0:T(8,128)(2,1)S(1)} %get-tuple-element.23), channel_id=1, source_target_pairs={{0,5},{1,6},{2,7},{3,0},{4,1},{5,2},{6,3},{7,4},{8,13},{9,14},{10,... | collective-permute-start | bytes 344072 | tf_op jit(solution)/shard_map/ppermute | solution.py:225
  16.1 12.0 %collective-permute-start.5 = (bf16[8,7168]{1,0:T(8,128)(2,1)S(1)}, bf16[8,7168]{1,0:T(8,128)(2,1)S(1)}, u32[]{:S(2)}, u32[]{:S(2)}) collective-permute-start(bf16[8,7168]{1,0:T(8,128)(2,1)S(1)} %get-tuple-element.22), channel_id=1, source_target_pairs={{0,6},{1,7},{2,0},{3,1},{4,2},{5,3},{6,4},{7,5},{8,14},{9,15},{10,... | collective-permute-start | bytes 344072 | tf_op jit(solution)/shard_map/ppermute | solution.py:225
  18.6 10.1 %collective-permute-start.6 = (bf16[8,7168]{1,0:T(8,128)(2,1)S(1)}, bf16[8,7168]{1,0:T(8,128)(2,1)S(1)}, u32[]{:S(2)}, u32[]{:S(2)}) collective-permute-start(bf16[8,7168]{1,0:T(8,128)(2,1)S(1)} %get-tuple-element.21), channel_id=1, source_target_pairs={{0,7},{1,0},{2,1},{3,2},{4,3},{5,4},{6,5},{7,6},{8,15},{9,8},{10,9... | collective-permute-start | bytes 344072 | tf_op jit(solution)/shard_map/ppermute | solution.py:225
  32.2 4.1 %collective-permute-start.7 = (bf16[8,8,7168]{2,1,0:T(8,128)(2,1)}, bf16[8,8,7168]{2,1,0:T(8,128)(2,1)}, u32[]{:S(2)}, u32[]{:S(2)}) collective-permute-start(bf16[8,8,7168]{2,1,0:T(8,128)(2,1)} %broadcast_select_fusion), channel_id=1, source_target_pairs={{0,1},{1,0},{2,3},{3,2},{4,5},{5,4},{6,7},{7,6},{8,9},{9,8},{10,11... | collective-permute-start | bytes 2752520 | tf_op jit(solution)/shard_map/ppermute | solution.py:268
  38.9 33.9 %copy-start.10 = (s32[128,8]{0,1:T(8,128)S(1)}, s32[128,8]{0,1:T(8,128)}, u32[]{:S(2)}) copy-start(s32[128,8]{0,1:T(8,128)} %param.15) | copy-start | bytes 12292
  71.0 7.9 %copy-start.9 = (s32[128,8]{0,1:T(8,128)S(1)}, s32[128,8]{0,1:T(8,128)}, u32[]{:S(2)}) copy-start(s32[128,8]{0,1:T(8,128)} %param.14) | copy-start | bytes 12292
  72.3 2.7 %collective-permute-start.8 = (bf16[64,7168]{1,0:T(8,128)(2,1)S(1)}, bf16[64,7168]{1,0:T(8,128)(2,1)}, u32[]{:S(2)}, u32[]{:S(2)}) collective-permute-start(bf16[64,7168]{1,0:T(8,128)(2,1)S(1)} %broadcast_select_fusion.1), channel_id=1, source_target_pairs={{0,1},{1,0},{2,3},{3,2},{4,5},{5,4},{6,7},{7,6},{8,9},{9,8},{10,11... | collective-permute-start | bytes 2752520 | tf_op jit(solution)/shard_map/ppermute | solution.py:275
  77.6 43.5 %copy-start.4 = (bf16[8,7168]{1,0:T(8,128)(2,1)}, bf16[8,7168]{1,0:T(8,128)(2,1)S(1)}, u32[]{:S(2)}) copy-start(bf16[8,7168]{1,0:T(8,128)(2,1)S(1)} %get-tuple-element.13) | copy-start | bytes 344068
  77.6 43.5 %copy-start.6 = (bf16[8,7168]{1,0:T(8,128)(2,1)}, bf16[8,7168]{1,0:T(8,128)(2,1)S(1)}, u32[]{:S(2)}) copy-start(bf16[8,7168]{1,0:T(8,128)(2,1)S(1)} %get-tuple-element.14) | copy-start | bytes 344068
  77.6 12.7 %collective-permute-start.16 = (bf16[8,7168]{1,0:T(8,128)(2,1)}, bf16[8,7168]{1,0:T(8,128)(2,1)S(1)}, u32[]{:S(2)}, u32[]{:S(2)}) collective-permute-start(bf16[8,7168]{1,0:T(8,128)(2,1)} %get-tuple-element.19), channel_id=1, source_target_pairs={{1,2},{3,4},{5,6},{7,0},{9,10},{11,12},{13,14},{15,8},{17,18},{19,... | collective-permute-start | bytes 344072 | tf_op jit(solution)/shard_map/ppermute | solution.py:248
  78.9 47.1 %collective-permute-start.9 = (bf16[8,7168]{1,0:T(8,128)(2,1)}, bf16[8,7168]{1,0:T(8,128)(2,1)}, u32[]{:S(2)}, u32[]{:S(2)}) collective-permute-start(bf16[8,7168]{1,0:T(8,128)(2,1)} %get-tuple-element.19), channel_id=1, source_target_pairs={{0,1},{2,3},{4,5},{6,7},{8,9},{10,11},{12,13},{14,15},{16,17},{18,... | collective-permute-start | bytes 344072 | tf_op jit(solution)/shard_map/ppermute | solution.py:248
  86.4 10.6 %collective-permute-start.17 = (bf16[8,7168]{1,0:T(8,128)(2,1)}, bf16[8,7168]{1,0:T(8,128)(2,1)S(1)}, u32[]{:S(2)}, u32[]{:S(2)}) collective-permute-start(bf16[8,7168]{1,0:T(8,128)(2,1)} %get-tuple-element.18), channel_id=1, source_target_pairs={{1,3},{3,5},{5,7},{7,1},{9,11},{11,13},{13,15},{15,9},{17,19},{19,... | collective-permute-start | bytes 344072 | tf_op jit(solution)/shard_map/ppermute | solution.py:248
  87.0 43.0 %collective-permute-start.10 = (bf16[8,7168]{1,0:T(8,128)(2,1)}, bf16[8,7168]{1,0:T(8,128)(2,1)S(1)}, u32[]{:S(2)}, u32[]{:S(2)}) collective-permute-start(bf16[8,7168]{1,0:T(8,128)(2,1)} %get-tuple-element.18), channel_id=1, source_target_pairs={{0,2},{2,4},{4,6},{6,0},{8,10},{10,12},{12,14},{14,8},{16,18},{18,... | collective-permute-start | bytes 344072 | tf_op jit(solution)/shard_map/ppermute | solution.py:248
  89.0 8.7 %collective-permute-start.18 = (bf16[8,7168]{1,0:T(8,128)(2,1)}, bf16[8,7168]{1,0:T(8,128)(2,1)S(1)}, u32[]{:S(2)}, u32[]{:S(2)}) collective-permute-start(bf16[8,7168]{1,0:T(8,128)(2,1)} %get-tuple-element.17), channel_id=1, source_target_pairs={{1,4},{3,6},{5,0},{7,2},{9,12},{11,14},{13,8},{15,10},{17,20},{19,... | collective-permute-start | bytes 344072 | tf_op jit(solution)/shard_map/ppermute | solution.py:248
  90.3 43.9 %collective-permute-start.11 = (bf16[8,7168]{1,0:T(8,128)(2,1)}, bf16[8,7168]{1,0:T(8,128)(2,1)S(1)}, u32[]{:S(2)}, u32[]{:S(2)}) collective-permute-start(bf16[8,7168]{1,0:T(8,128)(2,1)} %get-tuple-element.17), channel_id=1, source_target_pairs={{0,3},{2,5},{4,7},{6,1},{8,11},{10,13},{12,15},{14,9},{16,19},{18,... | collective-permute-start | bytes 344072 | tf_op jit(solution)/shard_map/ppermute | solution.py:248
  96.9 4.6 %collective-permute-start.19 = (bf16[8,7168]{1,0:T(8,128)(2,1)}, bf16[8,7168]{1,0:T(8,128)(2,1)S(1)}, u32[]{:S(2)}, u32[]{:S(2)}) collective-permute-start(bf16[8,7168]{1,0:T(8,128)(2,1)} %get-tuple-element.16), channel_id=1, source_target_pairs={{1,5},{3,7},{5,1},{7,3},{9,13},{11,15},{13,9},{15,11},{17,21},{19,... | collective-permute-start | bytes 344072 | tf_op jit(solution)/shard_map/ppermute | solution.py:248
  97.6 36.6 %collective-permute-start.12 = (bf16[8,7168]{1,0:T(8,128)(2,1)}, bf16[8,7168]{1,0:T(8,128)(2,1)}, u32[]{:S(2)}, u32[]{:S(2)}) collective-permute-start(bf16[8,7168]{1,0:T(8,128)(2,1)} %get-tuple-element.16), channel_id=1, source_target_pairs={{0,4},{2,6},{4,0},{6,2},{8,12},{10,14},{12,8},{14,10},{16,20},{18,... | collective-permute-start | bytes 344072 | tf_op jit(solution)/shard_map/ppermute | solution.py:248
  101.6 6.3 %collective-permute-start.20 = (bf16[8,7168]{1,0:T(8,128)(2,1)}, bf16[8,7168]{1,0:T(8,128)(2,1)S(1)}, u32[]{:S(2)}, u32[]{:S(2)}) collective-permute-start(bf16[8,7168]{1,0:T(8,128)(2,1)} %get-tuple-element.15), channel_id=1, source_target_pairs={{1,6},{3,0},{5,2},{7,4},{9,14},{11,8},{13,10},{15,12},{17,22},{19,... | collective-permute-start | bytes 344072 | tf_op jit(solution)/shard_map/ppermute | solution.py:248
  107.9 0.7 collective-permute-start.21
  108.6 8.1 %collective-permute-start.22 = (bf16[8,7168]{1,0:T(8,128)(2,1)S(1)}, bf16[8,7168]{1,0:T(8,128)(2,1)S(1)}, u32[]{:S(2)}, u32[]{:S(2)}) collective-permute-start(bf16[8,7168]{1,0:T(8,128)(2,1)S(1)} %get-tuple-element.13), channel_id=1, source_target_pairs={{1,0},{3,2},{5,4},{7,6},{9,8},{11,10},{13,12},{15,14},{17,16},{19,... | collective-permute-start | bytes 344072 | tf_op jit(solution)/shard_map/ppermute | solution.py:248
  116.7 19.5 %collective-permute-start.13 = (bf16[8,7168]{1,0:T(8,128)(2,1)}, bf16[8,7168]{1,0:T(8,128)(2,1)}, u32[]{:S(2)}, u32[]{:S(2)}) collective-permute-start(bf16[8,7168]{1,0:T(8,128)(2,1)} %get-tuple-element.15), channel_id=1, source_target_pairs={{0,5},{2,7},{4,1},{6,3},{8,13},{10,15},{12,9},{14,11},{16,21},{18,... | collective-permute-start | bytes 344072 | tf_op jit(solution)/shard_map/ppermute | solution.py:248
  121.1 0.9 copy-start.3
  123.8 2.2 %copy-start.7 = (bf16[8,7168]{1,0:T(8,128)(2,1)S(1)}, bf16[8,7168]{1,0:T(8,128)(2,1)}, u32[]{:S(2)}) copy-start(bf16[8,7168]{1,0:T(8,128)(2,1)} %copy-done.6) | copy-start | bytes 344068
  123.8 6.3 %copy-start.5 = (bf16[8,7168]{1,0:T(8,128)(2,1)S(1)}, bf16[8,7168]{1,0:T(8,128)(2,1)}, u32[]{:S(2)}) copy-start(bf16[8,7168]{1,0:T(8,128)(2,1)} %copy-done.4) | copy-start | bytes 344068
  123.8 7.8 %copy-start.1 = (bf16[128,7168]{1,0:T(8,128)(2,1)S(1)}, bf16[128,7168]{1,0:T(8,128)(2,1)}, u32[]{:S(2)}) copy-start(bf16[128,7168]{1,0:T(8,128)(2,1)} %param.19) | copy-start | bytes 5505028
  126.0 14.2 %collective-permute-start.14 = (bf16[8,7168]{1,0:T(8,128)(2,1)S(1)}, bf16[8,7168]{1,0:T(8,128)(2,1)S(1)}, u32[]{:S(2)}, u32[]{:S(2)}) collective-permute-start(bf16[8,7168]{1,0:T(8,128)(2,1)S(1)} %copy-done.7), channel_id=1, source_target_pairs={{0,6},{2,0},{4,2},{6,4},{8,14},{10,8},{12,10},{14,12},{16,22},{18,... | collective-permute-start | bytes 344072 | tf_op jit(solution)/shard_map/ppermute | solution.py:248
  130.0 14.4 %collective-permute-start.15 = (bf16[8,7168]{1,0:T(8,128)(2,1)S(1)}, bf16[8,7168]{1,0:T(8,128)(2,1)S(1)}, u32[]{:S(2)}, u32[]{:S(2)}) collective-permute-start(bf16[8,7168]{1,0:T(8,128)(2,1)S(1)} %copy-done.5), channel_id=1, source_target_pairs={{0,7},{2,1},{4,3},{6,5},{8,15},{10,9},{12,11},{14,13},{16,23},{18,... | collective-permute-start | bytes 344072 | tf_op jit(solution)/shard_map/ppermute | solution.py:248
  134.2 1.2 collective-permute-start.23
  135.4 3.9 %collective-permute-start.24 = (f32[7168]{0:T(1024)S(1)}, f32[7168]{0:T(1024)S(1)}, u32[]{:S(2)}, u32[]{:S(2)}) collective-permute-start(f32[7168]{0:T(1024)S(1)} %add.261), channel_id=1, source_target_pairs={{0,2},{1,3},{2,0},{3,1},{4,6},{5,7},{6,4},{7,5},{8,10},{9,11},{10,... | collective-permute-start | bytes 86024 | tf_op jit(solution)/shard_map/ppermute | solution.py:170
  139.3 4.8 %collective-permute-start.25 = (f32[7168]{0:T(1024)S(1)}, f32[7168]{0:T(1024)S(1)}, u32[]{:S(2)}, u32[]{:S(2)}) collective-permute-start(f32[7168]{0:T(1024)S(1)} %add.262), channel_id=1, source_target_pairs={{0,4},{1,5},{2,6},{3,7},{4,0},{5,1},{6,2},{7,3},{8,12},{9,13},{10,... | collective-permute-start | bytes 86024 | tf_op jit(solution)/shard_map/ppermute | solution.py:170
  144.1 3.9 %collective-permute-start.26 = (f32[7168]{0:T(1024)S(1)}, f32[7168]{0:T(1024)S(1)}, u32[]{:S(2)}, u32[]{:S(2)}) collective-permute-start(f32[7168]{0:T(1024)S(1)} %add.263), channel_id=1, source_target_pairs={{0,8},{8,0},{16,24},{24,16},{1,9},{9,1},{17,25},{25,17},{2,10},{10... | collective-permute-start | bytes 86024 | tf_op jit(solution)/shard_map/ppermute | solution.py:170
  147.9 3.9 %collective-permute-start.27 = (f32[7168]{0:T(1024)S(1)}, f32[7168]{0:T(1024)S(1)}, u32[]{:S(2)}, u32[]{:S(2)}) collective-permute-start(f32[7168]{0:T(1024)S(1)} %add.264), channel_id=1, source_target_pairs={{0,16},{8,24},{16,0},{24,8},{1,17},{9,25},{17,1},{25,9},{2,18},{10... | collective-permute-start | bytes 86024 | tf_op jit(solution)/shard_map/ppermute | solution.py:170

commit v8 on v6

--- a/solution.py
+++ b/solution.py
@@ -129,6 +129,74 @@
     )(x, y, gw, uw, dw)
 
 
+def _pair_kernel(
+    first_ref, a_ref, p_ref, g_ref, u_ref, d_ref, keep_ref, give_ref, xs, ys, acc_o, acc_b
+):
+    j = pl.program_id(0)
+    first = first_ref[0] == 1
+
+    @pl.when(j == 0)
+    def _():
+        xs[...] = jnp.where(first, a_ref[...], p_ref[...])
+        ys[...] = jnp.where(first, p_ref[...], a_ref[...])
+        acc_o[...] = jnp.zeros_like(acc_o)
+        acc_b[...] = jnp.zeros_like(acc_b)
+
+    x = xs[...]
+    y = ys[...]
+    gw = g_ref[...]
+    uw = u_ref[...]
+    dw = d_ref[...]
+    nt = (((1,), (1,)), ((), ()))
+    g = jnp.dot(x, gw, preferred_element_type=jnp.float32)
+    u = jnp.dot(x, uw, preferred_element_type=jnp.float32)
+    sig = jax.nn.sigmoid(g)
+    hidden = (g * sig * u).astype(jnp.bfloat16)
+    bh = lax.dot_general(y, dw, nt, preferred_element_type=jnp.float32)
+    back_up = (bh * g * sig).astype(jnp.bfloat16)
+    back_gate = (bh * u * sig * (1.0 + g * (1.0 - sig))).astype(jnp.bfloat16)
+    acc_o[...] += jnp.dot(hidden, dw, preferred_element_type=jnp.float32)
+    acc_b[...] += lax.dot_general(
+        back_gate, gw, nt, preferred_element_type=jnp.float32
+    ) + lax.dot_general(back_up, uw, nt, preferred_element_type=jnp.float32)
+
+    @pl.when(j == pl.num_programs(0) - 1)
+    def _():
+        out = acc_o[...].astype(keep_ref.dtype)
+        back = acc_b[...].astype(keep_ref.dtype)
+        keep_ref[...] = jnp.where(first, out, back)
+        give_ref[...] = jnp.where(first, back, out)
+
+
+def expert_pair(first, arrived, partner, gw, uw, dw):
+    rows, feat = arrived.shape
+    hid = gw.shape[1]
+    hb = min(hid, 256)
+    full = pl.BlockSpec((rows, feat), lambda j, f: (0, 0))
+    grid_spec = pltpu.PrefetchScalarGridSpec(
+        num_scalar_prefetch=1,
+        grid=(hid // hb,),
+        in_specs=[
+            full,
+            full,
+            pl.BlockSpec((feat, hb), lambda j, f: (0, j)),
+            pl.BlockSpec((feat, hb), lambda j, f: (0, j)),
+            pl.BlockSpec((hb, feat), lambda j, f: (j, 0)),
+        ],
+        out_specs=[full, full],
+        scratch_shapes=[pltpu.VMEM((rows, feat), arrived.dtype)] * 2
+        + [pltpu.VMEM((rows, feat), jnp.float32)] * 2,
+    )
+    return pl.pallas_call(
+        _pair_kernel,
+        grid_spec=grid_spec,
+        out_shape=[jax.ShapeDtypeStruct((rows, feat), jnp.bfloat16)] * 2,
+        compiler_params=pltpu.CompilerParams(
+            dimension_semantics=("arbitrary",), vmem_limit_bytes=56 * 1024 * 1024
+        ),
+    )(first, arrived, partner, gw, uw, dw)
+
+
 def apply_combine(combine, partial_sums):
     return jnp.dot(combine, partial_sums, precision=lax.Precision.HIGHEST)
 
@@ -250,12 +318,15 @@
     arrived = exchange(sending, "expert")
     swap = group_perm(expert_count, group_size, 1)
     partner = lax.ppermute(arrived, "expert", swap)
-    first = member == 0
-    local_rows = jnp.where(first, arrived, partner).reshape(expert_count * capacity, feature_count)
-    local_grads = jnp.where(first, partner, arrived).reshape(expert_count * capacity, feature_count)
-    forward, backward = expert_share(local_rows, local_grads, gate_weight, up_weight, down_weight)
-    keep = jnp.where(first, forward, backward)
-    give = jnp.where(first, backward, forward)
+    first = (member == 0).astype(jnp.int32).reshape(1)
+    keep, give = expert_pair(
+        first,
+        arrived.reshape(expert_count * capacity, feature_count),
+        partner.reshape(expert_count * capacity, feature_count),
+        gate_weight,
+        up_weight,
+        down_weight,
+    )
     total = keep.astype(jnp.float32) + lax.ppermute(give, "expert", swap).astype(jnp.float32)
     came = exchange(
         total.astype(jnp.bfloat16).reshape(expert_count, capacity, feature_count), "expert"

time: 130 us -> 126 us (0.969)
  other arithmetic: 13.4 us -> 9.58 us
  waiting for transfers between devices: 24.5 us -> 23.1 us
    reshape x1, other arithmetic: 2.59 us -> 1.07 us  [by_pair(): arrived.reshape(expert_count * capacity, feature_count)]
    ppermute x1, waiting for transfers between devices: 2.44 us -> 1.03 us  [by_pair(): partner = lax.ppermute(arrived, 'expert', swap)]
    select_n x1 -> x0, other arithmetic: 1.3 us -> none  [by_pair(): give = jnp.where(first, backward, forward)]
    unnamed x24 -> x26, local copies, waits for them, and re-layouts: 7.88 us -> 8.8 us
  transfers between devices with their start and end apart: 21 -> 21, of which waited for: 8 -> 8; matrix products, arithmetic and copies ran while one was open for 8% -> 9% of each run, Pallas kernels for 0% -> 0%
where the time goes in v8:
time: 126 us
  starting transfers between devices  36.7 us (29%)
  Pallas kernels  32.3 us (26%)
  waiting for transfers between devices  23.1 us (18%)
  local copies, waits for them, and re-layouts  15.4 us (12%)
  other arithmetic  9.58 us (8%)
  matrix products  7.84 us (6%)
    pallas_call x1, Pallas kernels, expert_pair(): pl.pallas_call(_pair_kernel, grid_spec=grid_spec, out_shape=[jax.ShapeDty...  32.3 us
    ppermute x14, starting transfers between devices, exchange(): lax.ppermute(part, axis, [(i, (i + shift) % size) for i in range(size)])  24.5 us
    ppermute x14, waiting for transfers between devices, exchange(): lax.ppermute(part, axis, [(i, (i + shift) % size) for i in range(size)])  11.2 us
    ppermute x5, starting transfers between devices, butterfly_sum(): lax.ppermute(value, axis, [(i, i ^ bit) for i in range(size)])  10.1 us
    unnamed x26, local copies, waits for them, and re-layouts  8.8 us
    ppermute x5, waiting for transfers between devices, butterfly_sum(): lax.ppermute(value, axis, [(i, i ^ bit) for i in range(size)])  8.5 us
    dot_general x2, matrix products, apply_combine(): return jnp.dot(combine, partial_sums, precision=lax.Precision.HIGHEST)  5.14 us
    gather x2, local copies, waits for them, and re-layouts, exchange(): return jnp.take(stacked, order, axis=0)  3.57 us
  transfers between devices with their start and end apart: 21, of which 8 were waited for; matrix products, arithmetic and copies ran while one was open for 9% of the time, Pallas kernels for 0%

profile of v8, /device:TPU:0, one launch (start us, length us, event | category | flops | bytes accessed | tf_op | source)
XLA Modules:
  0.0 125.9 jit_solution(2055062410726216253)
XLA Ops:
  0.8 0.8 fusion.15
  2.3 2.1 %multiply_reduce_fusion.1 = f32[128]{0:T(128)S(1)} fusion(bf16[128,7168]{1,0:T(8,128)(2,1)} %param.11, f32[7168]{0:T(1024)} %param.12), kind=kLoop, calls=%fused_computation.12 | loop fusion | flops 3669888 | bytes 1864192 | tf_op jit(solution)/shard_map/reduce_sum | solution.py:41
  4.3 1.9 %fusion.2 = bf16[4,1,8,7168]{3,2,0,1:T(8,128)(2,1)S(1)} fusion(bf16[128,7168]{1,0:T(8,128)(2,1)} %param.19, s32[4,8]{1,0:T(4,128)S(1)} %select_reduce_fusion, pred[4,8]{1,0:T(4,128)(4,1)S(1)} %fusion.14), kind=kOutput, calls=%fused_computation.8 | convolution fusion | flops 58957824 | bytes 2293920 | tf_op jit(solution)/shard_map/fct,td->fcd/dot_general | solution.py:302
  6.3 0.8 fusion.1
  7.3 0.8 dynamic-slice_bitcast_fusion.7
  8.5 2.6 %collective-permute-start.1 = (bf16[8,7168]{1,0:T(8,128)(2,1)S(1)}, bf16[8,7168]{1,0:T(8,128)(2,1)S(1)}, u32[]{:S(2)}, u32[]{:S(2)}) collective-permute-start(bf16[8,7168]{1,0:T(8,128)(2,1)S(1)} %get-tuple-element.23), channel_id=1, source_target_pairs={{0,2},{1,3},{2,4},{3,5},{4,6},{5,7},{6,0},{7,1},{8,10},{9,11},{10,... | collective-permute-start | bytes 344072 | tf_op jit(solution)/shard_map/ppermute | solution.py:293
  11.1 2.6 %collective-permute-start.2 = (bf16[8,7168]{1,0:T(8,128)(2,1)S(1)}, bf16[8,7168]{1,0:T(8,128)(2,1)S(1)}, u32[]{:S(2)}, u32[]{:S(2)}) collective-permute-start(bf16[8,7168]{1,0:T(8,128)(2,1)S(1)} %get-tuple-element.22), channel_id=1, source_target_pairs={{0,3},{1,4},{2,5},{3,6},{4,7},{5,0},{6,1},{7,2},{8,11},{9,12},{10,... | collective-permute-start | bytes 344072 | tf_op jit(solution)/shard_map/ppermute | solution.py:293
  13.7 1.2 collective-permute-start.3
  14.9 1.1 collective-permute-start.4
  16.1 2.3 %collective-permute-start.5 = (bf16[8,7168]{1,0:T(8,128)(2,1)S(1)}, bf16[8,7168]{1,0:T(8,128)(2,1)S(1)}, u32[]{:S(2)}, u32[]{:S(2)}) collective-permute-start(bf16[8,7168]{1,0:T(8,128)(2,1)S(1)} %get-tuple-element.19), channel_id=1, source_target_pairs={{0,6},{1,7},{2,0},{3,1},{4,2},{5,3},{6,4},{7,5},{8,14},{9,15},{10,... | collective-permute-start | bytes 344072 | tf_op jit(solution)/shard_map/ppermute | solution.py:293
  19.1 1.2 collective-permute-start.6
  20.9 5.3 %collective-permute-done.2 = bf16[8,7168]{1,0:T(8,128)(2,1)S(1)} collective-permute-done((bf16[8,7168]{1,0:T(8,128)(2,1)S(1)}, bf16[8,7168]{1,0:T(8,128)(2,1)S(1)}, u32[]{:S(2)}, u32[]{:S(2)}) %collective-permute-start.2) | collective-permute-done | bytes 114720 | tf_op jit(solution)/shard_map/ppermute | solution.py:293
  26.9 0.7 bitcast_dynamic-update-slice_fusion.10
  27.5 0.7 bitcast_dynamic-update-slice_fusion.9
  28.2 0.7 bitcast_dynamic-update-slice_fusion.8
  28.8 0.7 bitcast_dynamic-update-slice_fusion.7
  29.5 1.8 %gather_fusion = bf16[8,8,7168]{2,1,0:T(8,128)(2,1)S(1)} fusion(bf16[8,8,7168]{2,1,0:T(8,128)(2,1)} %bitcast_dynamic-update-slice_fusion.7, s32[1024]{0:T(1024)S(1)} %pad_clamp_fusion), kind=kCustom, calls=%fused_computation.clone | custom fusion | bytes 1835040 | tf_op jit(solution)/shard_map/jit(_take)/gather | solution.py:296
  31.4 1.7 %collective-permute-start.7 = (bf16[8,8,7168]{2,1,0:T(8,128)(2,1)S(1)}, bf16[8,8,7168]{2,1,0:T(8,128)(2,1)S(1)}, u32[]{:S(2)}, u32[]{:S(2)}) collective-permute-start(bf16[8,8,7168]{2,1,0:T(8,128)(2,1)S(1)} %broadcast_select_fusion), channel_id=1, source_target_pairs={{0,1},{1,0},{2,3},{3,2},{4,5},{5,4},{6,7},{7,6},{8,9},{9,8},{10,11... | collective-permute-start | bytes 2752520 | tf_op jit(solution)/shard_map/ppermute | solution.py:320
  33.1 1.1 fusion.33.a_ref
  34.2 1.0 collective-permute-done.7
  35.2 0.9 copy-done.2
  36.1 32.3 %shard_map.112 = (bf16[64,7168]{1,0:T(8,128)(2,1)}, bf16[64,7168]{1,0:T(8,128)(2,1)}) custom-call(s32[1]{0:T(128)} %bitcast.1.first_ref, bf16[64,7168]{1,0:T(8,128)(2,1)} %fusion.33.a_ref, bf16[64,7168]{1,0:T(8,128)(2,1)} %bitcast.92, bf16[7168,1024]{1,0:T(8,128)(2,1)} %g_ref.1, bf16[7168,1024]{1,0:T(8,128)(2,1)} %u_ref.1, bf16[1024,7168]{1,0:T(8,128)(2,1)} %d_ref.1), custom_call_target="tpu_custom_call" | custom-call | tf_op jit(solution)/shard_map/pallas_call | solution.py:190
  68.9 2.3 %collective-permute-done.8 = bf16[64,7168]{1,0:T(8,128)(2,1)S(1)} collective-permute-done((bf16[64,7168]{1,0:T(8,128)(2,1)}, bf16[64,7168]{1,0:T(8,128)(2,1)S(1)}, u32[]{:S(2)}, u32[]{:S(2)}) %collective-permute-start.8) | collective-permute-done | bytes 917536 | tf_op jit(solution)/shard_map/ppermute | solution.py:330
  71.2 1.4 %fusion.9 = bf16[8,8,7168]{2,1,0:T(8,128)(2,1)S(1)} fusion(bf16[64,7168]{1,0:T(8,128)(2,1)S(1)} %collective-permute-done.8, bf16[64,7168]{1,0:T(8,128)(2,1)} %get-tuple-element.6), kind=kLoop, calls=%fused_computation.20 | loop fusion | flops 1835008 | bytes 2752512 | tf_op jit(solution)/shard_map/reshape | solution.py:332
  72.6 0.7 dynamic-slice_bitcast_fusion
  73.8 4.4 %collective-permute-start.10 = (bf16[8,7168]{1,0:T(8,128)(2,1)S(1)}, bf16[8,7168]{1,0:T(8,128)(2,1)S(1)}, u32[]{:S(2)}, u32[]{:S(2)}) collective-permute-start(bf16[8,7168]{1,0:T(8,128)(2,1)S(1)} %get-tuple-element.15), channel_id=1, source_target_pairs={{0,2},{1,3},{2,4},{3,5},{4,6},{5,7},{6,0},{7,1},{8,10},{9,11},{10,... | collective-permute-start | bytes 344072 | tf_op jit(solution)/shard_map/ppermute | solution.py:293
  78.1 2.7 %collective-permute-start.11 = (bf16[8,7168]{1,0:T(8,128)(2,1)S(1)}, bf16[8,7168]{1,0:T(8,128)(2,1)S(1)}, u32[]{:S(2)}, u32[]{:S(2)}) collective-permute-start(bf16[8,7168]{1,0:T(8,128)(2,1)S(1)} %get-tuple-element.14), channel_id=1, source_target_pairs={{0,3},{1,4},{2,5},{3,6},{4,7},{5,0},{6,1},{7,2},{8,11},{9,12},{10,... | collective-permute-start | bytes 344072 | tf_op jit(solution)/shard_map/ppermute | solution.py:293
  80.9 0.7 collective-permute-start.12
  81.6 2.0 %collective-permute-start.13 = (bf16[8,7168]{1,0:T(8,128)(2,1)S(1)}, bf16[8,7168]{1,0:T(8,128)(2,1)S(1)}, u32[]{:S(2)}, u32[]{:S(2)}) collective-permute-start(bf16[8,7168]{1,0:T(8,128)(2,1)S(1)} %get-tuple-element.12), channel_id=1, source_target_pairs={{0,5},{1,6},{2,7},{3,0},{4,1},{5,2},{6,3},{7,4},{8,13},{9,14},{10,... | collective-permute-start | bytes 344072 | tf_op jit(solution)/shard_map/ppermute | solution.py:293
  83.6 1.0 collective-permute-start.14
  85.3 1.7 %collective-permute-start.15 = (bf16[8,7168]{1,0:T(8,128)(2,1)S(1)}, bf16[8,7168]{1,0:T(8,128)(2,1)S(1)}, u32[]{:S(2)}, u32[]{:S(2)}) collective-permute-start(bf16[8,7168]{1,0:T(8,128)(2,1)S(1)} %get-tuple-element.10), channel_id=1, source_target_pairs={{0,7},{1,0},{2,1},{3,2},{4,3},{5,4},{6,5},{7,6},{8,15},{9,8},{10,9... | collective-permute-start | bytes 344072 | tf_op jit(solution)/shard_map/ppermute | solution.py:293
  87.7 5.9 %collective-permute-done.11 = bf16[8,7168]{1,0:T(8,128)(2,1)S(1)} collective-permute-done((bf16[8,7168]{1,0:T(8,128)(2,1)S(1)}, bf16[8,7168]{1,0:T(8,128)(2,1)S(1)}, u32[]{:S(2)}, u32[]{:S(2)}) %collective-permute-start.11) | collective-permute-done | bytes 114720 | tf_op jit(solution)/shard_map/ppermute | solution.py:293
  94.3 0.7 bitcast_dynamic-update-slice_fusion.3
  94.9 0.7 bitcast_dynamic-update-slice_fusion.2
  95.6 0.7 bitcast_dynamic-update-slice_fusion.1
  96.9 1.8 %gather_fusion.1 = bf16[8,8,7168]{2,1,0:T(8,128)(2,1)S(1)} fusion(bf16[8,8,7168]{2,1,0:T(8,128)(2,1)} %bitcast_dynamic-update-slice_fusion, s32[1024]{0:T(1024)S(1)} %pad_clamp_fusion), kind=kCustom, calls=%fused_computation.1.clone | custom fusion | bytes 1835040 | tf_op jit(solution)/shard_map/jit(_take)/gather | solution.py:296
  98.9 2.2 %multiply_reduce_fusion = (f32[128]{0:T(128)S(1)}, f32[128,7168]{1,0:T(8,128)S(1)}) fusion(bf16[128,7168]{1,0:T(8,128)(2,1)S(1)} %copy-done, f32[7168]{0:T(1024)S(1)} %copy-done.3, f32[7168]{0:T(1024)S(1)} %copy-done.4, bf16[4,2,8,7168]{3,2,1,0:T(8,128)(2,1)S(1)} %bitcast.90, f32[128,4]{0,1:T(4,128)S(1)} %select_reduce_fusion.1, ...), kind=kOutput, calls=%fused_computation.10 | convolution fusion | flops 356917120 | bytes 6025728 | tf_op jit(solution)/shard_map/dot_general | solution.py:201
  101.0 2.6 %fusion.32 = (f32[7168]{0:T(1024)S(1)}, bf16[128,7168]{1,0:T(8,128)(2,1)}) fusion(f32[128]{0:T(128)S(1)} %broadcast_multiply_fusion, f32[128]{0:T(128)S(1)} %get-tuple-element.26, f32[7168]{0:T(1024)S(1)} %copy-done.3, bf16[128,7168]{1,0:T(8,128)(2,1)S(1)} %copy-done, f32[128,7168]{1,0:T(8,128)S(1)} %get-tuple-element.29, f32[128]{0:T(128)S(1)} %get-tuple-element.27, ...), kind=kLoop, calls=%fused_computation.92 | loop fusion | flops 9167872 | bytes 9233920 | tf_op jit(solution)/shard_map/reduce_sum | solution.py:373
  103.7 1.6 %collective-permute-start.16 = (f32[7168]{0:T(1024)S(1)}, f32[7168]{0:T(1024)S(1)}, u32[]{:S(2)}, u32[]{:S(2)}) collective-permute-start(f32[7168]{0:T(1024)S(1)} %get-tuple-element.8), channel_id=1, source_target_pairs={{0,1},{1,0},{2,3},{3,2},{4,5},{5,4},{6,7},{7,6},{8,9},{9,8},{10,11... | collective-permute-start | bytes 86024 | tf_op jit(solution)/shard_map/ppermute | solution.py:238
  105.3 0.9 collective-permute-done.16
  106.2 4.2 %collective-permute-start.17 = (f32[7168]{0:T(1024)S(1)}, f32[7168]{0:T(1024)S(1)}, u32[]{:S(2)}, u32[]{:S(2)}) collective-permute-start(f32[7168]{0:T(1024)S(1)} %add.186), channel_id=1, source_target_pairs={{0,2},{1,3},{2,0},{3,1},{4,6},{5,7},{6,4},{7,5},{8,10},{9,11},{10,... | collective-permute-start | bytes 86024 | tf_op jit(solution)/shard_map/ppermute | solution.py:238
  110.3 1.8 %collective-permute-done.17 = f32[7168]{0:T(1024)S(1)} collective-permute-done((f32[7168]{0:T(1024)S(1)}, f32[7168]{0:T(1024)S(1)}, u32[]{:S(2)}, u32[]{:S(2)}) %collective-permute-start.17) | collective-permute-done | bytes 28704 | tf_op jit(solution)/shard_map/ppermute | solution.py:238
  112.2 1.4 %collective-permute-start.18 = (f32[7168]{0:T(1024)S(1)}, f32[7168]{0:T(1024)S(1)}, u32[]{:S(2)}, u32[]{:S(2)}) collective-permute-start(f32[7168]{0:T(1024)S(1)} %add.187), channel_id=1, source_target_pairs={{0,4},{1,5},{2,6},{3,7},{4,0},{5,1},{6,2},{7,3},{8,12},{9,13},{10,... | collective-permute-start | bytes 86024 | tf_op jit(solution)/shard_map/ppermute | solution.py:238
  113.5 3.4 %collective-permute-done.18 = f32[7168]{0:T(1024)S(1)} collective-permute-done((f32[7168]{0:T(1024)S(1)}, f32[7168]{0:T(1024)S(1)}, u32[]{:S(2)}, u32[]{:S(2)}) %collective-permute-start.18) | collective-permute-done | bytes 28704 | tf_op jit(solution)/shard_map/ppermute | solution.py:238
  117.0 1.5 %collective-permute-start.19 = (f32[7168]{0:T(1024)S(1)}, f32[7168]{0:T(1024)S(1)}, u32[]{:S(2)}, u32[]{:S(2)}) collective-permute-start(f32[7168]{0:T(1024)S(1)} %add.188), channel_id=1, source_target_pairs={{0,8},{8,0},{16,24},{24,16},{1,9},{9,1},{17,25},{25,17},{2,10},{10... | collective-permute-start | bytes 86024 | tf_op jit(solution)/shard_map/ppermute | solution.py:238
  118.5 2.4 %collective-permute-done.19 = f32[7168]{0:T(1024)S(1)} collective-permute-done((f32[7168]{0:T(1024)S(1)}, f32[7168]{0:T(1024)S(1)}, u32[]{:S(2)}, u32[]{:S(2)}) %collective-permute-start.19) | collective-permute-done | bytes 28704 | tf_op jit(solution)/shard_map/ppermute | solution.py:238
  120.8 1.5 %collective-permute-start.20 = (f32[7168]{0:T(1024)S(1)}, f32[7168]{0:T(1024)S(1)}, u32[]{:S(2)}, u32[]{:S(2)}) collective-permute-start(f32[7168]{0:T(1024)S(1)} %add.189), channel_id=1, source_target_pairs={{0,16},{8,24},{16,0},{24,8},{1,17},{9,25},{17,1},{25,9},{2,18},{10... | collective-permute-start | bytes 86024 | tf_op jit(solution)/shard_map/ppermute | solution.py:238
  122.3 3.0 %fusion = bf16[128,7168]{1,0:T(8,128)(2,1)} fusion(bf16[128,7168]{1,0:T(8,128)(2,1)S(1)} %copy-done, f32[7168]{0:T(1024)S(1)} %copy-done.3, bf16[4,2,8,7168]{3,2,1,0:T(8,128)(2,1)S(1)} %bitcast.91, f32[128,4]{0,1:T(4,128)S(1)} %select_reduce_fusion.1, s32[128,4]{0,1:T(4,128)S(1)} %add_select_fusion), kind=kOutput, calls=%fused_computation.4 | convolution fusion | flops 355999744 | bytes 4161536 | tf_op jit(solution)/shard_map/dot_general | solution.py:201
  (59 shorter events, 7.8 us)
Async XLA Ops:
  0.6 5.6 %copy-start = (bf16[128,7168]{1,0:T(8,128)(2,1)S(1)}, bf16[128,7168]{1,0:T(8,128)(2,1)}, u32[]{:S(2)}) copy-start(bf16[128,7168]{1,0:T(8,128)(2,1)} %param.11) | copy-start | bytes 5505028
  0.6 5.6 %copy-start.3 = (f32[7168]{0:T(1024)S(1)}, f32[7168]{0:T(1024)}, u32[]{:S(2)}) copy-start(f32[7168]{0:T(1024)} %param.12) | copy-start | bytes 86020
  0.7 5.6 %copy-start.4 = (f32[7168]{0:T(1024)S(1)}, f32[7168]{0:T(1024)}, u32[]{:S(2)}) copy-start(f32[7168]{0:T(1024)} %param.13) | copy-start | bytes 86020
  8.0 8.1 %collective-permute-start = (bf16[8,7168]{1,0:T(8,128)(2,1)}, bf16[8,7168]{1,0:T(8,128)(2,1)S(1)}, u32[]{:S(2)}, u32[]{:S(2)}) collective-permute-start(bf16[8,7168]{1,0:T(8,128)(2,1)} %get-tuple-element.24), channel_id=1, source_target_pairs={{0,1},{1,2},{2,3},{3,4},{4,5},{5,6},{6,7},{7,0},{8,9},{9,10},{10,1... | collective-permute-start | bytes 344072 | tf_op jit(solution)/shard_map/ppermute | solution.py:293
  8.5 10.5 %collective-permute-start.1 = (bf16[8,7168]{1,0:T(8,128)(2,1)S(1)}, bf16[8,7168]{1,0:T(8,128)(2,1)S(1)}, u32[]{:S(2)}, u32[]{:S(2)}) collective-permute-start(bf16[8,7168]{1,0:T(8,128)(2,1)S(1)} %get-tuple-element.23), channel_id=1, source_target_pairs={{0,2},{1,3},{2,4},{3,5},{4,6},{5,7},{6,0},{7,1},{8,10},{9,11},{10,... | collective-permute-start | bytes 344072 | tf_op jit(solution)/shard_map/ppermute | solution.py:293
  11.1 15.1 %collective-permute-start.2 = (bf16[8,7168]{1,0:T(8,128)(2,1)S(1)}, bf16[8,7168]{1,0:T(8,128)(2,1)S(1)}, u32[]{:S(2)}, u32[]{:S(2)}) collective-permute-start(bf16[8,7168]{1,0:T(8,128)(2,1)S(1)} %get-tuple-element.22), channel_id=1, source_target_pairs={{0,3},{1,4},{2,5},{3,6},{4,7},{5,0},{6,1},{7,2},{8,11},{9,12},{10,... | collective-permute-start | bytes 344072 | tf_op jit(solution)/shard_map/ppermute | solution.py:293
  13.7 13.2 %collective-permute-start.3 = (bf16[8,7168]{1,0:T(8,128)(2,1)S(1)}, bf16[8,7168]{1,0:T(8,128)(2,1)S(1)}, u32[]{:S(2)}, u32[]{:S(2)}) collective-permute-start(bf16[8,7168]{1,0:T(8,128)(2,1)S(1)} %get-tuple-element.21), channel_id=1, source_target_pairs={{0,4},{1,5},{2,6},{3,7},{4,0},{5,1},{6,2},{7,3},{8,12},{9,13},{10,... | collective-permute-start | bytes 344072 | tf_op jit(solution)/shard_map/ppermute | solution.py:293
  14.9 12.6 %collective-permute-start.4 = (bf16[8,7168]{1,0:T(8,128)(2,1)S(1)}, bf16[8,7168]{1,0:T(8,128)(2,1)S(1)}, u32[]{:S(2)}, u32[]{:S(2)}) collective-permute-start(bf16[8,7168]{1,0:T(8,128)(2,1)S(1)} %get-tuple-element.20), channel_id=1, source_target_pairs={{0,5},{1,6},{2,7},{3,0},{4,1},{5,2},{6,3},{7,4},{8,13},{9,14},{10,... | collective-permute-start | bytes 344072 | tf_op jit(solution)/shard_map/ppermute | solution.py:293
  16.1 12.1 %collective-permute-start.5 = (bf16[8,7168]{1,0:T(8,128)(2,1)S(1)}, bf16[8,7168]{1,0:T(8,128)(2,1)S(1)}, u32[]{:S(2)}, u32[]{:S(2)}) collective-permute-start(bf16[8,7168]{1,0:T(8,128)(2,1)S(1)} %get-tuple-element.19), channel_id=1, source_target_pairs={{0,6},{1,7},{2,0},{3,1},{4,2},{5,3},{6,4},{7,5},{8,14},{9,15},{10,... | collective-permute-start | bytes 344072 | tf_op jit(solution)/shard_map/ppermute | solution.py:293
  19.1 9.8 %collective-permute-start.6 = (bf16[8,7168]{1,0:T(8,128)(2,1)S(1)}, bf16[8,7168]{1,0:T(8,128)(2,1)S(1)}, u32[]{:S(2)}, u32[]{:S(2)}) collective-permute-start(bf16[8,7168]{1,0:T(8,128)(2,1)S(1)} %get-tuple-element.18), channel_id=1, source_target_pairs={{0,7},{1,0},{2,1},{3,2},{4,3},{5,4},{6,5},{7,6},{8,15},{9,8},{10,9... | collective-permute-start | bytes 344072 | tf_op jit(solution)/shard_map/ppermute | solution.py:293
  31.4 3.8 %collective-permute-start.7 = (bf16[8,8,7168]{2,1,0:T(8,128)(2,1)S(1)}, bf16[8,8,7168]{2,1,0:T(8,128)(2,1)S(1)}, u32[]{:S(2)}, u32[]{:S(2)}) collective-permute-start(bf16[8,8,7168]{2,1,0:T(8,128)(2,1)S(1)} %broadcast_select_fusion), channel_id=1, source_target_pairs={{0,1},{1,0},{2,3},{3,2},{4,5},{5,4},{6,7},{7,6},{8,9},{9,8},{10,11... | collective-permute-start | bytes 2752520 | tf_op jit(solution)/shard_map/ppermute | solution.py:320
  35.2 0.9 copy-start.2
  68.5 5.3 %copy-start.6 = (s32[128,8]{0,1:T(8,128)S(1)}, s32[128,8]{0,1:T(8,128)}, u32[]{:S(2)}) copy-start(s32[128,8]{0,1:T(8,128)} %param.15) | copy-start | bytes 12292
  68.5 5.3 %copy-start.5 = (s32[128,8]{0,1:T(8,128)S(1)}, s32[128,8]{0,1:T(8,128)}, u32[]{:S(2)}) copy-start(s32[128,8]{0,1:T(8,128)} %param.14) | copy-start | bytes 12292
  68.5 2.7 %collective-permute-start.8 = (bf16[64,7168]{1,0:T(8,128)(2,1)}, bf16[64,7168]{1,0:T(8,128)(2,1)S(1)}, u32[]{:S(2)}, u32[]{:S(2)}) collective-permute-start(bf16[64,7168]{1,0:T(8,128)(2,1)} %get-tuple-element.7), channel_id=1, source_target_pairs={{0,1},{1,0},{2,3},{3,2},{4,5},{5,4},{6,7},{7,6},{8,9},{9,8},{10,11... | collective-permute-start | bytes 2752520 | tf_op jit(solution)/shard_map/ppermute | solution.py:330
  73.4 10.2 %collective-permute-start.9 = (bf16[8,7168]{1,0:T(8,128)(2,1)S(1)}, bf16[8,7168]{1,0:T(8,128)(2,1)S(1)}, u32[]{:S(2)}, u32[]{:S(2)}) collective-permute-start(bf16[8,7168]{1,0:T(8,128)(2,1)S(1)} %get-tuple-element.16), channel_id=1, source_target_pairs={{0,1},{1,2},{2,3},{3,4},{4,5},{5,6},{6,7},{7,0},{8,9},{9,10},{10,1... | collective-permute-start | bytes 344072 | tf_op jit(solution)/shard_map/ppermute | solution.py:293
  73.8 11.5 %collective-permute-start.10 = (bf16[8,7168]{1,0:T(8,128)(2,1)S(1)}, bf16[8,7168]{1,0:T(8,128)(2,1)S(1)}, u32[]{:S(2)}, u32[]{:S(2)}) collective-permute-start(bf16[8,7168]{1,0:T(8,128)(2,1)S(1)} %get-tuple-element.15), channel_id=1, source_target_pairs={{0,2},{1,3},{2,4},{3,5},{4,6},{5,7},{6,0},{7,1},{8,10},{9,11},{10,... | collective-permute-start | bytes 344072 | tf_op jit(solution)/shard_map/ppermute | solution.py:293
  78.1 15.5 %collective-permute-start.11 = (bf16[8,7168]{1,0:T(8,128)(2,1)S(1)}, bf16[8,7168]{1,0:T(8,128)(2,1)S(1)}, u32[]{:S(2)}, u32[]{:S(2)}) collective-permute-start(bf16[8,7168]{1,0:T(8,128)(2,1)S(1)} %get-tuple-element.14), channel_id=1, source_target_pairs={{0,3},{1,4},{2,5},{3,6},{4,7},{5,0},{6,1},{7,2},{8,11},{9,12},{10,... | collective-permute-start | bytes 344072 | tf_op jit(solution)/shard_map/ppermute | solution.py:293
  80.9 13.4 %collective-permute-start.12 = (bf16[8,7168]{1,0:T(8,128)(2,1)S(1)}, bf16[8,7168]{1,0:T(8,128)(2,1)S(1)}, u32[]{:S(2)}, u32[]{:S(2)}) collective-permute-start(bf16[8,7168]{1,0:T(8,128)(2,1)S(1)} %get-tuple-element.13), channel_id=1, source_target_pairs={{0,4},{1,5},{2,6},{3,7},{4,0},{5,1},{6,2},{7,3},{8,12},{9,13},{10,... | collective-permute-start | bytes 344072 | tf_op jit(solution)/shard_map/ppermute | solution.py:293
  81.6 13.3 %collective-permute-start.13 = (bf16[8,7168]{1,0:T(8,128)(2,1)S(1)}, bf16[8,7168]{1,0:T(8,128)(2,1)S(1)}, u32[]{:S(2)}, u32[]{:S(2)}) collective-permute-start(bf16[8,7168]{1,0:T(8,128)(2,1)S(1)} %get-tuple-element.12), channel_id=1, source_target_pairs={{0,5},{1,6},{2,7},{3,0},{4,1},{5,2},{6,3},{7,4},{8,13},{9,14},{10,... | collective-permute-start | bytes 344072 | tf_op jit(solution)/shard_map/ppermute | solution.py:293
  83.6 12.0 %collective-permute-start.14 = (bf16[8,7168]{1,0:T(8,128)(2,1)S(1)}, bf16[8,7168]{1,0:T(8,128)(2,1)S(1)}, u32[]{:S(2)}, u32[]{:S(2)}) collective-permute-start(bf16[8,7168]{1,0:T(8,128)(2,1)S(1)} %get-tuple-element.11), channel_id=1, source_target_pairs={{0,6},{1,7},{2,0},{3,1},{4,2},{5,3},{6,4},{7,5},{8,14},{9,15},{10,... | collective-permute-start | bytes 344072 | tf_op jit(solution)/shard_map/ppermute | solution.py:293
  85.3 11.0 %collective-permute-start.15 = (bf16[8,7168]{1,0:T(8,128)(2,1)S(1)}, bf16[8,7168]{1,0:T(8,128)(2,1)S(1)}, u32[]{:S(2)}, u32[]{:S(2)}) collective-permute-start(bf16[8,7168]{1,0:T(8,128)(2,1)S(1)} %get-tuple-element.10), channel_id=1, source_target_pairs={{0,7},{1,0},{2,1},{3,2},{4,3},{5,4},{6,5},{7,6},{8,15},{9,8},{10,9... | collective-permute-start | bytes 344072 | tf_op jit(solution)/shard_map/ppermute | solution.py:293
  98.7 2.3 %copy-start.1 = (bf16[128,7168]{1,0:T(8,128)(2,1)S(1)}, bf16[128,7168]{1,0:T(8,128)(2,1)}, u32[]{:S(2)}) copy-start(bf16[128,7168]{1,0:T(8,128)(2,1)} %param.19) | copy-start | bytes 5505028
  103.7 2.5 %collective-permute-start.16 = (f32[7168]{0:T(1024)S(1)}, f32[7168]{0:T(1024)S(1)}, u32[]{:S(2)}, u32[]{:S(2)}) collective-permute-start(f32[7168]{0:T(1024)S(1)} %get-tuple-element.8), channel_id=1, source_target_pairs={{0,1},{1,0},{2,3},{3,2},{4,5},{5,4},{6,7},{7,6},{8,9},{9,8},{10,11... | collective-permute-start | bytes 86024 | tf_op jit(solution)/shard_map/ppermute | solution.py:238
  106.2 6.0 %collective-permute-start.17 = (f32[7168]{0:T(1024)S(1)}, f32[7168]{0:T(1024)S(1)}, u32[]{:S(2)}, u32[]{:S(2)}) collective-permute-start(f32[7168]{0:T(1024)S(1)} %add.186), channel_id=1, source_target_pairs={{0,2},{1,3},{2,0},{3,1},{4,6},{5,7},{6,4},{7,5},{8,10},{9,11},{10,... | collective-permute-start | bytes 86024 | tf_op jit(solution)/shard_map/ppermute | solution.py:238
  112.2 4.8 %collective-permute-start.18 = (f32[7168]{0:T(1024)S(1)}, f32[7168]{0:T(1024)S(1)}, u32[]{:S(2)}, u32[]{:S(2)}) collective-permute-start(f32[7168]{0:T(1024)S(1)} %add.187), channel_id=1, source_target_pairs={{0,4},{1,5},{2,6},{3,7},{4,0},{5,1},{6,2},{7,3},{8,12},{9,13},{10,... | collective-permute-start | bytes 86024 | tf_op jit(solution)/shard_map/ppermute | solution.py:238
  117.0 3.9 %collective-permute-start.19 = (f32[7168]{0:T(1024)S(1)}, f32[7168]{0:T(1024)S(1)}, u32[]{:S(2)}, u32[]{:S(2)}) collective-permute-start(f32[7168]{0:T(1024)S(1)} %add.188), channel_id=1, source_target_pairs={{0,8},{8,0},{16,24},{24,16},{1,9},{9,1},{17,25},{25,17},{2,10},{10... | collective-permute-start | bytes 86024 | tf_op jit(solution)/shard_map/ppermute | solution.py:238
  120.8 4.5 %collective-permute-start.20 = (f32[7168]{0:T(1024)S(1)}, f32[7168]{0:T(1024)S(1)}, u32[]{:S(2)}, u32[]{:S(2)}) collective-permute-start(f32[7168]{0:T(1024)S(1)} %add.189), channel_id=1, source_target_pairs={{0,16},{8,24},{16,0},{24,8},{1,17},{9,25},{17,1},{25,9},{2,18},{10... | collective-permute-start | bytes 86024 | tf_op jit(solution)/shard_map/ppermute | solution.py:238

commit v9 on v8

--- a/solution.py
+++ b/solution.py
@@ -130,7 +130,7 @@
 
 
 def _pair_kernel(
-    first_ref, a_ref, p_ref, g_ref, u_ref, d_ref, keep_ref, give_ref, xs, ys, acc_o, acc_b
+    first_ref, a_ref, p_ref, g_ref, u_ref, d_ref, both_ref, xs, ys, acc_o, acc_b
 ):
     j = pl.program_id(0)
     first = first_ref[0] == 1
@@ -162,10 +162,8 @@
 
     @pl.when(j == pl.num_programs(0) - 1)
     def _():
-        out = acc_o[...].astype(keep_ref.dtype)
-        back = acc_b[...].astype(keep_ref.dtype)
-        keep_ref[...] = jnp.where(first, out, back)
-        give_ref[...] = jnp.where(first, back, out)
+        both_ref[0] = acc_o[...].astype(both_ref.dtype)
+        both_ref[1] = acc_b[...].astype(both_ref.dtype)
 
 
 def expert_pair(first, arrived, partner, gw, uw, dw):
@@ -183,14 +181,14 @@
             pl.BlockSpec((feat, hb), lambda j, f: (0, j)),
             pl.BlockSpec((hb, feat), lambda j, f: (j, 0)),
         ],
-        out_specs=[full, full],
+        out_specs=pl.BlockSpec((2, rows, feat), lambda j, f: (0, 0, 0)),
         scratch_shapes=[pltpu.VMEM((rows, feat), arrived.dtype)] * 2
         + [pltpu.VMEM((rows, feat), jnp.float32)] * 2,
     )
     return pl.pallas_call(
         _pair_kernel,
         grid_spec=grid_spec,
-        out_shape=[jax.ShapeDtypeStruct((rows, feat), jnp.bfloat16)] * 2,
+        out_shape=jax.ShapeDtypeStruct((2, rows, feat), jnp.bfloat16),
         compiler_params=pltpu.CompilerParams(
             dimension_semantics=("arbitrary",), vmem_limit_bytes=56 * 1024 * 1024
         ),
@@ -305,6 +303,23 @@
     return picked.astype(values.dtype)
 
 
+def by_parity(chunks, odd, flight, group_size):
+    size = lax.axis_size("expert")
+    me = lax.axis_index("expert")
+    moved = []
+    for shift in range(odd, size, group_size):
+        part = lax.dynamic_index_in_dim(chunks, (me + shift) % size, 0, keepdims=False)
+        if shift == 0:
+            moved.append(part)
+        else:
+            moved.append(lax.ppermute(part, "expert", [(i, (i + shift) % size) for i in range(size)]))
+    stacked = jnp.stack(moved)
+    chip = me // group_size
+    order = (chip - jnp.arange(flight, dtype=jnp.int32) + odd * (me % group_size - 1)) % flight
+    picked = jnp.take(stacked, order, axis=0)
+    return picked.reshape(flight * chunks.shape[1], chunks.shape[2])
+
+
 def by_pair(
     normed, out_grad, slot_table, filled, gate_weight, up_weight, down_weight,
     member, expert_count, group_size,
@@ -319,7 +334,7 @@
     swap = group_perm(expert_count, group_size, 1)
     partner = lax.ppermute(arrived, "expert", swap)
     first = (member == 0).astype(jnp.int32).reshape(1)
-    keep, give = expert_pair(
+    both = expert_pair(
         first,
         arrived.reshape(expert_count * capacity, feature_count),
         partner.reshape(expert_count * capacity, feature_count),
@@ -327,12 +342,10 @@
         up_weight,
         down_weight,
     )
-    total = keep.astype(jnp.float32) + lax.ppermute(give, "expert", swap).astype(jnp.float32)
-    came = exchange(
-        total.astype(jnp.bfloat16).reshape(expert_count, capacity, feature_count), "expert"
-    ).reshape(flight, 2, capacity, feature_count)
-    out_sums = came[:, 0].reshape(flight * capacity, feature_count).astype(jnp.float32)
-    grad_sums = came[:, 1].reshape(flight * capacity, feature_count).astype(jnp.float32)
+    sums = both.astype(jnp.float32) + lax.ppermute(both, "expert", swap).astype(jnp.float32)
+    sums = sums.astype(jnp.bfloat16).reshape(2, expert_count, capacity, feature_count)
+    grad_sums = by_parity(sums[1], 0, flight, group_size).astype(jnp.float32)
+    out_sums = by_parity(sums[0], 1, flight, group_size).astype(jnp.float32)
     return out_sums, grad_sums
 
 

time: 126 us -> 126 us (level)
  local copies, waits for them, and re-layouts: 15.4 us -> 10.8 us
  waiting for transfers between devices: 23.1 us -> 26.8 us
  other arithmetic: 9.58 us -> 12.4 us
  starting transfers between devices: 36.7 us -> 34.2 us
    ppermute x1 -> x8, starting transfers between devices: 0.44 us -> 13.5 us  [the longest x7 13.2 us: by_parity(): lax.ppermute(part, 'expert', [(i, (i + shift) % size) for i in range(size)])]
    ppermute x14 -> x7, starting transfers between devices: 24.5 us -> 11.4 us  [exchange(): lax.ppermute(part, axis, [(i, (i + shift) % size) for i in range(size)])]
    ppermute x1 -> x8, waiting for transfers between devices: 2.31 us -> 11.8 us  [the longest x7 8.04 us: by_parity(): lax.ppermute(part, 'expert', [(i, (i + shift) % size) for i in range(size)])]
    ppermute x14 -> x7, waiting for transfers between devices: 11.2 us -> 5.27 us  [exchange(): lax.ppermute(part, axis, [(i, (i + shift) % size) for i in range(size)])]
    unnamed x26 -> x20, local copies, waits for them, and re-layouts: 8.8 us -> 4.88 us
    ppermute x5, starting transfers between devices: 10.1 us -> 7.56 us  [butterfly_sum(): lax.ppermute(value, axis, [(i, i ^ bit) for i in range(size)])]
    convert_element_type x0 -> x1, other arithmetic: none -> 2.54 us  [by_pair(): sums.astype(jnp.bfloat16).reshape(2, expert_count, capacity, feature_count)]
    reshape x2 -> x0, other arithmetic: 2.46 us -> none  [the longest x1 1.39 us: by_pair(): total.astype(jnp.bfloat16).reshape(expert_count, capacity, feature_count)]
  transfers between devices with their start and end apart: 21 -> 21, of which waited for: 8 -> 8; matrix products, arithmetic and copies ran while one was open for 9% -> 7% of each run, Pallas kernels for 0% -> 0%
where the time goes in v9:
time: 126 us; the launch traced here: 125 us
  starting transfers between devices  34.2 us (27%)
  Pallas kernels  32.1 us (25%)
  waiting for transfers between devices  26.8 us (21%)
  other arithmetic  12.4 us (10%)
  local copies, waits for them, and re-layouts  10.8 us (9%)
  matrix products  7.88 us (6%)
    pallas_call x1, Pallas kernels, expert_pair(): pl.pallas_call(_pair_kernel, grid_spec=grid_spec, out_shape=jax.ShapeDtyp...  32.1 us
    ppermute x7, starting transfers between devices, by_parity(): lax.ppermute(part, 'expert', [(i, (i + shift) % size) for i in range(size)])  13.2 us
    ppermute x7, starting transfers between devices, exchange(): lax.ppermute(part, axis, [(i, (i + shift) % size) for i in range(size)])  11.4 us
    ppermute x5, waiting for transfers between devices, butterfly_sum(): lax.ppermute(value, axis, [(i, i ^ bit) for i in range(size)])  8.74 us
    ppermute x7, waiting for transfers between devices, by_parity(): lax.ppermute(part, 'expert', [(i, (i + shift) % size) for i in range(size)])  8.04 us
    ppermute x5, starting transfers between devices, butterfly_sum(): lax.ppermute(value, axis, [(i, i ^ bit) for i in range(size)])  7.56 us
    ppermute x7, waiting for transfers between devices, exchange(): lax.ppermute(part, axis, [(i, (i + shift) % size) for i in range(size)])  5.27 us
    dot_general x2, matrix products, apply_combine(): return jnp.dot(combine, partial_sums, precision=lax.Precision.HIGHEST)  5.19 us
  transfers between devices with their start and end apart: 21, of which 8 were waited for; matrix products, arithmetic and copies ran while one was open for 7% of the time, Pallas kernels for 0%

profile of v9, /device:TPU:0, one launch (start us, length us, event | category | flops | bytes accessed | tf_op | source)
XLA Modules:
  0.0 125.2 jit_solution(4559546753216298353)
XLA Ops:
  0.8 0.8 fusion.20
  2.3 2.1 %multiply_reduce_fusion.1 = f32[128]{0:T(128)S(1)} fusion(bf16[128,7168]{1,0:T(8,128)(2,1)} %param.11, f32[7168]{0:T(1024)} %param.12), kind=kLoop, calls=%fused_computation.16 | loop fusion | flops 3669888 | bytes 1864192 | tf_op jit(solution)/shard_map/reduce_sum | solution.py:41
  4.3 1.9 %fusion.4 = bf16[4,1,8,7168]{3,2,0,1:T(8,128)(2,1)S(1)} fusion(bf16[128,7168]{1,0:T(8,128)(2,1)} %param.19, s32[4,8]{1,0:T(4,128)S(1)} %select_reduce_fusion, pred[4,8]{1,0:T(4,128)(4,1)S(1)} %fusion.19), kind=kOutput, calls=%fused_computation.11 | convolution fusion | flops 58957824 | bytes 2293920 | tf_op jit(solution)/shard_map/fct,td->fcd/dot_general | solution.py:300
  6.3 0.8 fusion.3
  7.3 0.8 dynamic-slice_bitcast_fusion.7
  8.5 2.6 %collective-permute-start.1 = (bf16[8,7168]{1,0:T(8,128)(2,1)S(1)}, bf16[8,7168]{1,0:T(8,128)(2,1)S(1)}, u32[]{:S(2)}, u32[]{:S(2)}) collective-permute-start(bf16[8,7168]{1,0:T(8,128)(2,1)S(1)} %get-tuple-element.23), channel_id=1, source_target_pairs={{0,2},{1,3},{2,4},{3,5},{4,6},{5,7},{6,0},{7,1},{8,10},{9,11},{10,... | collective-permute-start | bytes 344072 | tf_op jit(solution)/shard_map/ppermute | solution.py:291
  11.1 2.6 %collective-permute-start.2 = (bf16[8,7168]{1,0:T(8,128)(2,1)S(1)}, bf16[8,7168]{1,0:T(8,128)(2,1)S(1)}, u32[]{:S(2)}, u32[]{:S(2)}) collective-permute-start(bf16[8,7168]{1,0:T(8,128)(2,1)S(1)} %get-tuple-element.22), channel_id=1, source_target_pairs={{0,3},{1,4},{2,5},{3,6},{4,7},{5,0},{6,1},{7,2},{8,11},{9,12},{10,... | collective-permute-start | bytes 344072 | tf_op jit(solution)/shard_map/ppermute | solution.py:291
  13.7 1.2 collective-permute-start.3
  14.9 1.1 collective-permute-start.4
  16.3 2.1 %collective-permute-start.5 = (bf16[8,7168]{1,0:T(8,128)(2,1)S(1)}, bf16[8,7168]{1,0:T(8,128)(2,1)S(1)}, u32[]{:S(2)}, u32[]{:S(2)}) collective-permute-start(bf16[8,7168]{1,0:T(8,128)(2,1)S(1)} %get-tuple-element.19), channel_id=1, source_target_pairs={{0,6},{1,7},{2,0},{3,1},{4,2},{5,3},{6,4},{7,5},{8,14},{9,15},{10,... | collective-permute-start | bytes 344072 | tf_op jit(solution)/shard_map/ppermute | solution.py:291
  18.4 0.7 bitcast_dynamic-update-slice_fusion.6
  19.1 1.2 collective-permute-start.6
  20.3 0.7 bitcast_dynamic-update-slice_fusion.5
  20.9 5.3 %collective-permute-done.2 = bf16[8,7168]{1,0:T(8,128)(2,1)S(1)} collective-permute-done((bf16[8,7168]{1,0:T(8,128)(2,1)S(1)}, bf16[8,7168]{1,0:T(8,128)(2,1)S(1)}, u32[]{:S(2)}, u32[]{:S(2)}) %collective-permute-start.2) | collective-permute-done | bytes 114720 | tf_op jit(solution)/shard_map/ppermute | solution.py:291
  26.2 0.7 bitcast_dynamic-update-slice_fusion.4
  26.9 0.7 bitcast_dynamic-update-slice_fusion.3
  27.5 0.7 bitcast_dynamic-update-slice_fusion.2
  28.2 0.7 bitcast_dynamic-update-slice_fusion.1
  28.8 0.7 bitcast_dynamic-update-slice_fusion
  29.5 1.8 %gather_fusion = bf16[8,8,7168]{2,1,0:T(8,128)(2,1)S(1)} fusion(bf16[8,8,7168]{2,1,0:T(8,128)(2,1)} %bitcast_dynamic-update-slice_fusion, s32[1024]{0:T(1024)S(1)} %pad_clamp_fusion.2), kind=kCustom, calls=%fused_computation.2 | custom fusion | bytes 1835040 | tf_op jit(solution)/shard_map/jit(_take)/gather | solution.py:294
  31.4 1.7 %collective-permute-start.7 = (bf16[8,8,7168]{2,1,0:T(8,128)(2,1)S(1)}, bf16[8,8,7168]{2,1,0:T(8,128)(2,1)S(1)}, u32[]{:S(2)}, u32[]{:S(2)}) collective-permute-start(bf16[8,8,7168]{2,1,0:T(8,128)(2,1)S(1)} %broadcast_select_fusion), channel_id=1, source_target_pairs={{0,1},{1,0},{2,3},{3,2},{4,5},{5,4},{6,7},{7,6},{8,9},{9,8},{10,11... | collective-permute-start | bytes 2752520 | tf_op jit(solution)/shard_map/ppermute | solution.py:335
  33.1 1.1 bitcast_select_fusion.a_ref
  34.2 1.0 collective-permute-done.7
  35.2 0.9 copy-done.2
  36.1 32.1 %shard_map.112 = bf16[2,64,7168]{2,1,0:T(8,128)(2,1)} custom-call(s32[1]{0:T(128)} %bitcast.first_ref, bf16[64,7168]{1,0:T(8,128)(2,1)} %bitcast_select_fusion.a_ref, bf16[64,7168]{1,0:T(8,128)(2,1)} %bitcast.81, bf16[7168,1024]{1,0:T(8,128)(2,1)} %g_ref.1, bf16[7168,1024]{1,0:T(8,128)(2,1)} %u_ref.1, bf16[1024,7168]{1,0:T(8,128)(2,1)} %d_ref.1), custom_call_target="tpu_custom_call" | custom-call | tf_op jit(solution)/shard_map/pallas_call | solution.py:188
  68.7 3.7 %collective-permute-done.8 = bf16[2,64,7168]{2,1,0:T(8,128)(2,1)} collective-permute-done((bf16[2,64,7168]{2,1,0:T(8,128)(2,1)}, bf16[2,64,7168]{2,1,0:T(8,128)(2,1)}, u32[]{:S(2)}, u32[]{:S(2)}) %collective-permute-start.8) | collective-permute-done | bytes 1835040 | tf_op jit(solution)/shard_map/ppermute | solution.py:345
  72.4 2.5 %add_convert_fusion = bf16[2,64,7168]{2,1,0:T(8,128)(2,1)S(1)} fusion(bf16[2,64,7168]{2,1,0:T(8,128)(2,1)} %collective-permute-done.8, bf16[2,64,7168]{2,1,0:T(8,128)(2,1)} %shard_map.112), kind=kLoop, calls=%fused_computation.14 | loop fusion | flops 3670016 | bytes 5505024 | tf_op jit(solution)/shard_map/convert_element_type | solution.py:346
  75.1 4.4 %collective-permute-start.13 = (bf16[8,7168]{1,0:T(8,128)(2,1)S(1)}, bf16[8,7168]{1,0:T(8,128)(2,1)S(1)}, u32[]{:S(2)}, u32[]{:S(2)}) collective-permute-start(bf16[8,7168]{1,0:T(8,128)(2,1)S(1)} %get-tuple-element.13), channel_id=1, source_target_pairs={{0,2},{1,3},{2,4},{3,5},{4,6},{5,7},{6,0},{7,1},{8,10},{9,11},{10,... | collective-permute-start | bytes 344072 | tf_op jit(solution)/shard_map/ppermute | solution.py:315
  79.5 3.1 %collective-permute-start.14 = (bf16[8,7168]{1,0:T(8,128)(2,1)S(1)}, bf16[8,7168]{1,0:T(8,128)(2,1)S(1)}, u32[]{:S(2)}, u32[]{:S(2)}) collective-permute-start(bf16[8,7168]{1,0:T(8,128)(2,1)S(1)} %get-tuple-element.12), channel_id=1, source_target_pairs={{0,4},{1,5},{2,6},{3,7},{4,0},{5,1},{6,2},{7,3},{8,12},{9,13},{10,... | collective-permute-start | bytes 344072 | tf_op jit(solution)/shard_map/ppermute | solution.py:315
  82.6 3.5 %collective-permute-done.13 = bf16[8,7168]{1,0:T(8,128)(2,1)S(1)} collective-permute-done((bf16[8,7168]{1,0:T(8,128)(2,1)S(1)}, bf16[8,7168]{1,0:T(8,128)(2,1)S(1)}, u32[]{:S(2)}, u32[]{:S(2)}) %collective-permute-start.13) | collective-permute-done | bytes 114720 | tf_op jit(solution)/shard_map/ppermute | solution.py:315
  86.1 4.5 %collective-permute-done.14 = bf16[8,7168]{1,0:T(8,128)(2,1)S(1)} collective-permute-done((bf16[8,7168]{1,0:T(8,128)(2,1)S(1)}, bf16[8,7168]{1,0:T(8,128)(2,1)S(1)}, u32[]{:S(2)}, u32[]{:S(2)}) %collective-permute-start.14) | collective-permute-done | bytes 114720 | tf_op jit(solution)/shard_map/ppermute | solution.py:315
  90.7 1.7 %pad_maximum_fusion.2 = bf16[4,8,7168]{2,1,0:T(8,128)(2,1)} fusion(bf16[1,8,7168]{2,1,0:T(8,128)(2,1)} %bitcast.39, bf16[1,8,7168]{2,1,0:T(8,128)(2,1)S(1)} %bitcast.87, bf16[1,8,7168]{2,1,0:T(8,128)(2,1)S(1)} %bitcast.86, bf16[1,8,7168]{2,1,0:T(8,128)(2,1)S(1)} %get-tuple-element.10), kind=kLoop, calls=%fused_computation.29 | loop fusion | flops 688128 | bytes 917504 | tf_op jit(solution)/shard_map/stack | solution.py:316
  92.4 1.6 %gather_fusion.2 = bf16[4,8,7168]{2,1,0:T(8,128)(2,1)S(1)} fusion(bf16[4,8,7168]{2,1,0:T(8,128)(2,1)} %pad_maximum_fusion.2, s32[1024]{0:T(1024)S(1)} %pad_clamp_fusion), kind=kCustom, calls=%fused_computation.1.clone | custom fusion | bytes 917520 | tf_op jit(solution)/shard_map/jit(_take)/gather | solution.py:319
  94.0 2.2 %multiply_reduce_fusion = (f32[128]{0:T(128)S(1)}, f32[128,7168]{1,0:T(8,128)S(1)}) fusion(bf16[128,7168]{1,0:T(8,128)(2,1)S(1)} %copy-done, f32[7168]{0:T(1024)S(1)} %copy-done.3, f32[7168]{0:T(1024)S(1)} %copy-done.4, bf16[4,8,7168]{2,1,0:T(8,128)(2,1)S(1)} %gather_fusion.2, pred[4]{0:T(512)(128)(4,1)S(1)} %compare_and_fusion, ...), kind=kOutput, calls=%fused_computation.13 | convolution fusion | flops 357146496 | bytes 6025732 | tf_op jit(solution)/shard_map/dot_general | solution.py:199
  96.2 2.6 %fusion.43 = (f32[7168]{0:T(1024)S(1)}, bf16[128,7168]{1,0:T(8,128)(2,1)}) fusion(f32[128]{0:T(128)S(1)} %broadcast_multiply_fusion, f32[128]{0:T(128)S(1)} %get-tuple-element.26, f32[7168]{0:T(1024)S(1)} %copy-done.3, bf16[128,7168]{1,0:T(8,128)(2,1)S(1)} %copy-done, f32[128,7168]{1,0:T(8,128)S(1)} %get-tuple-element.29, f32[128]{0:T(128)S(1)} %get-tuple-element.27, ...), kind=kLoop, calls=%fused_computation.116 | loop fusion | flops 9167872 | bytes 9233920 | tf_op jit(solution)/shard_map/reduce_sum | solution.py:386
  98.9 0.6 collective-permute-start.9
  99.4 2.7 %collective-permute-start.10 = (bf16[8,7168]{1,0:T(8,128)(2,1)S(1)}, bf16[8,7168]{1,0:T(8,128)(2,1)S(1)}, u32[]{:S(2)}, u32[]{:S(2)}) collective-permute-start(bf16[8,7168]{1,0:T(8,128)(2,1)S(1)} %get-tuple-element.17), channel_id=1, source_target_pairs={{0,3},{1,4},{2,5},{3,6},{4,7},{5,0},{6,1},{7,2},{8,11},{9,12},{10,... | collective-permute-start | bytes 344072 | tf_op jit(solution)/shard_map/ppermute | solution.py:315
  102.2 2.4 %collective-permute-start.12 = (bf16[8,7168]{1,0:T(8,128)(2,1)S(1)}, bf16[8,7168]{1,0:T(8,128)(2,1)S(1)}, u32[]{:S(2)}, u32[]{:S(2)}) collective-permute-start(bf16[8,7168]{1,0:T(8,128)(2,1)S(1)} %get-tuple-element.15), channel_id=1, source_target_pairs={{0,7},{1,0},{2,1},{3,2},{4,3},{5,4},{6,5},{7,6},{8,15},{9,8},{10,9... | collective-permute-start | bytes 344072 | tf_op jit(solution)/shard_map/ppermute | solution.py:315
  104.6 2.8 %collective-permute-start.17 = (f32[7168]{0:T(1024)S(1)}, f32[7168]{0:T(1024)S(1)}, u32[]{:S(2)}, u32[]{:S(2)}) collective-permute-start(f32[7168]{0:T(1024)S(1)} %add.243), channel_id=1, source_target_pairs={{0,2},{1,3},{2,0},{3,1},{4,6},{5,7},{6,4},{7,5},{8,10},{9,11},{10,... | collective-permute-start | bytes 86024 | tf_op jit(solution)/shard_map/ppermute | solution.py:236
  107.4 4.0 %collective-permute-done.17 = f32[7168]{0:T(1024)S(1)} collective-permute-done((f32[7168]{0:T(1024)S(1)}, f32[7168]{0:T(1024)S(1)}, u32[]{:S(2)}, u32[]{:S(2)}) %collective-permute-start.17) | collective-permute-done | bytes 28704 | tf_op jit(solution)/shard_map/ppermute | solution.py:236
  111.4 1.7 %collective-permute-start.18 = (f32[7168]{0:T(1024)S(1)}, f32[7168]{0:T(1024)S(1)}, u32[]{:S(2)}, u32[]{:S(2)}) collective-permute-start(f32[7168]{0:T(1024)S(1)} %add.244), channel_id=1, source_target_pairs={{0,4},{1,5},{2,6},{3,7},{4,0},{5,1},{6,2},{7,3},{8,12},{9,13},{10,... | collective-permute-start | bytes 86024 | tf_op jit(solution)/shard_map/ppermute | solution.py:236
  113.2 3.0 %collective-permute-done.18 = f32[7168]{0:T(1024)S(1)} collective-permute-done((f32[7168]{0:T(1024)S(1)}, f32[7168]{0:T(1024)S(1)}, u32[]{:S(2)}, u32[]{:S(2)}) %collective-permute-start.18) | collective-permute-done | bytes 28704 | tf_op jit(solution)/shard_map/ppermute | solution.py:236
  116.2 1.5 %collective-permute-start.19 = (f32[7168]{0:T(1024)S(1)}, f32[7168]{0:T(1024)S(1)}, u32[]{:S(2)}, u32[]{:S(2)}) collective-permute-start(f32[7168]{0:T(1024)S(1)} %add.245), channel_id=1, source_target_pairs={{0,8},{8,0},{16,24},{24,16},{1,9},{9,1},{17,25},{25,17},{2,10},{10... | collective-permute-start | bytes 86024 | tf_op jit(solution)/shard_map/ppermute | solution.py:236
  117.8 0.6 gather_fusion.1
  118.4 1.7 %collective-permute-done.19 = f32[7168]{0:T(1024)S(1)} collective-permute-done((f32[7168]{0:T(1024)S(1)}, f32[7168]{0:T(1024)S(1)}, u32[]{:S(2)}, u32[]{:S(2)}) %collective-permute-start.19) | collective-permute-done | bytes 28704 | tf_op jit(solution)/shard_map/ppermute | solution.py:236
  120.1 1.5 %collective-permute-start.20 = (f32[7168]{0:T(1024)S(1)}, f32[7168]{0:T(1024)S(1)}, u32[]{:S(2)}, u32[]{:S(2)}) collective-permute-start(f32[7168]{0:T(1024)S(1)} %add.246), channel_id=1, source_target_pairs={{0,16},{8,24},{16,0},{24,8},{1,17},{9,25},{17,1},{25,9},{2,18},{10... | collective-permute-start | bytes 86024 | tf_op jit(solution)/shard_map/ppermute | solution.py:236
  121.6 3.0 %fusion.2 = bf16[128,7168]{1,0:T(8,128)(2,1)} fusion(bf16[128,7168]{1,0:T(8,128)(2,1)S(1)} %copy-done, f32[7168]{0:T(1024)S(1)} %copy-done.3, bf16[4,8,7168]{2,1,0:T(8,128)(2,1)S(1)} %gather_fusion.1, pred[4]{0:T(512)(128)(4,1)S(1)} %get-tuple-element.6, f32[128,4]{0,1:T(4,128)S(1)} %select_reduce_fusion.1, s32[128,4]{0,1:T(4,128)S(1)} %add_select_fusion), kind=kOutput, calls=%fused_computation.7 | convolution fusion | flops 356229120 | bytes 4161540 | tf_op jit(solution)/shard_map/dot_general | solution.py:199
  124.6 0.6 add.247
  (63 shorter events, 2.5 us)
Async XLA Ops:
  0.6 5.6 %copy-start = (bf16[128,7168]{1,0:T(8,128)(2,1)S(1)}, bf16[128,7168]{1,0:T(8,128)(2,1)}, u32[]{:S(2)}) copy-start(bf16[128,7168]{1,0:T(8,128)(2,1)} %param.11) | copy-start | bytes 5505028
  0.6 5.6 %copy-start.3 = (f32[7168]{0:T(1024)S(1)}, f32[7168]{0:T(1024)}, u32[]{:S(2)}) copy-start(f32[7168]{0:T(1024)} %param.12) | copy-start | bytes 86020
  0.7 5.6 %copy-start.4 = (f32[7168]{0:T(1024)S(1)}, f32[7168]{0:T(1024)}, u32[]{:S(2)}) copy-start(f32[7168]{0:T(1024)} %param.13) | copy-start | bytes 86020
  8.0 8.2 %collective-permute-start = (bf16[8,7168]{1,0:T(8,128)(2,1)}, bf16[8,7168]{1,0:T(8,128)(2,1)S(1)}, u32[]{:S(2)}, u32[]{:S(2)}) collective-permute-start(bf16[8,7168]{1,0:T(8,128)(2,1)} %get-tuple-element.24), channel_id=1, source_target_pairs={{0,1},{1,2},{2,3},{3,4},{4,5},{5,6},{6,7},{7,0},{8,9},{9,10},{10,1... | collective-permute-start | bytes 344072 | tf_op jit(solution)/shard_map/ppermute | solution.py:291
  8.5 10.5 %collective-permute-start.1 = (bf16[8,7168]{1,0:T(8,128)(2,1)S(1)}, bf16[8,7168]{1,0:T(8,128)(2,1)S(1)}, u32[]{:S(2)}, u32[]{:S(2)}) collective-permute-start(bf16[8,7168]{1,0:T(8,128)(2,1)S(1)} %get-tuple-element.23), channel_id=1, source_target_pairs={{0,2},{1,3},{2,4},{3,5},{4,6},{5,7},{6,0},{7,1},{8,10},{9,11},{10,... | collective-permute-start | bytes 344072 | tf_op jit(solution)/shard_map/ppermute | solution.py:291
  11.1 15.1 %collective-permute-start.2 = (bf16[8,7168]{1,0:T(8,128)(2,1)S(1)}, bf16[8,7168]{1,0:T(8,128)(2,1)S(1)}, u32[]{:S(2)}, u32[]{:S(2)}) collective-permute-start(bf16[8,7168]{1,0:T(8,128)(2,1)S(1)} %get-tuple-element.22), channel_id=1, source_target_pairs={{0,3},{1,4},{2,5},{3,6},{4,7},{5,0},{6,1},{7,2},{8,11},{9,12},{10,... | collective-permute-start | bytes 344072 | tf_op jit(solution)/shard_map/ppermute | solution.py:291
  13.7 13.2 %collective-permute-start.3 = (bf16[8,7168]{1,0:T(8,128)(2,1)S(1)}, bf16[8,7168]{1,0:T(8,128)(2,1)S(1)}, u32[]{:S(2)}, u32[]{:S(2)}) collective-permute-start(bf16[8,7168]{1,0:T(8,128)(2,1)S(1)} %get-tuple-element.21), channel_id=1, source_target_pairs={{0,4},{1,5},{2,6},{3,7},{4,0},{5,1},{6,2},{7,3},{8,12},{9,13},{10,... | collective-permute-start | bytes 344072 | tf_op jit(solution)/shard_map/ppermute | solution.py:291
  14.9 12.6 %collective-permute-start.4 = (bf16[8,7168]{1,0:T(8,128)(2,1)S(1)}, bf16[8,7168]{1,0:T(8,128)(2,1)S(1)}, u32[]{:S(2)}, u32[]{:S(2)}) collective-permute-start(bf16[8,7168]{1,0:T(8,128)(2,1)S(1)} %get-tuple-element.20), channel_id=1, source_target_pairs={{0,5},{1,6},{2,7},{3,0},{4,1},{5,2},{6,3},{7,4},{8,13},{9,14},{10,... | collective-permute-start | bytes 344072 | tf_op jit(solution)/shard_map/ppermute | solution.py:291
  16.3 11.9 %collective-permute-start.5 = (bf16[8,7168]{1,0:T(8,128)(2,1)S(1)}, bf16[8,7168]{1,0:T(8,128)(2,1)S(1)}, u32[]{:S(2)}, u32[]{:S(2)}) collective-permute-start(bf16[8,7168]{1,0:T(8,128)(2,1)S(1)} %get-tuple-element.19), channel_id=1, source_target_pairs={{0,6},{1,7},{2,0},{3,1},{4,2},{5,3},{6,4},{7,5},{8,14},{9,15},{10,... | collective-permute-start | bytes 344072 | tf_op jit(solution)/shard_map/ppermute | solution.py:291
  19.1 9.8 %collective-permute-start.6 = (bf16[8,7168]{1,0:T(8,128)(2,1)S(1)}, bf16[8,7168]{1,0:T(8,128)(2,1)S(1)}, u32[]{:S(2)}, u32[]{:S(2)}) collective-permute-start(bf16[8,7168]{1,0:T(8,128)(2,1)S(1)} %get-tuple-element.18), channel_id=1, source_target_pairs={{0,7},{1,0},{2,1},{3,2},{4,3},{5,4},{6,5},{7,6},{8,15},{9,8},{10,9... | collective-permute-start | bytes 344072 | tf_op jit(solution)/shard_map/ppermute | solution.py:291
  31.4 3.8 %collective-permute-start.7 = (bf16[8,8,7168]{2,1,0:T(8,128)(2,1)S(1)}, bf16[8,8,7168]{2,1,0:T(8,128)(2,1)S(1)}, u32[]{:S(2)}, u32[]{:S(2)}) collective-permute-start(bf16[8,8,7168]{2,1,0:T(8,128)(2,1)S(1)} %broadcast_select_fusion), channel_id=1, source_target_pairs={{0,1},{1,0},{2,3},{3,2},{4,5},{5,4},{6,7},{7,6},{8,9},{9,8},{10,11... | collective-permute-start | bytes 2752520 | tf_op jit(solution)/shard_map/ppermute | solution.py:335
  35.2 0.9 copy-start.2
  36.1 32.5 %copy-start.6 = (s32[128,8]{0,1:T(8,128)S(1)}, s32[128,8]{0,1:T(8,128)}, u32[]{:S(2)}) copy-start(s32[128,8]{0,1:T(8,128)} %param.15) | copy-start | bytes 12292
  68.3 4.1 %collective-permute-start.8 = (bf16[2,64,7168]{2,1,0:T(8,128)(2,1)}, bf16[2,64,7168]{2,1,0:T(8,128)(2,1)}, u32[]{:S(2)}, u32[]{:S(2)}) collective-permute-start(bf16[2,64,7168]{2,1,0:T(8,128)(2,1)} %shard_map.112), channel_id=1, source_target_pairs={{0,1},{1,0},{2,3},{3,2},{4,5},{5,4},{6,7},{7,6},{8,9},{9,8},{10,11... | collective-permute-start | bytes 5505032 | tf_op jit(solution)/shard_map/ppermute | solution.py:345
  74.9 7.7 %copy-start.5 = (s32[128,8]{0,1:T(8,128)S(1)}, s32[128,8]{0,1:T(8,128)}, u32[]{:S(2)}) copy-start(s32[128,8]{0,1:T(8,128)} %param.14) | copy-start | bytes 12292
  75.1 11.0 %collective-permute-start.13 = (bf16[8,7168]{1,0:T(8,128)(2,1)S(1)}, bf16[8,7168]{1,0:T(8,128)(2,1)S(1)}, u32[]{:S(2)}, u32[]{:S(2)}) collective-permute-start(bf16[8,7168]{1,0:T(8,128)(2,1)S(1)} %get-tuple-element.13), channel_id=1, source_target_pairs={{0,2},{1,3},{2,4},{3,5},{4,6},{5,7},{6,0},{7,1},{8,10},{9,11},{10,... | collective-permute-start | bytes 344072 | tf_op jit(solution)/shard_map/ppermute | solution.py:315
  79.5 11.2 %collective-permute-start.14 = (bf16[8,7168]{1,0:T(8,128)(2,1)S(1)}, bf16[8,7168]{1,0:T(8,128)(2,1)S(1)}, u32[]{:S(2)}, u32[]{:S(2)}) collective-permute-start(bf16[8,7168]{1,0:T(8,128)(2,1)S(1)} %get-tuple-element.12), channel_id=1, source_target_pairs={{0,4},{1,5},{2,6},{3,7},{4,0},{5,1},{6,2},{7,3},{8,12},{9,13},{10,... | collective-permute-start | bytes 344072 | tf_op jit(solution)/shard_map/ppermute | solution.py:315
  82.6 8.1 %collective-permute-start.15 = (bf16[8,7168]{1,0:T(8,128)(2,1)S(1)}, bf16[8,7168]{1,0:T(8,128)(2,1)}, u32[]{:S(2)}, u32[]{:S(2)}) collective-permute-start(bf16[8,7168]{1,0:T(8,128)(2,1)S(1)} %get-tuple-element.11), channel_id=1, source_target_pairs={{0,6},{1,7},{2,0},{3,1},{4,2},{5,3},{6,4},{7,5},{8,14},{9,15},{10,... | collective-permute-start | bytes 344072 | tf_op jit(solution)/shard_map/ppermute | solution.py:315
  94.0 2.2 %copy-start.1 = (bf16[128,7168]{1,0:T(8,128)(2,1)S(1)}, bf16[128,7168]{1,0:T(8,128)(2,1)}, u32[]{:S(2)}) copy-start(bf16[128,7168]{1,0:T(8,128)(2,1)} %param.19) | copy-start | bytes 5505028
  98.8 5.8 %collective-permute-start.16 = (f32[7168]{0:T(1024)S(1)}, f32[7168]{0:T(1024)S(1)}, u32[]{:S(2)}, u32[]{:S(2)}) collective-permute-start(f32[7168]{0:T(1024)S(1)} %get-tuple-element.4), channel_id=1, source_target_pairs={{0,1},{1,0},{2,3},{3,2},{4,5},{5,4},{6,7},{7,6},{8,9},{9,8},{10,11... | collective-permute-start | bytes 86024 | tf_op jit(solution)/shard_map/ppermute | solution.py:236
  98.9 18.8 %collective-permute-start.9 = (bf16[8,7168]{1,0:T(8,128)(2,1)S(1)}, bf16[8,7168]{1,0:T(8,128)(2,1)S(1)}, u32[]{:S(2)}, u32[]{:S(2)}) collective-permute-start(bf16[8,7168]{1,0:T(8,128)(2,1)S(1)} %get-tuple-element.14), channel_id=1, source_target_pairs={{0,1},{1,2},{2,3},{3,4},{4,5},{5,6},{6,7},{7,0},{8,9},{9,10},{10,1... | collective-permute-start | bytes 344072 | tf_op jit(solution)/shard_map/ppermute | solution.py:315
  99.4 18.3 %collective-permute-start.10 = (bf16[8,7168]{1,0:T(8,128)(2,1)S(1)}, bf16[8,7168]{1,0:T(8,128)(2,1)S(1)}, u32[]{:S(2)}, u32[]{:S(2)}) collective-permute-start(bf16[8,7168]{1,0:T(8,128)(2,1)S(1)} %get-tuple-element.17), channel_id=1, source_target_pairs={{0,3},{1,4},{2,5},{3,6},{4,7},{5,0},{6,1},{7,2},{8,11},{9,12},{10,... | collective-permute-start | bytes 344072 | tf_op jit(solution)/shard_map/ppermute | solution.py:315
  102.2 15.5 %collective-permute-start.11 = (bf16[8,7168]{1,0:T(8,128)(2,1)S(1)}, bf16[8,7168]{1,0:T(8,128)(2,1)S(1)}, u32[]{:S(2)}, u32[]{:S(2)}) collective-permute-start(bf16[8,7168]{1,0:T(8,128)(2,1)S(1)} %get-tuple-element.16), channel_id=1, source_target_pairs={{0,5},{1,6},{2,7},{3,0},{4,1},{5,2},{6,3},{7,4},{8,13},{9,14},{10,... | collective-permute-start | bytes 344072 | tf_op jit(solution)/shard_map/ppermute | solution.py:315
  102.2 15.5 %collective-permute-start.12 = (bf16[8,7168]{1,0:T(8,128)(2,1)S(1)}, bf16[8,7168]{1,0:T(8,128)(2,1)S(1)}, u32[]{:S(2)}, u32[]{:S(2)}) collective-permute-start(bf16[8,7168]{1,0:T(8,128)(2,1)S(1)} %get-tuple-element.15), channel_id=1, source_target_pairs={{0,7},{1,0},{2,1},{3,2},{4,3},{5,4},{6,5},{7,6},{8,15},{9,8},{10,9... | collective-permute-start | bytes 344072 | tf_op jit(solution)/shard_map/ppermute | solution.py:315
  104.6 6.8 %collective-permute-start.17 = (f32[7168]{0:T(1024)S(1)}, f32[7168]{0:T(1024)S(1)}, u32[]{:S(2)}, u32[]{:S(2)}) collective-permute-start(f32[7168]{0:T(1024)S(1)} %add.243), channel_id=1, source_target_pairs={{0,2},{1,3},{2,0},{3,1},{4,6},{5,7},{6,4},{7,5},{8,10},{9,11},{10,... | collective-permute-start | bytes 86024 | tf_op jit(solution)/shard_map/ppermute | solution.py:236
  111.4 4.8 %collective-permute-start.18 = (f32[7168]{0:T(1024)S(1)}, f32[7168]{0:T(1024)S(1)}, u32[]{:S(2)}, u32[]{:S(2)}) collective-permute-start(f32[7168]{0:T(1024)S(1)} %add.244), channel_id=1, source_target_pairs={{0,4},{1,5},{2,6},{3,7},{4,0},{5,1},{6,2},{7,3},{8,12},{9,13},{10,... | collective-permute-start | bytes 86024 | tf_op jit(solution)/shard_map/ppermute | solution.py:236
  116.2 3.9 %collective-permute-start.19 = (f32[7168]{0:T(1024)S(1)}, f32[7168]{0:T(1024)S(1)}, u32[]{:S(2)}, u32[]{:S(2)}) collective-permute-start(f32[7168]{0:T(1024)S(1)} %add.245), channel_id=1, source_target_pairs={{0,8},{8,0},{16,24},{24,16},{1,9},{9,1},{17,25},{25,17},{2,10},{10... | collective-permute-start | bytes 86024 | tf_op jit(solution)/shard_map/ppermute | solution.py:236
  120.1 4.5 %collective-permute-start.20 = (f32[7168]{0:T(1024)S(1)}, f32[7168]{0:T(1024)S(1)}, u32[]{:S(2)}, u32[]{:S(2)}) collective-permute-start(f32[7168]{0:T(1024)S(1)} %add.246), channel_id=1, source_target_pairs={{0,16},{8,24},{16,0},{24,8},{1,17},{9,25},{17,1},{25,9},{2,18},{10... | collective-permute-start | bytes 86024 | tf_op jit(solution)/shard_map/ppermute | solution.py:236

commit v10 on v9

--- a/solution.py
+++ b/solution.py
@@ -303,21 +303,31 @@
     return picked.astype(values.dtype)
 
 
+def exchange_relative(chunks, first):
+    size = lax.axis_size("expert")
+    me = lax.axis_index("expert")
+    moved = [lax.dynamic_index_in_dim(chunks, me, 0, keepdims=False)]
+    for shift in range(1, size):
+        part = lax.dynamic_index_in_dim(chunks, (me + shift) % size, 0, keepdims=False)
+        moved.append(lax.ppermute(part, "expert", [(i, (i + shift) % size) for i in range(size)]))
+    return jnp.where(first, jnp.stack(moved), jnp.stack(moved[1:] + moved[:1]))
+
+
 def by_parity(chunks, odd, flight, group_size):
     size = lax.axis_size("expert")
     me = lax.axis_index("expert")
     moved = []
     for shift in range(odd, size, group_size):
-        part = lax.dynamic_index_in_dim(chunks, (me + shift) % size, 0, keepdims=False)
+        block = (size - me % group_size - shift) % size
+        part = lax.dynamic_index_in_dim(chunks, block, 0, keepdims=False)
         if shift == 0:
             moved.append(part)
         else:
             moved.append(lax.ppermute(part, "expert", [(i, (i + shift) % size) for i in range(size)]))
     stacked = jnp.stack(moved)
     chip = me // group_size
-    order = (chip - jnp.arange(flight, dtype=jnp.int32) + odd * (me % group_size - 1)) % flight
-    picked = jnp.take(stacked, order, axis=0)
-    return picked.reshape(flight * chunks.shape[1], chunks.shape[2])
+    order = (chip + odd * (me % group_size - 1) - jnp.arange(flight, dtype=jnp.int32)) % flight
+    return stacked.reshape(flight * chunks.shape[1], chunks.shape[2]), order
 
 
 def by_pair(
@@ -330,7 +340,7 @@
         [pick_rows(normed, slot_table, filled), pick_rows(out_grad, slot_table, filled)],
         axis=1,
     ).reshape(expert_count, capacity, feature_count)
-    arrived = exchange(sending, "expert")
+    arrived = exchange_relative(sending, member == 0)
     swap = group_perm(expert_count, group_size, 1)
     partner = lax.ppermute(arrived, "expert", swap)
     first = (member == 0).astype(jnp.int32).reshape(1)
@@ -344,9 +354,9 @@
     )
     sums = both.astype(jnp.float32) + lax.ppermute(both, "expert", swap).astype(jnp.float32)
     sums = sums.astype(jnp.bfloat16).reshape(2, expert_count, capacity, feature_count)
-    grad_sums = by_parity(sums[1], 0, flight, group_size).astype(jnp.float32)
-    out_sums = by_parity(sums[0], 1, flight, group_size).astype(jnp.float32)
-    return out_sums, grad_sums
+    grad_sums, grad_order = by_parity(sums[1], 0, flight, group_size)
+    out_sums, out_order = by_parity(sums[0], 1, flight, group_size)
+    return out_sums.astype(jnp.float32), grad_sums.astype(jnp.float32), out_order, grad_order
 
 
 def shards(
@@ -369,18 +379,23 @@
     member = lax.axis_index("expert") % group_size
     residual, inverse, normed = normalize(tokens, steering, norm_gain)
     slot_table, filled, combine = slot_tables(route_ids, route_gates, flight, capacity)
+    out_combine = combine
+    grad_combine = combine
     if group_size == 2:
-        out_sums, grad_sums = by_pair(
+        out_sums, grad_sums, out_order, grad_order = by_pair(
             normed, out_grad, slot_table, filled, gate_weight, up_weight, down_weight,
             member, expert_count, group_size,
         )
+        by_expert = combine.reshape(combine.shape[0], flight, capacity)
+        out_combine = jnp.take(by_expert, out_order, axis=1).reshape(combine.shape)
+        grad_combine = jnp.take(by_expert, grad_order, axis=1).reshape(combine.shape)
     else:
         out_sums, grad_sums = by_features(
             normed, out_grad, slot_table, filled, gate_weight, up_weight, down_weight,
             member, expert_count, group_size,
         )
-    mixture = apply_combine(combine, out_sums)
-    back_normed = apply_combine(combine, grad_sums)
+    mixture = apply_combine(out_combine, out_sums)
+    back_normed = apply_combine(grad_combine, grad_sums)
     layer_out = (residual + mixture).astype(jnp.bfloat16)
     total_grad = norm_backward(residual, inverse, norm_gain, back_normed, out_grad)
     steer_grad = butterfly_sum(jnp.sum(total_grad, axis=0), ("expert", "dp"))

time: 126 us -> 121 us (0.960)
  local copies, waits for them, and re-layouts: 10.8 us -> 2.58 us
  waiting for transfers between devices: 26.8 us -> 32.3 us
  other arithmetic: 12.4 us -> 9.48 us
    unnamed x20 -> x27, local copies, waits for them, and re-layouts: 4.88 us -> 0.16 us
    ppermute x5, waiting for transfers between devices: 8.74 us -> 12.7 us  [butterfly_sum(): lax.ppermute(value, axis, [(i, i ^ bit) for i in range(size)])]
    gather x3 -> x2, local copies, waits for them, and re-layouts: 3.95 us -> 1.1 us  [the longest x1 0.55 us: shards(): jnp.take(by_expert, grad_order, axis=1).reshape(combine.shape)]
    another operation x2 -> x0, other arithmetic: 1.79 us -> none  [by_parity(): stacked = jnp.stack(moved)]
    ppermute x5, starting transfers between devices: 7.56 us -> 6.12 us  [butterfly_sum(): lax.ppermute(value, axis, [(i, i ^ bit) for i in range(size)])]
  transfers between devices with their start and end apart: 21 -> 21, of which waited for: 8 -> 9; matrix products, arithmetic and copies ran while one was open for 7% -> 4% of each run, Pallas kernels for 0% -> 0%
where the time goes in v10:
time: 121 us; the launch traced here: 120 us
  starting transfers between devices  33.9 us (28%)
  waiting for transfers between devices  32.3 us (27%)
  Pallas kernels  32.1 us (27%)
  other arithmetic  9.48 us (8%)
  matrix products  8.88 us (7%)
  local copies, waits for them, and re-layouts  2.58 us (2%)
    pallas_call x1, Pallas kernels, expert_pair(): pl.pallas_call(_pair_kernel, grid_spec=grid_spec, out_shape=jax.ShapeDtyp...  32.1 us
    ppermute x7, starting transfers between devices, by_parity(): lax.ppermute(part, 'expert', [(i, (i + shift) % size) for i in range(size)])  13.2 us
    ppermute x5, waiting for transfers between devices, butterfly_sum(): lax.ppermute(value, axis, [(i, i ^ bit) for i in range(size)])  12.7 us
    ppermute x7, starting transfers between devices, exchange_relative(): lax.ppermute(part, 'expert', [(i, (i + shift) % size) for i in range(size)])  12 us
    ppermute x7, waiting for transfers between devices, by_parity(): lax.ppermute(part, 'expert', [(i, (i + shift) % size) for i in range(size)])  7.28 us
    ppermute x7, waiting for transfers between devices, exchange_relative(): lax.ppermute(part, 'expert', [(i, (i + shift) % size) for i in range(size)])  6.44 us
    dot_general x2, matrix products, apply_combine(): return jnp.dot(combine, partial_sums, precision=lax.Precision.HIGHEST)  6.18 us
    ppermute x5, starting transfers between devices, butterfly_sum(): lax.ppermute(value, axis, [(i, i ^ bit) for i in range(size)])  6.12 us
  transfers between devices with their start and end apart: 21, of which 9 were waited for; matrix products, arithmetic and copies ran while one was open for 4% of the time, Pallas kernels for 0%

profile of v10, /device:TPU:0, one launch (start us, length us, event | category | flops | bytes accessed | tf_op | source)
XLA Modules:
  0.0 120.4 jit_solution(9799605500308106274)
XLA Ops:
  0.8 0.8 fusion.31
  1.6 0.1 copy.22
  1.7 0.2 reduce_window_sum.11
  1.9 0.2 select_reduce_fusion
  2.1 0.2 fusion.29
  2.2 2.1 %multiply_reduce_fusion.1 = f32[128]{0:T(128)S(1)} fusion(bf16[128,7168]{1,0:T(8,128)(2,1)} %param.11, f32[7168]{0:T(1024)} %param.12), kind=kLoop, calls=%fused_computation.15 | loop fusion | flops 3669888 | bytes 1864192 | tf_op jit(solution)/shard_map/reduce_sum | solution.py:41
  4.3 1.9 %fusion.4 = bf16[4,1,8,7168]{3,2,0,1:T(8,128)(2,1)S(1)} fusion(bf16[128,7168]{1,0:T(8,128)(2,1)} %param.19, s32[4,8]{1,0:T(4,128)S(1)} %select_reduce_fusion, pred[4,8]{1,0:T(4,128)(4,1)S(1)} %fusion.29), kind=kOutput, calls=%fused_computation.10 | convolution fusion | flops 58957824 | bytes 2293920 | tf_op jit(solution)/shard_map/fct,td->fcd/dot_general | solution.py:300
  6.3 0.8 fusion.3
  7.1 0.1 pad_maximum_fusion
  7.3 0.9 dynamic-slice_bitcast_fusion.7
  8.1 0.5 collective-permute-start
  8.6 2.6 %collective-permute-start.1 = (bf16[8,7168]{1,0:T(8,128)(2,1)}, bf16[8,7168]{1,0:T(8,128)(2,1)S(1)}, u32[]{:S(2)}, u32[]{:S(2)}) collective-permute-start(bf16[8,7168]{1,0:T(8,128)(2,1)} %get-tuple-element.23), channel_id=1, source_target_pairs={{0,2},{1,3},{2,4},{3,5},{4,6},{5,7},{6,0},{7,1},{8,10},{9,11},{10,... | collective-permute-start | bytes 344072 | tf_op jit(solution)/shard_map/ppermute | solution.py:312
  11.2 2.6 %collective-permute-start.2 = (bf16[8,7168]{1,0:T(8,128)(2,1)}, bf16[8,7168]{1,0:T(8,128)(2,1)S(1)}, u32[]{:S(2)}, u32[]{:S(2)}) collective-permute-start(bf16[8,7168]{1,0:T(8,128)(2,1)} %get-tuple-element.22), channel_id=1, source_target_pairs={{0,3},{1,4},{2,5},{3,6},{4,7},{5,0},{6,1},{7,2},{8,11},{9,12},{10,... | collective-permute-start | bytes 344072 | tf_op jit(solution)/shard_map/ppermute | solution.py:312
  13.8 1.2 %collective-permute-start.3 = (bf16[8,7168]{1,0:T(8,128)(2,1)}, bf16[8,7168]{1,0:T(8,128)(2,1)S(1)}, u32[]{:S(2)}, u32[]{:S(2)}) collective-permute-start(bf16[8,7168]{1,0:T(8,128)(2,1)} %get-tuple-element.21), channel_id=1, source_target_pairs={{0,4},{1,5},{2,6},{3,7},{4,0},{5,1},{6,2},{7,3},{8,12},{9,13},{10,... | collective-permute-start | bytes 344072 | tf_op jit(solution)/shard_map/ppermute | solution.py:312
  15.0 1.1 collective-permute-start.4
  16.1 2.1 %collective-permute-start.5 = (bf16[8,7168]{1,0:T(8,128)(2,1)}, bf16[8,7168]{1,0:T(8,128)(2,1)S(1)}, u32[]{:S(2)}, u32[]{:S(2)}) collective-permute-start(bf16[8,7168]{1,0:T(8,128)(2,1)} %get-tuple-element.19), channel_id=1, source_target_pairs={{0,6},{1,7},{2,0},{3,1},{4,2},{5,3},{6,4},{7,5},{8,14},{9,15},{10,... | collective-permute-start | bytes 344072 | tf_op jit(solution)/shard_map/ppermute | solution.py:312
  18.3 1.9 %collective-permute-start.6 = (bf16[8,7168]{1,0:T(8,128)(2,1)S(1)}, bf16[8,7168]{1,0:T(8,128)(2,1)S(1)}, u32[]{:S(2)}, u32[]{:S(2)}) collective-permute-start(bf16[8,7168]{1,0:T(8,128)(2,1)S(1)} %get-tuple-element.18), channel_id=1, source_target_pairs={{0,7},{1,0},{2,1},{3,2},{4,3},{5,4},{6,5},{7,6},{8,15},{9,8},{10,9... | collective-permute-start | bytes 344072 | tf_op jit(solution)/shard_map/ppermute | solution.py:312
  20.2 6.2 %collective-permute-done.2 = bf16[8,7168]{1,0:T(8,128)(2,1)S(1)} collective-permute-done((bf16[8,7168]{1,0:T(8,128)(2,1)}, bf16[8,7168]{1,0:T(8,128)(2,1)S(1)}, u32[]{:S(2)}, u32[]{:S(2)}) %collective-permute-start.2) | collective-permute-done | bytes 114720 | tf_op jit(solution)/shard_map/ppermute | solution.py:312
  26.4 0.2 collective-permute-done.3
  26.9 0.1 broadcast_select_fusion
  27.0 2.2 %collective-permute-start.7 = (bf16[8,8,7168]{2,1,0:T(8,128)(2,1)S(1)}, bf16[8,8,7168]{2,1,0:T(8,128)(2,1)}, u32[]{:S(2)}, u32[]{:S(2)}) collective-permute-start(bf16[8,8,7168]{2,1,0:T(8,128)(2,1)S(1)} %broadcast_select_fusion), channel_id=1, source_target_pairs={{0,1},{1,0},{2,3},{3,2},{4,5},{5,4},{6,7},{7,6},{8,9},{9,8},{10,11... | collective-permute-start | bytes 2752520 | tf_op jit(solution)/shard_map/ppermute | solution.py:345
  29.2 2.2 %collective-permute-done.7 = bf16[8,8,7168]{2,1,0:T(8,128)(2,1)} collective-permute-done((bf16[8,8,7168]{2,1,0:T(8,128)(2,1)S(1)}, bf16[8,8,7168]{2,1,0:T(8,128)(2,1)}, u32[]{:S(2)}, u32[]{:S(2)}) %collective-permute-start.7) | collective-permute-done | bytes 917536 | tf_op jit(solution)/shard_map/ppermute | solution.py:345
  31.5 32.1 %shard_map.112 = bf16[2,64,7168]{2,1,0:T(8,128)(2,1)} custom-call(s32[1]{0:T(128)} %bitcast.1.first_ref, bf16[64,7168]{1,0:T(8,128)(2,1)} %bitcast.94, bf16[64,7168]{1,0:T(8,128)(2,1)} %bitcast.22.p_ref, bf16[7168,1024]{1,0:T(8,128)(2,1)} %g_ref.1, bf16[7168,1024]{1,0:T(8,128)(2,1)} %u_ref.1, bf16[1024,7168]{1,0:T(8,128)(2,1)} %d_ref.1), custom_call_target="tpu_custom_call" | custom-call | tf_op jit(solution)/shard_map/pallas_call | solution.py:188
  63.6 0.4 collective-permute-start.8
  64.0 3.7 %collective-permute-done.8 = bf16[2,64,7168]{2,1,0:T(8,128)(2,1)} collective-permute-done((bf16[2,64,7168]{2,1,0:T(8,128)(2,1)}, bf16[2,64,7168]{2,1,0:T(8,128)(2,1)}, u32[]{:S(2)}, u32[]{:S(2)}) %collective-permute-start.8) | collective-permute-done | bytes 1835040 | tf_op jit(solution)/shard_map/ppermute | solution.py:355
  67.7 2.5 %add_convert_fusion = bf16[2,64,7168]{2,1,0:T(8,128)(2,1)S(1)} fusion(bf16[2,64,7168]{2,1,0:T(8,128)(2,1)} %collective-permute-done.8, bf16[2,64,7168]{2,1,0:T(8,128)(2,1)} %shard_map.112), kind=kLoop, calls=%fused_computation.13 | loop fusion | flops 3670016 | bytes 5505024 | tf_op jit(solution)/shard_map/convert_element_type | solution.py:356
  70.2 0.1 slice_bitcast_fusion
  70.4 5.4 %collective-permute-start.13 = (bf16[8,7168]{1,0:T(8,128)(2,1)S(1)}, bf16[8,7168]{1,0:T(8,128)(2,1)S(1)}, u32[]{:S(2)}, u32[]{:S(2)}) collective-permute-start(bf16[8,7168]{1,0:T(8,128)(2,1)S(1)} %get-tuple-element.11), channel_id=1, source_target_pairs={{0,2},{1,3},{2,4},{3,5},{4,6},{5,7},{6,0},{7,1},{8,10},{9,11},{10,... | collective-permute-start | bytes 344072 | tf_op jit(solution)/shard_map/ppermute | solution.py:326
  75.8 2.2 %collective-permute-start.14 = (bf16[8,7168]{1,0:T(8,128)(2,1)S(1)}, bf16[8,7168]{1,0:T(8,128)(2,1)S(1)}, u32[]{:S(2)}, u32[]{:S(2)}) collective-permute-start(bf16[8,7168]{1,0:T(8,128)(2,1)S(1)} %get-tuple-element.10), channel_id=1, source_target_pairs={{0,4},{1,5},{2,6},{3,7},{4,0},{5,1},{6,2},{7,3},{8,12},{9,13},{10,... | collective-permute-start | bytes 344072 | tf_op jit(solution)/shard_map/ppermute | solution.py:326
  78.0 0.3 collective-permute-start.15
  78.3 0.5 gather_fusion.1
  78.8 2.7 %collective-permute-done.13 = bf16[8,7168]{1,0:T(8,128)(2,1)S(1)} collective-permute-done((bf16[8,7168]{1,0:T(8,128)(2,1)S(1)}, bf16[8,7168]{1,0:T(8,128)(2,1)S(1)}, u32[]{:S(2)}, u32[]{:S(2)}) %collective-permute-start.13) | collective-permute-done | bytes 114720 | tf_op jit(solution)/shard_map/ppermute | solution.py:326
  81.5 4.6 %collective-permute-done.14 = bf16[8,7168]{1,0:T(8,128)(2,1)S(1)} collective-permute-done((bf16[8,7168]{1,0:T(8,128)(2,1)S(1)}, bf16[8,7168]{1,0:T(8,128)(2,1)S(1)}, u32[]{:S(2)}, u32[]{:S(2)}) %collective-permute-start.14) | collective-permute-done | bytes 114720 | tf_op jit(solution)/shard_map/ppermute | solution.py:326
  86.1 3.1 %multiply_reduce_fusion = (f32[128]{0:T(128)S(1)}, f32[128,7168]{1,0:T(8,128)S(1)}) fusion(bf16[128,7168]{1,0:T(8,128)(2,1)S(1)} %copy-done, f32[7168]{0:T(1024)S(1)} %copy-done.3, f32[7168]{0:T(1024)S(1)} %copy-done.4, bf16[1,8,7168]{2,1,0:T(8,128)(2,1)} %bitcast.40, bf16[1,8,7168]{2,1,0:T(8,128)(2,1)S(1)} %bitcast.96, ...), kind=kOutput, calls=%fused_computation.12 | convolution fusion | flops 357601152 | bytes 6038020 | tf_op jit(solution)/shard_map/dot_general | solution.py:199
  89.3 2.6 %fusion.49 = (f32[7168]{0:T(1024)S(1)}, bf16[128,7168]{1,0:T(8,128)(2,1)}) fusion(f32[128]{0:T(128)S(1)} %broadcast_multiply_fusion, f32[128]{0:T(128)S(1)} %get-tuple-element.25, f32[7168]{0:T(1024)S(1)} %copy-done.3, bf16[128,7168]{1,0:T(8,128)(2,1)S(1)} %copy-done, f32[128,7168]{1,0:T(8,128)S(1)} %get-tuple-element.28, f32[128]{0:T(128)S(1)} %get-tuple-element.26, ...), kind=kLoop, calls=%fused_computation.115 | loop fusion | flops 9167872 | bytes 9233920 | tf_op jit(solution)/shard_map/reduce_sum | solution.py:401
  91.9 1.2 collective-permute-done.16
  93.1 3.0 %collective-permute-start.17 = (f32[7168]{0:T(1024)S(1)}, f32[7168]{0:T(1024)S(1)}, u32[]{:S(2)}, u32[]{:S(2)}) collective-permute-start(f32[7168]{0:T(1024)S(1)} %add.260), channel_id=1, source_target_pairs={{0,2},{1,3},{2,0},{3,1},{4,6},{5,7},{6,4},{7,5},{8,10},{9,11},{10,... | collective-permute-start | bytes 86024 | tf_op jit(solution)/shard_map/ppermute | solution.py:236
  96.2 0.9 collective-permute-start.10
  97.1 1.8 %collective-permute-start.11 = (bf16[8,7168]{1,0:T(8,128)(2,1)S(1)}, bf16[8,7168]{1,0:T(8,128)(2,1)S(1)}, u32[]{:S(2)}, u32[]{:S(2)}) collective-permute-start(bf16[8,7168]{1,0:T(8,128)(2,1)S(1)} %get-tuple-element.14), channel_id=1, source_target_pairs={{0,5},{1,6},{2,7},{3,0},{4,1},{5,2},{6,3},{7,4},{8,13},{9,14},{10,... | collective-permute-start | bytes 344072 | tf_op jit(solution)/shard_map/ppermute | solution.py:326
  98.9 2.6 %collective-permute-start.12 = (bf16[8,7168]{1,0:T(8,128)(2,1)S(1)}, bf16[8,7168]{1,0:T(8,128)(2,1)S(1)}, u32[]{:S(2)}, u32[]{:S(2)}) collective-permute-start(bf16[8,7168]{1,0:T(8,128)(2,1)S(1)} %get-tuple-element.13), channel_id=1, source_target_pairs={{0,7},{1,0},{2,1},{3,2},{4,3},{5,4},{6,5},{7,6},{8,15},{9,8},{10,9... | collective-permute-start | bytes 344072 | tf_op jit(solution)/shard_map/ppermute | solution.py:326
  101.5 0.1 collective-permute-start.18
  101.6 9.7 %collective-permute-done.18 = f32[7168]{0:T(1024)S(1)} collective-permute-done((f32[7168]{0:T(1024)S(1)}, f32[7168]{0:T(1024)S(1)}, u32[]{:S(2)}, u32[]{:S(2)}) %collective-permute-start.18) | collective-permute-done | bytes 28704 | tf_op jit(solution)/shard_map/ppermute | solution.py:236
  111.3 1.5 %collective-permute-start.19 = (f32[7168]{0:T(1024)S(1)}, f32[7168]{0:T(1024)S(1)}, u32[]{:S(2)}, u32[]{:S(2)}) collective-permute-start(f32[7168]{0:T(1024)S(1)} %add.262), channel_id=1, source_target_pairs={{0,8},{8,0},{16,24},{24,16},{1,9},{9,1},{17,25},{25,17},{2,10},{10... | collective-permute-start | bytes 86024 | tf_op jit(solution)/shard_map/ppermute | solution.py:236
  112.8 0.5 gather_fusion
  113.4 1.8 %collective-permute-done.19 = f32[7168]{0:T(1024)S(1)} collective-permute-done((f32[7168]{0:T(1024)S(1)}, f32[7168]{0:T(1024)S(1)}, u32[]{:S(2)}, u32[]{:S(2)}) %collective-permute-start.19) | collective-permute-done | bytes 28704 | tf_op jit(solution)/shard_map/ppermute | solution.py:236
  115.2 1.5 %collective-permute-start.20 = (f32[7168]{0:T(1024)S(1)}, f32[7168]{0:T(1024)S(1)}, u32[]{:S(2)}, u32[]{:S(2)}) collective-permute-start(f32[7168]{0:T(1024)S(1)} %add.263), channel_id=1, source_target_pairs={{0,16},{8,24},{16,0},{24,8},{1,17},{9,25},{17,1},{25,9},{2,18},{10... | collective-permute-start | bytes 86024 | tf_op jit(solution)/shard_map/ppermute | solution.py:236
  116.7 3.1 %fusion.2 = bf16[128,7168]{1,0:T(8,128)(2,1)} fusion(bf16[128,7168]{1,0:T(8,128)(2,1)S(1)} %copy-done, f32[7168]{0:T(1024)S(1)} %copy-done.3, bf16[1,8,7168]{2,1,0:T(8,128)(2,1)S(1)} %bitcast.100, bf16[1,8,7168]{2,1,0:T(8,128)(2,1)S(1)} %bitcast.99, bf16[1,8,7168]{2,1,0:T(8,128)(2,1)S(1)} %bitcast.98, bf16[1,8,7168]{2,1,0:T(8,128)(2,1)S(1)} %bitcast.97, ...), kind=kOutput, calls=%fused_computation.6 | convolution fusion | flops 356683776 | bytes 4173828 | tf_op jit(solution)/shard_map/dot_general | solution.py:199
  119.8 0.6 add.264
  (63 shorter events, 0.7 us)
Async XLA Ops:
  0.6 5.6 %copy-start = (bf16[128,7168]{1,0:T(8,128)(2,1)S(1)}, bf16[128,7168]{1,0:T(8,128)(2,1)}, u32[]{:S(2)}) copy-start(bf16[128,7168]{1,0:T(8,128)(2,1)} %param.11) | copy-start | bytes 5505028
  0.6 5.6 %copy-start.3 = (f32[7168]{0:T(1024)S(1)}, f32[7168]{0:T(1024)}, u32[]{:S(2)}) copy-start(f32[7168]{0:T(1024)} %param.12) | copy-start | bytes 86020
  0.7 5.6 %copy-start.4 = (f32[7168]{0:T(1024)S(1)}, f32[7168]{0:T(1024)}, u32[]{:S(2)}) copy-start(f32[7168]{0:T(1024)} %param.13) | copy-start | bytes 86020
  8.1 8.0 %collective-permute-start = (bf16[8,7168]{1,0:T(8,128)(2,1)}, bf16[8,7168]{1,0:T(8,128)(2,1)S(1)}, u32[]{:S(2)}, u32[]{:S(2)}) collective-permute-start(bf16[8,7168]{1,0:T(8,128)(2,1)} %get-tuple-element.24), channel_id=1, source_target_pairs={{0,1},{1,2},{2,3},{3,4},{4,5},{5,6},{6,7},{7,0},{8,9},{9,10},{10,1... | collective-permute-start | bytes 344072 | tf_op jit(solution)/shard_map/ppermute | solution.py:312
  8.6 9.7 %collective-permute-start.1 = (bf16[8,7168]{1,0:T(8,128)(2,1)}, bf16[8,7168]{1,0:T(8,128)(2,1)S(1)}, u32[]{:S(2)}, u32[]{:S(2)}) collective-permute-start(bf16[8,7168]{1,0:T(8,128)(2,1)} %get-tuple-element.23), channel_id=1, source_target_pairs={{0,2},{1,3},{2,4},{3,5},{4,6},{5,7},{6,0},{7,1},{8,10},{9,11},{10,... | collective-permute-start | bytes 344072 | tf_op jit(solution)/shard_map/ppermute | solution.py:312
  11.2 15.2 %collective-permute-start.2 = (bf16[8,7168]{1,0:T(8,128)(2,1)}, bf16[8,7168]{1,0:T(8,128)(2,1)S(1)}, u32[]{:S(2)}, u32[]{:S(2)}) collective-permute-start(bf16[8,7168]{1,0:T(8,128)(2,1)} %get-tuple-element.22), channel_id=1, source_target_pairs={{0,3},{1,4},{2,5},{3,6},{4,7},{5,0},{6,1},{7,2},{8,11},{9,12},{10,... | collective-permute-start | bytes 344072 | tf_op jit(solution)/shard_map/ppermute | solution.py:312
  13.8 12.8 %collective-permute-start.3 = (bf16[8,7168]{1,0:T(8,128)(2,1)}, bf16[8,7168]{1,0:T(8,128)(2,1)S(1)}, u32[]{:S(2)}, u32[]{:S(2)}) collective-permute-start(bf16[8,7168]{1,0:T(8,128)(2,1)} %get-tuple-element.21), channel_id=1, source_target_pairs={{0,4},{1,5},{2,6},{3,7},{4,0},{5,1},{6,2},{7,3},{8,12},{9,13},{10,... | collective-permute-start | bytes 344072 | tf_op jit(solution)/shard_map/ppermute | solution.py:312
  15.0 11.6 %collective-permute-start.4 = (bf16[8,7168]{1,0:T(8,128)(2,1)}, bf16[8,7168]{1,0:T(8,128)(2,1)S(1)}, u32[]{:S(2)}, u32[]{:S(2)}) collective-permute-start(bf16[8,7168]{1,0:T(8,128)(2,1)} %get-tuple-element.20), channel_id=1, source_target_pairs={{0,5},{1,6},{2,7},{3,0},{4,1},{5,2},{6,3},{7,4},{8,13},{9,14},{10,... | collective-permute-start | bytes 344072 | tf_op jit(solution)/shard_map/ppermute | solution.py:312
  16.1 10.5 %collective-permute-start.5 = (bf16[8,7168]{1,0:T(8,128)(2,1)}, bf16[8,7168]{1,0:T(8,128)(2,1)S(1)}, u32[]{:S(2)}, u32[]{:S(2)}) collective-permute-start(bf16[8,7168]{1,0:T(8,128)(2,1)} %get-tuple-element.19), channel_id=1, source_target_pairs={{0,6},{1,7},{2,0},{3,1},{4,2},{5,3},{6,4},{7,5},{8,14},{9,15},{10,... | collective-permute-start | bytes 344072 | tf_op jit(solution)/shard_map/ppermute | solution.py:312
  18.3 8.4 %collective-permute-start.6 = (bf16[8,7168]{1,0:T(8,128)(2,1)S(1)}, bf16[8,7168]{1,0:T(8,128)(2,1)S(1)}, u32[]{:S(2)}, u32[]{:S(2)}) collective-permute-start(bf16[8,7168]{1,0:T(8,128)(2,1)S(1)} %get-tuple-element.18), channel_id=1, source_target_pairs={{0,7},{1,0},{2,1},{3,2},{4,3},{5,4},{6,5},{7,6},{8,15},{9,8},{10,9... | collective-permute-start | bytes 344072 | tf_op jit(solution)/shard_map/ppermute | solution.py:312
  27.0 4.5 %copy-start.2 = (bf16[8,8,7168]{2,1,0:T(8,128)(2,1)}, bf16[8,8,7168]{2,1,0:T(8,128)(2,1)S(1)}, u32[]{:S(2)}) copy-start(bf16[8,8,7168]{2,1,0:T(8,128)(2,1)S(1)} %broadcast_select_fusion) | copy-start | bytes 2752516
  27.0 4.5 %collective-permute-start.7 = (bf16[8,8,7168]{2,1,0:T(8,128)(2,1)S(1)}, bf16[8,8,7168]{2,1,0:T(8,128)(2,1)}, u32[]{:S(2)}, u32[]{:S(2)}) collective-permute-start(bf16[8,8,7168]{2,1,0:T(8,128)(2,1)S(1)} %broadcast_select_fusion), channel_id=1, source_target_pairs={{0,1},{1,0},{2,3},{3,2},{4,5},{5,4},{6,7},{7,6},{8,9},{9,8},{10,11... | collective-permute-start | bytes 2752520 | tf_op jit(solution)/shard_map/ppermute | solution.py:345
  31.4 32.5 %copy-start.6 = (s32[128,8]{0,1:T(8,128)S(1)}, s32[128,8]{0,1:T(8,128)}, u32[]{:S(2)}) copy-start(s32[128,8]{0,1:T(8,128)} %param.15) | copy-start | bytes 12292
  31.5 32.5 %copy-start.5 = (s32[128,8]{0,1:T(8,128)S(1)}, s32[128,8]{0,1:T(8,128)}, u32[]{:S(2)}) copy-start(s32[128,8]{0,1:T(8,128)} %param.14) | copy-start | bytes 12292
  63.6 4.1 %collective-permute-start.8 = (bf16[2,64,7168]{2,1,0:T(8,128)(2,1)}, bf16[2,64,7168]{2,1,0:T(8,128)(2,1)}, u32[]{:S(2)}, u32[]{:S(2)}) collective-permute-start(bf16[2,64,7168]{2,1,0:T(8,128)(2,1)} %shard_map.112), channel_id=1, source_target_pairs={{0,1},{1,0},{2,3},{3,2},{4,5},{5,4},{6,7},{7,6},{8,9},{9,8},{10,11... | collective-permute-start | bytes 5505032 | tf_op jit(solution)/shard_map/ppermute | solution.py:355
  70.4 11.1 %collective-permute-start.13 = (bf16[8,7168]{1,0:T(8,128)(2,1)S(1)}, bf16[8,7168]{1,0:T(8,128)(2,1)S(1)}, u32[]{:S(2)}, u32[]{:S(2)}) collective-permute-start(bf16[8,7168]{1,0:T(8,128)(2,1)S(1)} %get-tuple-element.11), channel_id=1, source_target_pairs={{0,2},{1,3},{2,4},{3,5},{4,6},{5,7},{6,0},{7,1},{8,10},{9,11},{10,... | collective-permute-start | bytes 344072 | tf_op jit(solution)/shard_map/ppermute | solution.py:326
  75.8 10.3 %collective-permute-start.14 = (bf16[8,7168]{1,0:T(8,128)(2,1)S(1)}, bf16[8,7168]{1,0:T(8,128)(2,1)S(1)}, u32[]{:S(2)}, u32[]{:S(2)}) collective-permute-start(bf16[8,7168]{1,0:T(8,128)(2,1)S(1)} %get-tuple-element.10), channel_id=1, source_target_pairs={{0,4},{1,5},{2,6},{3,7},{4,0},{5,1},{6,2},{7,3},{8,12},{9,13},{10,... | collective-permute-start | bytes 344072 | tf_op jit(solution)/shard_map/ppermute | solution.py:326
  78.0 8.1 %collective-permute-start.15 = (bf16[8,7168]{1,0:T(8,128)(2,1)S(1)}, bf16[8,7168]{1,0:T(8,128)(2,1)}, u32[]{:S(2)}, u32[]{:S(2)}) collective-permute-start(bf16[8,7168]{1,0:T(8,128)(2,1)S(1)} %get-tuple-element.9), channel_id=1, source_target_pairs={{0,6},{1,7},{2,0},{3,1},{4,2},{5,3},{6,4},{7,5},{8,14},{9,15},{10,... | collective-permute-start | bytes 344072 | tf_op jit(solution)/shard_map/ppermute | solution.py:326
  78.8 10.4 %copy-start.1 = (bf16[128,7168]{1,0:T(8,128)(2,1)S(1)}, bf16[128,7168]{1,0:T(8,128)(2,1)}, u32[]{:S(2)}) copy-start(bf16[128,7168]{1,0:T(8,128)(2,1)} %param.19) | copy-start | bytes 5505028
  91.9 1.2 collective-permute-start.16
  93.1 8.4 %collective-permute-start.17 = (f32[7168]{0:T(1024)S(1)}, f32[7168]{0:T(1024)S(1)}, u32[]{:S(2)}, u32[]{:S(2)}) collective-permute-start(f32[7168]{0:T(1024)S(1)} %add.260), channel_id=1, source_target_pairs={{0,2},{1,3},{2,0},{3,1},{4,6},{5,7},{6,4},{7,5},{8,10},{9,11},{10,... | collective-permute-start | bytes 86024 | tf_op jit(solution)/shard_map/ppermute | solution.py:236
  96.2 20.5 %collective-permute-start.9 = (bf16[8,7168]{1,0:T(8,128)(2,1)S(1)}, bf16[8,7168]{1,0:T(8,128)(2,1)S(1)}, u32[]{:S(2)}, u32[]{:S(2)}) collective-permute-start(bf16[8,7168]{1,0:T(8,128)(2,1)S(1)} %get-tuple-element.12), channel_id=1, source_target_pairs={{0,1},{1,2},{2,3},{3,4},{4,5},{5,6},{6,7},{7,0},{8,9},{9,10},{10,1... | collective-permute-start | bytes 344072 | tf_op jit(solution)/shard_map/ppermute | solution.py:326
  96.2 20.5 %collective-permute-start.10 = (bf16[8,7168]{1,0:T(8,128)(2,1)S(1)}, bf16[8,7168]{1,0:T(8,128)(2,1)S(1)}, u32[]{:S(2)}, u32[]{:S(2)}) collective-permute-start(bf16[8,7168]{1,0:T(8,128)(2,1)S(1)} %get-tuple-element.15), channel_id=1, source_target_pairs={{0,3},{1,4},{2,5},{3,6},{4,7},{5,0},{6,1},{7,2},{8,11},{9,12},{10,... | collective-permute-start | bytes 344072 | tf_op jit(solution)/shard_map/ppermute | solution.py:326
  97.1 19.6 %collective-permute-start.11 = (bf16[8,7168]{1,0:T(8,128)(2,1)S(1)}, bf16[8,7168]{1,0:T(8,128)(2,1)S(1)}, u32[]{:S(2)}, u32[]{:S(2)}) collective-permute-start(bf16[8,7168]{1,0:T(8,128)(2,1)S(1)} %get-tuple-element.14), channel_id=1, source_target_pairs={{0,5},{1,6},{2,7},{3,0},{4,1},{5,2},{6,3},{7,4},{8,13},{9,14},{10,... | collective-permute-start | bytes 344072 | tf_op jit(solution)/shard_map/ppermute | solution.py:326
  98.9 17.8 %collective-permute-start.12 = (bf16[8,7168]{1,0:T(8,128)(2,1)S(1)}, bf16[8,7168]{1,0:T(8,128)(2,1)S(1)}, u32[]{:S(2)}, u32[]{:S(2)}) collective-permute-start(bf16[8,7168]{1,0:T(8,128)(2,1)S(1)} %get-tuple-element.13), channel_id=1, source_target_pairs={{0,7},{1,0},{2,1},{3,2},{4,3},{5,4},{6,5},{7,6},{8,15},{9,8},{10,9... | collective-permute-start | bytes 344072 | tf_op jit(solution)/shard_map/ppermute | solution.py:326
  101.5 9.8 %collective-permute-start.18 = (f32[7168]{0:T(1024)S(1)}, f32[7168]{0:T(1024)S(1)}, u32[]{:S(2)}, u32[]{:S(2)}) collective-permute-start(f32[7168]{0:T(1024)S(1)} %add.261), channel_id=1, source_target_pairs={{0,4},{1,5},{2,6},{3,7},{4,0},{5,1},{6,2},{7,3},{8,12},{9,13},{10,... | collective-permute-start | bytes 86024 | tf_op jit(solution)/shard_map/ppermute | solution.py:236
  111.3 3.9 %collective-permute-start.19 = (f32[7168]{0:T(1024)S(1)}, f32[7168]{0:T(1024)S(1)}, u32[]{:S(2)}, u32[]{:S(2)}) collective-permute-start(f32[7168]{0:T(1024)S(1)} %add.262), channel_id=1, source_target_pairs={{0,8},{8,0},{16,24},{24,16},{1,9},{9,1},{17,25},{25,17},{2,10},{10... | collective-permute-start | bytes 86024 | tf_op jit(solution)/shard_map/ppermute | solution.py:236
  115.2 4.6 %collective-permute-start.20 = (f32[7168]{0:T(1024)S(1)}, f32[7168]{0:T(1024)S(1)}, u32[]{:S(2)}, u32[]{:S(2)}) collective-permute-start(f32[7168]{0:T(1024)S(1)} %add.263), channel_id=1, source_target_pairs={{0,16},{8,24},{16,0},{24,8},{1,17},{9,25},{17,1},{25,9},{2,18},{10... | collective-permute-start | bytes 86024 | tf_op jit(solution)/shard_map/ppermute | solution.py:236

commit v11 on v10

--- a/solution.py
+++ b/solution.py
@@ -225,16 +225,20 @@
     return total
 
 
-def butterfly_sum(value, axes):
-    for axis in axes:
+def butterfly_sum(value, steps):
+    done = {}
+    for axis, limit in steps:
         size = lax.axis_size(axis)
         if size & (size - 1):
-            value = lax.psum(value, axis)
+            if axis not in done:
+                value = lax.psum(value, axis)
+                done[axis] = size
             continue
-        bit = 1
-        while bit < size:
+        bit = done.get(axis, 1)
+        while bit < size and (limit is None or bit < 2 * limit):
             value = value + lax.ppermute(value, axis, [(i, i ^ bit) for i in range(size)])
             bit *= 2
+        done[axis] = bit
     return value
 
 
@@ -398,7 +402,9 @@
     back_normed = apply_combine(grad_combine, grad_sums)
     layer_out = (residual + mixture).astype(jnp.bfloat16)
     total_grad = norm_backward(residual, inverse, norm_gain, back_normed, out_grad)
-    steer_grad = butterfly_sum(jnp.sum(total_grad, axis=0), ("expert", "dp"))
+    steer_grad = butterfly_sum(
+        jnp.sum(total_grad, axis=0), (("expert", 1), ("dp", None), ("expert", None))
+    )
     return (layer_out, total_grad.astype(jnp.bfloat16), steer_grad)
 
 

time: 121 us -> 114 us (0.942)
  waiting for transfers between devices: 32.3 us -> 25.8 us
    ppermute x5, waiting for transfers between devices: 12.7 us -> 6.12 us  [butterfly_sum(): lax.ppermute(value, axis, [(i, i ^ bit) for i in range(size)])]
  transfers between devices with their start and end apart: 21 -> 21, of which waited for: 9 -> 10; matrix products, arithmetic and copies ran while one was open for 4% -> 4% of each run, Pallas kernels for 0% -> 0%
where the time goes in v11:
time: 114 us
  starting transfers between devices  34.3 us (30%)
  Pallas kernels  32.1 us (28%)
  waiting for transfers between devices  25.8 us (23%)
  other arithmetic  9.48 us (8%)
  matrix products  8.88 us (8%)
  local copies, waits for them, and re-layouts  2.58 us (2%)
    pallas_call x1, Pallas kernels, expert_pair(): pl.pallas_call(_pair_kernel, grid_spec=grid_spec, out_shape=jax.ShapeDtyp...  32.1 us
    ppermute x7, starting transfers between devices, by_parity(): lax.ppermute(part, 'expert', [(i, (i + shift) % size) for i in range(size)])  13.2 us
    ppermute x7, starting transfers between devices, exchange_relative(): lax.ppermute(part, 'expert', [(i, (i + shift) % size) for i in range(size)])  12 us
    ppermute x7, waiting for transfers between devices, by_parity(): lax.ppermute(part, 'expert', [(i, (i + shift) % size) for i in range(size)])  7.28 us
    ppermute x5, starting transfers between devices, butterfly_sum(): lax.ppermute(value, axis, [(i, i ^ bit) for i in range(size)])  6.52 us
    ppermute x7, waiting for transfers between devices, exchange_relative(): lax.ppermute(part, 'expert', [(i, (i + shift) % size) for i in range(size)])  6.44 us
    dot_general x2, matrix products, apply_combine(): return jnp.dot(combine, partial_sums, precision=lax.Precision.HIGHEST)  6.18 us
    ppermute x5, waiting for transfers between devices, butterfly_sum(): lax.ppermute(value, axis, [(i, i ^ bit) for i in range(size)])  6.12 us
  transfers between devices with their start and end apart: 21, of which 10 were waited for; matrix products, arithmetic and copies ran while one was open for 4% of the time, Pallas kernels for 0%

profile of v11, /device:TPU:0, one launch (start us, length us, event | category | flops | bytes accessed | tf_op | source)
XLA Modules:
  0.0 114.2 jit_solution(7665685419742188268)
XLA Ops:
  0.8 0.8 fusion.31
  1.6 0.1 copy.22
  1.7 0.2 reduce_window_sum.11
  1.9 0.2 select_reduce_fusion
  2.1 0.2 fusion.29
  2.2 2.1 %multiply_reduce_fusion.1 = f32[128]{0:T(128)S(1)} fusion(bf16[128,7168]{1,0:T(8,128)(2,1)} %param.11, f32[7168]{0:T(1024)} %param.12), kind=kLoop, calls=%fused_computation.15 | loop fusion | flops 3669888 | bytes 1864192 | tf_op jit(solution)/shard_map/reduce_sum | solution.py:41
  4.3 1.9 %fusion.4 = bf16[4,1,8,7168]{3,2,0,1:T(8,128)(2,1)S(1)} fusion(bf16[128,7168]{1,0:T(8,128)(2,1)} %param.19, s32[4,8]{1,0:T(4,128)S(1)} %select_reduce_fusion, pred[4,8]{1,0:T(4,128)(4,1)S(1)} %fusion.29), kind=kOutput, calls=%fused_computation.10 | convolution fusion | flops 58957824 | bytes 2293920 | tf_op jit(solution)/shard_map/fct,td->fcd/dot_general | solution.py:304
  6.3 0.8 fusion.3
  7.3 0.9 dynamic-slice_bitcast_fusion.7
  8.1 0.5 collective-permute-start
  8.6 2.6 %collective-permute-start.1 = (bf16[8,7168]{1,0:T(8,128)(2,1)}, bf16[8,7168]{1,0:T(8,128)(2,1)S(1)}, u32[]{:S(2)}, u32[]{:S(2)}) collective-permute-start(bf16[8,7168]{1,0:T(8,128)(2,1)} %get-tuple-element.23), channel_id=1, source_target_pairs={{0,2},{1,3},{2,4},{3,5},{4,6},{5,7},{6,0},{7,1},{8,10},{9,11},{10,... | collective-permute-start | bytes 344072 | tf_op jit(solution)/shard_map/ppermute | solution.py:316
  11.2 2.6 %collective-permute-start.2 = (bf16[8,7168]{1,0:T(8,128)(2,1)}, bf16[8,7168]{1,0:T(8,128)(2,1)S(1)}, u32[]{:S(2)}, u32[]{:S(2)}) collective-permute-start(bf16[8,7168]{1,0:T(8,128)(2,1)} %get-tuple-element.22), channel_id=1, source_target_pairs={{0,3},{1,4},{2,5},{3,6},{4,7},{5,0},{6,1},{7,2},{8,11},{9,12},{10,... | collective-permute-start | bytes 344072 | tf_op jit(solution)/shard_map/ppermute | solution.py:316
  13.8 1.2 %collective-permute-start.3 = (bf16[8,7168]{1,0:T(8,128)(2,1)}, bf16[8,7168]{1,0:T(8,128)(2,1)S(1)}, u32[]{:S(2)}, u32[]{:S(2)}) collective-permute-start(bf16[8,7168]{1,0:T(8,128)(2,1)} %get-tuple-element.21), channel_id=1, source_target_pairs={{0,4},{1,5},{2,6},{3,7},{4,0},{5,1},{6,2},{7,3},{8,12},{9,13},{10,... | collective-permute-start | bytes 344072 | tf_op jit(solution)/shard_map/ppermute | solution.py:316
  15.0 1.1 collective-permute-start.4
  16.1 2.1 %collective-permute-start.5 = (bf16[8,7168]{1,0:T(8,128)(2,1)}, bf16[8,7168]{1,0:T(8,128)(2,1)S(1)}, u32[]{:S(2)}, u32[]{:S(2)}) collective-permute-start(bf16[8,7168]{1,0:T(8,128)(2,1)} %get-tuple-element.19), channel_id=1, source_target_pairs={{0,6},{1,7},{2,0},{3,1},{4,2},{5,3},{6,4},{7,5},{8,14},{9,15},{10,... | collective-permute-start | bytes 344072 | tf_op jit(solution)/shard_map/ppermute | solution.py:316
  18.3 1.9 %collective-permute-start.6 = (bf16[8,7168]{1,0:T(8,128)(2,1)S(1)}, bf16[8,7168]{1,0:T(8,128)(2,1)S(1)}, u32[]{:S(2)}, u32[]{:S(2)}) collective-permute-start(bf16[8,7168]{1,0:T(8,128)(2,1)S(1)} %get-tuple-element.18), channel_id=1, source_target_pairs={{0,7},{1,0},{2,1},{3,2},{4,3},{5,4},{6,5},{7,6},{8,15},{9,8},{10,9... | collective-permute-start | bytes 344072 | tf_op jit(solution)/shard_map/ppermute | solution.py:316
  20.2 6.2 %collective-permute-done.2 = bf16[8,7168]{1,0:T(8,128)(2,1)S(1)} collective-permute-done((bf16[8,7168]{1,0:T(8,128)(2,1)}, bf16[8,7168]{1,0:T(8,128)(2,1)S(1)}, u32[]{:S(2)}, u32[]{:S(2)}) %collective-permute-start.2) | collective-permute-done | bytes 114720 | tf_op jit(solution)/shard_map/ppermute | solution.py:316
  26.4 0.2 collective-permute-done.3
  26.9 0.1 broadcast_select_fusion
  27.0 2.2 %collective-permute-start.7 = (bf16[8,8,7168]{2,1,0:T(8,128)(2,1)S(1)}, bf16[8,8,7168]{2,1,0:T(8,128)(2,1)}, u32[]{:S(2)}, u32[]{:S(2)}) collective-permute-start(bf16[8,8,7168]{2,1,0:T(8,128)(2,1)S(1)} %broadcast_select_fusion), channel_id=1, source_target_pairs={{0,1},{1,0},{2,3},{3,2},{4,5},{5,4},{6,7},{7,6},{8,9},{9,8},{10,11... | collective-permute-start | bytes 2752520 | tf_op jit(solution)/shard_map/ppermute | solution.py:349
  29.2 2.2 %collective-permute-done.7 = bf16[8,8,7168]{2,1,0:T(8,128)(2,1)} collective-permute-done((bf16[8,8,7168]{2,1,0:T(8,128)(2,1)S(1)}, bf16[8,8,7168]{2,1,0:T(8,128)(2,1)}, u32[]{:S(2)}, u32[]{:S(2)}) %collective-permute-start.7) | collective-permute-done | bytes 917536 | tf_op jit(solution)/shard_map/ppermute | solution.py:349
  31.5 32.1 %shard_map.112 = bf16[2,64,7168]{2,1,0:T(8,128)(2,1)} custom-call(s32[1]{0:T(128)} %bitcast.1.first_ref, bf16[64,7168]{1,0:T(8,128)(2,1)} %bitcast.94, bf16[64,7168]{1,0:T(8,128)(2,1)} %bitcast.22.p_ref, bf16[7168,1024]{1,0:T(8,128)(2,1)} %g_ref.1, bf16[7168,1024]{1,0:T(8,128)(2,1)} %u_ref.1, bf16[1024,7168]{1,0:T(8,128)(2,1)} %d_ref.1), custom_call_target="tpu_custom_call" | custom-call | tf_op jit(solution)/shard_map/pallas_call | solution.py:188
  63.6 0.4 collective-permute-start.8
  64.0 3.7 %collective-permute-done.8 = bf16[2,64,7168]{2,1,0:T(8,128)(2,1)} collective-permute-done((bf16[2,64,7168]{2,1,0:T(8,128)(2,1)}, bf16[2,64,7168]{2,1,0:T(8,128)(2,1)}, u32[]{:S(2)}, u32[]{:S(2)}) %collective-permute-start.8) | collective-permute-done | bytes 1835040 | tf_op jit(solution)/shard_map/ppermute | solution.py:359
  67.7 2.5 %add_convert_fusion = bf16[2,64,7168]{2,1,0:T(8,128)(2,1)S(1)} fusion(bf16[2,64,7168]{2,1,0:T(8,128)(2,1)} %collective-permute-done.8, bf16[2,64,7168]{2,1,0:T(8,128)(2,1)} %shard_map.112), kind=kLoop, calls=%fused_computation.13 | loop fusion | flops 3670016 | bytes 5505024 | tf_op jit(solution)/shard_map/convert_element_type | solution.py:360
  70.2 0.1 slice_bitcast_fusion
  70.4 5.4 %collective-permute-start.13 = (bf16[8,7168]{1,0:T(8,128)(2,1)S(1)}, bf16[8,7168]{1,0:T(8,128)(2,1)S(1)}, u32[]{:S(2)}, u32[]{:S(2)}) collective-permute-start(bf16[8,7168]{1,0:T(8,128)(2,1)S(1)} %get-tuple-element.11), channel_id=1, source_target_pairs={{0,2},{1,3},{2,4},{3,5},{4,6},{5,7},{6,0},{7,1},{8,10},{9,11},{10,... | collective-permute-start | bytes 344072 | tf_op jit(solution)/shard_map/ppermute | solution.py:330
  75.8 2.2 %collective-permute-start.14 = (bf16[8,7168]{1,0:T(8,128)(2,1)S(1)}, bf16[8,7168]{1,0:T(8,128)(2,1)S(1)}, u32[]{:S(2)}, u32[]{:S(2)}) collective-permute-start(bf16[8,7168]{1,0:T(8,128)(2,1)S(1)} %get-tuple-element.10), channel_id=1, source_target_pairs={{0,4},{1,5},{2,6},{3,7},{4,0},{5,1},{6,2},{7,3},{8,12},{9,13},{10,... | collective-permute-start | bytes 344072 | tf_op jit(solution)/shard_map/ppermute | solution.py:330
  78.0 0.3 collective-permute-start.15
  78.3 0.5 gather_fusion.1
  78.8 2.7 %collective-permute-done.13 = bf16[8,7168]{1,0:T(8,128)(2,1)S(1)} collective-permute-done((bf16[8,7168]{1,0:T(8,128)(2,1)S(1)}, bf16[8,7168]{1,0:T(8,128)(2,1)S(1)}, u32[]{:S(2)}, u32[]{:S(2)}) %collective-permute-start.13) | collective-permute-done | bytes 114720 | tf_op jit(solution)/shard_map/ppermute | solution.py:330
  81.5 4.6 %collective-permute-done.14 = bf16[8,7168]{1,0:T(8,128)(2,1)S(1)} collective-permute-done((bf16[8,7168]{1,0:T(8,128)(2,1)S(1)}, bf16[8,7168]{1,0:T(8,128)(2,1)S(1)}, u32[]{:S(2)}, u32[]{:S(2)}) %collective-permute-start.14) | collective-permute-done | bytes 114720 | tf_op jit(solution)/shard_map/ppermute | solution.py:330
  86.1 3.1 %multiply_reduce_fusion = (f32[128]{0:T(128)S(1)}, f32[128,7168]{1,0:T(8,128)S(1)}) fusion(bf16[128,7168]{1,0:T(8,128)(2,1)S(1)} %copy-done, f32[7168]{0:T(1024)S(1)} %copy-done.3, f32[7168]{0:T(1024)S(1)} %copy-done.4, bf16[1,8,7168]{2,1,0:T(8,128)(2,1)} %bitcast.40, bf16[1,8,7168]{2,1,0:T(8,128)(2,1)S(1)} %bitcast.96, ...), kind=kOutput, calls=%fused_computation.12 | convolution fusion | flops 357601152 | bytes 6038020 | tf_op jit(solution)/shard_map/dot_general | solution.py:199
  89.3 2.6 %fusion.49 = (f32[7168]{0:T(1024)S(1)}, bf16[128,7168]{1,0:T(8,128)(2,1)}) fusion(f32[128]{0:T(128)S(1)} %broadcast_multiply_fusion, f32[128]{0:T(128)S(1)} %get-tuple-element.25, f32[7168]{0:T(1024)S(1)} %copy-done.3, bf16[128,7168]{1,0:T(8,128)(2,1)S(1)} %copy-done, f32[128,7168]{1,0:T(8,128)S(1)} %get-tuple-element.28, f32[128]{0:T(128)S(1)} %get-tuple-element.26, ...), kind=kLoop, calls=%fused_computation.115 | loop fusion | flops 9167872 | bytes 9233920 | tf_op jit(solution)/shard_map/reduce_sum | solution.py:406
  91.9 1.2 %collective-permute-done.16 = f32[7168]{0:T(1024)S(1)} collective-permute-done((f32[7168]{0:T(1024)S(1)}, f32[7168]{0:T(1024)S(1)}, u32[]{:S(2)}, u32[]{:S(2)}) %collective-permute-start.16) | collective-permute-done | bytes 28704 | tf_op jit(solution)/shard_map/ppermute | solution.py:239
  93.1 1.5 %collective-permute-start.17 = (f32[7168]{0:T(1024)S(1)}, f32[7168]{0:T(1024)S(1)}, u32[]{:S(2)}, u32[]{:S(2)}) collective-permute-start(f32[7168]{0:T(1024)S(1)} %add.260), channel_id=1, source_target_pairs={{0,8},{8,0},{16,24},{24,16},{1,9},{9,1},{17,25},{25,17},{2,10},{10... | collective-permute-start | bytes 86024 | tf_op jit(solution)/shard_map/ppermute | solution.py:239
  94.7 2.6 %collective-permute-start.10 = (bf16[8,7168]{1,0:T(8,128)(2,1)S(1)}, bf16[8,7168]{1,0:T(8,128)(2,1)S(1)}, u32[]{:S(2)}, u32[]{:S(2)}) collective-permute-start(bf16[8,7168]{1,0:T(8,128)(2,1)S(1)} %get-tuple-element.15), channel_id=1, source_target_pairs={{0,3},{1,4},{2,5},{3,6},{4,7},{5,0},{6,1},{7,2},{8,11},{9,12},{10,... | collective-permute-start | bytes 344072 | tf_op jit(solution)/shard_map/ppermute | solution.py:330
  97.3 1.2 %collective-permute-start.11 = (bf16[8,7168]{1,0:T(8,128)(2,1)S(1)}, bf16[8,7168]{1,0:T(8,128)(2,1)S(1)}, u32[]{:S(2)}, u32[]{:S(2)}) collective-permute-start(bf16[8,7168]{1,0:T(8,128)(2,1)S(1)} %get-tuple-element.14), channel_id=1, source_target_pairs={{0,5},{1,6},{2,7},{3,0},{4,1},{5,2},{6,3},{7,4},{8,13},{9,14},{10,... | collective-permute-start | bytes 344072 | tf_op jit(solution)/shard_map/ppermute | solution.py:330
  98.5 1.4 %collective-permute-start.12 = (bf16[8,7168]{1,0:T(8,128)(2,1)S(1)}, bf16[8,7168]{1,0:T(8,128)(2,1)S(1)}, u32[]{:S(2)}, u32[]{:S(2)}) collective-permute-start(bf16[8,7168]{1,0:T(8,128)(2,1)S(1)} %get-tuple-element.13), channel_id=1, source_target_pairs={{0,7},{1,0},{2,1},{3,2},{4,3},{5,4},{6,5},{7,6},{8,15},{9,8},{10,9... | collective-permute-start | bytes 344072 | tf_op jit(solution)/shard_map/ppermute | solution.py:330
  100.0 1.6 %collective-permute-start.18 = (f32[7168]{0:T(1024)S(1)}, f32[7168]{0:T(1024)S(1)}, u32[]{:S(2)}, u32[]{:S(2)}) collective-permute-start(f32[7168]{0:T(1024)S(1)} %add.261), channel_id=1, source_target_pairs={{0,16},{8,24},{16,0},{24,8},{1,17},{9,25},{17,1},{25,9},{2,18},{10... | collective-permute-start | bytes 86024 | tf_op jit(solution)/shard_map/ppermute | solution.py:239
  101.6 2.3 %collective-permute-done.18 = f32[7168]{0:T(1024)S(1)} collective-permute-done((f32[7168]{0:T(1024)S(1)}, f32[7168]{0:T(1024)S(1)}, u32[]{:S(2)}, u32[]{:S(2)}) %collective-permute-start.18) | collective-permute-done | bytes 28704 | tf_op jit(solution)/shard_map/ppermute | solution.py:239
  103.9 3.0 %collective-permute-start.19 = (f32[7168]{0:T(1024)S(1)}, f32[7168]{0:T(1024)S(1)}, u32[]{:S(2)}, u32[]{:S(2)}) collective-permute-start(f32[7168]{0:T(1024)S(1)} %add.262), channel_id=1, source_target_pairs={{0,2},{1,3},{2,0},{3,1},{4,6},{5,7},{6,4},{7,5},{8,10},{9,11},{10,... | collective-permute-start | bytes 86024 | tf_op jit(solution)/shard_map/ppermute | solution.py:239
  107.0 0.5 gather_fusion
  107.5 1.3 %collective-permute-done.19 = f32[7168]{0:T(1024)S(1)} collective-permute-done((f32[7168]{0:T(1024)S(1)}, f32[7168]{0:T(1024)S(1)}, u32[]{:S(2)}, u32[]{:S(2)}) %collective-permute-start.19) | collective-permute-done | bytes 28704 | tf_op jit(solution)/shard_map/ppermute | solution.py:239
  108.8 0.4 collective-permute-start.20
  109.2 3.1 %fusion.2 = bf16[128,7168]{1,0:T(8,128)(2,1)} fusion(bf16[128,7168]{1,0:T(8,128)(2,1)S(1)} %copy-done, f32[7168]{0:T(1024)S(1)} %copy-done.3, bf16[1,8,7168]{2,1,0:T(8,128)(2,1)S(1)} %bitcast.100, bf16[1,8,7168]{2,1,0:T(8,128)(2,1)S(1)} %bitcast.99, bf16[1,8,7168]{2,1,0:T(8,128)(2,1)S(1)} %bitcast.98, bf16[1,8,7168]{2,1,0:T(8,128)(2,1)S(1)} %bitcast.97, ...), kind=kOutput, calls=%fused_computation.6 | convolution fusion | flops 356683776 | bytes 4173828 | tf_op jit(solution)/shard_map/dot_general | solution.py:199
  112.3 1.3 %collective-permute-done.20 = f32[7168]{0:T(1024)S(1)} collective-permute-done((f32[7168]{0:T(1024)S(1)}, f32[7168]{0:T(1024)S(1)}, u32[]{:S(2)}, u32[]{:S(2)}) %collective-permute-start.20) | collective-permute-done | bytes 28704 | tf_op jit(solution)/shard_map/ppermute | solution.py:239
  113.6 0.6 add.264
  (63 shorter events, 0.7 us)
Async XLA Ops:
  0.6 5.6 %copy-start = (bf16[128,7168]{1,0:T(8,128)(2,1)S(1)}, bf16[128,7168]{1,0:T(8,128)(2,1)}, u32[]{:S(2)}) copy-start(bf16[128,7168]{1,0:T(8,128)(2,1)} %param.11) | copy-start | bytes 5505028
  0.6 5.6 %copy-start.3 = (f32[7168]{0:T(1024)S(1)}, f32[7168]{0:T(1024)}, u32[]{:S(2)}) copy-start(f32[7168]{0:T(1024)} %param.12) | copy-start | bytes 86020
  0.7 5.6 %copy-start.4 = (f32[7168]{0:T(1024)S(1)}, f32[7168]{0:T(1024)}, u32[]{:S(2)}) copy-start(f32[7168]{0:T(1024)} %param.13) | copy-start | bytes 86020
  8.1 8.0 %collective-permute-start = (bf16[8,7168]{1,0:T(8,128)(2,1)}, bf16[8,7168]{1,0:T(8,128)(2,1)S(1)}, u32[]{:S(2)}, u32[]{:S(2)}) collective-permute-start(bf16[8,7168]{1,0:T(8,128)(2,1)} %get-tuple-element.24), channel_id=1, source_target_pairs={{0,1},{1,2},{2,3},{3,4},{4,5},{5,6},{6,7},{7,0},{8,9},{9,10},{10,1... | collective-permute-start | bytes 344072 | tf_op jit(solution)/shard_map/ppermute | solution.py:316
  8.6 9.7 %collective-permute-start.1 = (bf16[8,7168]{1,0:T(8,128)(2,1)}, bf16[8,7168]{1,0:T(8,128)(2,1)S(1)}, u32[]{:S(2)}, u32[]{:S(2)}) collective-permute-start(bf16[8,7168]{1,0:T(8,128)(2,1)} %get-tuple-element.23), channel_id=1, source_target_pairs={{0,2},{1,3},{2,4},{3,5},{4,6},{5,7},{6,0},{7,1},{8,10},{9,11},{10,... | collective-permute-start | bytes 344072 | tf_op jit(solution)/shard_map/ppermute | solution.py:316
  11.2 15.2 %collective-permute-start.2 = (bf16[8,7168]{1,0:T(8,128)(2,1)}, bf16[8,7168]{1,0:T(8,128)(2,1)S(1)}, u32[]{:S(2)}, u32[]{:S(2)}) collective-permute-start(bf16[8,7168]{1,0:T(8,128)(2,1)} %get-tuple-element.22), channel_id=1, source_target_pairs={{0,3},{1,4},{2,5},{3,6},{4,7},{5,0},{6,1},{7,2},{8,11},{9,12},{10,... | collective-permute-start | bytes 344072 | tf_op jit(solution)/shard_map/ppermute | solution.py:316
  13.8 12.8 %collective-permute-start.3 = (bf16[8,7168]{1,0:T(8,128)(2,1)}, bf16[8,7168]{1,0:T(8,128)(2,1)S(1)}, u32[]{:S(2)}, u32[]{:S(2)}) collective-permute-start(bf16[8,7168]{1,0:T(8,128)(2,1)} %get-tuple-element.21), channel_id=1, source_target_pairs={{0,4},{1,5},{2,6},{3,7},{4,0},{5,1},{6,2},{7,3},{8,12},{9,13},{10,... | collective-permute-start | bytes 344072 | tf_op jit(solution)/shard_map/ppermute | solution.py:316
  15.0 11.6 %collective-permute-start.4 = (bf16[8,7168]{1,0:T(8,128)(2,1)}, bf16[8,7168]{1,0:T(8,128)(2,1)S(1)}, u32[]{:S(2)}, u32[]{:S(2)}) collective-permute-start(bf16[8,7168]{1,0:T(8,128)(2,1)} %get-tuple-element.20), channel_id=1, source_target_pairs={{0,5},{1,6},{2,7},{3,0},{4,1},{5,2},{6,3},{7,4},{8,13},{9,14},{10,... | collective-permute-start | bytes 344072 | tf_op jit(solution)/shard_map/ppermute | solution.py:316
  16.1 10.5 %collective-permute-start.5 = (bf16[8,7168]{1,0:T(8,128)(2,1)}, bf16[8,7168]{1,0:T(8,128)(2,1)S(1)}, u32[]{:S(2)}, u32[]{:S(2)}) collective-permute-start(bf16[8,7168]{1,0:T(8,128)(2,1)} %get-tuple-element.19), channel_id=1, source_target_pairs={{0,6},{1,7},{2,0},{3,1},{4,2},{5,3},{6,4},{7,5},{8,14},{9,15},{10,... | collective-permute-start | bytes 344072 | tf_op jit(solution)/shard_map/ppermute | solution.py:316
  18.3 8.4 %collective-permute-start.6 = (bf16[8,7168]{1,0:T(8,128)(2,1)S(1)}, bf16[8,7168]{1,0:T(8,128)(2,1)S(1)}, u32[]{:S(2)}, u32[]{:S(2)}) collective-permute-start(bf16[8,7168]{1,0:T(8,128)(2,1)S(1)} %get-tuple-element.18), channel_id=1, source_target_pairs={{0,7},{1,0},{2,1},{3,2},{4,3},{5,4},{6,5},{7,6},{8,15},{9,8},{10,9... | collective-permute-start | bytes 344072 | tf_op jit(solution)/shard_map/ppermute | solution.py:316
  27.0 4.5 %copy-start.2 = (bf16[8,8,7168]{2,1,0:T(8,128)(2,1)}, bf16[8,8,7168]{2,1,0:T(8,128)(2,1)S(1)}, u32[]{:S(2)}) copy-start(bf16[8,8,7168]{2,1,0:T(8,128)(2,1)S(1)} %broadcast_select_fusion) | copy-start | bytes 2752516
  27.0 4.5 %collective-permute-start.7 = (bf16[8,8,7168]{2,1,0:T(8,128)(2,1)S(1)}, bf16[8,8,7168]{2,1,0:T(8,128)(2,1)}, u32[]{:S(2)}, u32[]{:S(2)}) collective-permute-start(bf16[8,8,7168]{2,1,0:T(8,128)(2,1)S(1)} %broadcast_select_fusion), channel_id=1, source_target_pairs={{0,1},{1,0},{2,3},{3,2},{4,5},{5,4},{6,7},{7,6},{8,9},{9,8},{10,11... | collective-permute-start | bytes 2752520 | tf_op jit(solution)/shard_map/ppermute | solution.py:349
  31.4 32.5 %copy-start.6 = (s32[128,8]{0,1:T(8,128)S(1)}, s32[128,8]{0,1:T(8,128)}, u32[]{:S(2)}) copy-start(s32[128,8]{0,1:T(8,128)} %param.15) | copy-start | bytes 12292
  31.5 32.5 %copy-start.5 = (s32[128,8]{0,1:T(8,128)S(1)}, s32[128,8]{0,1:T(8,128)}, u32[]{:S(2)}) copy-start(s32[128,8]{0,1:T(8,128)} %param.14) | copy-start | bytes 12292
  63.6 4.1 %collective-permute-start.8 = (bf16[2,64,7168]{2,1,0:T(8,128)(2,1)}, bf16[2,64,7168]{2,1,0:T(8,128)(2,1)}, u32[]{:S(2)}, u32[]{:S(2)}) collective-permute-start(bf16[2,64,7168]{2,1,0:T(8,128)(2,1)} %shard_map.112), channel_id=1, source_target_pairs={{0,1},{1,0},{2,3},{3,2},{4,5},{5,4},{6,7},{7,6},{8,9},{9,8},{10,11... | collective-permute-start | bytes 5505032 | tf_op jit(solution)/shard_map/ppermute | solution.py:359
  70.4 11.1 %collective-permute-start.13 = (bf16[8,7168]{1,0:T(8,128)(2,1)S(1)}, bf16[8,7168]{1,0:T(8,128)(2,1)S(1)}, u32[]{:S(2)}, u32[]{:S(2)}) collective-permute-start(bf16[8,7168]{1,0:T(8,128)(2,1)S(1)} %get-tuple-element.11), channel_id=1, source_target_pairs={{0,2},{1,3},{2,4},{3,5},{4,6},{5,7},{6,0},{7,1},{8,10},{9,11},{10,... | collective-permute-start | bytes 344072 | tf_op jit(solution)/shard_map/ppermute | solution.py:330
  75.8 10.3 %collective-permute-start.14 = (bf16[8,7168]{1,0:T(8,128)(2,1)S(1)}, bf16[8,7168]{1,0:T(8,128)(2,1)S(1)}, u32[]{:S(2)}, u32[]{:S(2)}) collective-permute-start(bf16[8,7168]{1,0:T(8,128)(2,1)S(1)} %get-tuple-element.10), channel_id=1, source_target_pairs={{0,4},{1,5},{2,6},{3,7},{4,0},{5,1},{6,2},{7,3},{8,12},{9,13},{10,... | collective-permute-start | bytes 344072 | tf_op jit(solution)/shard_map/ppermute | solution.py:330
  78.0 8.1 %collective-permute-start.15 = (bf16[8,7168]{1,0:T(8,128)(2,1)S(1)}, bf16[8,7168]{1,0:T(8,128)(2,1)}, u32[]{:S(2)}, u32[]{:S(2)}) collective-permute-start(bf16[8,7168]{1,0:T(8,128)(2,1)S(1)} %get-tuple-element.9), channel_id=1, source_target_pairs={{0,6},{1,7},{2,0},{3,1},{4,2},{5,3},{6,4},{7,5},{8,14},{9,15},{10,... | collective-permute-start | bytes 344072 | tf_op jit(solution)/shard_map/ppermute | solution.py:330
  78.8 10.4 %copy-start.1 = (bf16[128,7168]{1,0:T(8,128)(2,1)S(1)}, bf16[128,7168]{1,0:T(8,128)(2,1)}, u32[]{:S(2)}) copy-start(bf16[128,7168]{1,0:T(8,128)(2,1)} %param.19) | copy-start | bytes 5505028
  91.9 1.2 %collective-permute-start.16 = (f32[7168]{0:T(1024)S(1)}, f32[7168]{0:T(1024)S(1)}, u32[]{:S(2)}, u32[]{:S(2)}) collective-permute-start(f32[7168]{0:T(1024)S(1)} %get-tuple-element.4), channel_id=1, source_target_pairs={{0,1},{1,0},{2,3},{3,2},{4,5},{5,4},{6,7},{7,6},{8,9},{9,8},{10,11... | collective-permute-start | bytes 86024 | tf_op jit(solution)/shard_map/ppermute | solution.py:239
  93.1 6.9 %collective-permute-start.17 = (f32[7168]{0:T(1024)S(1)}, f32[7168]{0:T(1024)S(1)}, u32[]{:S(2)}, u32[]{:S(2)}) collective-permute-start(f32[7168]{0:T(1024)S(1)} %add.260), channel_id=1, source_target_pairs={{0,8},{8,0},{16,24},{24,16},{1,9},{9,1},{17,25},{25,17},{2,10},{10... | collective-permute-start | bytes 86024 | tf_op jit(solution)/shard_map/ppermute | solution.py:239
  94.6 14.6 %collective-permute-start.9 = (bf16[8,7168]{1,0:T(8,128)(2,1)S(1)}, bf16[8,7168]{1,0:T(8,128)(2,1)S(1)}, u32[]{:S(2)}, u32[]{:S(2)}) collective-permute-start(bf16[8,7168]{1,0:T(8,128)(2,1)S(1)} %get-tuple-element.12), channel_id=1, source_target_pairs={{0,1},{1,2},{2,3},{3,4},{4,5},{5,6},{6,7},{7,0},{8,9},{9,10},{10,1... | collective-permute-start | bytes 344072 | tf_op jit(solution)/shard_map/ppermute | solution.py:330
  94.7 14.5 %collective-permute-start.10 = (bf16[8,7168]{1,0:T(8,128)(2,1)S(1)}, bf16[8,7168]{1,0:T(8,128)(2,1)S(1)}, u32[]{:S(2)}, u32[]{:S(2)}) collective-permute-start(bf16[8,7168]{1,0:T(8,128)(2,1)S(1)} %get-tuple-element.15), channel_id=1, source_target_pairs={{0,3},{1,4},{2,5},{3,6},{4,7},{5,0},{6,1},{7,2},{8,11},{9,12},{10,... | collective-permute-start | bytes 344072 | tf_op jit(solution)/shard_map/ppermute | solution.py:330
  97.3 12.0 %collective-permute-start.11 = (bf16[8,7168]{1,0:T(8,128)(2,1)S(1)}, bf16[8,7168]{1,0:T(8,128)(2,1)S(1)}, u32[]{:S(2)}, u32[]{:S(2)}) collective-permute-start(bf16[8,7168]{1,0:T(8,128)(2,1)S(1)} %get-tuple-element.14), channel_id=1, source_target_pairs={{0,5},{1,6},{2,7},{3,0},{4,1},{5,2},{6,3},{7,4},{8,13},{9,14},{10,... | collective-permute-start | bytes 344072 | tf_op jit(solution)/shard_map/ppermute | solution.py:330
  98.5 10.7 %collective-permute-start.12 = (bf16[8,7168]{1,0:T(8,128)(2,1)S(1)}, bf16[8,7168]{1,0:T(8,128)(2,1)S(1)}, u32[]{:S(2)}, u32[]{:S(2)}) collective-permute-start(bf16[8,7168]{1,0:T(8,128)(2,1)S(1)} %get-tuple-element.13), channel_id=1, source_target_pairs={{0,7},{1,0},{2,1},{3,2},{4,3},{5,4},{6,5},{7,6},{8,15},{9,8},{10,9... | collective-permute-start | bytes 344072 | tf_op jit(solution)/shard_map/ppermute | solution.py:330
  100.0 3.9 %collective-permute-start.18 = (f32[7168]{0:T(1024)S(1)}, f32[7168]{0:T(1024)S(1)}, u32[]{:S(2)}, u32[]{:S(2)}) collective-permute-start(f32[7168]{0:T(1024)S(1)} %add.261), channel_id=1, source_target_pairs={{0,16},{8,24},{16,0},{24,8},{1,17},{9,25},{17,1},{25,9},{2,18},{10... | collective-permute-start | bytes 86024 | tf_op jit(solution)/shard_map/ppermute | solution.py:239
  103.9 4.9 %collective-permute-start.19 = (f32[7168]{0:T(1024)S(1)}, f32[7168]{0:T(1024)S(1)}, u32[]{:S(2)}, u32[]{:S(2)}) collective-permute-start(f32[7168]{0:T(1024)S(1)} %add.262), channel_id=1, source_target_pairs={{0,2},{1,3},{2,0},{3,1},{4,6},{5,7},{6,4},{7,5},{8,10},{9,11},{10,... | collective-permute-start | bytes 86024 | tf_op jit(solution)/shard_map/ppermute | solution.py:239
  108.8 4.8 %collective-permute-start.20 = (f32[7168]{0:T(1024)S(1)}, f32[7168]{0:T(1024)S(1)}, u32[]{:S(2)}, u32[]{:S(2)}) collective-permute-start(f32[7168]{0:T(1024)S(1)} %add.263), channel_id=1, source_target_pairs={{0,4},{1,5},{2,6},{3,7},{4,0},{5,1},{6,2},{7,3},{8,12},{9,13},{10,... | collective-permute-start | bytes 86024 | tf_op jit(solution)/shard_map/ppermute | solution.py:239

commit v12 on v11

--- a/solution.py
+++ b/solution.py
@@ -130,7 +130,7 @@
 
 
 def _pair_kernel(
-    first_ref, a_ref, p_ref, g_ref, u_ref, d_ref, both_ref, xs, ys, acc_o, acc_b
+    first_ref, a_ref, p_ref, g_ref, u_ref, d_ref, fwd_ref, bwd_ref, xs, ys, acc_o, acc_b
 ):
     j = pl.program_id(0)
     first = first_ref[0] == 1
@@ -162,8 +162,8 @@
 
     @pl.when(j == pl.num_programs(0) - 1)
     def _():
-        both_ref[0] = acc_o[...].astype(both_ref.dtype)
-        both_ref[1] = acc_b[...].astype(both_ref.dtype)
+        fwd_ref[...] = acc_o[...].astype(fwd_ref.dtype)
+        bwd_ref[...] = acc_b[...].astype(bwd_ref.dtype)
 
 
 def expert_pair(first, arrived, partner, gw, uw, dw):
@@ -181,14 +181,14 @@
             pl.BlockSpec((feat, hb), lambda j, f: (0, j)),
             pl.BlockSpec((hb, feat), lambda j, f: (j, 0)),
         ],
-        out_specs=pl.BlockSpec((2, rows, feat), lambda j, f: (0, 0, 0)),
+        out_specs=[full, full],
         scratch_shapes=[pltpu.VMEM((rows, feat), arrived.dtype)] * 2
         + [pltpu.VMEM((rows, feat), jnp.float32)] * 2,
     )
     return pl.pallas_call(
         _pair_kernel,
         grid_spec=grid_spec,
-        out_shape=jax.ShapeDtypeStruct((2, rows, feat), jnp.bfloat16),
+        out_shape=[jax.ShapeDtypeStruct((rows, feat), jnp.bfloat16)] * 2,
         compiler_params=pltpu.CompilerParams(
             dimension_semantics=("arbitrary",), vmem_limit_bytes=56 * 1024 * 1024
         ),
@@ -348,7 +348,7 @@
     swap = group_perm(expert_count, group_size, 1)
     partner = lax.ppermute(arrived, "expert", swap)
     first = (member == 0).astype(jnp.int32).reshape(1)
-    both = expert_pair(
+    forward, backward = expert_pair(
         first,
         arrived.reshape(expert_count * capacity, feature_count),
         partner.reshape(expert_count * capacity, feature_count),
@@ -356,10 +356,19 @@
         up_weight,
         down_weight,
     )
-    sums = both.astype(jnp.float32) + lax.ppermute(both, "expert", swap).astype(jnp.float32)
-    sums = sums.astype(jnp.bfloat16).reshape(2, expert_count, capacity, feature_count)
-    grad_sums, grad_order = by_parity(sums[1], 0, flight, group_size)
-    out_sums, out_order = by_parity(sums[0], 1, flight, group_size)
+    shape = (expert_count, capacity, feature_count)
+    grad_total = backward.astype(jnp.float32) + lax.ppermute(backward, "expert", swap).astype(
+        jnp.float32
+    )
+    grad_sums, grad_order = by_parity(
+        grad_total.astype(jnp.bfloat16).reshape(shape), 0, flight, group_size
+    )
+    out_total = forward.astype(jnp.float32) + lax.ppermute(forward, "expert", swap).astype(
+        jnp.float32
+    )
+    out_sums, out_order = by_parity(
+        out_total.astype(jnp.bfloat16).reshape(shape), 1, flight, group_size
+    )
     return out_sums.astype(jnp.float32), grad_sums.astype(jnp.float32), out_order, grad_order
 
 

time: 114 us -> 112 us (0.982)
  waiting for transfers between devices: 25.8 us -> 24.1 us
    convert_element_type x1 -> x0, other arithmetic: 2.54 us -> none  [by_pair(): sums.astype(jnp.bfloat16).reshape(2, expert_count, capacity, feature_count)]
    reshape x0 -> x2, other arithmetic: none -> 1.88 us  [the longest x1 1.67 us: by_pair(): grad_total.astype(jnp.bfloat16).reshape(shape)]
    ppermute x1 -> x2, waiting for transfers between devices: 3.68 us -> 2.35 us  [the longest x1 2.35 us: by_pair(): lax.ppermute(backward, 'expert', swap).astype(jnp.float32)]
  transfers between devices with their start and end apart: 21 -> 22, of which waited for: 10 -> 10; matrix products, arithmetic and copies ran while one was open for 4% -> 9% of each run, Pallas kernels for 0% -> 0%
where the time goes in v12:
time: 112 us
  starting transfers between devices  34.4 us (31%)
  Pallas kernels  32.2 us (29%)
  waiting for transfers between devices  24.1 us (22%)
  matrix products  8.89 us (8%)
  other arithmetic  8.79 us (8%)
  local copies, waits for them, and re-layouts  2.46 us (2%)
  between operations  1.15 us (1%)
    pallas_call x1, Pallas kernels, expert_pair(): pl.pallas_call(_pair_kernel, grid_spec=grid_spec, out_shape=[jax.ShapeDty...  32.2 us
    ppermute x7, starting transfers between devices, by_parity(): lax.ppermute(part, 'expert', [(i, (i + shift) % size) for i in range(size)])  13.2 us
    ppermute x7, starting transfers between devices, exchange_relative(): lax.ppermute(part, 'expert', [(i, (i + shift) % size) for i in range(size)])  12 us
    ppermute x7, waiting for transfers between devices, by_parity(): lax.ppermute(part, 'expert', [(i, (i + shift) % size) for i in range(size)])  7.27 us
    ppermute x5, starting transfers between devices, butterfly_sum(): lax.ppermute(value, axis, [(i, i ^ bit) for i in range(size)])  6.51 us
    ppermute x7, waiting for transfers between devices, exchange_relative(): lax.ppermute(part, 'expert', [(i, (i + shift) % size) for i in range(size)])  6.44 us
    dot_general x2, matrix products, apply_combine(): return jnp.dot(combine, partial_sums, precision=lax.Precision.HIGHEST)  6.19 us
    ppermute x5, waiting for transfers between devices, butterfly_sum(): lax.ppermute(value, axis, [(i, i ^ bit) for i in range(size)])  5.81 us
  transfers between devices with their start and end apart: 22, of which 10 were waited for; matrix products, arithmetic and copies ran while one was open for 9% of the time, Pallas kernels for 0%

profile of v12, /device:TPU:0, one launch (start us, length us, event | category | flops | bytes accessed | tf_op | source)
XLA Modules:
  0.0 111.9 jit_solution(17649342871020069561)
XLA Ops:
  0.8 0.8 fusion.33
  1.6 0.1 copy.22
  1.7 0.2 reduce_window_sum.11
  1.9 0.2 select_reduce_fusion
  2.1 0.2 fusion.31
  2.2 2.1 %multiply_reduce_fusion.1 = f32[128]{0:T(128)S(1)} fusion(bf16[128,7168]{1,0:T(8,128)(2,1)} %param.11, f32[7168]{0:T(1024)} %param.12), kind=kLoop, calls=%fused_computation.14 | loop fusion | flops 3669888 | bytes 1864192 | tf_op jit(solution)/shard_map/reduce_sum | solution.py:41
  4.3 1.9 %fusion.4 = bf16[4,1,8,7168]{3,2,0,1:T(8,128)(2,1)S(1)} fusion(bf16[128,7168]{1,0:T(8,128)(2,1)} %param.19, s32[4,8]{1,0:T(4,128)S(1)} %select_reduce_fusion, pred[4,8]{1,0:T(4,128)(4,1)S(1)} %fusion.31), kind=kOutput, calls=%fused_computation.10 | convolution fusion | flops 58957824 | bytes 2293920 | tf_op jit(solution)/shard_map/fct,td->fcd/dot_general | solution.py:304
  6.3 0.8 fusion.3
  7.3 0.8 dynamic-slice_bitcast_fusion.7
  8.1 0.5 collective-permute-start
  8.6 2.6 %collective-permute-start.1 = (bf16[8,7168]{1,0:T(8,128)(2,1)}, bf16[8,7168]{1,0:T(8,128)(2,1)S(1)}, u32[]{:S(2)}, u32[]{:S(2)}) collective-permute-start(bf16[8,7168]{1,0:T(8,128)(2,1)} %get-tuple-element.25), channel_id=1, source_target_pairs={{0,2},{1,3},{2,4},{3,5},{4,6},{5,7},{6,0},{7,1},{8,10},{9,11},{10,... | collective-permute-start | bytes 344072 | tf_op jit(solution)/shard_map/ppermute | solution.py:316
  11.2 2.6 %collective-permute-start.2 = (bf16[8,7168]{1,0:T(8,128)(2,1)}, bf16[8,7168]{1,0:T(8,128)(2,1)S(1)}, u32[]{:S(2)}, u32[]{:S(2)}) collective-permute-start(bf16[8,7168]{1,0:T(8,128)(2,1)} %get-tuple-element.24), channel_id=1, source_target_pairs={{0,3},{1,4},{2,5},{3,6},{4,7},{5,0},{6,1},{7,2},{8,11},{9,12},{10,... | collective-permute-start | bytes 344072 | tf_op jit(solution)/shard_map/ppermute | solution.py:316
  13.8 1.2 %collective-permute-start.3 = (bf16[8,7168]{1,0:T(8,128)(2,1)}, bf16[8,7168]{1,0:T(8,128)(2,1)S(1)}, u32[]{:S(2)}, u32[]{:S(2)}) collective-permute-start(bf16[8,7168]{1,0:T(8,128)(2,1)} %get-tuple-element.23), channel_id=1, source_target_pairs={{0,4},{1,5},{2,6},{3,7},{4,0},{5,1},{6,2},{7,3},{8,12},{9,13},{10,... | collective-permute-start | bytes 344072 | tf_op jit(solution)/shard_map/ppermute | solution.py:316
  15.0 1.1 %collective-permute-start.4 = (bf16[8,7168]{1,0:T(8,128)(2,1)}, bf16[8,7168]{1,0:T(8,128)(2,1)S(1)}, u32[]{:S(2)}, u32[]{:S(2)}) collective-permute-start(bf16[8,7168]{1,0:T(8,128)(2,1)} %get-tuple-element.22), channel_id=1, source_target_pairs={{0,5},{1,6},{2,7},{3,0},{4,1},{5,2},{6,3},{7,4},{8,13},{9,14},{10,... | collective-permute-start | bytes 344072 | tf_op jit(solution)/shard_map/ppermute | solution.py:316
  16.1 2.1 %collective-permute-start.5 = (bf16[8,7168]{1,0:T(8,128)(2,1)}, bf16[8,7168]{1,0:T(8,128)(2,1)S(1)}, u32[]{:S(2)}, u32[]{:S(2)}) collective-permute-start(bf16[8,7168]{1,0:T(8,128)(2,1)} %get-tuple-element.21), channel_id=1, source_target_pairs={{0,6},{1,7},{2,0},{3,1},{4,2},{5,3},{6,4},{7,5},{8,14},{9,15},{10,... | collective-permute-start | bytes 344072 | tf_op jit(solution)/shard_map/ppermute | solution.py:316
  18.3 1.9 %collective-permute-start.6 = (bf16[8,7168]{1,0:T(8,128)(2,1)S(1)}, bf16[8,7168]{1,0:T(8,128)(2,1)S(1)}, u32[]{:S(2)}, u32[]{:S(2)}) collective-permute-start(bf16[8,7168]{1,0:T(8,128)(2,1)S(1)} %get-tuple-element.20), channel_id=1, source_target_pairs={{0,7},{1,0},{2,1},{3,2},{4,3},{5,4},{6,5},{7,6},{8,15},{9,8},{10,9... | collective-permute-start | bytes 344072 | tf_op jit(solution)/shard_map/ppermute | solution.py:316
  20.2 6.2 %collective-permute-done.2 = bf16[8,7168]{1,0:T(8,128)(2,1)S(1)} collective-permute-done((bf16[8,7168]{1,0:T(8,128)(2,1)}, bf16[8,7168]{1,0:T(8,128)(2,1)S(1)}, u32[]{:S(2)}, u32[]{:S(2)}) %collective-permute-start.2) | collective-permute-done | bytes 114720 | tf_op jit(solution)/shard_map/ppermute | solution.py:316
  26.4 0.2 collective-permute-done.3
  26.9 0.1 broadcast_select_fusion
  27.0 2.2 %collective-permute-start.7 = (bf16[8,8,7168]{2,1,0:T(8,128)(2,1)S(1)}, bf16[8,8,7168]{2,1,0:T(8,128)(2,1)}, u32[]{:S(2)}, u32[]{:S(2)}) collective-permute-start(bf16[8,8,7168]{2,1,0:T(8,128)(2,1)S(1)} %broadcast_select_fusion), channel_id=1, source_target_pairs={{0,1},{1,0},{2,3},{3,2},{4,5},{5,4},{6,7},{7,6},{8,9},{9,8},{10,11... | collective-permute-start | bytes 2752520 | tf_op jit(solution)/shard_map/ppermute | solution.py:349
  29.2 2.2 %collective-permute-done.7 = bf16[8,8,7168]{2,1,0:T(8,128)(2,1)} collective-permute-done((bf16[8,8,7168]{2,1,0:T(8,128)(2,1)S(1)}, bf16[8,8,7168]{2,1,0:T(8,128)(2,1)}, u32[]{:S(2)}, u32[]{:S(2)}) %collective-permute-start.7) | collective-permute-done | bytes 917536 | tf_op jit(solution)/shard_map/ppermute | solution.py:349
  31.4 32.2 %shard_map.112 = (bf16[64,7168]{1,0:T(8,128)(2,1)}, bf16[64,7168]{1,0:T(8,128)(2,1)}) custom-call(s32[1]{0:T(128)} %bitcast.1.first_ref, bf16[64,7168]{1,0:T(8,128)(2,1)} %bitcast.94, bf16[64,7168]{1,0:T(8,128)(2,1)} %bitcast.22.p_ref, bf16[7168,1024]{1,0:T(8,128)(2,1)} %g_ref.1, bf16[7168,1024]{1,0:T(8,128)(2,1)} %u_ref.1, bf16[1024,7168]{1,0:T(8,128)(2,1)} %d_ref.1), custom_call_target="tpu_custom_call" | custom-call | tf_op jit(solution)/shard_map/pallas_call | solution.py:188
  63.6 0.4 collective-permute-start.13
  64.1 2.4 %collective-permute-done.13 = bf16[64,7168]{1,0:T(8,128)(2,1)} collective-permute-done((bf16[64,7168]{1,0:T(8,128)(2,1)}, bf16[64,7168]{1,0:T(8,128)(2,1)}, u32[]{:S(2)}, u32[]{:S(2)}) %collective-permute-start.13) | collective-permute-done | bytes 917536 | tf_op jit(solution)/shard_map/ppermute | solution.py:360
  66.4 1.7 %fusion.12 = bf16[8,8,7168]{2,1,0:T(8,128)(2,1)S(1)} fusion(bf16[64,7168]{1,0:T(8,128)(2,1)} %collective-permute-done.13, bf16[64,7168]{1,0:T(8,128)(2,1)} %get-tuple-element.7), kind=kLoop, calls=%fused_computation.24 | loop fusion | flops 1835008 | bytes 2752512 | tf_op jit(solution)/shard_map/reshape | solution.py:364
  68.2 5.4 %collective-permute-start.14 = (bf16[8,7168]{1,0:T(8,128)(2,1)S(1)}, bf16[8,7168]{1,0:T(8,128)(2,1)S(1)}, u32[]{:S(2)}, u32[]{:S(2)}) collective-permute-start(bf16[8,7168]{1,0:T(8,128)(2,1)S(1)} %get-tuple-element.13), channel_id=1, source_target_pairs={{0,2},{1,3},{2,4},{3,5},{4,6},{5,7},{6,0},{7,1},{8,10},{9,11},{10,... | collective-permute-start | bytes 344072 | tf_op jit(solution)/shard_map/ppermute | solution.py:330
  73.5 2.2 %collective-permute-start.15 = (bf16[8,7168]{1,0:T(8,128)(2,1)S(1)}, bf16[8,7168]{1,0:T(8,128)(2,1)}, u32[]{:S(2)}, u32[]{:S(2)}) collective-permute-start(bf16[8,7168]{1,0:T(8,128)(2,1)S(1)} %get-tuple-element.12), channel_id=1, source_target_pairs={{0,4},{1,5},{2,6},{3,7},{4,0},{5,1},{6,2},{7,3},{8,12},{9,13},{10,... | collective-permute-start | bytes 344072 | tf_op jit(solution)/shard_map/ppermute | solution.py:330
  75.7 0.3 collective-permute-start.16
  76.0 0.5 gather_fusion.1
  76.7 2.6 %collective-permute-done.14 = bf16[8,7168]{1,0:T(8,128)(2,1)S(1)} collective-permute-done((bf16[8,7168]{1,0:T(8,128)(2,1)S(1)}, bf16[8,7168]{1,0:T(8,128)(2,1)S(1)}, u32[]{:S(2)}, u32[]{:S(2)}) %collective-permute-start.14) | collective-permute-done | bytes 114720 | tf_op jit(solution)/shard_map/ppermute | solution.py:330
  79.3 4.7 %collective-permute-done.15 = bf16[8,7168]{1,0:T(8,128)(2,1)} collective-permute-done((bf16[8,7168]{1,0:T(8,128)(2,1)S(1)}, bf16[8,7168]{1,0:T(8,128)(2,1)}, u32[]{:S(2)}, u32[]{:S(2)}) %collective-permute-start.15) | collective-permute-done | bytes 114720 | tf_op jit(solution)/shard_map/ppermute | solution.py:330
  84.0 3.1 %multiply_reduce_fusion = (f32[128]{0:T(128)S(1)}, f32[128,7168]{1,0:T(8,128)S(1)}) fusion(bf16[128,7168]{1,0:T(8,128)(2,1)S(1)} %copy-done, f32[7168]{0:T(1024)S(1)} %copy-done.4, f32[7168]{0:T(1024)S(1)} %copy-done.5, bf16[1,8,7168]{2,1,0:T(8,128)(2,1)} %bitcast.40, bf16[1,8,7168]{2,1,0:T(8,128)(2,1)} %bitcast.38, bf16[1,8,7168]{2,1,0:T(8,128)(2,1)S(1)} %bitcast.95, ...), kind=kOutput, calls=%fused_computation.12 | convolution fusion | flops 357601152 | bytes 6038020 | tf_op jit(solution)/shard_map/dot_general | solution.py:199
  87.1 2.6 %fusion.51 = (f32[7168]{0:T(1024)S(1)}, bf16[128,7168]{1,0:T(8,128)(2,1)}) fusion(f32[128]{0:T(128)S(1)} %broadcast_multiply_fusion, f32[128]{0:T(128)S(1)} %get-tuple-element.27, f32[7168]{0:T(1024)S(1)} %copy-done.4, bf16[128,7168]{1,0:T(8,128)(2,1)S(1)} %copy-done, f32[128,7168]{1,0:T(8,128)S(1)} %get-tuple-element.30, f32[128]{0:T(128)S(1)} %get-tuple-element.28, ...), kind=kLoop, calls=%fused_computation.116 | loop fusion | flops 9167872 | bytes 9233920 | tf_op jit(solution)/shard_map/reduce_sum | solution.py:415
  89.7 0.2 fusion.11
  90.0 1.0 collective-permute-done.17
  90.9 1.5 %collective-permute-start.18 = (f32[7168]{0:T(1024)S(1)}, f32[7168]{0:T(1024)S(1)}, u32[]{:S(2)}, u32[]{:S(2)}) collective-permute-start(f32[7168]{0:T(1024)S(1)} %add.264), channel_id=1, source_target_pairs={{0,8},{8,0},{16,24},{24,16},{1,9},{9,1},{17,25},{25,17},{2,10},{10... | collective-permute-start | bytes 86024 | tf_op jit(solution)/shard_map/ppermute | solution.py:239
  92.5 2.5 %collective-permute-start.10 = (bf16[8,7168]{1,0:T(8,128)(2,1)S(1)}, bf16[8,7168]{1,0:T(8,128)(2,1)S(1)}, u32[]{:S(2)}, u32[]{:S(2)}) collective-permute-start(bf16[8,7168]{1,0:T(8,128)(2,1)S(1)} %get-tuple-element.17), channel_id=1, source_target_pairs={{0,3},{1,4},{2,5},{3,6},{4,7},{5,0},{6,1},{7,2},{8,11},{9,12},{10,... | collective-permute-start | bytes 344072 | tf_op jit(solution)/shard_map/ppermute | solution.py:330
  95.0 1.3 %collective-permute-start.11 = (bf16[8,7168]{1,0:T(8,128)(2,1)S(1)}, bf16[8,7168]{1,0:T(8,128)(2,1)S(1)}, u32[]{:S(2)}, u32[]{:S(2)}) collective-permute-start(bf16[8,7168]{1,0:T(8,128)(2,1)S(1)} %get-tuple-element.16), channel_id=1, source_target_pairs={{0,5},{1,6},{2,7},{3,0},{4,1},{5,2},{6,3},{7,4},{8,13},{9,14},{10,... | collective-permute-start | bytes 344072 | tf_op jit(solution)/shard_map/ppermute | solution.py:330
  96.4 1.5 %collective-permute-start.12 = (bf16[8,7168]{1,0:T(8,128)(2,1)S(1)}, bf16[8,7168]{1,0:T(8,128)(2,1)S(1)}, u32[]{:S(2)}, u32[]{:S(2)}) collective-permute-start(bf16[8,7168]{1,0:T(8,128)(2,1)S(1)} %get-tuple-element.15), channel_id=1, source_target_pairs={{0,7},{1,0},{2,1},{3,2},{4,3},{5,4},{6,5},{7,6},{8,15},{9,8},{10,9... | collective-permute-start | bytes 344072 | tf_op jit(solution)/shard_map/ppermute | solution.py:330
  97.8 1.6 %collective-permute-start.19 = (f32[7168]{0:T(1024)S(1)}, f32[7168]{0:T(1024)S(1)}, u32[]{:S(2)}, u32[]{:S(2)}) collective-permute-start(f32[7168]{0:T(1024)S(1)} %add.265), channel_id=1, source_target_pairs={{0,16},{8,24},{16,0},{24,8},{1,17},{9,25},{17,1},{25,9},{2,18},{10... | collective-permute-start | bytes 86024 | tf_op jit(solution)/shard_map/ppermute | solution.py:239
  99.4 2.4 %collective-permute-done.19 = f32[7168]{0:T(1024)S(1)} collective-permute-done((f32[7168]{0:T(1024)S(1)}, f32[7168]{0:T(1024)S(1)}, u32[]{:S(2)}, u32[]{:S(2)}) %collective-permute-start.19) | collective-permute-done | bytes 28704 | tf_op jit(solution)/shard_map/ppermute | solution.py:239
  101.8 2.9 %collective-permute-start.20 = (f32[7168]{0:T(1024)S(1)}, f32[7168]{0:T(1024)S(1)}, u32[]{:S(2)}, u32[]{:S(2)}) collective-permute-start(f32[7168]{0:T(1024)S(1)} %add.266), channel_id=1, source_target_pairs={{0,2},{1,3},{2,0},{3,1},{4,6},{5,7},{6,4},{7,5},{8,10},{9,11},{10,... | collective-permute-start | bytes 86024 | tf_op jit(solution)/shard_map/ppermute | solution.py:239
  104.7 0.5 gather_fusion
  105.3 1.3 %collective-permute-done.20 = f32[7168]{0:T(1024)S(1)} collective-permute-done((f32[7168]{0:T(1024)S(1)}, f32[7168]{0:T(1024)S(1)}, u32[]{:S(2)}, u32[]{:S(2)}) %collective-permute-start.20) | collective-permute-done | bytes 28704 | tf_op jit(solution)/shard_map/ppermute | solution.py:239
  106.6 0.5 collective-permute-start.21
  107.1 3.1 %fusion.2 = bf16[128,7168]{1,0:T(8,128)(2,1)} fusion(bf16[128,7168]{1,0:T(8,128)(2,1)S(1)} %copy-done, f32[7168]{0:T(1024)S(1)} %copy-done.4, bf16[1,8,7168]{2,1,0:T(8,128)(2,1)S(1)} %bitcast.99, bf16[1,8,7168]{2,1,0:T(8,128)(2,1)S(1)} %bitcast.98, bf16[1,8,7168]{2,1,0:T(8,128)(2,1)S(1)} %bitcast.97, bf16[1,8,7168]{2,1,0:T(8,128)(2,1)S(1)} %bitcast.96, ...), kind=kOutput, calls=%fused_computation.6 | convolution fusion | flops 356683776 | bytes 4173828 | tf_op jit(solution)/shard_map/dot_general | solution.py:199
  110.1 1.2 %collective-permute-done.21 = f32[7168]{0:T(1024)S(1)} collective-permute-done((f32[7168]{0:T(1024)S(1)}, f32[7168]{0:T(1024)S(1)}, u32[]{:S(2)}, u32[]{:S(2)}) %collective-permute-start.21) | collective-permute-done | bytes 28704 | tf_op jit(solution)/shard_map/ppermute | solution.py:239
  111.3 0.6 add.268
  (67 shorter events, 0.8 us)
Async XLA Ops:
  0.6 5.6 %copy-start = (bf16[128,7168]{1,0:T(8,128)(2,1)S(1)}, bf16[128,7168]{1,0:T(8,128)(2,1)}, u32[]{:S(2)}) copy-start(bf16[128,7168]{1,0:T(8,128)(2,1)} %param.11) | copy-start | bytes 5505028
  0.6 5.6 %copy-start.4 = (f32[7168]{0:T(1024)S(1)}, f32[7168]{0:T(1024)}, u32[]{:S(2)}) copy-start(f32[7168]{0:T(1024)} %param.12) | copy-start | bytes 86020
  0.7 5.6 %copy-start.5 = (f32[7168]{0:T(1024)S(1)}, f32[7168]{0:T(1024)}, u32[]{:S(2)}) copy-start(f32[7168]{0:T(1024)} %param.13) | copy-start | bytes 86020
  8.1 8.0 %collective-permute-start = (bf16[8,7168]{1,0:T(8,128)(2,1)}, bf16[8,7168]{1,0:T(8,128)(2,1)S(1)}, u32[]{:S(2)}, u32[]{:S(2)}) collective-permute-start(bf16[8,7168]{1,0:T(8,128)(2,1)} %get-tuple-element.26), channel_id=1, source_target_pairs={{0,1},{1,2},{2,3},{3,4},{4,5},{5,6},{6,7},{7,0},{8,9},{9,10},{10,1... | collective-permute-start | bytes 344072 | tf_op jit(solution)/shard_map/ppermute | solution.py:316
  8.6 9.7 %collective-permute-start.1 = (bf16[8,7168]{1,0:T(8,128)(2,1)}, bf16[8,7168]{1,0:T(8,128)(2,1)S(1)}, u32[]{:S(2)}, u32[]{:S(2)}) collective-permute-start(bf16[8,7168]{1,0:T(8,128)(2,1)} %get-tuple-element.25), channel_id=1, source_target_pairs={{0,2},{1,3},{2,4},{3,5},{4,6},{5,7},{6,0},{7,1},{8,10},{9,11},{10,... | collective-permute-start | bytes 344072 | tf_op jit(solution)/shard_map/ppermute | solution.py:316
  11.2 15.2 %collective-permute-start.2 = (bf16[8,7168]{1,0:T(8,128)(2,1)}, bf16[8,7168]{1,0:T(8,128)(2,1)S(1)}, u32[]{:S(2)}, u32[]{:S(2)}) collective-permute-start(bf16[8,7168]{1,0:T(8,128)(2,1)} %get-tuple-element.24), channel_id=1, source_target_pairs={{0,3},{1,4},{2,5},{3,6},{4,7},{5,0},{6,1},{7,2},{8,11},{9,12},{10,... | collective-permute-start | bytes 344072 | tf_op jit(solution)/shard_map/ppermute | solution.py:316
  13.8 12.8 %collective-permute-start.3 = (bf16[8,7168]{1,0:T(8,128)(2,1)}, bf16[8,7168]{1,0:T(8,128)(2,1)S(1)}, u32[]{:S(2)}, u32[]{:S(2)}) collective-permute-start(bf16[8,7168]{1,0:T(8,128)(2,1)} %get-tuple-element.23), channel_id=1, source_target_pairs={{0,4},{1,5},{2,6},{3,7},{4,0},{5,1},{6,2},{7,3},{8,12},{9,13},{10,... | collective-permute-start | bytes 344072 | tf_op jit(solution)/shard_map/ppermute | solution.py:316
  15.0 11.6 %collective-permute-start.4 = (bf16[8,7168]{1,0:T(8,128)(2,1)}, bf16[8,7168]{1,0:T(8,128)(2,1)S(1)}, u32[]{:S(2)}, u32[]{:S(2)}) collective-permute-start(bf16[8,7168]{1,0:T(8,128)(2,1)} %get-tuple-element.22), channel_id=1, source_target_pairs={{0,5},{1,6},{2,7},{3,0},{4,1},{5,2},{6,3},{7,4},{8,13},{9,14},{10,... | collective-permute-start | bytes 344072 | tf_op jit(solution)/shard_map/ppermute | solution.py:316
  16.1 10.5 %collective-permute-start.5 = (bf16[8,7168]{1,0:T(8,128)(2,1)}, bf16[8,7168]{1,0:T(8,128)(2,1)S(1)}, u32[]{:S(2)}, u32[]{:S(2)}) collective-permute-start(bf16[8,7168]{1,0:T(8,128)(2,1)} %get-tuple-element.21), channel_id=1, source_target_pairs={{0,6},{1,7},{2,0},{3,1},{4,2},{5,3},{6,4},{7,5},{8,14},{9,15},{10,... | collective-permute-start | bytes 344072 | tf_op jit(solution)/shard_map/ppermute | solution.py:316
  18.3 8.4 %collective-permute-start.6 = (bf16[8,7168]{1,0:T(8,128)(2,1)S(1)}, bf16[8,7168]{1,0:T(8,128)(2,1)S(1)}, u32[]{:S(2)}, u32[]{:S(2)}) collective-permute-start(bf16[8,7168]{1,0:T(8,128)(2,1)S(1)} %get-tuple-element.20), channel_id=1, source_target_pairs={{0,7},{1,0},{2,1},{3,2},{4,3},{5,4},{6,5},{7,6},{8,15},{9,8},{10,9... | collective-permute-start | bytes 344072 | tf_op jit(solution)/shard_map/ppermute | solution.py:316
  27.0 4.5 %copy-start.2 = (bf16[8,8,7168]{2,1,0:T(8,128)(2,1)}, bf16[8,8,7168]{2,1,0:T(8,128)(2,1)S(1)}, u32[]{:S(2)}) copy-start(bf16[8,8,7168]{2,1,0:T(8,128)(2,1)S(1)} %broadcast_select_fusion) | copy-start | bytes 2752516
  27.0 4.5 %collective-permute-start.7 = (bf16[8,8,7168]{2,1,0:T(8,128)(2,1)S(1)}, bf16[8,8,7168]{2,1,0:T(8,128)(2,1)}, u32[]{:S(2)}, u32[]{:S(2)}) collective-permute-start(bf16[8,8,7168]{2,1,0:T(8,128)(2,1)S(1)} %broadcast_select_fusion), channel_id=1, source_target_pairs={{0,1},{1,0},{2,3},{3,2},{4,5},{5,4},{6,7},{7,6},{8,9},{9,8},{10,11... | collective-permute-start | bytes 2752520 | tf_op jit(solution)/shard_map/ppermute | solution.py:349
  31.4 32.6 %copy-start.7 = (s32[128,8]{0,1:T(8,128)S(1)}, s32[128,8]{0,1:T(8,128)}, u32[]{:S(2)}) copy-start(s32[128,8]{0,1:T(8,128)} %param.15) | copy-start | bytes 12292
  31.4 32.6 %copy-start.6 = (s32[128,8]{0,1:T(8,128)S(1)}, s32[128,8]{0,1:T(8,128)}, u32[]{:S(2)}) copy-start(s32[128,8]{0,1:T(8,128)} %param.14) | copy-start | bytes 12292
  63.6 13.0 %copy-start.3 = (bf16[64,7168]{1,0:T(8,128)(2,1)S(1)}, bf16[64,7168]{1,0:T(8,128)(2,1)}, u32[]{:S(2)}) copy-start(bf16[64,7168]{1,0:T(8,128)(2,1)} %get-tuple-element.6) | copy-start | bytes 2752516
  63.6 2.8 %collective-permute-start.13 = (bf16[64,7168]{1,0:T(8,128)(2,1)}, bf16[64,7168]{1,0:T(8,128)(2,1)}, u32[]{:S(2)}, u32[]{:S(2)}) collective-permute-start(bf16[64,7168]{1,0:T(8,128)(2,1)} %get-tuple-element.7), channel_id=1, source_target_pairs={{0,1},{1,0},{2,3},{3,2},{4,5},{5,4},{6,7},{7,6},{8,9},{9,8},{10,11... | collective-permute-start | bytes 2752520 | tf_op jit(solution)/shard_map/ppermute | solution.py:360
  68.2 11.1 %collective-permute-start.14 = (bf16[8,7168]{1,0:T(8,128)(2,1)S(1)}, bf16[8,7168]{1,0:T(8,128)(2,1)S(1)}, u32[]{:S(2)}, u32[]{:S(2)}) collective-permute-start(bf16[8,7168]{1,0:T(8,128)(2,1)S(1)} %get-tuple-element.13), channel_id=1, source_target_pairs={{0,2},{1,3},{2,4},{3,5},{4,6},{5,7},{6,0},{7,1},{8,10},{9,11},{10,... | collective-permute-start | bytes 344072 | tf_op jit(solution)/shard_map/ppermute | solution.py:330
  73.5 10.4 %collective-permute-start.15 = (bf16[8,7168]{1,0:T(8,128)(2,1)S(1)}, bf16[8,7168]{1,0:T(8,128)(2,1)}, u32[]{:S(2)}, u32[]{:S(2)}) collective-permute-start(bf16[8,7168]{1,0:T(8,128)(2,1)S(1)} %get-tuple-element.12), channel_id=1, source_target_pairs={{0,4},{1,5},{2,6},{3,7},{4,0},{5,1},{6,2},{7,3},{8,12},{9,13},{10,... | collective-permute-start | bytes 344072 | tf_op jit(solution)/shard_map/ppermute | solution.py:330
  75.7 8.2 %collective-permute-start.16 = (bf16[8,7168]{1,0:T(8,128)(2,1)S(1)}, bf16[8,7168]{1,0:T(8,128)(2,1)}, u32[]{:S(2)}, u32[]{:S(2)}) collective-permute-start(bf16[8,7168]{1,0:T(8,128)(2,1)S(1)} %get-tuple-element.11), channel_id=1, source_target_pairs={{0,6},{1,7},{2,0},{3,1},{4,2},{5,3},{6,4},{7,5},{8,14},{9,15},{10,... | collective-permute-start | bytes 344072 | tf_op jit(solution)/shard_map/ppermute | solution.py:330
  76.6 10.5 %copy-start.1 = (bf16[128,7168]{1,0:T(8,128)(2,1)S(1)}, bf16[128,7168]{1,0:T(8,128)(2,1)}, u32[]{:S(2)}) copy-start(bf16[128,7168]{1,0:T(8,128)(2,1)} %param.19) | copy-start | bytes 5505028
  76.6 13.1 %collective-permute-start.8 = (bf16[64,7168]{1,0:T(8,128)(2,1)S(1)}, bf16[64,7168]{1,0:T(8,128)(2,1)S(1)}, u32[]{:S(2)}, u32[]{:S(2)}) collective-permute-start(bf16[64,7168]{1,0:T(8,128)(2,1)S(1)} %copy-done.3), channel_id=1, source_target_pairs={{0,1},{1,0},{2,3},{3,2},{4,5},{5,4},{6,7},{7,6},{8,9},{9,8},{10,11... | collective-permute-start | bytes 2752520 | tf_op jit(solution)/shard_map/ppermute | solution.py:366
  89.7 1.2 %collective-permute-start.17 = (f32[7168]{0:T(1024)S(1)}, f32[7168]{0:T(1024)S(1)}, u32[]{:S(2)}, u32[]{:S(2)}) collective-permute-start(f32[7168]{0:T(1024)S(1)} %get-tuple-element.8), channel_id=1, source_target_pairs={{0,1},{1,0},{2,3},{3,2},{4,5},{5,4},{6,7},{7,6},{8,9},{9,8},{10,11... | collective-permute-start | bytes 86024 | tf_op jit(solution)/shard_map/ppermute | solution.py:239
  90.9 6.9 %collective-permute-start.18 = (f32[7168]{0:T(1024)S(1)}, f32[7168]{0:T(1024)S(1)}, u32[]{:S(2)}, u32[]{:S(2)}) collective-permute-start(f32[7168]{0:T(1024)S(1)} %add.264), channel_id=1, source_target_pairs={{0,8},{8,0},{16,24},{24,16},{1,9},{9,1},{17,25},{25,17},{2,10},{10... | collective-permute-start | bytes 86024 | tf_op jit(solution)/shard_map/ppermute | solution.py:239
  92.5 14.6 %collective-permute-start.9 = (bf16[8,7168]{1,0:T(8,128)(2,1)S(1)}, bf16[8,7168]{1,0:T(8,128)(2,1)S(1)}, u32[]{:S(2)}, u32[]{:S(2)}) collective-permute-start(bf16[8,7168]{1,0:T(8,128)(2,1)S(1)} %get-tuple-element.14), channel_id=1, source_target_pairs={{0,1},{1,2},{2,3},{3,4},{4,5},{5,6},{6,7},{7,0},{8,9},{9,10},{10,1... | collective-permute-start | bytes 344072 | tf_op jit(solution)/shard_map/ppermute | solution.py:330
  92.5 14.5 %collective-permute-start.10 = (bf16[8,7168]{1,0:T(8,128)(2,1)S(1)}, bf16[8,7168]{1,0:T(8,128)(2,1)S(1)}, u32[]{:S(2)}, u32[]{:S(2)}) collective-permute-start(bf16[8,7168]{1,0:T(8,128)(2,1)S(1)} %get-tuple-element.17), channel_id=1, source_target_pairs={{0,3},{1,4},{2,5},{3,6},{4,7},{5,0},{6,1},{7,2},{8,11},{9,12},{10,... | collective-permute-start | bytes 344072 | tf_op jit(solution)/shard_map/ppermute | solution.py:330
  95.0 12.1 %collective-permute-start.11 = (bf16[8,7168]{1,0:T(8,128)(2,1)S(1)}, bf16[8,7168]{1,0:T(8,128)(2,1)S(1)}, u32[]{:S(2)}, u32[]{:S(2)}) collective-permute-start(bf16[8,7168]{1,0:T(8,128)(2,1)S(1)} %get-tuple-element.16), channel_id=1, source_target_pairs={{0,5},{1,6},{2,7},{3,0},{4,1},{5,2},{6,3},{7,4},{8,13},{9,14},{10,... | collective-permute-start | bytes 344072 | tf_op jit(solution)/shard_map/ppermute | solution.py:330
  96.4 10.7 %collective-permute-start.12 = (bf16[8,7168]{1,0:T(8,128)(2,1)S(1)}, bf16[8,7168]{1,0:T(8,128)(2,1)S(1)}, u32[]{:S(2)}, u32[]{:S(2)}) collective-permute-start(bf16[8,7168]{1,0:T(8,128)(2,1)S(1)} %get-tuple-element.15), channel_id=1, source_target_pairs={{0,7},{1,0},{2,1},{3,2},{4,3},{5,4},{6,5},{7,6},{8,15},{9,8},{10,9... | collective-permute-start | bytes 344072 | tf_op jit(solution)/shard_map/ppermute | solution.py:330
  97.8 3.9 %collective-permute-start.19 = (f32[7168]{0:T(1024)S(1)}, f32[7168]{0:T(1024)S(1)}, u32[]{:S(2)}, u32[]{:S(2)}) collective-permute-start(f32[7168]{0:T(1024)S(1)} %add.265), channel_id=1, source_target_pairs={{0,16},{8,24},{16,0},{24,8},{1,17},{9,25},{17,1},{25,9},{2,18},{10... | collective-permute-start | bytes 86024 | tf_op jit(solution)/shard_map/ppermute | solution.py:239
  101.8 4.8 %collective-permute-start.20 = (f32[7168]{0:T(1024)S(1)}, f32[7168]{0:T(1024)S(1)}, u32[]{:S(2)}, u32[]{:S(2)}) collective-permute-start(f32[7168]{0:T(1024)S(1)} %add.266), channel_id=1, source_target_pairs={{0,2},{1,3},{2,0},{3,1},{4,6},{5,7},{6,4},{7,5},{8,10},{9,11},{10,... | collective-permute-start | bytes 86024 | tf_op jit(solution)/shard_map/ppermute | solution.py:239
  106.6 4.8 %collective-permute-start.21 = (f32[7168]{0:T(1024)S(1)}, f32[7168]{0:T(1024)S(1)}, u32[]{:S(2)}, u32[]{:S(2)}) collective-permute-start(f32[7168]{0:T(1024)S(1)} %add.267), channel_id=1, source_target_pairs={{0,4},{1,5},{2,6},{3,7},{4,0},{5,1},{6,2},{7,3},{8,12},{9,13},{10,... | collective-permute-start | bytes 86024 | tf_op jit(solution)/shard_map/ppermute | solution.py:239

commit v13 on v12

--- a/solution.py
+++ b/solution.py
@@ -340,18 +340,29 @@
 ):
     flight, capacity = slot_table.shape
     feature_count = normed.shape[1]
-    sending = jnp.stack(
-        [pick_rows(normed, slot_table, filled), pick_rows(out_grad, slot_table, filled)],
-        axis=1,
-    ).reshape(expert_count, capacity, feature_count)
-    arrived = exchange_relative(sending, member == 0)
+    picked = (pick_rows(normed, slot_table, filled), pick_rows(out_grad, slot_table, filled))
+    me = lax.axis_index("expert")
+    own = []
+    for shift in range(expert_count):
+        expert = ((me + shift) % expert_count) // group_size
+        part = lax.dynamic_index_in_dim(picked[shift % 2], expert, 0, keepdims=False)
+        if shift:
+            pairs = [(i, (i + shift) % expert_count) for i in range(expert_count)]
+            part = lax.ppermute(part, "expert", pairs)
+        own.append(part)
+    own = jnp.stack(own)
     swap = group_perm(expert_count, group_size, 1)
-    partner = lax.ppermute(arrived, "expert", swap)
-    first = (member == 0).astype(jnp.int32).reshape(1)
+    partner = lax.ppermute(own, "expert", swap)
+    first = member == 0
+    even = jnp.where(first, own, partner)
+    odd = jnp.where(first, partner, own)
+    blocks = range(0, expert_count, 2)
+    rows_x = jnp.stack(sum([[even[k], odd[(k + 2) % expert_count]] for k in blocks], []))
+    rows_y = jnp.stack(sum([[odd[k + 1], even[k + 1]] for k in blocks], []))
     forward, backward = expert_pair(
-        first,
-        arrived.reshape(expert_count * capacity, feature_count),
-        partner.reshape(expert_count * capacity, feature_count),
+        jnp.ones((1,), jnp.int32),
+        rows_x.reshape(expert_count * capacity, feature_count),
+        rows_y.reshape(expert_count * capacity, feature_count),
         gate_weight,
         up_weight,
         down_weight,

time: 112 us -> 112 us (level)
    reduce_sum x1, other arithmetic: 2.07 us -> 0.57 us  [normalize(): jnp.mean(residual * residual, axis=-1, keepdims=True) + EPSILON]
    unnamed x29 -> x31, local copies, waits for them, and re-layouts: 0.16 us -> 1.39 us
    select_n x1, other arithmetic: 0.1 us -> 1.3 us  [by_pair(): odd = jnp.where(first, partner, own)]
  transfers between devices with their start and end apart: 22 -> 22, of which waited for: 10 -> 10; matrix products, arithmetic and copies ran while one was open for 9% -> 11% of each run, Pallas kernels for 0% -> 0%
where the time goes in v13:
time: 112 us; the launch traced here: 111 us
  starting transfers between devices  33.4 us (30%)
  Pallas kernels  32.2 us (29%)
  waiting for transfers between devices  24.4 us (22%)
  matrix products  8.87 us (8%)
  other arithmetic  8.42 us (8%)
  local copies, waits for them, and re-layouts  2.85 us (3%)
  between operations  1.22 us (1%)
    pallas_call x1, Pallas kernels, expert_pair(): pl.pallas_call(_pair_kernel, grid_spec=grid_spec, out_shape=[jax.ShapeDty...  32.2 us
    ppermute x7, starting transfers between devices, by_parity(): lax.ppermute(part, 'expert', [(i, (i + shift) % size) for i in range(size)])  13 us
    ppermute x7, starting transfers between devices, by_pair(): part = lax.ppermute(part, 'expert', pairs)  11 us
    ppermute x7, waiting for transfers between devices, by_pair(): part = lax.ppermute(part, 'expert', pairs)  7.12 us
    ppermute x7, waiting for transfers between devices, by_parity(): lax.ppermute(part, 'expert', [(i, (i + shift) % size) for i in range(size)])  6.89 us
    ppermute x5, starting transfers between devices, butterfly_sum(): lax.ppermute(value, axis, [(i, i ^ bit) for i in range(size)])  6.57 us
    dot_general x2, matrix products, apply_combine(): return jnp.dot(combine, partial_sums, precision=lax.Precision.HIGHEST)  6.18 us
    ppermute x5, waiting for transfers between devices, butterfly_sum(): lax.ppermute(value, axis, [(i, i ^ bit) for i in range(size)])  5.84 us
  transfers between devices with their start and end apart: 22, of which 10 were waited for; matrix products, arithmetic and copies ran while one was open for 11% of the time, Pallas kernels for 0%

profile of v13, /device:TPU:0, one launch (start us, length us, event | category | flops | bytes accessed | tf_op | source)
XLA Modules:
  0.0 111.4 jit_solution(14581077846199106299)
XLA Ops:
  0.8 0.8 fusion.31
  1.7 0.2 reduce_window_sum.11
  2.0 0.2 select_reduce_fusion
  2.1 0.2 fusion.29
  2.3 1.9 %convolution_convert_fusion = bf16[4,8,7168]{2,1,0:T(8,128)(2,1)S(1)} fusion(bf16[128,7168]{1,0:T(8,128)(2,1)} %param.19, s32[4,8]{1,0:T(4,128)S(1)} %select_reduce_fusion, pred[4,8]{1,0:T(4,128)(4,1)S(1)} %fusion.29), kind=kOutput, calls=%fused_computation.7 | convolution fusion | flops 58957824 | bytes 2293920 | tf_op jit(solution)/shard_map/fct,td->fcd/dot_general | solution.py:304
  4.3 0.5 collective-permute-start
  4.8 0.6 multiply_reduce_fusion.1
  5.4 0.8 convolution_convert_fusion.1
  6.3 2.8 %collective-permute-start.1 = (bf16[8,7168]{1,0:T(8,128)(2,1)S(1)}, bf16[8,7168]{1,0:T(8,128)(2,1)S(1)}, u32[]{:S(2)}, u32[]{:S(2)}) collective-permute-start(bf16[8,7168]{1,0:T(8,128)(2,1)S(1)} %get-tuple-element.40), channel_id=1, source_target_pairs={{0,2},{1,3},{2,4},{3,5},{4,6},{5,7},{6,0},{7,1},{8,10},{9,11},{10,... | collective-permute-start | bytes 344072 | tf_op jit(solution)/shard_map/ppermute | solution.py:351
  9.0 2.4 %collective-permute-start.2 = (bf16[8,7168]{1,0:T(8,128)(2,1)S(1)}, bf16[8,7168]{1,0:T(8,128)(2,1)S(1)}, u32[]{:S(2)}, u32[]{:S(2)}) collective-permute-start(bf16[8,7168]{1,0:T(8,128)(2,1)S(1)} %get-tuple-element.36), channel_id=1, source_target_pairs={{0,3},{1,4},{2,5},{3,6},{4,7},{5,0},{6,1},{7,2},{8,11},{9,12},{10,... | collective-permute-start | bytes 344072 | tf_op jit(solution)/shard_map/ppermute | solution.py:351
  11.5 1.2 %collective-permute-start.3 = (bf16[8,7168]{1,0:T(8,128)(2,1)S(1)}, bf16[8,7168]{1,0:T(8,128)(2,1)S(1)}, u32[]{:S(2)}, u32[]{:S(2)}) collective-permute-start(bf16[8,7168]{1,0:T(8,128)(2,1)S(1)} %get-tuple-element.39), channel_id=1, source_target_pairs={{0,4},{1,5},{2,6},{3,7},{4,0},{5,1},{6,2},{7,3},{8,12},{9,13},{10,... | collective-permute-start | bytes 344072 | tf_op jit(solution)/shard_map/ppermute | solution.py:351
  12.7 1.3 %collective-permute-start.4 = (bf16[8,7168]{1,0:T(8,128)(2,1)S(1)}, bf16[8,7168]{1,0:T(8,128)(2,1)S(1)}, u32[]{:S(2)}, u32[]{:S(2)}) collective-permute-start(bf16[8,7168]{1,0:T(8,128)(2,1)S(1)} %get-tuple-element.35), channel_id=1, source_target_pairs={{0,5},{1,6},{2,7},{3,0},{4,1},{5,2},{6,3},{7,4},{8,13},{9,14},{10,... | collective-permute-start | bytes 344072 | tf_op jit(solution)/shard_map/ppermute | solution.py:351
  14.0 1.3 %collective-permute-start.5 = (bf16[8,7168]{1,0:T(8,128)(2,1)S(1)}, bf16[8,7168]{1,0:T(8,128)(2,1)S(1)}, u32[]{:S(2)}, u32[]{:S(2)}) collective-permute-start(bf16[8,7168]{1,0:T(8,128)(2,1)S(1)} %get-tuple-element.38), channel_id=1, source_target_pairs={{0,6},{1,7},{2,0},{3,1},{4,2},{5,3},{6,4},{7,5},{8,14},{9,15},{10,... | collective-permute-start | bytes 344072 | tf_op jit(solution)/shard_map/ppermute | solution.py:351
  15.4 1.4 %collective-permute-start.6 = (bf16[8,7168]{1,0:T(8,128)(2,1)S(1)}, bf16[8,7168]{1,0:T(8,128)(2,1)S(1)}, u32[]{:S(2)}, u32[]{:S(2)}) collective-permute-start(bf16[8,7168]{1,0:T(8,128)(2,1)S(1)} %get-tuple-element.34), channel_id=1, source_target_pairs={{0,7},{1,0},{2,1},{3,2},{4,3},{5,4},{6,5},{7,6},{8,15},{9,8},{10,9... | collective-permute-start | bytes 344072 | tf_op jit(solution)/shard_map/ppermute | solution.py:351
  16.7 6.9 %collective-permute-done.2 = bf16[8,7168]{1,0:T(8,128)(2,1)S(1)} collective-permute-done((bf16[8,7168]{1,0:T(8,128)(2,1)S(1)}, bf16[8,7168]{1,0:T(8,128)(2,1)S(1)}, u32[]{:S(2)}, u32[]{:S(2)}) %collective-permute-start.2) | collective-permute-done | bytes 114720 | tf_op jit(solution)/shard_map/ppermute | solution.py:351
  23.7 0.2 collective-permute-done.3
  24.0 2.4 %collective-permute-start.7 = (bf16[8,8,7168]{2,1,0:T(8,128)(2,1)S(1)}, bf16[8,8,7168]{2,1,0:T(8,128)(2,1)}, u32[]{:S(2)}, u32[]{:S(2)}) collective-permute-start(bf16[8,8,7168]{2,1,0:T(8,128)(2,1)S(1)} %bitcast_dynamic-update-slice_fusion), channel_id=1, source_target_pairs={{0,1},{1,0},{2,3},{3,2},{4,5},{5,4},{6,7},{7,6},{8,9},{9,8},{10,11... | collective-permute-start | bytes 2752520 | tf_op jit(solution)/shard_map/ppermute | solution.py:355
  26.4 2.2 %collective-permute-done.7 = bf16[8,8,7168]{2,1,0:T(8,128)(2,1)} collective-permute-done((bf16[8,8,7168]{2,1,0:T(8,128)(2,1)S(1)}, bf16[8,8,7168]{2,1,0:T(8,128)(2,1)}, u32[]{:S(2)}, u32[]{:S(2)}) %collective-permute-start.7) | collective-permute-done | bytes 917536 | tf_op jit(solution)/shard_map/ppermute | solution.py:355
  28.6 1.3 %broadcast_select_fusion = (bf16[8,8,7168]{2,1,0:T(8,128)(2,1)S(1)}, bf16[8,8,7168]{2,1,0:T(8,128)(2,1)S(1)}) fusion(bf16[8,8,7168]{2,1,0:T(8,128)(2,1)} %collective-permute-done.7, bf16[8,8,7168]{2,1,0:T(8,128)(2,1)S(1)} %bitcast_dynamic-update-slice_fusion, pred[]{:T(512)S(6)} %eq.85), kind=kLoop, calls=%fused_computation.23 | loop fusion | flops 917504 | bytes 3670017 | tf_op jit(solution)/shard_map/jit(_where)/select_n | solution.py:358
  30.1 0.9 copy-done.3
  31.0 0.3 copy-done.2
  31.3 32.2 %shard_map.112 = (bf16[64,7168]{1,0:T(8,128)(2,1)}, bf16[64,7168]{1,0:T(8,128)(2,1)}) custom-call(s32[1]{0:T(128)} %constant.275.clone.1.first_ref, bf16[64,7168]{1,0:T(8,128)(2,1)} %bitcast.79, bf16[64,7168]{1,0:T(8,128)(2,1)} %bitcast.80, bf16[7168,1024]{1,0:T(8,128)(2,1)} %g_ref.1, bf16[7168,1024]{1,0:T(8,128)(2,1)} %u_ref.1, bf16[1024,7168]{1,0:T(8,128)(2,1)} %d_ref.1), custom_call_target="tpu_custom_call" | custom-call | tf_op jit(solution)/shard_map/pallas_call | solution.py:188
  63.5 0.4 collective-permute-start.13
  64.0 2.4 %collective-permute-done.13 = bf16[64,7168]{1,0:T(8,128)(2,1)} collective-permute-done((bf16[64,7168]{1,0:T(8,128)(2,1)}, bf16[64,7168]{1,0:T(8,128)(2,1)}, u32[]{:S(2)}, u32[]{:S(2)}) %collective-permute-start.13) | collective-permute-done | bytes 917536 | tf_op jit(solution)/shard_map/ppermute | solution.py:371
  66.4 1.7 %fusion.10 = bf16[8,8,7168]{2,1,0:T(8,128)(2,1)S(1)} fusion(bf16[64,7168]{1,0:T(8,128)(2,1)} %collective-permute-done.13, bf16[64,7168]{1,0:T(8,128)(2,1)} %get-tuple-element.7), kind=kLoop, calls=%fused_computation.22 | loop fusion | flops 1835008 | bytes 2752512 | tf_op jit(solution)/shard_map/reshape | solution.py:375
  68.1 5.2 %collective-permute-start.14 = (bf16[8,7168]{1,0:T(8,128)(2,1)S(1)}, bf16[8,7168]{1,0:T(8,128)(2,1)S(1)}, u32[]{:S(2)}, u32[]{:S(2)}) collective-permute-start(bf16[8,7168]{1,0:T(8,128)(2,1)S(1)} %get-tuple-element.15), channel_id=1, source_target_pairs={{0,2},{1,3},{2,4},{3,5},{4,6},{5,7},{6,0},{7,1},{8,10},{9,11},{10,... | collective-permute-start | bytes 344072 | tf_op jit(solution)/shard_map/ppermute | solution.py:330
  73.3 1.9 %collective-permute-start.15 = (bf16[8,7168]{1,0:T(8,128)(2,1)S(1)}, bf16[8,7168]{1,0:T(8,128)(2,1)S(1)}, u32[]{:S(2)}, u32[]{:S(2)}) collective-permute-start(bf16[8,7168]{1,0:T(8,128)(2,1)S(1)} %get-tuple-element.14), channel_id=1, source_target_pairs={{0,4},{1,5},{2,6},{3,7},{4,0},{5,1},{6,2},{7,3},{8,12},{9,13},{10,... | collective-permute-start | bytes 344072 | tf_op jit(solution)/shard_map/ppermute | solution.py:330
  75.2 0.5 collective-permute-start.16
  75.8 0.5 gather_fusion.1
  76.5 2.3 %collective-permute-done.14 = bf16[8,7168]{1,0:T(8,128)(2,1)S(1)} collective-permute-done((bf16[8,7168]{1,0:T(8,128)(2,1)S(1)}, bf16[8,7168]{1,0:T(8,128)(2,1)S(1)}, u32[]{:S(2)}, u32[]{:S(2)}) %collective-permute-start.14) | collective-permute-done | bytes 114720 | tf_op jit(solution)/shard_map/ppermute | solution.py:330
  78.8 4.6 %collective-permute-done.15 = bf16[8,7168]{1,0:T(8,128)(2,1)S(1)} collective-permute-done((bf16[8,7168]{1,0:T(8,128)(2,1)S(1)}, bf16[8,7168]{1,0:T(8,128)(2,1)S(1)}, u32[]{:S(2)}, u32[]{:S(2)}) %collective-permute-start.15) | collective-permute-done | bytes 114720 | tf_op jit(solution)/shard_map/ppermute | solution.py:330
  83.4 3.1 %multiply_reduce_fusion = (f32[128]{0:T(128)S(1)}, f32[128,7168]{1,0:T(8,128)S(1)}) fusion(bf16[128,7168]{1,0:T(8,128)(2,1)S(1)} %copy-done, f32[7168]{0:T(1024)S(1)} %copy-done.5, f32[7168]{0:T(1024)S(1)} %copy-done.6, bf16[1,8,7168]{2,1,0:T(8,128)(2,1)} %bitcast.36, bf16[1,8,7168]{2,1,0:T(8,128)(2,1)S(1)} %bitcast.82, ...), kind=kOutput, calls=%fused_computation.10 | convolution fusion | flops 357601152 | bytes 6038020 | tf_op jit(solution)/shard_map/dot_general | solution.py:199
  86.5 2.6 %fusion.49 = (f32[7168]{0:T(1024)S(1)}, bf16[128,7168]{1,0:T(8,128)(2,1)}) fusion(f32[128]{0:T(128)S(1)} %broadcast_multiply_fusion, f32[128]{0:T(128)S(1)} %get-tuple-element.42, f32[7168]{0:T(1024)S(1)} %copy-done.5, bf16[128,7168]{1,0:T(8,128)(2,1)S(1)} %copy-done, f32[128,7168]{1,0:T(8,128)S(1)} %get-tuple-element.45, f32[128]{0:T(128)S(1)} %get-tuple-element.43, ...), kind=kLoop, calls=%fused_computation.122 | loop fusion | flops 9167872 | bytes 9233920 | tf_op jit(solution)/shard_map/reduce_sum | solution.py:426
  89.1 0.2 fusion.9
  89.4 1.0 collective-permute-done.17
  90.3 1.5 %collective-permute-start.18 = (f32[7168]{0:T(1024)S(1)}, f32[7168]{0:T(1024)S(1)}, u32[]{:S(2)}, u32[]{:S(2)}) collective-permute-start(f32[7168]{0:T(1024)S(1)} %add.277), channel_id=1, source_target_pairs={{0,8},{8,0},{16,24},{24,16},{1,9},{9,1},{17,25},{25,17},{2,10},{10... | collective-permute-start | bytes 86024 | tf_op jit(solution)/shard_map/ppermute | solution.py:239
  91.9 2.6 %collective-permute-start.10 = (bf16[8,7168]{1,0:T(8,128)(2,1)S(1)}, bf16[8,7168]{1,0:T(8,128)(2,1)S(1)}, u32[]{:S(2)}, u32[]{:S(2)}) collective-permute-start(bf16[8,7168]{1,0:T(8,128)(2,1)S(1)} %get-tuple-element.19), channel_id=1, source_target_pairs={{0,3},{1,4},{2,5},{3,6},{4,7},{5,0},{6,1},{7,2},{8,11},{9,12},{10,... | collective-permute-start | bytes 344072 | tf_op jit(solution)/shard_map/ppermute | solution.py:330
  94.5 1.3 %collective-permute-start.11 = (bf16[8,7168]{1,0:T(8,128)(2,1)S(1)}, bf16[8,7168]{1,0:T(8,128)(2,1)S(1)}, u32[]{:S(2)}, u32[]{:S(2)}) collective-permute-start(bf16[8,7168]{1,0:T(8,128)(2,1)S(1)} %get-tuple-element.18), channel_id=1, source_target_pairs={{0,5},{1,6},{2,7},{3,0},{4,1},{5,2},{6,3},{7,4},{8,13},{9,14},{10,... | collective-permute-start | bytes 344072 | tf_op jit(solution)/shard_map/ppermute | solution.py:330
  95.8 1.4 %collective-permute-start.12 = (bf16[8,7168]{1,0:T(8,128)(2,1)S(1)}, bf16[8,7168]{1,0:T(8,128)(2,1)S(1)}, u32[]{:S(2)}, u32[]{:S(2)}) collective-permute-start(bf16[8,7168]{1,0:T(8,128)(2,1)S(1)} %get-tuple-element.17), channel_id=1, source_target_pairs={{0,7},{1,0},{2,1},{3,2},{4,3},{5,4},{6,5},{7,6},{8,15},{9,8},{10,9... | collective-permute-start | bytes 344072 | tf_op jit(solution)/shard_map/ppermute | solution.py:330
  97.2 1.6 %collective-permute-start.19 = (f32[7168]{0:T(1024)S(1)}, f32[7168]{0:T(1024)S(1)}, u32[]{:S(2)}, u32[]{:S(2)}) collective-permute-start(f32[7168]{0:T(1024)S(1)} %add.278), channel_id=1, source_target_pairs={{0,16},{8,24},{16,0},{24,8},{1,17},{9,25},{17,1},{25,9},{2,18},{10... | collective-permute-start | bytes 86024 | tf_op jit(solution)/shard_map/ppermute | solution.py:239
  98.8 2.3 %collective-permute-done.19 = f32[7168]{0:T(1024)S(1)} collective-permute-done((f32[7168]{0:T(1024)S(1)}, f32[7168]{0:T(1024)S(1)}, u32[]{:S(2)}, u32[]{:S(2)}) %collective-permute-start.19) | collective-permute-done | bytes 28704 | tf_op jit(solution)/shard_map/ppermute | solution.py:239
  101.2 3.0 %collective-permute-start.20 = (f32[7168]{0:T(1024)S(1)}, f32[7168]{0:T(1024)S(1)}, u32[]{:S(2)}, u32[]{:S(2)}) collective-permute-start(f32[7168]{0:T(1024)S(1)} %add.279), channel_id=1, source_target_pairs={{0,2},{1,3},{2,0},{3,1},{4,6},{5,7},{6,4},{7,5},{8,10},{9,11},{10,... | collective-permute-start | bytes 86024 | tf_op jit(solution)/shard_map/ppermute | solution.py:239
  104.2 0.5 gather_fusion
  104.8 1.3 %collective-permute-done.20 = f32[7168]{0:T(1024)S(1)} collective-permute-done((f32[7168]{0:T(1024)S(1)}, f32[7168]{0:T(1024)S(1)}, u32[]{:S(2)}, u32[]{:S(2)}) %collective-permute-start.20) | collective-permute-done | bytes 28704 | tf_op jit(solution)/shard_map/ppermute | solution.py:239
  106.1 0.4 collective-permute-start.21
  106.5 3.1 %fusion.2 = bf16[128,7168]{1,0:T(8,128)(2,1)} fusion(bf16[128,7168]{1,0:T(8,128)(2,1)S(1)} %copy-done, f32[7168]{0:T(1024)S(1)} %copy-done.5, bf16[1,8,7168]{2,1,0:T(8,128)(2,1)S(1)} %bitcast.86, bf16[1,8,7168]{2,1,0:T(8,128)(2,1)S(1)} %bitcast.85, bf16[1,8,7168]{2,1,0:T(8,128)(2,1)S(1)} %bitcast.84, bf16[1,8,7168]{2,1,0:T(8,128)(2,1)S(1)} %bitcast.83, ...), kind=kOutput, calls=%fused_computation.6 | convolution fusion | flops 356683776 | bytes 4173828 | tf_op jit(solution)/shard_map/dot_general | solution.py:199
  109.6 1.2 %collective-permute-done.21 = f32[7168]{0:T(1024)S(1)} collective-permute-done((f32[7168]{0:T(1024)S(1)}, f32[7168]{0:T(1024)S(1)}, u32[]{:S(2)}, u32[]{:S(2)}) %collective-permute-start.21) | collective-permute-done | bytes 28704 | tf_op jit(solution)/shard_map/ppermute | solution.py:239
  110.8 0.6 add.281
  (69 shorter events, 0.9 us)
Async XLA Ops:
  0.6 4.2 %copy-start = (bf16[128,7168]{1,0:T(8,128)(2,1)S(1)}, bf16[128,7168]{1,0:T(8,128)(2,1)}, u32[]{:S(2)}) copy-start(bf16[128,7168]{1,0:T(8,128)(2,1)} %param.11) | copy-start | bytes 5505028
  0.6 4.2 %copy-start.5 = (f32[7168]{0:T(1024)S(1)}, f32[7168]{0:T(1024)}, u32[]{:S(2)}) copy-start(f32[7168]{0:T(1024)} %param.12) | copy-start | bytes 86020
  0.7 4.8 %copy-start.6 = (f32[7168]{0:T(1024)S(1)}, f32[7168]{0:T(1024)}, u32[]{:S(2)}) copy-start(f32[7168]{0:T(1024)} %param.13) | copy-start | bytes 86020
  4.3 9.7 %collective-permute-start = (bf16[8,7168]{1,0:T(8,128)(2,1)S(1)}, bf16[8,7168]{1,0:T(8,128)(2,1)S(1)}, u32[]{:S(2)}, u32[]{:S(2)}) collective-permute-start(bf16[8,7168]{1,0:T(8,128)(2,1)S(1)} %get-tuple-element.37), channel_id=1, source_target_pairs={{0,1},{1,2},{2,3},{3,4},{4,5},{5,6},{6,7},{7,0},{8,9},{9,10},{10,1... | collective-permute-start | bytes 344072 | tf_op jit(solution)/shard_map/ppermute | solution.py:351
  6.3 9.1 %collective-permute-start.1 = (bf16[8,7168]{1,0:T(8,128)(2,1)S(1)}, bf16[8,7168]{1,0:T(8,128)(2,1)S(1)}, u32[]{:S(2)}, u32[]{:S(2)}) collective-permute-start(bf16[8,7168]{1,0:T(8,128)(2,1)S(1)} %get-tuple-element.40), channel_id=1, source_target_pairs={{0,2},{1,3},{2,4},{3,5},{4,6},{5,7},{6,0},{7,1},{8,10},{9,11},{10,... | collective-permute-start | bytes 344072 | tf_op jit(solution)/shard_map/ppermute | solution.py:351
  9.0 14.6 %collective-permute-start.2 = (bf16[8,7168]{1,0:T(8,128)(2,1)S(1)}, bf16[8,7168]{1,0:T(8,128)(2,1)S(1)}, u32[]{:S(2)}, u32[]{:S(2)}) collective-permute-start(bf16[8,7168]{1,0:T(8,128)(2,1)S(1)} %get-tuple-element.36), channel_id=1, source_target_pairs={{0,3},{1,4},{2,5},{3,6},{4,7},{5,0},{6,1},{7,2},{8,11},{9,12},{10,... | collective-permute-start | bytes 344072 | tf_op jit(solution)/shard_map/ppermute | solution.py:351
  11.5 12.4 %collective-permute-start.3 = (bf16[8,7168]{1,0:T(8,128)(2,1)S(1)}, bf16[8,7168]{1,0:T(8,128)(2,1)S(1)}, u32[]{:S(2)}, u32[]{:S(2)}) collective-permute-start(bf16[8,7168]{1,0:T(8,128)(2,1)S(1)} %get-tuple-element.39), channel_id=1, source_target_pairs={{0,4},{1,5},{2,6},{3,7},{4,0},{5,1},{6,2},{7,3},{8,12},{9,13},{10,... | collective-permute-start | bytes 344072 | tf_op jit(solution)/shard_map/ppermute | solution.py:351
  12.7 11.2 %collective-permute-start.4 = (bf16[8,7168]{1,0:T(8,128)(2,1)S(1)}, bf16[8,7168]{1,0:T(8,128)(2,1)S(1)}, u32[]{:S(2)}, u32[]{:S(2)}) collective-permute-start(bf16[8,7168]{1,0:T(8,128)(2,1)S(1)} %get-tuple-element.35), channel_id=1, source_target_pairs={{0,5},{1,6},{2,7},{3,0},{4,1},{5,2},{6,3},{7,4},{8,13},{9,14},{10,... | collective-permute-start | bytes 344072 | tf_op jit(solution)/shard_map/ppermute | solution.py:351
  14.0 9.9 %collective-permute-start.5 = (bf16[8,7168]{1,0:T(8,128)(2,1)S(1)}, bf16[8,7168]{1,0:T(8,128)(2,1)S(1)}, u32[]{:S(2)}, u32[]{:S(2)}) collective-permute-start(bf16[8,7168]{1,0:T(8,128)(2,1)S(1)} %get-tuple-element.38), channel_id=1, source_target_pairs={{0,6},{1,7},{2,0},{3,1},{4,2},{5,3},{6,4},{7,5},{8,14},{9,15},{10,... | collective-permute-start | bytes 344072 | tf_op jit(solution)/shard_map/ppermute | solution.py:351
  15.4 8.6 %collective-permute-start.6 = (bf16[8,7168]{1,0:T(8,128)(2,1)S(1)}, bf16[8,7168]{1,0:T(8,128)(2,1)S(1)}, u32[]{:S(2)}, u32[]{:S(2)}) collective-permute-start(bf16[8,7168]{1,0:T(8,128)(2,1)S(1)} %get-tuple-element.34), channel_id=1, source_target_pairs={{0,7},{1,0},{2,1},{3,2},{4,3},{5,4},{6,5},{7,6},{8,15},{9,8},{10,9... | collective-permute-start | bytes 344072 | tf_op jit(solution)/shard_map/ppermute | solution.py:351
  24.0 4.6 %collective-permute-start.7 = (bf16[8,8,7168]{2,1,0:T(8,128)(2,1)S(1)}, bf16[8,8,7168]{2,1,0:T(8,128)(2,1)}, u32[]{:S(2)}, u32[]{:S(2)}) collective-permute-start(bf16[8,8,7168]{2,1,0:T(8,128)(2,1)S(1)} %bitcast_dynamic-update-slice_fusion), channel_id=1, source_target_pairs={{0,1},{1,0},{2,3},{3,2},{4,5},{5,4},{6,7},{7,6},{8,9},{9,8},{10,11... | collective-permute-start | bytes 2752520 | tf_op jit(solution)/shard_map/ppermute | solution.py:355
  30.1 0.9 copy-start.3
  30.1 1.2 %copy-start.2 = (bf16[8,8,7168]{2,1,0:T(8,128)(2,1)}, bf16[8,8,7168]{2,1,0:T(8,128)(2,1)S(1)}, u32[]{:S(2)}) copy-start(bf16[8,8,7168]{2,1,0:T(8,128)(2,1)S(1)} %slice_dynamic-update-slice_fusion.8) | copy-start | bytes 2752516
  31.3 32.6 %copy-start.8 = (s32[128,8]{0,1:T(8,128)S(1)}, s32[128,8]{0,1:T(8,128)}, u32[]{:S(2)}) copy-start(s32[128,8]{0,1:T(8,128)} %param.15) | copy-start | bytes 12292
  31.3 32.6 %copy-start.7 = (s32[128,8]{0,1:T(8,128)S(1)}, s32[128,8]{0,1:T(8,128)}, u32[]{:S(2)}) copy-start(s32[128,8]{0,1:T(8,128)} %param.14) | copy-start | bytes 12292
  63.5 12.8 %copy-start.4 = (bf16[64,7168]{1,0:T(8,128)(2,1)S(1)}, bf16[64,7168]{1,0:T(8,128)(2,1)}, u32[]{:S(2)}) copy-start(bf16[64,7168]{1,0:T(8,128)(2,1)} %get-tuple-element.6) | copy-start | bytes 2752516
  63.5 2.8 %collective-permute-start.13 = (bf16[64,7168]{1,0:T(8,128)(2,1)}, bf16[64,7168]{1,0:T(8,128)(2,1)}, u32[]{:S(2)}, u32[]{:S(2)}) collective-permute-start(bf16[64,7168]{1,0:T(8,128)(2,1)} %get-tuple-element.7), channel_id=1, source_target_pairs={{0,1},{1,0},{2,3},{3,2},{4,5},{5,4},{6,7},{7,6},{8,9},{9,8},{10,11... | collective-permute-start | bytes 2752520 | tf_op jit(solution)/shard_map/ppermute | solution.py:371
  68.1 10.7 %collective-permute-start.14 = (bf16[8,7168]{1,0:T(8,128)(2,1)S(1)}, bf16[8,7168]{1,0:T(8,128)(2,1)S(1)}, u32[]{:S(2)}, u32[]{:S(2)}) collective-permute-start(bf16[8,7168]{1,0:T(8,128)(2,1)S(1)} %get-tuple-element.15), channel_id=1, source_target_pairs={{0,2},{1,3},{2,4},{3,5},{4,6},{5,7},{6,0},{7,1},{8,10},{9,11},{10,... | collective-permute-start | bytes 344072 | tf_op jit(solution)/shard_map/ppermute | solution.py:330
  73.3 10.0 %collective-permute-start.15 = (bf16[8,7168]{1,0:T(8,128)(2,1)S(1)}, bf16[8,7168]{1,0:T(8,128)(2,1)S(1)}, u32[]{:S(2)}, u32[]{:S(2)}) collective-permute-start(bf16[8,7168]{1,0:T(8,128)(2,1)S(1)} %get-tuple-element.14), channel_id=1, source_target_pairs={{0,4},{1,5},{2,6},{3,7},{4,0},{5,1},{6,2},{7,3},{8,12},{9,13},{10,... | collective-permute-start | bytes 344072 | tf_op jit(solution)/shard_map/ppermute | solution.py:330
  75.2 8.1 %collective-permute-start.16 = (bf16[8,7168]{1,0:T(8,128)(2,1)S(1)}, bf16[8,7168]{1,0:T(8,128)(2,1)}, u32[]{:S(2)}, u32[]{:S(2)}) collective-permute-start(bf16[8,7168]{1,0:T(8,128)(2,1)S(1)} %get-tuple-element.13), channel_id=1, source_target_pairs={{0,6},{1,7},{2,0},{3,1},{4,2},{5,3},{6,4},{7,5},{8,14},{9,15},{10,... | collective-permute-start | bytes 344072 | tf_op jit(solution)/shard_map/ppermute | solution.py:330
  76.4 10.1 %copy-start.1 = (bf16[128,7168]{1,0:T(8,128)(2,1)S(1)}, bf16[128,7168]{1,0:T(8,128)(2,1)}, u32[]{:S(2)}) copy-start(bf16[128,7168]{1,0:T(8,128)(2,1)} %param.19) | copy-start | bytes 5505028
  76.4 12.7 %collective-permute-start.8 = (bf16[64,7168]{1,0:T(8,128)(2,1)S(1)}, bf16[64,7168]{1,0:T(8,128)(2,1)S(1)}, u32[]{:S(2)}, u32[]{:S(2)}) collective-permute-start(bf16[64,7168]{1,0:T(8,128)(2,1)S(1)} %copy-done.4), channel_id=1, source_target_pairs={{0,1},{1,0},{2,3},{3,2},{4,5},{5,4},{6,7},{7,6},{8,9},{9,8},{10,11... | collective-permute-start | bytes 2752520 | tf_op jit(solution)/shard_map/ppermute | solution.py:377
  89.1 1.2 %collective-permute-start.17 = (f32[7168]{0:T(1024)S(1)}, f32[7168]{0:T(1024)S(1)}, u32[]{:S(2)}, u32[]{:S(2)}) collective-permute-start(f32[7168]{0:T(1024)S(1)} %get-tuple-element.8), channel_id=1, source_target_pairs={{0,1},{1,0},{2,3},{3,2},{4,5},{5,4},{6,7},{7,6},{8,9},{9,8},{10,11... | collective-permute-start | bytes 86024 | tf_op jit(solution)/shard_map/ppermute | solution.py:239
  90.3 6.9 %collective-permute-start.18 = (f32[7168]{0:T(1024)S(1)}, f32[7168]{0:T(1024)S(1)}, u32[]{:S(2)}, u32[]{:S(2)}) collective-permute-start(f32[7168]{0:T(1024)S(1)} %add.277), channel_id=1, source_target_pairs={{0,8},{8,0},{16,24},{24,16},{1,9},{9,1},{17,25},{25,17},{2,10},{10... | collective-permute-start | bytes 86024 | tf_op jit(solution)/shard_map/ppermute | solution.py:239
  91.9 14.6 %collective-permute-start.9 = (bf16[8,7168]{1,0:T(8,128)(2,1)S(1)}, bf16[8,7168]{1,0:T(8,128)(2,1)S(1)}, u32[]{:S(2)}, u32[]{:S(2)}) collective-permute-start(bf16[8,7168]{1,0:T(8,128)(2,1)S(1)} %get-tuple-element.16), channel_id=1, source_target_pairs={{0,1},{1,2},{2,3},{3,4},{4,5},{5,6},{6,7},{7,0},{8,9},{9,10},{10,1... | collective-permute-start | bytes 344072 | tf_op jit(solution)/shard_map/ppermute | solution.py:330
  91.9 14.6 %collective-permute-start.10 = (bf16[8,7168]{1,0:T(8,128)(2,1)S(1)}, bf16[8,7168]{1,0:T(8,128)(2,1)S(1)}, u32[]{:S(2)}, u32[]{:S(2)}) collective-permute-start(bf16[8,7168]{1,0:T(8,128)(2,1)S(1)} %get-tuple-element.19), channel_id=1, source_target_pairs={{0,3},{1,4},{2,5},{3,6},{4,7},{5,0},{6,1},{7,2},{8,11},{9,12},{10,... | collective-permute-start | bytes 344072 | tf_op jit(solution)/shard_map/ppermute | solution.py:330
  94.5 12.0 %collective-permute-start.11 = (bf16[8,7168]{1,0:T(8,128)(2,1)S(1)}, bf16[8,7168]{1,0:T(8,128)(2,1)S(1)}, u32[]{:S(2)}, u32[]{:S(2)}) collective-permute-start(bf16[8,7168]{1,0:T(8,128)(2,1)S(1)} %get-tuple-element.18), channel_id=1, source_target_pairs={{0,5},{1,6},{2,7},{3,0},{4,1},{5,2},{6,3},{7,4},{8,13},{9,14},{10,... | collective-permute-start | bytes 344072 | tf_op jit(solution)/shard_map/ppermute | solution.py:330
  95.8 10.7 %collective-permute-start.12 = (bf16[8,7168]{1,0:T(8,128)(2,1)S(1)}, bf16[8,7168]{1,0:T(8,128)(2,1)S(1)}, u32[]{:S(2)}, u32[]{:S(2)}) collective-permute-start(bf16[8,7168]{1,0:T(8,128)(2,1)S(1)} %get-tuple-element.17), channel_id=1, source_target_pairs={{0,7},{1,0},{2,1},{3,2},{4,3},{5,4},{6,5},{7,6},{8,15},{9,8},{10,9... | collective-permute-start | bytes 344072 | tf_op jit(solution)/shard_map/ppermute | solution.py:330
  97.2 3.9 %collective-permute-start.19 = (f32[7168]{0:T(1024)S(1)}, f32[7168]{0:T(1024)S(1)}, u32[]{:S(2)}, u32[]{:S(2)}) collective-permute-start(f32[7168]{0:T(1024)S(1)} %add.278), channel_id=1, source_target_pairs={{0,16},{8,24},{16,0},{24,8},{1,17},{9,25},{17,1},{25,9},{2,18},{10... | collective-permute-start | bytes 86024 | tf_op jit(solution)/shard_map/ppermute | solution.py:239
  101.2 4.9 %collective-permute-start.20 = (f32[7168]{0:T(1024)S(1)}, f32[7168]{0:T(1024)S(1)}, u32[]{:S(2)}, u32[]{:S(2)}) collective-permute-start(f32[7168]{0:T(1024)S(1)} %add.279), channel_id=1, source_target_pairs={{0,2},{1,3},{2,0},{3,1},{4,6},{5,7},{6,4},{7,5},{8,10},{9,11},{10,... | collective-permute-start | bytes 86024 | tf_op jit(solution)/shard_map/ppermute | solution.py:239
  106.1 4.8 %collective-permute-start.21 = (f32[7168]{0:T(1024)S(1)}, f32[7168]{0:T(1024)S(1)}, u32[]{:S(2)}, u32[]{:S(2)}) collective-permute-start(f32[7168]{0:T(1024)S(1)} %add.280), channel_id=1, source_target_pairs={{0,4},{1,5},{2,6},{3,7},{4,0},{5,1},{6,2},{7,3},{8,12},{9,13},{10,... | collective-permute-start | bytes 86024 | tf_op jit(solution)/shard_map/ppermute | solution.py:239

commit v14 on v13

--- a/solution.py
+++ b/solution.py
@@ -193,6 +193,16 @@
             dimension_semantics=("arbitrary",), vmem_limit_bytes=56 * 1024 * 1024
         ),
     )(first, arrived, partner, gw, uw, dw)
+
+
+def split_combine(combine, rows):
+    high = combine.astype(jnp.bfloat16)
+    rest = combine - high.astype(jnp.float32)
+    mid = rest.astype(jnp.bfloat16)
+    low = (rest - mid.astype(jnp.float32)).astype(jnp.bfloat16)
+    total = jnp.dot(high, rows, preferred_element_type=jnp.float32)
+    total = total + jnp.dot(mid, rows, preferred_element_type=jnp.float32)
+    return total + jnp.dot(low, rows, preferred_element_type=jnp.float32)
 
 
 def apply_combine(combine, partial_sums):
@@ -380,7 +390,7 @@
     out_sums, out_order = by_parity(
         out_total.astype(jnp.bfloat16).reshape(shape), 1, flight, group_size
     )
-    return out_sums.astype(jnp.float32), grad_sums.astype(jnp.float32), out_order, grad_order
+    return out_sums, grad_sums, out_order, grad_order
 
 
 def shards(
@@ -413,13 +423,15 @@
         by_expert = combine.reshape(combine.shape[0], flight, capacity)
         out_combine = jnp.take(by_expert, out_order, axis=1).reshape(combine.shape)
         grad_combine = jnp.take(by_expert, grad_order, axis=1).reshape(combine.shape)
+        mixture = split_combine(out_combine, out_sums)
+        back_normed = split_combine(grad_combine, grad_sums)
     else:
         out_sums, grad_sums = by_features(
             normed, out_grad, slot_table, filled, gate_weight, up_weight, down_weight,
             member, expert_count, group_size,
         )
-    mixture = apply_combine(out_combine, out_sums)
-    back_normed = apply_combine(grad_combine, grad_sums)
+        mixture = apply_combine(out_combine, out_sums)
+        back_normed = apply_combine(grad_combine, grad_sums)
     layer_out = (residual + mixture).astype(jnp.bfloat16)
     total_grad = norm_backward(residual, inverse, norm_gain, back_normed, out_grad)
     steer_grad = butterfly_sum(

time: 112 us -> 115 us (1.027)
  starting transfers between devices: 33.4 us -> 38.4 us
  waiting for transfers between devices: 24.4 us -> 20.8 us
  local copies, waits for them, and re-layouts: 2.85 us -> 4.55 us
    ppermute x5, starting transfers between devices: 6.57 us -> 12.8 us  [butterfly_sum(): lax.ppermute(value, axis, [(i, i ^ bit) for i in range(size)])]
    ppermute x7, starting transfers between devices: 13 us -> 11.4 us  [by_parity(): lax.ppermute(part, 'expert', [(i, (i + shift) % size) for i in range(size)])]
    dot_general x2 -> x6, matrix products: 6.18 us -> 6.79 us  [the longest x2 3.8 us: split_combine(): total = jnp.dot(high, rows, preferred_element_type=jnp.float32)]
  transfers between devices with their start and end apart: 22 -> 22, of which waited for: 10 -> 9; matrix products, arithmetic and copies ran while one was open for 11% -> 13% of each run, Pallas kernels for 0% -> 0%
where the time goes in v14:
time: 115 us
  starting transfers between devices  38.4 us (33%)
  Pallas kernels  32.2 us (28%)
  waiting for transfers between devices  20.8 us (18%)
  matrix products  9.49 us (8%)
  other arithmetic  8.45 us (7%)
  local copies, waits for them, and re-layouts  4.55 us (4%)
  between operations  1.17 us (1%)
    pallas_call x1, Pallas kernels, expert_pair(): pl.pallas_call(_pair_kernel, grid_spec=grid_spec, out_shape=[jax.ShapeDty...  32.2 us
    ppermute x5, starting transfers between devices, butterfly_sum(): lax.ppermute(value, axis, [(i, i ^ bit) for i in range(size)])  12.8 us
    ppermute x7, starting transfers between devices, by_parity(): lax.ppermute(part, 'expert', [(i, (i + shift) % size) for i in range(size)])  11.4 us
    ppermute x7, starting transfers between devices, by_pair(): part = lax.ppermute(part, 'expert', pairs)  10.9 us
    ppermute x7, waiting for transfers between devices, by_parity(): lax.ppermute(part, 'expert', [(i, (i + shift) % size) for i in range(size)])  6.24 us
    ppermute x7, waiting for transfers between devices, by_pair(): part = lax.ppermute(part, 'expert', pairs)  6.08 us
    ppermute x5, waiting for transfers between devices, butterfly_sum(): lax.ppermute(value, axis, [(i, i ^ bit) for i in range(size)])  4.73 us
    dot_general x2, matrix products, split_combine(): total = jnp.dot(high, rows, preferred_element_type=jnp.float32)  3.8 us
  transfers between devices with their start and end apart: 22, of which 9 were waited for; matrix products, arithmetic and copies ran while one was open for 13% of the time, Pallas kernels for 0%

profile of v14, /device:TPU:0, one launch (start us, length us, event | category | flops | bytes accessed | tf_op | source)
XLA Modules:
  0.0 115.1 jit_solution(10652226068532366681)
XLA Ops:
  0.7 0.8 fusion.17
  2.3 1.9 %convolution_convert_fusion = bf16[4,8,7168]{2,1,0:T(8,128)(2,1)S(1)} fusion(bf16[128,7168]{1,0:T(8,128)(2,1)} %param.19, s32[4,8]{1,0:T(4,128)S(1)} %select_reduce_fusion, pred[4,8]{1,0:T(4,128)(4,1)S(1)} %fusion.15), kind=kOutput, calls=%fused_computation.15 | convolution fusion | flops 58957824 | bytes 2293920 | tf_op jit(solution)/shard_map/fct,td->fcd/dot_general | solution.py:314
  4.2 0.7 dynamic-slice_bitcast_fusion.7
  5.0 0.5 collective-permute-start
  5.5 0.6 multiply_reduce_fusion.1
  6.1 0.8 convolution_convert_fusion.1
  6.9 2.6 %collective-permute-start.1 = (bf16[8,7168]{1,0:T(8,128)(2,1)S(1)}, bf16[8,7168]{1,0:T(8,128)(2,1)S(1)}, u32[]{:S(2)}, u32[]{:S(2)}) collective-permute-start(bf16[8,7168]{1,0:T(8,128)(2,1)S(1)} %get-tuple-element.40), channel_id=1, source_target_pairs={{0,2},{1,3},{2,4},{3,5},{4,6},{5,7},{6,0},{7,1},{8,10},{9,11},{10,... | collective-permute-start | bytes 344072 | tf_op jit(solution)/shard_map/ppermute | solution.py:361
  9.5 2.6 %collective-permute-start.2 = (bf16[8,7168]{1,0:T(8,128)(2,1)}, bf16[8,7168]{1,0:T(8,128)(2,1)S(1)}, u32[]{:S(2)}, u32[]{:S(2)}) collective-permute-start(bf16[8,7168]{1,0:T(8,128)(2,1)} %get-tuple-element.36), channel_id=1, source_target_pairs={{0,3},{1,4},{2,5},{3,6},{4,7},{5,0},{6,1},{7,2},{8,11},{9,12},{10,... | collective-permute-start | bytes 344072 | tf_op jit(solution)/shard_map/ppermute | solution.py:361
  12.1 1.2 %collective-permute-start.3 = (bf16[8,7168]{1,0:T(8,128)(2,1)S(1)}, bf16[8,7168]{1,0:T(8,128)(2,1)S(1)}, u32[]{:S(2)}, u32[]{:S(2)}) collective-permute-start(bf16[8,7168]{1,0:T(8,128)(2,1)S(1)} %get-tuple-element.39), channel_id=1, source_target_pairs={{0,4},{1,5},{2,6},{3,7},{4,0},{5,1},{6,2},{7,3},{8,12},{9,13},{10,... | collective-permute-start | bytes 344072 | tf_op jit(solution)/shard_map/ppermute | solution.py:361
  13.3 1.1 collective-permute-start.4
  14.5 1.3 %collective-permute-start.5 = (bf16[8,7168]{1,0:T(8,128)(2,1)S(1)}, bf16[8,7168]{1,0:T(8,128)(2,1)S(1)}, u32[]{:S(2)}, u32[]{:S(2)}) collective-permute-start(bf16[8,7168]{1,0:T(8,128)(2,1)S(1)} %get-tuple-element.38), channel_id=1, source_target_pairs={{0,6},{1,7},{2,0},{3,1},{4,2},{5,3},{6,4},{7,5},{8,14},{9,15},{10,... | collective-permute-start | bytes 344072 | tf_op jit(solution)/shard_map/ppermute | solution.py:361
  15.8 0.9 bitcast_dynamic-update-slice_fusion.6
  16.7 1.5 %collective-permute-start.6 = (bf16[8,7168]{1,0:T(8,128)(2,1)S(1)}, bf16[8,7168]{1,0:T(8,128)(2,1)S(1)}, u32[]{:S(2)}, u32[]{:S(2)}) collective-permute-start(bf16[8,7168]{1,0:T(8,128)(2,1)S(1)} %get-tuple-element.34), channel_id=1, source_target_pairs={{0,7},{1,0},{2,1},{3,2},{4,3},{5,4},{6,5},{7,6},{8,15},{9,8},{10,9... | collective-permute-start | bytes 344072 | tf_op jit(solution)/shard_map/ppermute | solution.py:361
  18.2 5.9 %collective-permute-done.2 = bf16[8,7168]{1,0:T(8,128)(2,1)S(1)} collective-permute-done((bf16[8,7168]{1,0:T(8,128)(2,1)}, bf16[8,7168]{1,0:T(8,128)(2,1)S(1)}, u32[]{:S(2)}, u32[]{:S(2)}) %collective-permute-start.2) | collective-permute-done | bytes 114720 | tf_op jit(solution)/shard_map/ppermute | solution.py:361
  24.4 2.7 %collective-permute-start.7 = (bf16[8,8,7168]{2,1,0:T(8,128)(2,1)S(1)}, bf16[8,8,7168]{2,1,0:T(8,128)(2,1)}, u32[]{:S(2)}, u32[]{:S(2)}) collective-permute-start(bf16[8,8,7168]{2,1,0:T(8,128)(2,1)S(1)} %bitcast_dynamic-update-slice_fusion), channel_id=1, source_target_pairs={{0,1},{1,0},{2,3},{3,2},{4,5},{5,4},{6,7},{7,6},{8,9},{9,8},{10,11... | collective-permute-start | bytes 2752520 | tf_op jit(solution)/shard_map/ppermute | solution.py:365
  27.1 2.2 %collective-permute-done.7 = bf16[8,8,7168]{2,1,0:T(8,128)(2,1)} collective-permute-done((bf16[8,8,7168]{2,1,0:T(8,128)(2,1)S(1)}, bf16[8,8,7168]{2,1,0:T(8,128)(2,1)}, u32[]{:S(2)}, u32[]{:S(2)}) %collective-permute-start.7) | collective-permute-done | bytes 917536 | tf_op jit(solution)/shard_map/ppermute | solution.py:365
  29.3 1.3 %broadcast_select_fusion = (bf16[8,8,7168]{2,1,0:T(8,128)(2,1)S(1)}, bf16[8,8,7168]{2,1,0:T(8,128)(2,1)S(1)}) fusion(bf16[8,8,7168]{2,1,0:T(8,128)(2,1)} %collective-permute-done.7, bf16[8,8,7168]{2,1,0:T(8,128)(2,1)S(1)} %bitcast_dynamic-update-slice_fusion, pred[]{:T(512)S(6)} %eq.85), kind=kLoop, calls=%fused_computation.31 | loop fusion | flops 917504 | bytes 3670017 | tf_op jit(solution)/shard_map/jit(_where)/select_n | solution.py:368
  30.9 0.9 copy-done.3
  31.7 0.3 copy-done.2
  32.0 32.2 %shard_map.112 = (bf16[64,7168]{1,0:T(8,128)(2,1)}, bf16[64,7168]{1,0:T(8,128)(2,1)}) custom-call(s32[1]{0:T(128)} %constant.275.clone.1.first_ref, bf16[64,7168]{1,0:T(8,128)(2,1)} %bitcast.117, bf16[64,7168]{1,0:T(8,128)(2,1)} %bitcast.118, bf16[7168,1024]{1,0:T(8,128)(2,1)} %g_ref.1, bf16[7168,1024]{1,0:T(8,128)(2,1)} %u_ref.1, bf16[1024,7168]{1,0:T(8,128)(2,1)} %d_ref.1), custom_call_target="tpu_custom_call" | custom-call | tf_op jit(solution)/shard_map/pallas_call | solution.py:188
  64.3 0.4 collective-permute-start.13
  64.7 0.6 gather_fusion.1
  65.3 0.2 collective-permute-start.8
  65.5 1.5 %collective-permute-done.13 = bf16[64,7168]{1,0:T(8,128)(2,1)} collective-permute-done((bf16[64,7168]{1,0:T(8,128)(2,1)}, bf16[64,7168]{1,0:T(8,128)(2,1)}, u32[]{:S(2)}, u32[]{:S(2)}) %collective-permute-start.13) | collective-permute-done | bytes 917536 | tf_op jit(solution)/shard_map/ppermute | solution.py:381
  67.1 1.7 %fusion.14 = bf16[8,8,7168]{2,1,0:T(8,128)(2,1)S(1)} fusion(bf16[64,7168]{1,0:T(8,128)(2,1)} %collective-permute-done.13, bf16[64,7168]{1,0:T(8,128)(2,1)} %get-tuple-element.7), kind=kLoop, calls=%fused_computation.30 | loop fusion | flops 1835008 | bytes 2752512 | tf_op jit(solution)/shard_map/reshape | solution.py:385
  68.8 6.3 %collective-permute-start.16 = (bf16[8,7168]{1,0:T(8,128)(2,1)S(1)}, bf16[8,7168]{1,0:T(8,128)(2,1)S(1)}, u32[]{:S(2)}, u32[]{:S(2)}) collective-permute-start(bf16[8,7168]{1,0:T(8,128)(2,1)S(1)} %get-tuple-element.13), channel_id=1, source_target_pairs={{0,6},{1,7},{2,0},{3,1},{4,2},{5,3},{6,4},{7,5},{8,14},{9,15},{10,... | collective-permute-start | bytes 344072 | tf_op jit(solution)/shard_map/ppermute | solution.py:340
  75.2 0.5 collective-permute-start.14
  75.8 0.2 fusion.13
  76.1 2.7 %collective-permute-start.12 = (bf16[8,7168]{1,0:T(8,128)(2,1)S(1)}, bf16[8,7168]{1,0:T(8,128)(2,1)S(1)}, u32[]{:S(2)}, u32[]{:S(2)}) collective-permute-start(bf16[8,7168]{1,0:T(8,128)(2,1)S(1)} %get-tuple-element.17), channel_id=1, source_target_pairs={{0,7},{1,0},{2,1},{3,2},{4,3},{5,4},{6,5},{7,6},{8,15},{9,8},{10,9... | collective-permute-start | bytes 344072 | tf_op jit(solution)/shard_map/ppermute | solution.py:340
  78.7 1.7 %collective-permute-start.10 = (bf16[8,7168]{1,0:T(8,128)(2,1)S(1)}, bf16[8,7168]{1,0:T(8,128)(2,1)S(1)}, u32[]{:S(2)}, u32[]{:S(2)}) collective-permute-start(bf16[8,7168]{1,0:T(8,128)(2,1)S(1)} %get-tuple-element.19), channel_id=1, source_target_pairs={{0,3},{1,4},{2,5},{3,6},{4,7},{5,0},{6,1},{7,2},{8,11},{9,12},{10,... | collective-permute-start | bytes 344072 | tf_op jit(solution)/shard_map/ppermute | solution.py:340
  80.5 6.2 %collective-permute-done.15 = bf16[8,7168]{1,0:T(8,128)(2,1)S(1)} collective-permute-done((bf16[8,7168]{1,0:T(8,128)(2,1)S(1)}, bf16[8,7168]{1,0:T(8,128)(2,1)S(1)}, u32[]{:S(2)}, u32[]{:S(2)}) %collective-permute-start.15) | collective-permute-done | bytes 114720 | tf_op jit(solution)/shard_map/ppermute | solution.py:340
  86.7 0.7 convolution_bitcast_fusion
  87.4 0.7 convolution_bitcast_fusion.1
  88.2 1.4 %multiply_reduce_fusion = (f32[128]{0:T(128)S(1)}, f32[128,7168]{1,0:T(8,128)S(1)}) fusion(bf16[128,7168]{1,0:T(8,128)(2,1)S(1)} %copy-done, f32[7168]{0:T(1024)S(1)} %copy-done.5, f32[7168]{0:T(1024)S(1)} %copy-done.6, f32[128,7168]{1,0:T(8,128)S(1)} %convolution_bitcast_fusion, f32[128,7168]{1,0:T(8,128)S(1)} %convolution_bitcast_fusion.1, ...), kind=kOutput, calls=%fused_computation.18 | convolution fusion | flops 65834880 | bytes 13378052 | tf_op jit(solution)/shard_map/dot_general | solution.py:203
  89.7 2.6 %fusion.49 = (f32[7168]{0:T(1024)S(1)}, bf16[128,7168]{1,0:T(8,128)(2,1)}) fusion(f32[128]{0:T(128)S(1)} %broadcast_multiply_fusion, f32[128]{0:T(128)S(1)} %get-tuple-element.42, f32[7168]{0:T(1024)S(1)} %copy-done.5, bf16[128,7168]{1,0:T(8,128)(2,1)S(1)} %copy-done, f32[128,7168]{1,0:T(8,128)S(1)} %get-tuple-element.45, f32[128]{0:T(128)S(1)} %get-tuple-element.43, ...), kind=kLoop, calls=%fused_computation.132 | loop fusion | flops 9167872 | bytes 9233920 | tf_op jit(solution)/shard_map/reduce_sum | solution.py:438
  92.3 1.2 %collective-permute-done.17 = f32[7168]{0:T(1024)S(1)} collective-permute-done((f32[7168]{0:T(1024)S(1)}, f32[7168]{0:T(1024)S(1)}, u32[]{:S(2)}, u32[]{:S(2)}) %collective-permute-start.17) | collective-permute-done | bytes 28704 | tf_op jit(solution)/shard_map/ppermute | solution.py:249
  93.5 5.0 %collective-permute-start.18 = (f32[7168]{0:T(1024)S(1)}, f32[7168]{0:T(1024)S(1)}, u32[]{:S(2)}, u32[]{:S(2)}) collective-permute-start(f32[7168]{0:T(1024)S(1)} %add.293), channel_id=1, source_target_pairs={{0,8},{8,0},{16,24},{24,16},{1,9},{9,1},{17,25},{25,17},{2,10},{10... | collective-permute-start | bytes 86024 | tf_op jit(solution)/shard_map/ppermute | solution.py:249
  98.5 0.5 gather_fusion
  99.1 1.3 %collective-permute-done.18 = f32[7168]{0:T(1024)S(1)} collective-permute-done((f32[7168]{0:T(1024)S(1)}, f32[7168]{0:T(1024)S(1)}, u32[]{:S(2)}, u32[]{:S(2)}) %collective-permute-start.18) | collective-permute-done | bytes 28704 | tf_op jit(solution)/shard_map/ppermute | solution.py:249
  100.4 2.1 %collective-permute-start.19 = (f32[7168]{0:T(1024)S(1)}, f32[7168]{0:T(1024)S(1)}, u32[]{:S(2)}, u32[]{:S(2)}) collective-permute-start(f32[7168]{0:T(1024)S(1)} %add.294), channel_id=1, source_target_pairs={{0,16},{8,24},{16,0},{24,8},{1,17},{9,25},{17,1},{25,9},{2,18},{10... | collective-permute-start | bytes 86024 | tf_op jit(solution)/shard_map/ppermute | solution.py:249
  102.5 0.7 convolution_bitcast_fusion.3
  103.2 1.1 collective-permute-done.19
  104.3 1.9 %collective-permute-start.20 = (f32[7168]{0:T(1024)S(1)}, f32[7168]{0:T(1024)S(1)}, u32[]{:S(2)}, u32[]{:S(2)}) collective-permute-start(f32[7168]{0:T(1024)S(1)} %add.295), channel_id=1, source_target_pairs={{0,2},{1,3},{2,0},{3,1},{4,6},{5,7},{6,4},{7,5},{8,10},{9,11},{10,... | collective-permute-start | bytes 86024 | tf_op jit(solution)/shard_map/ppermute | solution.py:249
  106.2 0.7 convolution_bitcast_fusion.4
  107.0 1.2 %collective-permute-done.20 = f32[7168]{0:T(1024)S(1)} collective-permute-done((f32[7168]{0:T(1024)S(1)}, f32[7168]{0:T(1024)S(1)}, u32[]{:S(2)}, u32[]{:S(2)}) %collective-permute-start.20) | collective-permute-done | bytes 28704 | tf_op jit(solution)/shard_map/ppermute | solution.py:249
  108.2 3.8 %collective-permute-start.21 = (f32[7168]{0:T(1024)S(1)}, f32[7168]{0:T(1024)S(1)}, u32[]{:S(2)}, u32[]{:S(2)}) collective-permute-start(f32[7168]{0:T(1024)S(1)} %add.296), channel_id=1, source_target_pairs={{0,4},{1,5},{2,6},{3,7},{4,0},{5,1},{6,2},{7,3},{8,12},{9,13},{10,... | collective-permute-start | bytes 86024 | tf_op jit(solution)/shard_map/ppermute | solution.py:249
  112.0 2.4 %fusion.6 = bf16[128,7168]{1,0:T(8,128)(2,1)} fusion(f32[128,7168]{1,0:T(8,128)S(1)} %convolution_bitcast_fusion.3, f32[128,7168]{1,0:T(8,128)S(1)} %convolution_bitcast_fusion.4, bf16[128,7168]{1,0:T(8,128)(2,1)S(1)} %copy-done, f32[7168]{0:T(1024)S(1)} %copy-done.5, f32[4,128,8]{1,2,0:T(8,128)S(1)} %gather_fusion, pred[4]{0:T(512)(128)(4,1)S(1)} %compare_and_fusion.1, ...), kind=kOutput, calls=%fused_computation.14 | convolution fusion | flops 64917504 | bytes 11513860 | tf_op jit(solution)/shard_map/dot_general | solution.py:203
  114.5 0.6 add.297
  (73 shorter events, 1.6 us)
Async XLA Ops:
  0.6 4.8 %copy-start = (bf16[128,7168]{1,0:T(8,128)(2,1)S(1)}, bf16[128,7168]{1,0:T(8,128)(2,1)}, u32[]{:S(2)}) copy-start(bf16[128,7168]{1,0:T(8,128)(2,1)} %param.11) | copy-start | bytes 5505028
  0.6 4.8 %copy-start.5 = (f32[7168]{0:T(1024)S(1)}, f32[7168]{0:T(1024)}, u32[]{:S(2)}) copy-start(f32[7168]{0:T(1024)} %param.12) | copy-start | bytes 86020
  0.7 5.4 %copy-start.6 = (f32[7168]{0:T(1024)S(1)}, f32[7168]{0:T(1024)}, u32[]{:S(2)}) copy-start(f32[7168]{0:T(1024)} %param.13) | copy-start | bytes 86020
  5.0 9.5 %collective-permute-start = (bf16[8,7168]{1,0:T(8,128)(2,1)}, bf16[8,7168]{1,0:T(8,128)(2,1)}, u32[]{:S(2)}, u32[]{:S(2)}) collective-permute-start(bf16[8,7168]{1,0:T(8,128)(2,1)} %get-tuple-element.37), channel_id=1, source_target_pairs={{0,1},{1,2},{2,3},{3,4},{4,5},{5,6},{6,7},{7,0},{8,9},{9,10},{10,1... | collective-permute-start | bytes 344072 | tf_op jit(solution)/shard_map/ppermute | solution.py:361
  6.9 9.8 %collective-permute-start.1 = (bf16[8,7168]{1,0:T(8,128)(2,1)S(1)}, bf16[8,7168]{1,0:T(8,128)(2,1)S(1)}, u32[]{:S(2)}, u32[]{:S(2)}) collective-permute-start(bf16[8,7168]{1,0:T(8,128)(2,1)S(1)} %get-tuple-element.40), channel_id=1, source_target_pairs={{0,2},{1,3},{2,4},{3,5},{4,6},{5,7},{6,0},{7,1},{8,10},{9,11},{10,... | collective-permute-start | bytes 344072 | tf_op jit(solution)/shard_map/ppermute | solution.py:361
  9.5 14.6 %collective-permute-start.2 = (bf16[8,7168]{1,0:T(8,128)(2,1)}, bf16[8,7168]{1,0:T(8,128)(2,1)S(1)}, u32[]{:S(2)}, u32[]{:S(2)}) collective-permute-start(bf16[8,7168]{1,0:T(8,128)(2,1)} %get-tuple-element.36), channel_id=1, source_target_pairs={{0,3},{1,4},{2,5},{3,6},{4,7},{5,0},{6,1},{7,2},{8,11},{9,12},{10,... | collective-permute-start | bytes 344072 | tf_op jit(solution)/shard_map/ppermute | solution.py:361
  12.1 12.2 %collective-permute-start.3 = (bf16[8,7168]{1,0:T(8,128)(2,1)S(1)}, bf16[8,7168]{1,0:T(8,128)(2,1)S(1)}, u32[]{:S(2)}, u32[]{:S(2)}) collective-permute-start(bf16[8,7168]{1,0:T(8,128)(2,1)S(1)} %get-tuple-element.39), channel_id=1, source_target_pairs={{0,4},{1,5},{2,6},{3,7},{4,0},{5,1},{6,2},{7,3},{8,12},{9,13},{10,... | collective-permute-start | bytes 344072 | tf_op jit(solution)/shard_map/ppermute | solution.py:361
  13.3 11.0 %collective-permute-start.4 = (bf16[8,7168]{1,0:T(8,128)(2,1)S(1)}, bf16[8,7168]{1,0:T(8,128)(2,1)S(1)}, u32[]{:S(2)}, u32[]{:S(2)}) collective-permute-start(bf16[8,7168]{1,0:T(8,128)(2,1)S(1)} %get-tuple-element.35), channel_id=1, source_target_pairs={{0,5},{1,6},{2,7},{3,0},{4,1},{5,2},{6,3},{7,4},{8,13},{9,14},{10,... | collective-permute-start | bytes 344072 | tf_op jit(solution)/shard_map/ppermute | solution.py:361
  14.5 9.9 %collective-permute-start.5 = (bf16[8,7168]{1,0:T(8,128)(2,1)S(1)}, bf16[8,7168]{1,0:T(8,128)(2,1)S(1)}, u32[]{:S(2)}, u32[]{:S(2)}) collective-permute-start(bf16[8,7168]{1,0:T(8,128)(2,1)S(1)} %get-tuple-element.38), channel_id=1, source_target_pairs={{0,6},{1,7},{2,0},{3,1},{4,2},{5,3},{6,4},{7,5},{8,14},{9,15},{10,... | collective-permute-start | bytes 344072 | tf_op jit(solution)/shard_map/ppermute | solution.py:361
  16.7 7.7 %collective-permute-start.6 = (bf16[8,7168]{1,0:T(8,128)(2,1)S(1)}, bf16[8,7168]{1,0:T(8,128)(2,1)S(1)}, u32[]{:S(2)}, u32[]{:S(2)}) collective-permute-start(bf16[8,7168]{1,0:T(8,128)(2,1)S(1)} %get-tuple-element.34), channel_id=1, source_target_pairs={{0,7},{1,0},{2,1},{3,2},{4,3},{5,4},{6,5},{7,6},{8,15},{9,8},{10,9... | collective-permute-start | bytes 344072 | tf_op jit(solution)/shard_map/ppermute | solution.py:361
  24.4 4.9 %collective-permute-start.7 = (bf16[8,8,7168]{2,1,0:T(8,128)(2,1)S(1)}, bf16[8,8,7168]{2,1,0:T(8,128)(2,1)}, u32[]{:S(2)}, u32[]{:S(2)}) collective-permute-start(bf16[8,8,7168]{2,1,0:T(8,128)(2,1)S(1)} %bitcast_dynamic-update-slice_fusion), channel_id=1, source_target_pairs={{0,1},{1,0},{2,3},{3,2},{4,5},{5,4},{6,7},{7,6},{8,9},{9,8},{10,11... | collective-permute-start | bytes 2752520 | tf_op jit(solution)/shard_map/ppermute | solution.py:365
  30.8 0.9 copy-start.3
  30.8 1.2 %copy-start.2 = (bf16[8,8,7168]{2,1,0:T(8,128)(2,1)}, bf16[8,8,7168]{2,1,0:T(8,128)(2,1)S(1)}, u32[]{:S(2)}) copy-start(bf16[8,8,7168]{2,1,0:T(8,128)(2,1)S(1)} %slice_dynamic-update-slice_fusion.8) | copy-start | bytes 2752516
  32.0 32.6 %copy-start.8 = (s32[128,8]{0,1:T(8,128)S(1)}, s32[128,8]{0,1:T(8,128)}, u32[]{:S(2)}) copy-start(s32[128,8]{0,1:T(8,128)} %param.15) | copy-start | bytes 12292
  32.0 32.6 %copy-start.7 = (s32[128,8]{0,1:T(8,128)S(1)}, s32[128,8]{0,1:T(8,128)}, u32[]{:S(2)}) copy-start(s32[128,8]{0,1:T(8,128)} %param.14) | copy-start | bytes 12292
  64.3 11.5 %copy-start.4 = (bf16[64,7168]{1,0:T(8,128)(2,1)S(1)}, bf16[64,7168]{1,0:T(8,128)(2,1)}, u32[]{:S(2)}) copy-start(bf16[64,7168]{1,0:T(8,128)(2,1)} %get-tuple-element.6) | copy-start | bytes 2752516
  64.3 2.8 %collective-permute-start.13 = (bf16[64,7168]{1,0:T(8,128)(2,1)}, bf16[64,7168]{1,0:T(8,128)(2,1)}, u32[]{:S(2)}, u32[]{:S(2)}) collective-permute-start(bf16[64,7168]{1,0:T(8,128)(2,1)} %get-tuple-element.7), channel_id=1, source_target_pairs={{0,1},{1,0},{2,3},{3,2},{4,5},{5,4},{6,7},{7,6},{8,9},{9,8},{10,11... | collective-permute-start | bytes 2752520 | tf_op jit(solution)/shard_map/ppermute | solution.py:381
  65.3 10.5 %collective-permute-start.8 = (bf16[64,7168]{1,0:T(8,128)(2,1)}, bf16[64,7168]{1,0:T(8,128)(2,1)S(1)}, u32[]{:S(2)}, u32[]{:S(2)}) collective-permute-start(bf16[64,7168]{1,0:T(8,128)(2,1)} %get-tuple-element.6), channel_id=1, source_target_pairs={{0,1},{1,0},{2,3},{3,2},{4,5},{5,4},{6,7},{7,6},{8,9},{9,8},{10,11... | collective-permute-start | bytes 2752520 | tf_op jit(solution)/shard_map/ppermute | solution.py:387
  68.8 9.9 %collective-permute-start.16 = (bf16[8,7168]{1,0:T(8,128)(2,1)S(1)}, bf16[8,7168]{1,0:T(8,128)(2,1)S(1)}, u32[]{:S(2)}, u32[]{:S(2)}) collective-permute-start(bf16[8,7168]{1,0:T(8,128)(2,1)S(1)} %get-tuple-element.13), channel_id=1, source_target_pairs={{0,6},{1,7},{2,0},{3,1},{4,2},{5,3},{6,4},{7,5},{8,14},{9,15},{10,... | collective-permute-start | bytes 344072 | tf_op jit(solution)/shard_map/ppermute | solution.py:340
  75.1 11.5 %collective-permute-start.15 = (bf16[8,7168]{1,0:T(8,128)(2,1)S(1)}, bf16[8,7168]{1,0:T(8,128)(2,1)S(1)}, u32[]{:S(2)}, u32[]{:S(2)}) collective-permute-start(bf16[8,7168]{1,0:T(8,128)(2,1)S(1)} %get-tuple-element.14), channel_id=1, source_target_pairs={{0,4},{1,5},{2,6},{3,7},{4,0},{5,1},{6,2},{7,3},{8,12},{9,13},{10,... | collective-permute-start | bytes 344072 | tf_op jit(solution)/shard_map/ppermute | solution.py:340
  75.2 11.4 %collective-permute-start.14 = (bf16[8,7168]{1,0:T(8,128)(2,1)S(1)}, bf16[8,7168]{1,0:T(8,128)(2,1)S(1)}, u32[]{:S(2)}, u32[]{:S(2)}) collective-permute-start(bf16[8,7168]{1,0:T(8,128)(2,1)S(1)} %get-tuple-element.15), channel_id=1, source_target_pairs={{0,2},{1,3},{2,4},{3,5},{4,6},{5,7},{6,0},{7,1},{8,10},{9,11},{10,... | collective-permute-start | bytes 344072 | tf_op jit(solution)/shard_map/ppermute | solution.py:340
  76.1 26.4 %collective-permute-start.12 = (bf16[8,7168]{1,0:T(8,128)(2,1)S(1)}, bf16[8,7168]{1,0:T(8,128)(2,1)S(1)}, u32[]{:S(2)}, u32[]{:S(2)}) collective-permute-start(bf16[8,7168]{1,0:T(8,128)(2,1)S(1)} %get-tuple-element.17), channel_id=1, source_target_pairs={{0,7},{1,0},{2,1},{3,2},{4,3},{5,4},{6,5},{7,6},{8,15},{9,8},{10,9... | collective-permute-start | bytes 344072 | tf_op jit(solution)/shard_map/ppermute | solution.py:340
  78.7 23.7 %collective-permute-start.11 = (bf16[8,7168]{1,0:T(8,128)(2,1)S(1)}, bf16[8,7168]{1,0:T(8,128)(2,1)S(1)}, u32[]{:S(2)}, u32[]{:S(2)}) collective-permute-start(bf16[8,7168]{1,0:T(8,128)(2,1)S(1)} %get-tuple-element.18), channel_id=1, source_target_pairs={{0,5},{1,6},{2,7},{3,0},{4,1},{5,2},{6,3},{7,4},{8,13},{9,14},{10,... | collective-permute-start | bytes 344072 | tf_op jit(solution)/shard_map/ppermute | solution.py:340
  78.7 23.7 %collective-permute-start.10 = (bf16[8,7168]{1,0:T(8,128)(2,1)S(1)}, bf16[8,7168]{1,0:T(8,128)(2,1)S(1)}, u32[]{:S(2)}, u32[]{:S(2)}) collective-permute-start(bf16[8,7168]{1,0:T(8,128)(2,1)S(1)} %get-tuple-element.19), channel_id=1, source_target_pairs={{0,3},{1,4},{2,5},{3,6},{4,7},{5,0},{6,1},{7,2},{8,11},{9,12},{10,... | collective-permute-start | bytes 344072 | tf_op jit(solution)/shard_map/ppermute | solution.py:340
  86.7 15.8 %collective-permute-start.9 = (bf16[8,7168]{1,0:T(8,128)(2,1)S(1)}, bf16[8,7168]{1,0:T(8,128)(2,1)S(1)}, u32[]{:S(2)}, u32[]{:S(2)}) collective-permute-start(bf16[8,7168]{1,0:T(8,128)(2,1)S(1)} %get-tuple-element.16), channel_id=1, source_target_pairs={{0,1},{1,2},{2,3},{3,4},{4,5},{5,6},{6,7},{7,0},{8,9},{9,10},{10,1... | collective-permute-start | bytes 344072 | tf_op jit(solution)/shard_map/ppermute | solution.py:340
  88.2 1.5 %copy-start.1 = (bf16[128,7168]{1,0:T(8,128)(2,1)S(1)}, bf16[128,7168]{1,0:T(8,128)(2,1)}, u32[]{:S(2)}) copy-start(bf16[128,7168]{1,0:T(8,128)(2,1)} %param.19) | copy-start | bytes 5505028
  92.3 1.2 %collective-permute-start.17 = (f32[7168]{0:T(1024)S(1)}, f32[7168]{0:T(1024)S(1)}, u32[]{:S(2)}, u32[]{:S(2)}) collective-permute-start(f32[7168]{0:T(1024)S(1)} %get-tuple-element.8), channel_id=1, source_target_pairs={{0,1},{1,0},{2,3},{3,2},{4,5},{5,4},{6,7},{7,6},{8,9},{9,8},{10,11... | collective-permute-start | bytes 86024 | tf_op jit(solution)/shard_map/ppermute | solution.py:249
  93.5 6.9 %collective-permute-start.18 = (f32[7168]{0:T(1024)S(1)}, f32[7168]{0:T(1024)S(1)}, u32[]{:S(2)}, u32[]{:S(2)}) collective-permute-start(f32[7168]{0:T(1024)S(1)} %add.293), channel_id=1, source_target_pairs={{0,8},{8,0},{16,24},{24,16},{1,9},{9,1},{17,25},{25,17},{2,10},{10... | collective-permute-start | bytes 86024 | tf_op jit(solution)/shard_map/ppermute | solution.py:249
  100.4 3.9 %collective-permute-start.19 = (f32[7168]{0:T(1024)S(1)}, f32[7168]{0:T(1024)S(1)}, u32[]{:S(2)}, u32[]{:S(2)}) collective-permute-start(f32[7168]{0:T(1024)S(1)} %add.294), channel_id=1, source_target_pairs={{0,16},{8,24},{16,0},{24,8},{1,17},{9,25},{17,1},{25,9},{2,18},{10... | collective-permute-start | bytes 86024 | tf_op jit(solution)/shard_map/ppermute | solution.py:249
  104.3 3.9 %collective-permute-start.20 = (f32[7168]{0:T(1024)S(1)}, f32[7168]{0:T(1024)S(1)}, u32[]{:S(2)}, u32[]{:S(2)}) collective-permute-start(f32[7168]{0:T(1024)S(1)} %add.295), channel_id=1, source_target_pairs={{0,2},{1,3},{2,0},{3,1},{4,6},{5,7},{6,4},{7,5},{8,10},{9,11},{10,... | collective-permute-start | bytes 86024 | tf_op jit(solution)/shard_map/ppermute | solution.py:249
  108.2 6.3 %collective-permute-start.21 = (f32[7168]{0:T(1024)S(1)}, f32[7168]{0:T(1024)S(1)}, u32[]{:S(2)}, u32[]{:S(2)}) collective-permute-start(f32[7168]{0:T(1024)S(1)} %add.296), channel_id=1, source_target_pairs={{0,4},{1,5},{2,6},{3,7},{4,0},{5,1},{6,2},{7,3},{8,12},{9,13},{10,... | collective-permute-start | bytes 86024 | tf_op jit(solution)/shard_map/ppermute | solution.py:249
